TPU v7x, 256 devices: a whole 4x4x8 slice. The times are simulated.
256 devices in a mesh: expert: 16 (over z, core), tensor: 16 (over y, x).
Axes of the slice: x: 4, y: 4, z: 8, core: 2. Of those that a mesh axis runs over, the one named last changes fastest.
Arguments:
- residual_in: bfloat16 [22528, 1024], P(('expert', 'tensor')), may hold values from -6 to 6
- attn_heads: bfloat16 [1024, 22528], P('tensor', 'expert'), may hold values from -6 to 6
- out_proj: bfloat16 [1024, 1024], P('tensor'), may hold values from -0.1875 to 0.1875
- gain_first: float32 [1024], replicated, may hold values from 0.25 to 1.75
- router_weight: float32 [1024, 16], replicated, may hold values from -0.046875 to 0.046875
- routes: int32 [22528, 2], P(('expert', 'tensor')), may hold values from 0 to 15, all different within a row; in each aligned block of 88 rows (0 to 87, 88 to 175, ...) at most 22 rows name the same one
- w_gate: bfloat16 [16, 2816, 1024], P('expert', 'tensor'), may hold values from -0.1875 to 0.1875
- w_upward: bfloat16 [16, 2816, 1024], P('expert', 'tensor'), may hold values from -0.1875 to 0.1875
- w_downward: bfloat16 [16, 2816, 1024], P('expert', 'tensor'), may hold values from -0.21875 to 0.21875
- gain_second: float32 [1024], replicated, may hold values from 0.25 to 1.75
Outputs:
- residual_out: bfloat16 [22528, 1024], P(('expert', 'tensor'))
- next_normed: bfloat16 [22528, 1024], P(('expert', 'tensor'))
Inputs may be any that keep to these rules, and one draw needn't show every extreme that they name: `routes`: each row names two different experts; among the rows of one device no expert is named more than 22 times, and some expert reaches 22.
All inputs are finite; a program needn't handle non-finite values.
Results may differ from a plain program's by a relative error of at most 0.012.
Values may be sent and summed in bfloat16 or wider, within the bound.
No kernel may reach another device: no remote copies, remote signals or barrier semaphores. Data moves between devices by JAX's collectives and lax.ppermute only.
A program may use at most 128 MiB of HBM per device.

v0:
```python
import jax
import jax.numpy as jnp
from jax import lax
from jax.sharding import PartitionSpec as P


def rms_scale(values, gain):
    wide = values.astype(jnp.float32)
    scale = lax.rsqrt(jnp.mean(wide * wide, axis=-1, keepdims=True) + 1e-06)
    return (wide * scale * gain).astype(jnp.bfloat16)


def expert_block(inputs, gate_rows, up_rows, down_rows):
    gate_part = lax.dot_general(
        inputs, gate_rows, (((1,), (1,)), ((), ())), preferred_element_type=jnp.float32
    )
    up_part = lax.dot_general(
        inputs, up_rows, (((1,), (1,)), ((), ())), preferred_element_type=jnp.float32
    )
    hid = (jax.nn.gelu(gate_part, approximate=True) * up_part).astype(jnp.bfloat16)
    return jnp.dot(hid, down_rows, preferred_element_type=jnp.float32)


def per_device(
    residual_in,
    attn_heads,
    out_proj,
    gain_first,
    router_weight,
    routes,
    w_gate,
    w_upward,
    w_downward,
    gain_second,
):
    row_count = residual_in.shape[0]
    width = residual_in.shape[1]
    n_expert = lax.axis_size("expert")
    capacity = 4 * row_count // n_expert
    block = attn_heads
    projected = lax.psum_scatter(
        lax.dot_general(
            block, out_proj, (((0,), (0,)), ((), ())), preferred_element_type=jnp.float32
        ),
        "tensor",
        scatter_dimension=0,
        tiled=True,
    )
    hidden_one = (residual_in.astype(jnp.float32) + projected).astype(jnp.bfloat16)
    normed = rms_scale(hidden_one, gain_first)
    logits = jnp.dot(normed.astype(jnp.float32), router_weight, precision=lax.Precision.HIGHEST)
    router_probs = jax.nn.softmax(logits, axis=-1)
    picked = jnp.take_along_axis(router_probs, routes, axis=1)
    gate_weights = picked / jnp.sum(picked, axis=1, keepdims=True)
    flat_ids = routes.reshape(-1)
    expert_iota = jnp.arange(n_expert, dtype=jnp.int32)
    onehot = (flat_ids[:, None] == expert_iota[None, :]).astype(jnp.int32)
    earlier = jnp.cumsum(onehot, axis=0) - onehot
    slot_index = jnp.sum(earlier * onehot, axis=1)
    target = flat_ids * capacity + slot_index
    slot_iota = jnp.arange(n_expert * capacity, dtype=jnp.int32)
    placing = (slot_iota[:, None] == target[None, :]).astype(jnp.bfloat16)
    repeated = jnp.repeat(normed, 2, axis=0)
    send_slots = jnp.dot(placing, repeated, preferred_element_type=jnp.float32).astype(jnp.bfloat16)
    send_slots = send_slots.reshape(n_expert, capacity, width)
    received = lax.all_to_all(send_slots, "expert", split_axis=0, concat_axis=0, tiled=True)
    slot_total = n_expert * capacity
    rows_in = received.reshape(slot_total, width)
    gate_rows = w_gate[0]
    up_rows = w_upward[0]
    down_rows = w_downward[0]
    all_rows = lax.all_gather(rows_in, "tensor", axis=0, tiled=True)
    block = all_rows
    expert_sum = lax.psum_scatter(
        expert_block(block, gate_rows, up_rows, down_rows).astype(jnp.bfloat16),
        "tensor",
        scatter_dimension=0,
        tiled=True,
    )
    expert_out = expert_sum.reshape(n_expert, capacity, width)
    returned = lax.all_to_all(expert_out, "expert", split_axis=0, concat_axis=0, tiled=True)
    returned = returned.reshape(slot_total, width)
    per_route = lax.dot_general(
        placing, returned, (((0,), (0,)), ((), ())), preferred_element_type=jnp.float32
    )
    per_route = per_route.reshape(row_count, 2, width)
    mixed = jnp.sum(gate_weights[:, :, None] * per_route, axis=1)
    residual_out = (hidden_one.astype(jnp.float32) + mixed).astype(jnp.bfloat16)
    next_normed = rms_scale(residual_out, gain_second)
    return (residual_out, next_normed)


def solution(mesh):
    placed = (
        P(("expert", "tensor"), None),
        P("tensor", "expert"),
        P("tensor", None),
        P(),
        P(),
        P(("expert", "tensor"), None),
        P("expert", "tensor", None),
        P("expert", "tensor", None),
        P("expert", "tensor", None),
        P(),
    )
    return jax.shard_map(
        per_device,
        mesh=mesh,
        in_specs=placed,
        out_specs=(P(("expert", "tensor"), None), P(("expert", "tensor"), None)),
        check_vma=False,
    )
```

profile of v0, /device:TPU:1, one launch (start us, length us, event | category | flops | bytes accessed | tf_op | source)
XLA Modules:
  0.0 380.7 jit_solution(14872669456772548435)
XLA Ops:
  7.2 0.0 copy-start
  7.2 0.0 reduce-scatter.7.cloned.1.call-start
  7.2 4.4 %fusion.38 = f32[1408,1024]{1,0:T(8,128)} fusion(bf16[64,1408]{1,0:T(8,128)(2,1)} %param.11, bf16[64,1024]{1,0:T(8,128)(2,1)} %param.12), kind=kOutput, calls=%fused_computation.66 | convolution fusion | flops 184549376 | bytes 6078464 | tf_op jit(solution)/shard_map/dot_general | solution.py:42
  11.7 0.0 copy-start.5
  11.7 0.0 copy-start.3
  11.7 0.0 copy-start.6
  11.7 0.0 reduce-scatter.7.cloned.1.call-update
  11.7 0.0 all-gather.2.cloned.1.call-start
  11.7 0.6 copy-done.5
  12.3 0.1 copy.34
  12.4 0.1 reshape.109
  12.6 0.6 reduce-window.6
  13.2 0.2 slice_reduce_fusion
  13.4 0.1 bitcast_bitcast_fusion
  13.5 86.2 %reduce-scatter.7.cloned.1.call-done = f32[88,1024]{1,0:T(8,128)} async-done(((f32[1408,1024]{1,0:T(8,128)}), f32[88,1024]{1,0:T(8,128)}) %reduce-scatter.7.cloned.1.call-update) | async-done | bytes 360464
  99.7 0.0 copy-done.3
  99.7 1.1 fusion.16
  100.9 0.0 copy-done.6
  100.9 0.0 copy-start.2
  100.9 0.1 fusion.18
  101.0 0.2 broadcast_in_dim.7
  101.2 0.1 reshape.112
  101.4 0.3 convolution_convert_fusion.1
  101.7 0.2 reshape.113
  101.9 32.1 %all_to_all.10 = bf16[16,22,1024]{2,1,0:T(8,128)(2,1)S(1)} all-to-all(bf16[16,22,1024]{2,1,0:T(8,128)(2,1)S(1)} %reshape.113), channel_id=1, replica_groups=mesh['expert'=16,'tensor'=16] {'expert'}, dimensions={0} | all-to-all | bytes 1441792 | tf_op jit(solution)/shard_map/all_to_all | solution.py:66
  134.1 1.1 reshape.114
  135.1 0.0 all-gather.2.cloned.1.call-update
  135.1 0.0 copy-start.8
  135.2 0.0 reduce-scatter.5.cloned.1.call-start
  135.2 84.5 %all-gather.2.cloned.1.call-done = bf16[5632,1024]{1,0:T(8,128)(2,1)} async-done(((bf16[352,1024]{1,0:T(8,128)(2,1)}), bf16[5632,1024]{1,0:T(8,128)(2,1)}) %all-gather.2.cloned.1.call-update) | async-done | bytes 11534352 | tf_op jit(solution)/shard_map/all_gather | solution.py:72
  219.7 0.0 copy-done.2
  219.7 10.2 %fusion.23 = f32[5632,176]{0,1:T(8,128)} fusion(bf16[5632,1024]{1,0:T(8,128)(2,1)} %all-gather.2.cloned.1.call-done, bf16[1,176,1024]{2,1,0:T(8,128)(2,1)S(1)} %copy-done.2), kind=kOutput, calls=%fused_computation.33 | convolution fusion | flops 2030043136 | bytes 15859712 | tf_op jit(solution)/shard_map/dot_general | solution.py:14
  229.9 0.0 copy-done
  229.9 0.0 copy-done.8
  229.9 13.1 %convolution_convert_fusion = bf16[5632,1024]{1,0:T(8,128)(2,1)} fusion(bf16[5632,1024]{1,0:T(8,128)(2,1)} %all-gather.2.cloned.1.call-done, f32[5632,176]{0,1:T(8,128)} %fusion.23, bf16[1,176,1024]{2,1,0:T(8,128)(2,1)S(1)} %copy-done, bf16[1,176,1024]{2,1,0:T(8,128)(2,1)S(1)} %copy-done.8), kind=kOutput, calls=%fused_computation.1 | convolution fusion | flops 4075765760 | bytes 27754496 | tf_op jit(solution)/shard_map/dot_general | solution.py:21
  243.0 0.0 copy-start.4
  243.0 0.0 reduce-scatter.5.cloned.1.call-update
  243.0 96.4 %reduce-scatter.5.cloned.1.call-done = bf16[352,1024]{1,0:T(8,128)(2,1)} async-done(((bf16[5632,1024]{1,0:T(8,128)(2,1)}), bf16[352,1024]{1,0:T(8,128)(2,1)}) %reduce-scatter.5.cloned.1.call-update) | async-done | bytes 720912 | tf_op jit(solution)/shard_map/reduce_scatter | solution.py:74
  339.5 2.1 reshape.115
  341.6 8.3 %all-to-all-start.1 = ((bf16[16,22,1024]{2,1,0:T(8,128)(2,1)}), bf16[16,22,1024]{2,1,0:T(8,128)(2,1)S(1)}, u32[]{:S(2)}, u32[]{:S(2)}) async-start(bf16[16,22,1024]{2,1,0:T(8,128)(2,1)} %reshape.115), calls=%async_computation.2 | async-start | bytes 1572864 | tf_op jit(solution)/shard_map/all_to_all | solution.py:81
  349.9 0.1 copy.32
  350.0 0.1 reshape.118
  350.1 0.1 iota_compare_fusion.2
  350.3 0.1 eq.57
  350.4 0.0 copy-done.4
  350.4 0.3 fusion.37
  350.7 0.0 copy-start.7
  350.7 2.3 gather_fusion
  353.0 0.1 reshape.121
  353.1 0.1 copy.33
  353.2 19.4 %all-to-all-done.1 = bf16[16,22,1024]{2,1,0:T(8,128)(2,1)S(1)} async-done(((bf16[16,22,1024]{2,1,0:T(8,128)(2,1)}), bf16[16,22,1024]{2,1,0:T(8,128)(2,1)S(1)}, u32[]{:S(2)}, u32[]{:S(2)}) %all-to-all-start.1) | async-done | bytes 720928 | tf_op jit(solution)/shard_map/all_to_all | solution.py:81
  372.6 0.2 reshape.129
  372.8 0.4 fusion.12
  373.2 0.2 fusion.13
  373.3 0.0 copy-start.1
  373.4 0.0 copy-done.7
  373.4 0.8 fusion.15
  374.1 0.0 copy-done.1
  (13 shorter events, 0.2 us)
Async XLA Ops:
  7.2 222.7 %copy-start = (bf16[1,176,1024]{2,1,0:T(8,128)(2,1)S(1)}, bf16[1,176,1024]{2,1,0:T(8,128)(2,1)}, u32[]{:S(2)}) copy-start(bf16[1,176,1024]{2,1,0:T(8,128)(2,1)} %param.18) | copy-start | bytes 1081348
  7.2 92.5 %reduce-scatter.7.cloned.1.call-start = ((), (), s32[]{:S(2)}) async-start(), calls=%async_computation.6 | async-start | bytes 6127616
  11.7 0.7 copy-start.5
  11.7 88.1 %copy-start.3 = (bf16[88,1024]{1,0:T(8,128)(2,1)S(1)}, bf16[88,1024]{1,0:T(8,128)(2,1)}, u32[]{:S(2)}) copy-start(bf16[88,1024]{1,0:T(8,128)(2,1)} %param.10) | copy-start | bytes 540676
  11.7 89.2 %copy-start.6 = (f32[1024]{0:T(1024)S(1)}, f32[1024]{0:T(1024)}, u32[]{:S(2)}) copy-start(f32[1024]{0:T(1024)} %param.13) | copy-start | bytes 12292
  11.7 208.0 %all-gather.2.cloned.1.call-start = ((), (), s32[]{:S(2)}) async-start(), calls=%async_computation.4 | async-start | bytes 12255232 | tf_op jit(solution)/shard_map/all_gather | solution.py:72
  100.9 118.8 %copy-start.2 = (bf16[1,176,1024]{2,1,0:T(8,128)(2,1)S(1)}, bf16[1,176,1024]{2,1,0:T(8,128)(2,1)}, u32[]{:S(2)}) copy-start(bf16[1,176,1024]{2,1,0:T(8,128)(2,1)} %param.16) | copy-start | bytes 1081348
  135.1 94.8 %copy-start.8 = (bf16[1,176,1024]{2,1,0:T(8,128)(2,1)S(1)}, bf16[1,176,1024]{2,1,0:T(8,128)(2,1)}, u32[]{:S(2)}) copy-start(bf16[1,176,1024]{2,1,0:T(8,128)(2,1)} %param.17) | copy-start | bytes 1081348
  135.2 204.3 %reduce-scatter.5.cloned.1.call-start = ((), (), s32[]{:S(2)}) async-start(), calls=%async_computation.5 | async-start | bytes 12255232 | tf_op jit(solution)/shard_map/reduce_scatter | solution.py:74
  243.0 107.4 %copy-start.4 = (f32[1024,16]{0,1:T(8,128)S(1)}, f32[1024,16]{0,1:T(8,128)}, u32[]{:S(2)}) copy-start(f32[1024,16]{0,1:T(8,128)} %param.14) | copy-start | bytes 196612
  341.6 31.1 %all-to-all-start.1 = ((bf16[16,22,1024]{2,1,0:T(8,128)(2,1)}), bf16[16,22,1024]{2,1,0:T(8,128)(2,1)S(1)}, u32[]{:S(2)}, u32[]{:S(2)}) async-start(bf16[16,22,1024]{2,1,0:T(8,128)(2,1)} %reshape.115), calls=%async_computation.2 | async-start | bytes 1572864 | tf_op jit(solution)/shard_map/all_to_all | solution.py:81
  350.7 22.7 %copy-start.7 = (f32[1024]{0:T(1024)S(1)}, f32[1024]{0:T(1024)}, u32[]{:S(2)}) copy-start(f32[1024]{0:T(1024)} %param.19) | copy-start | bytes 12292
  373.3 0.8 copy-start.1
Sparse Core Ops, SparseCore 0:
  11.8 87.8 reduce-scatter.6
  135.3 84.3 all-gather.1
  243.2 96.2 reduce-scatter.4
where the time goes:
time: 381 us
  waiting for transfers between devices  287 us (75%)
  blocking collectives  32.1 us (8%)
  matrix products  28.7 us (8%)
  between operations  14 us (4%)
  starting transfers between devices  8.46 us (2%)
  local copies, waits for them, and re-layouts  7.73 us (2%)
    reduce_scatter x1, waiting for transfers between devices, per_device(): lax.psum_scatter(expert_block(block, gate_rows, up_rows, down_rows).astyp...  96.4 us
    unnamed x4, waiting for transfers between devices  86.2 us
    all_gather x1, waiting for transfers between devices, per_device(): all_rows = lax.all_gather(rows_in, 'tensor', axis=0, tiled=True)  84.5 us
    all_to_all x1, blocking collectives, per_device(): lax.all_to_all(send_slots, 'expert', split_axis=0, concat_axis=0, tiled=T...  32.1 us
    all_to_all x1, waiting for transfers between devices, per_device(): lax.all_to_all(expert_out, 'expert', split_axis=0, concat_axis=0, tiled=T...  19.4 us
    dot_general x1, matrix products, expert_block(): return jnp.dot(hid, down_rows, preferred_element_type=jnp.float32)  13.1 us
    dot_general x1, matrix products, expert_block(): lax.dot_general(inputs, gate_rows, (((1,), (1,)), ((), ())), preferred_el...  10.2 us
    all_to_all x1, starting transfers between devices, per_device(): lax.all_to_all(expert_out, 'expert', split_axis=0, concat_axis=0, tiled=T...  8.33 us
  transfers between devices with their start and end apart: 4, of which 4 were waited for; matrix products, arithmetic and copies ran while one was open for 1% of the time, Pallas kernels for 0%

commit v1 on v0

--- a/solution.py
+++ b/solution.py
@@ -1,7 +1,13 @@
+import math
+
 import jax
 import jax.numpy as jnp
 from jax import lax
+from jax.sharding import Mesh
 from jax.sharding import PartitionSpec as P
+
+ROWS_AXES = ("expert", "ty", "tx")
+TENSOR_AXES = ("ty", "tx")
 
 
 def rms_scale(values, gain):
@@ -37,15 +43,17 @@
     width = residual_in.shape[1]
     n_expert = lax.axis_size("expert")
     capacity = 4 * row_count // n_expert
-    block = attn_heads
-    projected = lax.psum_scatter(
-        lax.dot_general(
-            block, out_proj, (((0,), (0,)), ((), ())), preferred_element_type=jnp.float32
-        ),
-        "tensor",
-        scatter_dimension=0,
-        tiled=True,
+
+    full_proj = lax.all_gather(out_proj, TENSOR_AXES, axis=0, tiled=True)
+    own_heads = lax.all_to_all(attn_heads, TENSOR_AXES, 1, 0, tiled=True)
+    projected = lax.dot_general(
+        own_heads, full_proj, (((0,), (0,)), ((), ())), preferred_element_type=jnp.float32
     )
+
+    stacked = jnp.concatenate([w_gate, w_upward, w_downward], axis=0)
+    weights = lax.all_gather(stacked, "tx", axis=1, tiled=True)
+    gate_rows, up_rows, down_rows = weights[0], weights[1], weights[2]
+
     hidden_one = (residual_in.astype(jnp.float32) + projected).astype(jnp.bfloat16)
     normed = rms_scale(hidden_one, gain_first)
     logits = jnp.dot(normed.astype(jnp.float32), router_weight, precision=lax.Precision.HIGHEST)
@@ -66,14 +74,10 @@
     received = lax.all_to_all(send_slots, "expert", split_axis=0, concat_axis=0, tiled=True)
     slot_total = n_expert * capacity
     rows_in = received.reshape(slot_total, width)
-    gate_rows = w_gate[0]
-    up_rows = w_upward[0]
-    down_rows = w_downward[0]
-    all_rows = lax.all_gather(rows_in, "tensor", axis=0, tiled=True)
-    block = all_rows
+    all_rows = lax.all_gather(rows_in, "ty", axis=0, tiled=True)
     expert_sum = lax.psum_scatter(
-        expert_block(block, gate_rows, up_rows, down_rows).astype(jnp.bfloat16),
-        "tensor",
+        expert_block(all_rows, gate_rows, up_rows, down_rows).astype(jnp.bfloat16),
+        "ty",
         scatter_dimension=0,
         tiled=True,
     )
@@ -90,23 +94,34 @@
     return (residual_out, next_normed)
 
 
+def split_tensor(n):
+    inner = int(math.isqrt(n))
+    while n % inner:
+        inner -= 1
+    return n // inner, inner
+
+
 def solution(mesh):
+    n_expert = mesh.shape["expert"]
+    n_ty, n_tx = split_tensor(mesh.shape["tensor"])
+    grid = Mesh(mesh.devices.reshape(n_expert, n_ty, n_tx), ROWS_AXES)
+    rows = P(ROWS_AXES, None)
     placed = (
-        P(("expert", "tensor"), None),
-        P("tensor", "expert"),
-        P("tensor", None),
+        rows,
+        P(TENSOR_AXES, "expert"),
+        P(TENSOR_AXES, None),
         P(),
         P(),
-        P(("expert", "tensor"), None),
-        P("expert", "tensor", None),
-        P("expert", "tensor", None),
-        P("expert", "tensor", None),
+        rows,
+        P("expert", TENSOR_AXES, None),
+        P("expert", TENSOR_AXES, None),
+        P("expert", TENSOR_AXES, None),
         P(),
     )
     return jax.shard_map(
         per_device,
-        mesh=mesh,
+        mesh=grid,
         in_specs=placed,
-        out_specs=(P(("expert", "tensor"), None), P(("expert", "tensor"), None)),
+        out_specs=(rows, rows),
         check_vma=False,
     )

time: 381 us -> 256 us (0.67)
  waiting for transfers between devices: 287 us -> 162 us
  matrix products: 28.7 us -> 19.4 us
  starting transfers between devices: 8.46 us -> 15.5 us
    unnamed x4, waiting for transfers between devices: 86.2 us -> 0.73 us
    reduce_scatter x1, waiting for transfers between devices: 96.4 us -> 39.1 us  [per_device(): lax.psum_scatter(expert_block(all_rows, gate_rows, up_rows, down_rows).as...]
    all_gather x1 -> x3, waiting for transfers between devices: 84.5 us -> 96.2 us  [the longest x1 42.1 us: per_device(): all_rows = lax.all_gather(rows_in, 'ty', axis=0, tiled=True)]
    all_to_all x0 -> x1, starting transfers between devices: none -> 7.57 us  [per_device(): own_heads = lax.all_to_all(attn_heads, TENSOR_AXES, 1, 0, tiled=True)]
    all_to_all x0 -> x1, waiting for transfers between devices: none -> 6.28 us  [per_device(): own_heads = lax.all_to_all(attn_heads, TENSOR_AXES, 1, 0, tiled=True)]
  transfers between devices with their start and end apart: 4 -> 6, of which waited for: 4 -> 6; matrix products, arithmetic and copies ran while one was open for 1% -> 5% of each run, Pallas kernels for 0% -> 0%
where the time goes in v1:
time: 256 us; the launch traced here: 255 us
  waiting for transfers between devices  162 us (63%)
  blocking collectives  31.9 us (12%)
  matrix products  19.4 us (8%)
  starting transfers between devices  15.5 us (6%)
  between operations  14 us (5%)
  local copies, waits for them, and re-layouts  8.4 us (3%)
  other arithmetic  4.3 us (2%)
    all_gather x1, waiting for transfers between devices, per_device(): all_rows = lax.all_gather(rows_in, 'ty', axis=0, tiled=True)  42.1 us
    reduce_scatter x1, waiting for transfers between devices, per_device(): lax.psum_scatter(expert_block(all_rows, gate_rows, up_rows, down_rows).as...  39.1 us
    all_gather x1, waiting for transfers between devices, per_device(): full_proj = lax.all_gather(out_proj, TENSOR_AXES, axis=0, tiled=True)  35.9 us
    all_to_all x1, blocking collectives, per_device(): lax.all_to_all(send_slots, 'expert', split_axis=0, concat_axis=0, tiled=T...  31.9 us
    all_to_all x1, waiting for transfers between devices, per_device(): lax.all_to_all(expert_out, 'expert', split_axis=0, concat_axis=0, tiled=T...  19.4 us
    all_gather x1, waiting for transfers between devices, per_device(): weights = lax.all_gather(stacked, 'tx', axis=1, tiled=True)  18.2 us
    dot_general x1, matrix products, expert_block(): return jnp.dot(hid, down_rows, preferred_element_type=jnp.float32)  9.54 us
    all_to_all x1, starting transfers between devices, per_device(): lax.all_to_all(expert_out, 'expert', split_axis=0, concat_axis=0, tiled=T...  7.76 us
  transfers between devices with their start and end apart: 6, of which 6 were waited for; matrix products, arithmetic and copies ran while one was open for 5% of the time, Pallas kernels for 0%

profile of v1, /device:TPU:1, one launch (start us, length us, event | category | flops | bytes accessed | tf_op | source)
XLA Modules:
  0.0 255.2 jit_solution(3978086841994874409)
XLA Ops:
  7.2 0.0 copy-start
  7.2 0.0 copy-start.2
  7.2 0.0 copy-start.4
  7.2 0.0 copy-start.3
  7.2 0.0 all-gather.4.cloned.1.call-start
  7.3 0.7 all-gather.4.cloned.1.call-update
  7.9 0.0 all-gather.8.cloned.1.call-start
  8.0 2.3 pad_maximum_fusion
  10.3 0.0 copy-start.5
  10.3 0.0 all-gather.8.cloned.1.call-update
  10.3 0.0 copy-done.2
  10.3 0.5 all_to_all.20
  10.8 0.8 copy.23
  11.6 7.6 %all-to-all-start = ((bf16[64,16,88]{2,0,1:T(8,128)(2,1)}), bf16[64,16,88]{2,0,1:T(8,128)(2,1)S(1)}, u32[]{:S(2)}, u32[]{:S(2)}) async-start(bf16[64,16,88]{2,0,1:T(8,128)(2,1)} %copy.23), calls=%async_computation | async-start | bytes 524288 | tf_op jit(solution)/shard_map/all_to_all | solution.py:48
  19.2 0.0 all-gather.6.cloned.1.call-start
  19.2 0.0 copy-done.4
  19.3 0.1 copy.26
  19.4 0.1 reshape.112
  19.5 0.6 reduce-window.6
  20.1 0.2 slice_reduce_fusion
  20.3 0.1 bitcast_bitcast_fusion
  20.5 6.3 %all-to-all-done = bf16[64,16,88]{2,0,1:T(8,128)(2,1)S(1)} async-done(((bf16[64,16,88]{2,0,1:T(8,128)(2,1)}), bf16[64,16,88]{2,0,1:T(8,128)(2,1)S(1)}, u32[]{:S(2)}, u32[]{:S(2)}) %all-to-all-start) | async-done | bytes 180256 | tf_op jit(solution)/shard_map/all_to_all | solution.py:48
  26.7 35.9 %all-gather.4.cloned.1.call-done = bf16[1024,1024]{1,0:T(8,128)(2,1)} async-done(((bf16[64,1024]{1,0:T(8,128)(2,1)}), bf16[1024,1024]{1,0:T(8,128)(2,1)}) %all-gather.4.cloned.1.call-update) | async-done | bytes 2097168 | tf_op jit(solution)/shard_map/all_gather | solution.py:47
  62.6 0.0 copy-done.3
  62.6 2.2 multiply_reduce_fusion
  64.8 0.0 copy-done.5
  64.8 0.1 multiply_convert_fusion
  65.0 0.2 broadcast_in_dim.7
  65.1 0.1 reshape.115
  65.3 0.3 convolution_convert_fusion.1
  65.6 0.2 reshape.116
  65.9 31.9 %all_to_all.29 = bf16[16,22,1024]{2,1,0:T(8,128)(2,1)S(1)} all-to-all(bf16[16,22,1024]{2,1,0:T(8,128)(2,1)S(1)} %reshape.116), channel_id=1, replica_groups=mesh['expert'=16,'ty'=4,'tx'=4] {'expert'}, dimensions={0} | all-to-all | bytes 1441792 | tf_op jit(solution)/shard_map/all_to_all | solution.py:74
  97.7 1.1 reshape.117
  98.8 0.0 all-gather.6.cloned.1.call-update
  98.8 0.0 reduce-scatter.2.cloned.1.call-start
  98.9 18.2 %all-gather.8.cloned.1.call-done = bf16[3,704,1024]{2,1,0:T(8,128)(2,1)} async-done(((bf16[3,176,1024]{2,1,0:T(8,128)(2,1)}), bf16[3,704,1024]{2,1,0:T(8,128)(2,1)}) %all-gather.8.cloned.1.call-update) | async-done | bytes 4325392 | tf_op jit(solution)/shard_map/all_gather | solution.py:54
  117.1 42.1 %all-gather.6.cloned.1.call-done = bf16[1408,1024]{1,0:T(8,128)(2,1)} async-done(((bf16[352,1024]{1,0:T(8,128)(2,1)}), bf16[1408,1024]{1,0:T(8,128)(2,1)}) %all-gather.6.cloned.1.call-update) | async-done | bytes 2883600 | tf_op jit(solution)/shard_map/all_gather | solution.py:77
  159.2 0.0 copy-start.7
  159.2 6.7 %fusion.9 = f32[1408,704]{0,1:T(8,128)} fusion(bf16[1408,1024]{1,0:T(8,128)(2,1)} %all-gather.6.cloned.1.call-done, bf16[3,704,1024]{2,1,0:T(8,128)(2,1)} %all-gather.8.cloned.1.call-done), kind=kOutput, calls=%fused_computation.15 | convolution fusion | flops 2030043136 | bytes 8290304 | tf_op jit(solution)/shard_map/dot_general | solution.py:20
  165.9 0.0 copy-done.7
  165.9 9.5 %convolution_convert_fusion = bf16[1408,1024]{1,0:T(8,128)(2,1)} fusion(bf16[3,704,1024]{2,1,0:T(8,128)(2,1)} %all-gather.8.cloned.1.call-done, f32[1408,704]{0,1:T(8,128)} %fusion.9, bf16[1408,1024]{1,0:T(8,128)(2,1)S(1)} %copy-done.7), kind=kOutput, calls=%fused_computation.11 | convolution fusion | flops 4071440384 | bytes 12615680 | tf_op jit(solution)/shard_map/dot_general | solution.py:27
  175.5 0.0 reduce-scatter.2.cloned.1.call-update
  175.5 39.1 %reduce-scatter.2.cloned.1.call-done = bf16[352,1024]{1,0:T(8,128)(2,1)} async-done(((bf16[1408,1024]{1,0:T(8,128)(2,1)}), bf16[352,1024]{1,0:T(8,128)(2,1)}) %reduce-scatter.2.cloned.1.call-update) | async-done | bytes 720912 | tf_op jit(solution)/shard_map/reduce_scatter | solution.py:78
  214.6 2.1 reshape.118
  216.7 7.8 %all-to-all-start.2 = ((bf16[16,22,1024]{2,1,0:T(8,128)(2,1)}), bf16[16,22,1024]{2,1,0:T(8,128)(2,1)S(1)}, u32[]{:S(2)}, u32[]{:S(2)}) async-start(bf16[16,22,1024]{2,1,0:T(8,128)(2,1)} %reshape.118), calls=%async_computation.3 | async-start | bytes 1572864 | tf_op jit(solution)/shard_map/all_to_all | solution.py:85
  224.5 0.1 copy.24
  224.6 0.1 reshape.121
  224.7 0.1 iota_compare_fusion.2
  224.8 0.1 eq.57
  224.9 0.0 copy-done
  224.9 0.3 fusion.27
  225.2 2.3 gather_fusion
  227.5 0.0 copy-start.6
  227.5 0.1 reshape.124
  227.7 0.1 copy.25
  227.8 19.4 %all-to-all-done.2 = bf16[16,22,1024]{2,1,0:T(8,128)(2,1)S(1)} async-done(((bf16[16,22,1024]{2,1,0:T(8,128)(2,1)}), bf16[16,22,1024]{2,1,0:T(8,128)(2,1)S(1)}, u32[]{:S(2)}, u32[]{:S(2)}) %all-to-all-start.2) | async-done | bytes 720928 | tf_op jit(solution)/shard_map/all_to_all | solution.py:85
  247.2 0.2 reshape.132
  247.4 0.4 fusion.10
  247.7 0.2 fusion.13
  247.9 0.0 copy-start.1
  247.9 0.0 copy-done.6
  247.9 0.8 fusion.15
  248.7 0.0 copy-done.1
  (13 shorter events, 0.2 us)
Async XLA Ops:
  7.2 217.7 %copy-start = (f32[1024,16]{0,1:T(8,128)S(1)}, f32[1024,16]{0,1:T(8,128)}, u32[]{:S(2)}) copy-start(f32[1024,16]{0,1:T(8,128)} %param.14) | copy-start | bytes 196612
  7.2 3.2 %copy-start.2 = (bf16[64,1408]{1,0:T(8,128)(2,1)S(1)}, bf16[64,1408]{1,0:T(8,128)(2,1)}, u32[]{:S(2)}) copy-start(bf16[64,1408]{1,0:T(8,128)(2,1)} %param.11) | copy-start | bytes 540676
  7.2 12.1 %copy-start.4 = (s32[88,2]{0,1:T(2,128)S(1)}, s32[88,2]{0,1:T(2,128)}, u32[]{:S(2)}) copy-start(s32[88,2]{0,1:T(2,128)} %param.15) | copy-start | bytes 2116
  7.2 55.4 %copy-start.3 = (bf16[88,1024]{1,0:T(8,128)(2,1)S(1)}, bf16[88,1024]{1,0:T(8,128)(2,1)}, u32[]{:S(2)}) copy-start(bf16[88,1024]{1,0:T(8,128)(2,1)} %param.10) | copy-start | bytes 540676
  7.2 55.4 %all-gather.4.cloned.1.call-start = ((), (), s32[]{:S(2)}) async-start(), calls=%async_computation.4 | async-start | bytes 2228224 | tf_op jit(solution)/shard_map/all_gather | solution.py:47
  7.9 109.1 %all-gather.8.cloned.1.call-start = ((), (), s32[]{:S(2)}) async-start(), calls=%async_computation.6 | async-start | bytes 5406720 | tf_op jit(solution)/shard_map/all_gather | solution.py:54
  10.3 54.5 %copy-start.5 = (f32[1024]{0:T(1024)S(1)}, f32[1024]{0:T(1024)}, u32[]{:S(2)}) copy-start(f32[1024]{0:T(1024)} %param.13) | copy-start | bytes 12292
  11.6 15.1 %all-to-all-start = ((bf16[64,16,88]{2,0,1:T(8,128)(2,1)}), bf16[64,16,88]{2,0,1:T(8,128)(2,1)S(1)}, u32[]{:S(2)}, u32[]{:S(2)}) async-start(bf16[64,16,88]{2,0,1:T(8,128)(2,1)} %copy.23), calls=%async_computation | async-start | bytes 524288 | tf_op jit(solution)/shard_map/all_to_all | solution.py:48
  19.2 140.0 %all-gather.6.cloned.1.call-start = ((), (), s32[]{:S(2)}) async-start(), calls=%async_computation.5 | async-start | bytes 3604480 | tf_op jit(solution)/shard_map/all_gather | solution.py:77
  98.8 115.8 %reduce-scatter.2.cloned.1.call-start = ((), (), s32[]{:S(2)}) async-start(), calls=%async_computation.7 | async-start | bytes 3604480 | tf_op jit(solution)/shard_map/reduce_scatter | solution.py:78
  159.2 6.7 %copy-start.7 = (bf16[1408,1024]{1,0:T(8,128)(2,1)S(1)}, bf16[1408,1024]{1,0:T(8,128)(2,1)}, u32[]{:S(2)}) copy-start(bf16[1408,1024]{1,0:T(8,128)(2,1)} %all-gather.6.cloned.1.call-done) | copy-start | bytes 8650756
  216.7 30.5 %all-to-all-start.2 = ((bf16[16,22,1024]{2,1,0:T(8,128)(2,1)}), bf16[16,22,1024]{2,1,0:T(8,128)(2,1)S(1)}, u32[]{:S(2)}, u32[]{:S(2)}) async-start(bf16[16,22,1024]{2,1,0:T(8,128)(2,1)} %reshape.118), calls=%async_computation.3 | async-start | bytes 1572864 | tf_op jit(solution)/shard_map/all_to_all | solution.py:85
  227.5 20.4 %copy-start.6 = (f32[1024]{0:T(1024)S(1)}, f32[1024]{0:T(1024)}, u32[]{:S(2)}) copy-start(f32[1024]{0:T(1024)} %param.19) | copy-start | bytes 12292
  247.9 0.8 copy-start.1
Sparse Core Ops, SparseCore 0:
  10.4 52.1 all-gather.3
  64.4 52.6 all-gather.7
  118.9 40.2 all-gather.5
  175.6 38.9 reduce-scatter.1

commit v2 on v1

--- a/solution.py
+++ b/solution.py
@@ -44,15 +44,26 @@
     n_expert = lax.axis_size("expert")
     capacity = 4 * row_count // n_expert
 
-    full_proj = lax.all_gather(out_proj, TENSOR_AXES, axis=0, tiled=True)
+    core = lax.axis_index("expert") % 2
+    half = width // 2
+    my_cols = lax.dynamic_slice_in_dim(out_proj, core * half, half, axis=1)
+    my_half = lax.all_gather(my_cols, TENSOR_AXES, axis=0, tiled=True)
+    other_half = lax.ppermute(my_half, "expert", [(i, i ^ 1) for i in range(n_expert)])
     own_heads = lax.all_to_all(attn_heads, TENSOR_AXES, 1, 0, tiled=True)
-    projected = lax.dot_general(
-        own_heads, full_proj, (((0,), (0,)), ((), ())), preferred_element_type=jnp.float32
+    contract = (((0,), (0,)), ((), ()))
+    proj_mine = lax.dot_general(own_heads, my_half, contract, preferred_element_type=jnp.float32)
+    proj_other = lax.dot_general(own_heads, other_half, contract, preferred_element_type=jnp.float32)
+    projected = jnp.where(
+        core == 0,
+        jnp.concatenate([proj_mine, proj_other], axis=1),
+        jnp.concatenate([proj_other, proj_mine], axis=1),
     )
 
     stacked = jnp.concatenate([w_gate, w_upward, w_downward], axis=0)
-    weights = lax.all_gather(stacked, "tx", axis=1, tiled=True)
-    gate_rows, up_rows, down_rows = weights[0], weights[1], weights[2]
+    n_tx = lax.axis_size("tx")
+    pieces = [stacked]
+    for shift in range(1, n_tx):
+        pieces.append(lax.ppermute(stacked, "tx", [(i, (i + shift) % n_tx) for i in range(n_tx)]))
 
     hidden_one = (residual_in.astype(jnp.float32) + projected).astype(jnp.bfloat16)
     normed = rms_scale(hidden_one, gain_first)
@@ -71,6 +82,9 @@
     repeated = jnp.repeat(normed, 2, axis=0)
     send_slots = jnp.dot(placing, repeated, preferred_element_type=jnp.float32).astype(jnp.bfloat16)
     send_slots = send_slots.reshape(n_expert, capacity, width)
+    send_slots, *pieces = lax.optimization_barrier((send_slots, *pieces))
+    weights = jnp.concatenate(pieces, axis=1)
+    gate_rows, up_rows, down_rows = weights[0], weights[1], weights[2]
     received = lax.all_to_all(send_slots, "expert", split_axis=0, concat_axis=0, tiled=True)
     slot_total = n_expert * capacity
     rows_in = received.reshape(slot_total, width)

time: 256 us -> 261 us (1.020)
  local copies, waits for them, and re-layouts: 8.4 us -> 22.5 us
  waiting for transfers between devices: 162 us -> 152 us
  starting transfers between devices: 15.5 us -> 20.5 us
    all_gather x1, waiting for transfers between devices: 42.1 us -> 26.3 us  [per_device(): all_rows = lax.all_gather(rows_in, 'ty', axis=0, tiled=True)]
    all_gather x2 -> x1, waiting for transfers between devices: 54.1 us -> 66.8 us  [per_device(): my_half = lax.all_gather(my_cols, TENSOR_AXES, axis=0, tiled=True)]
    unnamed x17 -> x20, local copies, waits for them, and re-layouts: 0.14 us -> 9.27 us
    ppermute x0 -> x4, starting transfers between devices: none -> 8.15 us  [the longest x3 5.71 us: per_device(): lax.ppermute(stacked, 'tx', [(i, (i + shift) % n_tx) for i in range(n_tx)])]
    all_to_all x1, waiting for transfers between devices: 6.28 us -> 0.01 us  [per_device(): own_heads = lax.all_to_all(attn_heads, TENSOR_AXES, 1, 0, tiled=True)]
    concatenate x0 -> x2, local copies, waits for them, and re-layouts: none -> 3.38 us  [the longest x1 2.37 us: per_device(): weights = jnp.concatenate(pieces, axis=1)]
    all_to_all x1, starting transfers between devices: 7.57 us -> 4.32 us  [per_device(): own_heads = lax.all_to_all(attn_heads, TENSOR_AXES, 1, 0, tiled=True)]
  transfers between devices with their start and end apart: 6 -> 9, of which waited for: 6 -> 4; matrix products, arithmetic and copies ran while one was open for 5% -> 8% of each run, Pallas kernels for 0% -> 0%
where the time goes in v2:
time: 261 us
  waiting for transfers between devices  152 us (58%)
  blocking collectives  30 us (11%)
  local copies, waits for them, and re-layouts  22.5 us (9%)
  starting transfers between devices  20.5 us (8%)
  matrix products  19.7 us (8%)
  between operations  14 us (5%)
    all_gather x1, waiting for transfers between devices, per_device(): my_half = lax.all_gather(my_cols, TENSOR_AXES, axis=0, tiled=True)  66.8 us
    reduce_scatter x1, waiting for transfers between devices, per_device(): lax.psum_scatter(expert_block(all_rows, gate_rows, up_rows, down_rows).as...  39.1 us
    all_to_all x1, blocking collectives, per_device(): lax.all_to_all(send_slots, 'expert', split_axis=0, concat_axis=0, tiled=T...  30 us
    all_gather x1, waiting for transfers between devices, per_device(): all_rows = lax.all_gather(rows_in, 'ty', axis=0, tiled=True)  26.3 us
    all_to_all x1, waiting for transfers between devices, per_device(): lax.all_to_all(expert_out, 'expert', split_axis=0, concat_axis=0, tiled=T...  19.4 us
    dot_general x1, matrix products, expert_block(): return jnp.dot(hid, down_rows, preferred_element_type=jnp.float32)  10.3 us
    unnamed x20, local copies, waits for them, and re-layouts  9.27 us
    all_to_all x1, starting transfers between devices, per_device(): lax.all_to_all(expert_out, 'expert', split_axis=0, concat_axis=0, tiled=T...  7.76 us
  transfers between devices with their start and end apart: 9, of which 4 were waited for; matrix products, arithmetic and copies ran while one was open for 8% of the time, Pallas kernels for 0%

profile of v2, /device:TPU:1, one launch (start us, length us, event | category | flops | bytes accessed | tf_op | source)
XLA Modules:
  0.0 260.6 jit_solution(8388557563514807960)
XLA Ops:
  7.2 0.0 copy-start
  7.2 0.0 all-gather.3.cloned.1.call-start
  7.3 0.8 copy-done
  8.1 0.6 constant_dynamic-slice_fusion
  8.7 0.0 all-gather.3.cloned.1.call-update
  8.7 1.0 constant_dynamic-update-slice_fusion.2
  9.7 1.0 constant_dynamic-update-slice_fusion.1
  10.8 1.0 constant_dynamic-update-slice_fusion
  11.8 2.1 collective-permute-start.1
  13.9 2.5 collective-permute-start.2
  16.3 1.2 collective-permute-start.3
  17.5 1.4 all_to_all.20
  18.9 0.8 copy.23
  19.7 4.3 %all-to-all-start = ((bf16[64,16,88]{2,0,1:T(8,128)(2,1)}), bf16[64,16,88]{2,0,1:T(8,128)(2,1)S(1)}, u32[]{:S(2)}, u32[]{:S(2)}) async-start(bf16[64,16,88]{2,0,1:T(8,128)(2,1)} %copy.23), calls=%async_computation | async-start | bytes 524288 | tf_op jit(solution)/shard_map/all_to_all | solution.py:52
  24.0 0.0 all-gather.5.cloned.1.call-start
  24.1 0.8 copy.26
  24.9 0.1 reshape.112
  25.0 66.8 %all-gather.3.cloned.1.call-done = bf16[1024,512]{1,0:T(8,128)(2,1)} async-done(((bf16[64,512]{1,0:T(8,128)(2,1)}), bf16[1024,512]{1,0:T(8,128)(2,1)}) %all-gather.3.cloned.1.call-update) | async-done | bytes 1048592 | tf_op jit(solution)/shard_map/all_gather | solution.py:50
  91.8 2.4 collective-permute-start
  94.2 0.6 reduce-window.6
  94.8 0.2 slice_reduce_fusion
  95.0 0.1 bitcast_bitcast_fusion
  95.2 0.0 all-to-all-done
  95.2 1.6 convolution_bitcast_fusion.1
  96.7 0.0 collective-permute-done
  96.7 0.3 convolution_bitcast_fusion
  97.1 0.2 fusion.14
  97.3 0.1 fusion.16
  97.4 0.2 broadcast_in_dim.7
  97.6 0.1 reshape.115
  97.7 0.3 convolution_convert_fusion.1
  98.1 0.2 reshape.116
  98.3 0.0 collective-permute-done.1
  98.3 0.0 collective-permute-done.2
  98.3 0.0 collective-permute-done.3
  98.3 30.0 %all_to_all.29 = bf16[16,22,1024]{2,1,0:T(8,128)(2,1)S(1)} all-to-all(bf16[16,22,1024]{2,1,0:T(8,128)(2,1)S(1)} %reshape.116), channel_id=1, replica_groups=mesh['expert'=16,'ty'=4,'tx'=4] {'expert'}, dimensions={0} | all-to-all | bytes 1441792 | tf_op jit(solution)/shard_map/all_to_all | solution.py:88
  128.3 1.1 reshape.117
  129.4 0.0 all-gather.5.cloned.1.call-update
  129.4 0.2 reduce-scatter.2.cloned.1.call-start
  129.6 1.1 constant_dynamic-update-slice_fusion.6
  130.7 2.3 constant_dynamic-update-slice_fusion.5
  133.0 2.3 constant_dynamic-update-slice_fusion.4
  135.3 2.4 constant_dynamic-update-slice_fusion.3
  137.6 26.3 %all-gather.5.cloned.1.call-done = bf16[1408,1024]{1,0:T(8,128)(2,1)} async-done(((bf16[352,1024]{1,0:T(8,128)(2,1)}), bf16[1408,1024]{1,0:T(8,128)(2,1)}) %all-gather.5.cloned.1.call-update) | async-done | bytes 2883600 | tf_op jit(solution)/shard_map/all_gather | solution.py:91
  164.0 6.6 %fusion.9 = f32[1408,704]{0,1:T(8,128)} fusion(bf16[1408,1024]{1,0:T(8,128)(2,1)} %all-gather.5.cloned.1.call-done, bf16[3,704,1024]{2,1,0:T(8,128)(2,1)} %constant_dynamic-update-slice_fusion.3), kind=kOutput, calls=%fused_computation.15 | convolution fusion | flops 2030043136 | bytes 8290304 | tf_op jit(solution)/shard_map/dot_general | solution.py:20
  170.5 10.3 %convolution_convert_fusion = bf16[1408,1024]{1,0:T(8,128)(2,1)} fusion(bf16[3,704,1024]{2,1,0:T(8,128)(2,1)} %constant_dynamic-update-slice_fusion.3, f32[1408,704]{0,1:T(8,128)} %fusion.9, bf16[1408,1024]{1,0:T(8,128)(2,1)} %all-gather.5.cloned.1.call-done), kind=kOutput, calls=%fused_computation.11 | convolution fusion | flops 4071440384 | bytes 12615680 | tf_op jit(solution)/shard_map/dot_general | solution.py:27
  180.8 0.0 reduce-scatter.2.cloned.1.call-update
  180.9 39.1 %reduce-scatter.2.cloned.1.call-done = bf16[352,1024]{1,0:T(8,128)(2,1)} async-done(((bf16[1408,1024]{1,0:T(8,128)(2,1)}), bf16[352,1024]{1,0:T(8,128)(2,1)}) %reduce-scatter.2.cloned.1.call-update) | async-done | bytes 720912 | tf_op jit(solution)/shard_map/reduce_scatter | solution.py:92
  220.0 2.1 reshape.118
  222.1 7.8 %all-to-all-start.2 = ((bf16[16,22,1024]{2,1,0:T(8,128)(2,1)}), bf16[16,22,1024]{2,1,0:T(8,128)(2,1)S(1)}, u32[]{:S(2)}, u32[]{:S(2)}) async-start(bf16[16,22,1024]{2,1,0:T(8,128)(2,1)} %reshape.118), calls=%async_computation.3 | async-start | bytes 1572864 | tf_op jit(solution)/shard_map/all_to_all | solution.py:99
  229.8 0.1 copy.24
  229.9 0.1 reshape.121
  230.1 0.1 iota_compare_fusion.2
  230.2 0.1 eq.63
  230.3 0.3 fusion.33
  230.6 0.0 copy-start.6
  230.6 2.3 gather_fusion
  232.9 0.1 reshape.124
  233.0 0.1 copy.25
  233.2 19.4 %all-to-all-done.2 = bf16[16,22,1024]{2,1,0:T(8,128)(2,1)S(1)} async-done(((bf16[16,22,1024]{2,1,0:T(8,128)(2,1)}), bf16[16,22,1024]{2,1,0:T(8,128)(2,1)S(1)}, u32[]{:S(2)}, u32[]{:S(2)}) %all-to-all-start.2) | async-done | bytes 720928 | tf_op jit(solution)/shard_map/all_to_all | solution.py:99
  252.5 0.2 reshape.132
  252.8 0.4 fusion.10
  253.1 0.2 fusion.11
  253.3 0.8 fusion.13
  (24 shorter events, 0.2 us)
Async XLA Ops:
  7.2 0.9 copy-start
  7.2 89.9 %copy-start.2 = (bf16[88,1024]{1,0:T(8,128)(2,1)S(1)}, bf16[88,1024]{1,0:T(8,128)(2,1)}, u32[]{:S(2)}) copy-start(bf16[88,1024]{1,0:T(8,128)(2,1)} %param.10) | copy-start | bytes 540676
  7.2 90.1 %copy-start.5 = (f32[1024]{0:T(1024)S(1)}, f32[1024]{0:T(1024)}, u32[]{:S(2)}) copy-start(f32[1024]{0:T(1024)} %param.13) | copy-start | bytes 12292
  7.2 84.6 %all-gather.3.cloned.1.call-start = ((), (), s32[]{:S(2)}) async-start(), calls=%async_computation.4 | async-start | bytes 1114112 | tf_op jit(solution)/shard_map/all_gather | solution.py:50
  11.8 86.5 %collective-permute-start.1 = (bf16[3,176,1024]{2,1,0:T(8,128)(2,1)S(1)}, bf16[3,176,1024]{2,1,0:T(8,128)(2,1)}, u32[]{:S(2)}, u32[]{:S(2)}) collective-permute-start(bf16[3,176,1024]{2,1,0:T(8,128)(2,1)S(1)} %constant_dynamic-update-slice_fusion), channel_id=1, source_target_pairs={{0,1},{1,2},{2,3},{3,0},{4,5},{5,6},{6,7},{7,4},{8,9},{9,10},{10,1... | collective-permute-start | bytes 3244040 | tf_op jit(solution)/shard_map/ppermute | solution.py:66
  13.9 84.4 %collective-permute-start.2 = (bf16[3,176,1024]{2,1,0:T(8,128)(2,1)S(1)}, bf16[3,176,1024]{2,1,0:T(8,128)(2,1)}, u32[]{:S(2)}, u32[]{:S(2)}) collective-permute-start(bf16[3,176,1024]{2,1,0:T(8,128)(2,1)S(1)} %constant_dynamic-update-slice_fusion), channel_id=1, source_target_pairs={{0,2},{1,3},{2,0},{3,1},{4,6},{5,7},{6,4},{7,5},{8,10},{9,11},{10,... | collective-permute-start | bytes 3244040 | tf_op jit(solution)/shard_map/ppermute | solution.py:66
  16.3 82.0 %collective-permute-start.3 = (bf16[3,176,1024]{2,1,0:T(8,128)(2,1)S(1)}, bf16[3,176,1024]{2,1,0:T(8,128)(2,1)}, u32[]{:S(2)}, u32[]{:S(2)}) collective-permute-start(bf16[3,176,1024]{2,1,0:T(8,128)(2,1)S(1)} %constant_dynamic-update-slice_fusion), channel_id=1, source_target_pairs={{0,3},{1,0},{2,1},{3,2},{4,7},{5,4},{6,5},{7,6},{8,11},{9,8},{10,9... | collective-permute-start | bytes 3244040 | tf_op jit(solution)/shard_map/ppermute | solution.py:66
  19.7 75.5 %all-to-all-start = ((bf16[64,16,88]{2,0,1:T(8,128)(2,1)}), bf16[64,16,88]{2,0,1:T(8,128)(2,1)S(1)}, u32[]{:S(2)}, u32[]{:S(2)}) async-start(bf16[64,16,88]{2,0,1:T(8,128)(2,1)} %copy.23), calls=%async_computation | async-start | bytes 524288 | tf_op jit(solution)/shard_map/all_to_all | solution.py:52
  24.0 140.0 %all-gather.5.cloned.1.call-start = ((), (), s32[]{:S(2)}) async-start(), calls=%async_computation.5 | async-start | bytes 3604480 | tf_op jit(solution)/shard_map/all_gather | solution.py:91
  91.8 4.9 %collective-permute-start = (bf16[1024,512]{1,0:T(8,128)(2,1)}, bf16[1024,512]{1,0:T(8,128)(2,1)S(1)}, u32[]{:S(2)}, u32[]{:S(2)}) collective-permute-start(bf16[1024,512]{1,0:T(8,128)(2,1)} %all-gather.3.cloned.1.call-done), channel_id=1, source_target_pairs={{0,16},{16,0},{32,48},{48,32},{64,80},{80,64},{96,112},{112,96},{1... | collective-permute-start | bytes 3145736 | tf_op jit(solution)/shard_map/ppermute | solution.py:51
  129.4 90.6 %reduce-scatter.2.cloned.1.call-start = ((), (), s32[]{:S(2)}) async-start(), calls=%async_computation.6 | async-start | bytes 3604480 | tf_op jit(solution)/shard_map/reduce_scatter | solution.py:92
  180.8 49.0 %copy-start.4 = (s32[88,2]{0,1:T(2,128)S(1)}, s32[88,2]{0,1:T(2,128)}, u32[]{:S(2)}) copy-start(s32[88,2]{0,1:T(2,128)} %param.15) | copy-start | bytes 2116
  180.8 49.5 %copy-start.3 = (f32[1024,16]{0,1:T(8,128)S(1)}, f32[1024,16]{0,1:T(8,128)}, u32[]{:S(2)}) copy-start(f32[1024,16]{0,1:T(8,128)} %param.14) | copy-start | bytes 196612
  222.1 30.5 %all-to-all-start.2 = ((bf16[16,22,1024]{2,1,0:T(8,128)(2,1)}), bf16[16,22,1024]{2,1,0:T(8,128)(2,1)S(1)}, u32[]{:S(2)}, u32[]{:S(2)}) async-start(bf16[16,22,1024]{2,1,0:T(8,128)(2,1)} %reshape.118), calls=%async_computation.3 | async-start | bytes 1572864 | tf_op jit(solution)/shard_map/all_to_all | solution.py:99
  230.6 22.7 %copy-start.6 = (f32[1024]{0:T(1024)S(1)}, f32[1024]{0:T(1024)}, u32[]{:S(2)}) copy-start(f32[1024]{0:T(1024)} %param.19) | copy-start | bytes 12292
  253.3 0.8 copy-start.1
Sparse Core Ops, SparseCore 0:
  11.0 80.7 all-gather.2
  129.5 34.4 all-gather.4
  181.0 38.9 reduce-scatter.1

commit v3 on v1

--- a/solution.py
+++ b/solution.py
@@ -44,15 +44,29 @@
     n_expert = lax.axis_size("expert")
     capacity = 4 * row_count // n_expert
 
-    full_proj = lax.all_gather(out_proj, TENSOR_AXES, axis=0, tiled=True)
+    n_ty = lax.axis_size("ty")
+    n_tx = lax.axis_size("tx")
+    ty = lax.axis_index("ty")
+    tx = lax.axis_index("tx")
+    near = [out_proj] + [
+        lax.ppermute(out_proj, "tx", shift_pairs(n_tx, s)) for s in range(1, n_tx)
+    ]
+    near = jnp.stack(near)
+    full_proj = [near] + [lax.ppermute(near, "ty", shift_pairs(n_ty, s)) for s in range(1, n_ty)]
+    full_proj = jnp.stack(full_proj)
     own_heads = lax.all_to_all(attn_heads, TENSOR_AXES, 1, 0, tiled=True)
+    own_heads = own_heads.reshape(n_ty, n_tx, -1, row_count)
+    from_y = (ty - jnp.arange(n_ty)) % n_ty
+    from_x = (tx - jnp.arange(n_tx)) % n_tx
+    own_heads = jnp.take(jnp.take(own_heads, from_y, axis=0), from_x, axis=1)
     projected = lax.dot_general(
-        own_heads, full_proj, (((0,), (0,)), ((), ())), preferred_element_type=jnp.float32
+        own_heads, full_proj, (((0, 1, 2), (0, 1, 2)), ((), ())), preferred_element_type=jnp.float32
     )
 
     stacked = jnp.concatenate([w_gate, w_upward, w_downward], axis=0)
-    weights = lax.all_gather(stacked, "tx", axis=1, tiled=True)
-    gate_rows, up_rows, down_rows = weights[0], weights[1], weights[2]
+    pieces = [stacked] + [
+        lax.ppermute(stacked, "tx", shift_pairs(n_tx, s)) for s in range(1, n_tx)
+    ]
 
     hidden_one = (residual_in.astype(jnp.float32) + projected).astype(jnp.bfloat16)
     normed = rms_scale(hidden_one, gain_first)
@@ -71,16 +85,20 @@
     repeated = jnp.repeat(normed, 2, axis=0)
     send_slots = jnp.dot(placing, repeated, preferred_element_type=jnp.float32).astype(jnp.bfloat16)
     send_slots = send_slots.reshape(n_expert, capacity, width)
+    weights = jnp.concatenate(pieces, axis=1)
+    gate_rows, up_rows, down_rows = weights[0], weights[1], weights[2]
     received = lax.all_to_all(send_slots, "expert", split_axis=0, concat_axis=0, tiled=True)
     slot_total = n_expert * capacity
     rows_in = received.reshape(slot_total, width)
-    all_rows = lax.all_gather(rows_in, "ty", axis=0, tiled=True)
-    expert_sum = lax.psum_scatter(
-        expert_block(all_rows, gate_rows, up_rows, down_rows).astype(jnp.bfloat16),
-        "ty",
-        scatter_dimension=0,
-        tiled=True,
-    )
+    all_rows = [rows_in] + [lax.ppermute(rows_in, "ty", shift_pairs(n_ty, s)) for s in range(1, n_ty)]
+    all_rows = jnp.concatenate(all_rows, axis=0)
+    partial = expert_block(all_rows, gate_rows, up_rows, down_rows).astype(jnp.bfloat16)
+    partial = partial.reshape(n_ty, slot_total, width)
+    expert_sum = partial[0].astype(jnp.float32)
+    for s in range(1, n_ty):
+        back = lax.ppermute(partial[s], "ty", shift_pairs(n_ty, -s))
+        expert_sum = expert_sum + back.astype(jnp.float32)
+    expert_sum = expert_sum.astype(jnp.bfloat16)
     expert_out = expert_sum.reshape(n_expert, capacity, width)
     returned = lax.all_to_all(expert_out, "expert", split_axis=0, concat_axis=0, tiled=True)
     returned = returned.reshape(slot_total, width)
@@ -92,6 +110,10 @@
     residual_out = (hidden_one.astype(jnp.float32) + mixed).astype(jnp.bfloat16)
     next_normed = rms_scale(residual_out, gain_second)
     return (residual_out, next_normed)
+
+
+def shift_pairs(n, shift):
+    return [(i, (i + shift) % n) for i in range(n)]
 
 
 def split_tensor(n):

time: 256 us -> 204 us (0.80); the launches traced: 255 us -> 200 us
  waiting for transfers between devices: 162 us -> 113 us
  starting transfers between devices: 15.5 us -> 50.1 us
  blocking collectives: 31.9 us -> 0 us
  between operations: 14 us -> 1.14 us
  local copies, waits for them, and re-layouts: 8.4 us -> 12.7 us
  matrix products: 19.4 us -> 15.7 us
  other arithmetic: 4.3 us -> 6.96 us
    all_gather x3 -> x0, waiting for transfers between devices: 96.2 us -> none  [the longest x1 42.1 us: per_device(): all_rows = lax.all_gather(rows_in, 'ty', axis=0, tiled=True)]
    ppermute x0 -> x15, waiting for transfers between devices: none -> 74.2 us  [the longest x3 26.6 us: per_device(): back = lax.ppermute(partial[s], 'ty', shift_pairs(n_ty, -s))]
    reduce_scatter x1 -> x0, waiting for transfers between devices: 39.1 us -> none  [per_device(): lax.psum_scatter(expert_block(all_rows, gate_rows, up_rows, down_rows).as...]
    all_to_all x1 -> x0, blocking collectives: 31.9 us -> none  [per_device(): lax.all_to_all(send_slots, 'expert', split_axis=0, concat_axis=0, tiled=T...]
    ppermute x0 -> x15, starting transfers between devices: none -> 21.7 us  [the longest x3 5.63 us: per_device(): lax.ppermute(near, 'ty', shift_pairs(n_ty, s))]
    all_to_all x0 -> x1, waiting for transfers between devices: none -> 19.5 us  [per_device(): lax.all_to_all(send_slots, 'expert', split_axis=0, concat_axis=0, tiled=T...]
    all_to_all x0 -> x1, starting transfers between devices: none -> 8.87 us  [per_device(): lax.all_to_all(send_slots, 'expert', split_axis=0, concat_axis=0, tiled=T...]
    all_to_all x1, starting transfers between devices: 7.76 us -> 14.2 us  [per_device(): lax.all_to_all(expert_out, 'expert', split_axis=0, concat_axis=0, tiled=T...]
  transfers between devices with their start and end apart: 6 -> 18, of which waited for: 6 -> 10; matrix products, arithmetic and copies ran while one was open for 5% -> 5% of each run, Pallas kernels for 0% -> 0%
where the time goes in v3:
time: 204 us; the launch traced here: 200 us
  waiting for transfers between devices  113 us (55%)
  starting transfers between devices  50.1 us (25%)
  matrix products  15.7 us (8%)
  local copies, waits for them, and re-layouts  12.7 us (6%)
  other arithmetic  6.96 us (3%)
    ppermute x3, waiting for transfers between devices, per_device(): back = lax.ppermute(partial[s], 'ty', shift_pairs(n_ty, -s))  26.6 us
    ppermute x3, waiting for transfers between devices, per_device(): lax.ppermute(stacked, 'tx', shift_pairs(n_tx, s))  25.1 us
    ppermute x3, waiting for transfers between devices, per_device(): lax.ppermute(near, 'ty', shift_pairs(n_ty, s))  21 us
    all_to_all x1, waiting for transfers between devices, per_device(): lax.all_to_all(send_slots, 'expert', split_axis=0, concat_axis=0, tiled=T...  19.5 us
    all_to_all x1, waiting for transfers between devices, per_device(): lax.all_to_all(expert_out, 'expert', split_axis=0, concat_axis=0, tiled=T...  19.4 us
    all_to_all x1, starting transfers between devices, per_device(): lax.all_to_all(expert_out, 'expert', split_axis=0, concat_axis=0, tiled=T...  14.2 us
    all_to_all x1, starting transfers between devices, per_device(): lax.all_to_all(send_slots, 'expert', split_axis=0, concat_axis=0, tiled=T...  8.87 us
    dot_general x1, matrix products, expert_block(): return jnp.dot(hid, down_rows, preferred_element_type=jnp.float32)  8.6 us
  transfers between devices with their start and end apart: 18, of which 10 were waited for; matrix products, arithmetic and copies ran while one was open for 5% of the time, Pallas kernels for 0%

profile of v3, /device:TPU:1, one launch (start us, length us, event | category | flops | bytes accessed | tf_op | source)
XLA Modules:
  0.0 199.8 jit_solution(11590121160816478813)
XLA Ops:
  0.7 2.1 %collective-permute-start = (bf16[64,1024]{1,0:T(8,128)(2,1)}, bf16[64,1024]{1,0:T(8,128)(2,1)S(1)}, u32[]{:S(2)}, u32[]{:S(2)}) collective-permute-start(bf16[64,1024]{1,0:T(8,128)(2,1)} %param.12), channel_id=1, source_target_pairs={{0,1},{1,2},{2,3},{3,0},{4,5},{5,6},{6,7},{7,4},{8,9},{9,10},{10,1... | collective-permute-start | bytes 393224 | tf_op jit(solution)/shard_map/ppermute | solution.py:52
  2.8 1.4 collective-permute-start.2
  4.1 1.6 collective-permute-start.1
  5.8 1.4 all_to_all.18
  7.2 0.8 copy.25
  8.0 5.4 %all-to-all-start = ((bf16[64,16,88]{2,0,1:T(8,128)(2,1)}), bf16[64,16,88]{2,0,1:T(8,128)(2,1)S(1)}, u32[]{:S(2)}, u32[]{:S(2)}) async-start(bf16[64,16,88]{2,0,1:T(8,128)(2,1)} %copy.25), calls=%async_computation | async-start | bytes 524288 | tf_op jit(solution)/shard_map/all_to_all | solution.py:57
  13.5 0.8 copy.29
  14.3 0.1 reshape.234
  14.4 0.6 reduce-window.6
  15.0 0.2 slice_reduce_fusion
  15.2 0.1 bitcast_bitcast_fusion
  15.4 1.0 fusion.58
  16.4 3.0 %collective-permute-start.4 = (bf16[4,64,1024]{2,1,0:T(8,128)(2,1)S(1)}, bf16[4,64,1024]{2,1,0:T(8,128)(2,1)S(1)}, u32[]{:S(2)}, u32[]{:S(2)}) collective-permute-start(bf16[4,64,1024]{2,1,0:T(8,128)(2,1)S(1)} %get-tuple-element.10), channel_id=1, source_target_pairs={{0,8},{4,12},{8,0},{12,4},{1,9},{5,13},{9,1},{13,5},{2,10},{6,14},... | collective-permute-start | bytes 1572872 | tf_op jit(solution)/shard_map/ppermute | solution.py:55
  19.3 0.3 collective-permute-start.3
  19.6 2.4 %collective-permute-start.5 = (bf16[4,64,1024]{2,1,0:T(8,128)(2,1)S(1)}, bf16[4,64,1024]{2,1,0:T(8,128)(2,1)}, u32[]{:S(2)}, u32[]{:S(2)}) collective-permute-start(bf16[4,64,1024]{2,1,0:T(8,128)(2,1)S(1)} %get-tuple-element.10), channel_id=1, source_target_pairs={{0,12},{4,0},{8,4},{12,8},{1,13},{5,1},{9,5},{13,9},{2,14},{6,2},{... | collective-permute-start | bytes 1572872 | tf_op jit(solution)/shard_map/ppermute | solution.py:55
  22.1 0.6 gather_fusion
  22.7 0.1 broadcast_select_fusion
  22.8 0.6 gather_fusion.1
  23.4 8.6 %collective-permute-done.4 = bf16[4,64,1024]{2,1,0:T(8,128)(2,1)S(1)} collective-permute-done((bf16[4,64,1024]{2,1,0:T(8,128)(2,1)S(1)}, bf16[4,64,1024]{2,1,0:T(8,128)(2,1)S(1)}, u32[]{:S(2)}, u32[]{:S(2)}) %collective-permute-start.4) | collective-permute-done | bytes 524320 | tf_op jit(solution)/shard_map/ppermute | solution.py:55
  32.0 12.4 %collective-permute-done.3 = bf16[4,64,1024]{2,1,0:T(8,128)(2,1)S(1)} collective-permute-done((bf16[4,64,1024]{2,1,0:T(8,128)(2,1)S(1)}, bf16[4,64,1024]{2,1,0:T(8,128)(2,1)S(1)}, u32[]{:S(2)}, u32[]{:S(2)}) %collective-permute-start.3) | collective-permute-done | bytes 524320 | tf_op jit(solution)/shard_map/ppermute | solution.py:55
  44.4 1.8 multiply_reduce_fusion
  46.2 0.1 multiply_convert_fusion
  46.3 0.2 broadcast_in_dim.40
  46.5 0.1 reshape.237
  46.7 0.3 convolution_convert_fusion.1
  47.1 1.1 reshape.238
  48.2 8.9 %all-to-all-start.1 = ((bf16[16,22,1024]{2,1,0:T(8,128)(2,1)}), bf16[16,22,1024]{2,1,0:T(8,128)(2,1)S(1)}, u32[]{:S(2)}, u32[]{:S(2)}) async-start(bf16[16,22,1024]{2,1,0:T(8,128)(2,1)} %reshape.238), calls=%async_computation.1 | async-start | bytes 1572864 | tf_op jit(solution)/shard_map/all_to_all | solution.py:90
  57.2 2.1 %collective-permute-start.11 = (bf16[3,176,1024]{2,1,0:T(8,128)(2,1)S(1)}, bf16[3,176,1024]{2,1,0:T(8,128)(2,1)}, u32[]{:S(2)}, u32[]{:S(2)}) collective-permute-start(bf16[3,176,1024]{2,1,0:T(8,128)(2,1)S(1)} %constant_dynamic-update-slice_fusion.4), channel_id=1, source_target_pairs={{0,3},{1,0},{2,1},{3,2},{4,7},{5,4},{6,5},{7,6},{8,11},{9,8},{10,9... | collective-permute-start | bytes 3244040 | tf_op jit(solution)/shard_map/ppermute | solution.py:68
  59.3 0.8 collective-permute-start.10
  60.0 0.2 collective-permute-start.9
  60.2 19.5 %all-to-all-done.1 = bf16[16,22,1024]{2,1,0:T(8,128)(2,1)S(1)} async-done(((bf16[16,22,1024]{2,1,0:T(8,128)(2,1)}), bf16[16,22,1024]{2,1,0:T(8,128)(2,1)S(1)}, u32[]{:S(2)}, u32[]{:S(2)}) %all-to-all-start.1) | async-done | bytes 720928 | tf_op jit(solution)/shard_map/all_to_all | solution.py:90
  79.8 0.2 reshape.239
  80.0 1.2 collective-permute-start.6
  81.1 2.1 %collective-permute-start.7 = (bf16[352,1024]{1,0:T(8,128)(2,1)S(1)}, bf16[352,1024]{1,0:T(8,128)(2,1)S(1)}, u32[]{:S(2)}, u32[]{:S(2)}) collective-permute-start(bf16[352,1024]{1,0:T(8,128)(2,1)S(1)} %reshape.239), channel_id=1, source_target_pairs={{0,8},{4,12},{8,0},{12,4},{1,9},{5,13},{9,1},{13,5},{2,10},{6,14},... | collective-permute-start | bytes 2162696 | tf_op jit(solution)/shard_map/ppermute | solution.py:93
  83.2 1.4 collective-permute-start.8
  84.7 1.3 collective-permute-done.10
  85.9 23.9 %collective-permute-done.9 = bf16[3,176,1024]{2,1,0:T(8,128)(2,1)} collective-permute-done((bf16[3,176,1024]{2,1,0:T(8,128)(2,1)S(1)}, bf16[3,176,1024]{2,1,0:T(8,128)(2,1)}, u32[]{:S(2)}, u32[]{:S(2)}) %collective-permute-start.9) | collective-permute-done | bytes 1081376 | tf_op jit(solution)/shard_map/ppermute | solution.py:68
  109.8 2.2 %pad_maximum_fusion = bf16[3,704,1024]{2,1,0:T(8,128)(2,1)S(1)} fusion(bf16[3,176,1024]{2,1,0:T(8,128)(2,1)} %collective-permute-done.11, bf16[3,176,1024]{2,1,0:T(8,128)(2,1)} %collective-permute-done.10, bf16[3,176,1024]{2,1,0:T(8,128)(2,1)} %collective-permute-done.9, bf16[3,176,1024]{2,1,0:T(8,128)(2,1)S(1)} %constant_dynamic-update-slice_fusion.4), kind=kLoop, calls=%fused_computation.4 | loop fusion | flops 17301504 | bytes 8650752 | tf_op jit(solution)/shard_map/concatenate | solution.py:88
  112.1 1.4 collective-permute-done.7
  113.6 0.4 copy-done.1
  114.0 1.7 copy-done.7
  115.7 4.4 %fusion.23 = f32[1408,704]{0,1:T(8,128)} fusion(bf16[1408,1024]{1,0:T(8,128)(2,1)S(1)} %constant_dynamic-update-slice_fusion, bf16[3,704,1024]{2,1,0:T(8,128)(2,1)S(1)} %pad_maximum_fusion), kind=kOutput, calls=%fused_computation.31 | convolution fusion | flops 2030043136 | bytes 8290304 | tf_op jit(solution)/shard_map/dot_general | solution.py:20
  120.0 8.6 %convolution_convert_fusion = bf16[1408,1024]{1,0:T(8,128)(2,1)S(1)} fusion(f32[1408,704]{0,1:T(8,128)} %fusion.23, bf16[3,704,1024]{2,1,0:T(8,128)(2,1)} %copy-done.1, bf16[1408,1024]{1,0:T(8,128)(2,1)} %copy-done.7), kind=kOutput, calls=%fused_computation.14 | convolution fusion | flops 4071440384 | bytes 12615680 | tf_op jit(solution)/shard_map/dot_general | solution.py:27
  128.7 0.2 fusion.60
  128.9 1.9 collective-permute-start.12
  130.7 1.3 collective-permute-start.13
  132.0 10.7 %collective-permute-done.12 = bf16[352,1024]{1,0:T(8,128)(2,1)S(1)} collective-permute-done((bf16[352,1024]{1,0:T(8,128)(2,1)S(1)}, bf16[352,1024]{1,0:T(8,128)(2,1)S(1)}, u32[]{:S(2)}, u32[]{:S(2)}) %collective-permute-start.12) | collective-permute-done | bytes 720928 | tf_op jit(solution)/shard_map/ppermute | solution.py:99
  142.7 2.6 %collective-permute-done.14 = bf16[352,1024]{1,0:T(8,128)(2,1)S(1)} collective-permute-done((bf16[352,1024]{1,0:T(8,128)(2,1)S(1)}, bf16[352,1024]{1,0:T(8,128)(2,1)S(1)}, u32[]{:S(2)}, u32[]{:S(2)}) %collective-permute-start.14) | collective-permute-done | bytes 720928 | tf_op jit(solution)/shard_map/ppermute | solution.py:99
  145.4 13.3 %collective-permute-done.13 = bf16[352,1024]{1,0:T(8,128)(2,1)S(1)} collective-permute-done((bf16[352,1024]{1,0:T(8,128)(2,1)S(1)}, bf16[352,1024]{1,0:T(8,128)(2,1)S(1)}, u32[]{:S(2)}, u32[]{:S(2)}) %collective-permute-start.13) | collective-permute-done | bytes 720928 | tf_op jit(solution)/shard_map/ppermute | solution.py:99
  158.6 1.7 add_convert_fusion
  160.3 1.1 reshape.240
  161.4 14.2 %all-to-all-start.2 = ((bf16[16,22,1024]{2,1,0:T(8,128)(2,1)}), bf16[16,22,1024]{2,1,0:T(8,128)(2,1)S(1)}, u32[]{:S(2)}, u32[]{:S(2)}) async-start(bf16[16,22,1024]{2,1,0:T(8,128)(2,1)} %reshape.240), calls=%async_computation.2 | async-start | bytes 1572864 | tf_op jit(solution)/shard_map/all_to_all | solution.py:103
  175.6 0.1 copy.27
  175.7 0.1 reshape.259
  175.8 0.1 iota_compare_fusion.2
  175.9 0.1 eq.60
  176.0 0.3 fusion.61
  176.4 2.3 %gather_fusion.2 = f32[176]{0:T(256)S(1)} fusion(f32[88,16]{0,1:T(8,128)S(1)} %fusion.45, s32[176]{0:T(256)S(1)} %reshape.259), kind=kCustom, calls=%fused_computation.2 | custom fusion | bytes 2816 | tf_op jit(solution)/shard_map/jit(take_along_axis)/gather | solution.py:75
  178.6 0.1 reshape.262
  178.9 19.4 %all-to-all-done.2 = bf16[16,22,1024]{2,1,0:T(8,128)(2,1)S(1)} async-done(((bf16[16,22,1024]{2,1,0:T(8,128)(2,1)}), bf16[16,22,1024]{2,1,0:T(8,128)(2,1)S(1)}, u32[]{:S(2)}, u32[]{:S(2)}) %all-to-all-start.2) | async-done | bytes 720928 | tf_op jit(solution)/shard_map/all_to_all | solution.py:103
  198.3 0.2 reshape.271
  198.5 0.4 fusion.24
  198.8 0.1 fusion.37
  199.0 0.8 fusion.39
  (62 shorter events, 0.7 us)
Async XLA Ops:
  0.6 175.4 %copy-start = (f32[1024,16]{0,1:T(8,128)S(1)}, f32[1024,16]{0,1:T(8,128)}, u32[]{:S(2)}) copy-start(f32[1024,16]{0,1:T(8,128)} %param.14) | copy-start | bytes 196612
  0.6 43.8 %copy-start.13 = (bf16[88,1024]{1,0:T(8,128)(2,1)S(1)}, bf16[88,1024]{1,0:T(8,128)(2,1)}, u32[]{:S(2)}) copy-start(bf16[88,1024]{1,0:T(8,128)(2,1)} %param.10) | copy-start | bytes 540676
  0.7 14.7 %collective-permute-start = (bf16[64,1024]{1,0:T(8,128)(2,1)}, bf16[64,1024]{1,0:T(8,128)(2,1)S(1)}, u32[]{:S(2)}, u32[]{:S(2)}) collective-permute-start(bf16[64,1024]{1,0:T(8,128)(2,1)} %param.12), channel_id=1, source_target_pairs={{0,1},{1,2},{2,3},{3,0},{4,5},{5,6},{6,7},{7,4},{8,9},{9,10},{10,1... | collective-permute-start | bytes 393224 | tf_op jit(solution)/shard_map/ppermute | solution.py:52
  2.8 12.6 %collective-permute-start.2 = (bf16[64,1024]{1,0:T(8,128)(2,1)}, bf16[64,1024]{1,0:T(8,128)(2,1)S(1)}, u32[]{:S(2)}, u32[]{:S(2)}) collective-permute-start(bf16[64,1024]{1,0:T(8,128)(2,1)} %param.12), channel_id=1, source_target_pairs={{0,3},{1,0},{2,1},{3,2},{4,7},{5,4},{6,5},{7,6},{8,11},{9,8},{10,9... | collective-permute-start | bytes 393224 | tf_op jit(solution)/shard_map/ppermute | solution.py:52
  4.1 11.3 %collective-permute-start.1 = (bf16[64,1024]{1,0:T(8,128)(2,1)}, bf16[64,1024]{1,0:T(8,128)(2,1)S(1)}, u32[]{:S(2)}, u32[]{:S(2)}) collective-permute-start(bf16[64,1024]{1,0:T(8,128)(2,1)} %param.12), channel_id=1, source_target_pairs={{0,2},{1,3},{2,0},{3,1},{4,6},{5,7},{6,4},{7,5},{8,10},{9,11},{10,... | collective-permute-start | bytes 393224 | tf_op jit(solution)/shard_map/ppermute | solution.py:52
  8.0 14.1 %all-to-all-start = ((bf16[64,16,88]{2,0,1:T(8,128)(2,1)}), bf16[64,16,88]{2,0,1:T(8,128)(2,1)S(1)}, u32[]{:S(2)}, u32[]{:S(2)}) async-start(bf16[64,16,88]{2,0,1:T(8,128)(2,1)} %copy.25), calls=%async_computation | async-start | bytes 524288 | tf_op jit(solution)/shard_map/all_to_all | solution.py:57
  16.4 15.6 %collective-permute-start.4 = (bf16[4,64,1024]{2,1,0:T(8,128)(2,1)S(1)}, bf16[4,64,1024]{2,1,0:T(8,128)(2,1)S(1)}, u32[]{:S(2)}, u32[]{:S(2)}) collective-permute-start(bf16[4,64,1024]{2,1,0:T(8,128)(2,1)S(1)} %get-tuple-element.10), channel_id=1, source_target_pairs={{0,8},{4,12},{8,0},{12,4},{1,9},{5,13},{9,1},{13,5},{2,10},{6,14},... | collective-permute-start | bytes 1572872 | tf_op jit(solution)/shard_map/ppermute | solution.py:55
  19.3 25.1 %collective-permute-start.3 = (bf16[4,64,1024]{2,1,0:T(8,128)(2,1)S(1)}, bf16[4,64,1024]{2,1,0:T(8,128)(2,1)S(1)}, u32[]{:S(2)}, u32[]{:S(2)}) collective-permute-start(bf16[4,64,1024]{2,1,0:T(8,128)(2,1)S(1)} %get-tuple-element.10), channel_id=1, source_target_pairs={{0,4},{4,8},{8,12},{12,0},{1,5},{5,9},{9,13},{13,1},{2,6},{6,10},{... | collective-permute-start | bytes 1572872 | tf_op jit(solution)/shard_map/ppermute | solution.py:55
  19.6 24.8 %collective-permute-start.5 = (bf16[4,64,1024]{2,1,0:T(8,128)(2,1)S(1)}, bf16[4,64,1024]{2,1,0:T(8,128)(2,1)}, u32[]{:S(2)}, u32[]{:S(2)}) collective-permute-start(bf16[4,64,1024]{2,1,0:T(8,128)(2,1)S(1)} %get-tuple-element.10), channel_id=1, source_target_pairs={{0,12},{4,0},{8,4},{12,8},{1,13},{5,1},{9,5},{13,9},{2,14},{6,2},{... | collective-permute-start | bytes 1572872 | tf_op jit(solution)/shard_map/ppermute | solution.py:55
  22.0 24.6 %copy-start.8 = (s32[176]{0:T(256)}, s32[176]{0:T(256)S(1)}, u32[]{:S(2)}) copy-start(s32[176]{0:T(256)S(1)} %multiply_add_fusion) | copy-start | bytes 2116
  44.4 1.8 copy-start.11
  46.2 10.8 %copy-start.4 = (bf16[1,176,1024]{2,1,0:T(8,128)(2,1)S(1)}, bf16[1,176,1024]{2,1,0:T(8,128)(2,1)}, u32[]{:S(2)}) copy-start(bf16[1,176,1024]{2,1,0:T(8,128)(2,1)} %param.16) | copy-start | bytes 1081348
  46.5 10.5 %copy-start.5 = (bf16[1,176,1024]{2,1,0:T(8,128)(2,1)S(1)}, bf16[1,176,1024]{2,1,0:T(8,128)(2,1)}, u32[]{:S(2)}) copy-start(bf16[1,176,1024]{2,1,0:T(8,128)(2,1)} %param.17) | copy-start | bytes 1081348
  46.7 10.4 %copy-start.6 = (bf16[1,176,1024]{2,1,0:T(8,128)(2,1)S(1)}, bf16[1,176,1024]{2,1,0:T(8,128)(2,1)}, u32[]{:S(2)}) copy-start(bf16[1,176,1024]{2,1,0:T(8,128)(2,1)} %param.18) | copy-start | bytes 1081348
  48.2 31.6 %all-to-all-start.1 = ((bf16[16,22,1024]{2,1,0:T(8,128)(2,1)}), bf16[16,22,1024]{2,1,0:T(8,128)(2,1)S(1)}, u32[]{:S(2)}, u32[]{:S(2)}) async-start(bf16[16,22,1024]{2,1,0:T(8,128)(2,1)} %reshape.238), calls=%async_computation.1 | async-start | bytes 1572864 | tf_op jit(solution)/shard_map/all_to_all | solution.py:90
  57.2 26.1 %collective-permute-start.11 = (bf16[3,176,1024]{2,1,0:T(8,128)(2,1)S(1)}, bf16[3,176,1024]{2,1,0:T(8,128)(2,1)}, u32[]{:S(2)}, u32[]{:S(2)}) collective-permute-start(bf16[3,176,1024]{2,1,0:T(8,128)(2,1)S(1)} %constant_dynamic-update-slice_fusion.4), channel_id=1, source_target_pairs={{0,3},{1,0},{2,1},{3,2},{4,7},{5,4},{6,5},{7,6},{8,11},{9,8},{10,9... | collective-permute-start | bytes 3244040 | tf_op jit(solution)/shard_map/ppermute | solution.py:68
  59.3 26.7 %collective-permute-start.10 = (bf16[3,176,1024]{2,1,0:T(8,128)(2,1)S(1)}, bf16[3,176,1024]{2,1,0:T(8,128)(2,1)}, u32[]{:S(2)}, u32[]{:S(2)}) collective-permute-start(bf16[3,176,1024]{2,1,0:T(8,128)(2,1)S(1)} %constant_dynamic-update-slice_fusion.4), channel_id=1, source_target_pairs={{0,2},{1,3},{2,0},{3,1},{4,6},{5,7},{6,4},{7,5},{8,10},{9,11},{10,... | collective-permute-start | bytes 3244040 | tf_op jit(solution)/shard_map/ppermute | solution.py:68
  60.0 49.8 %collective-permute-start.9 = (bf16[3,176,1024]{2,1,0:T(8,128)(2,1)S(1)}, bf16[3,176,1024]{2,1,0:T(8,128)(2,1)}, u32[]{:S(2)}, u32[]{:S(2)}) collective-permute-start(bf16[3,176,1024]{2,1,0:T(8,128)(2,1)S(1)} %constant_dynamic-update-slice_fusion.4), channel_id=1, source_target_pairs={{0,1},{1,2},{2,3},{3,0},{4,5},{5,6},{6,7},{7,4},{8,9},{9,10},{10,1... | collective-permute-start | bytes 3244040 | tf_op jit(solution)/shard_map/ppermute | solution.py:68
  80.0 32.1 %collective-permute-start.6 = (bf16[352,1024]{1,0:T(8,128)(2,1)S(1)}, bf16[352,1024]{1,0:T(8,128)(2,1)S(1)}, u32[]{:S(2)}, u32[]{:S(2)}) collective-permute-start(bf16[352,1024]{1,0:T(8,128)(2,1)S(1)} %reshape.239), channel_id=1, source_target_pairs={{0,4},{4,8},{8,12},{12,0},{1,5},{5,9},{9,13},{13,1},{2,6},{6,10},{... | collective-permute-start | bytes 2162696 | tf_op jit(solution)/shard_map/ppermute | solution.py:93
  81.1 32.4 %collective-permute-start.7 = (bf16[352,1024]{1,0:T(8,128)(2,1)S(1)}, bf16[352,1024]{1,0:T(8,128)(2,1)S(1)}, u32[]{:S(2)}, u32[]{:S(2)}) collective-permute-start(bf16[352,1024]{1,0:T(8,128)(2,1)S(1)} %reshape.239), channel_id=1, source_target_pairs={{0,8},{4,12},{8,0},{12,4},{1,9},{5,13},{9,1},{13,5},{2,10},{6,14},... | collective-permute-start | bytes 2162696 | tf_op jit(solution)/shard_map/ppermute | solution.py:93
  83.2 30.3 %collective-permute-start.8 = (bf16[352,1024]{1,0:T(8,128)(2,1)S(1)}, bf16[352,1024]{1,0:T(8,128)(2,1)S(1)}, u32[]{:S(2)}, u32[]{:S(2)}) collective-permute-start(bf16[352,1024]{1,0:T(8,128)(2,1)S(1)} %reshape.239), channel_id=1, source_target_pairs={{0,12},{4,0},{8,4},{12,8},{1,13},{5,1},{9,5},{13,9},{2,14},{6,2},{... | collective-permute-start | bytes 2162696 | tf_op jit(solution)/shard_map/ppermute | solution.py:93
  112.0 2.0 copy-start.1
  114.0 1.7 copy-start.7
  128.7 16.7 %copy-start.2 = (bf16[1408,1024]{1,0:T(8,128)(2,1)}, bf16[1408,1024]{1,0:T(8,128)(2,1)S(1)}, u32[]{:S(2)}) copy-start(bf16[1408,1024]{1,0:T(8,128)(2,1)S(1)} %convolution_convert_fusion) | copy-start | bytes 8650756
  128.9 13.9 %collective-permute-start.12 = (bf16[352,1024]{1,0:T(8,128)(2,1)S(1)}, bf16[352,1024]{1,0:T(8,128)(2,1)S(1)}, u32[]{:S(2)}, u32[]{:S(2)}) collective-permute-start(bf16[352,1024]{1,0:T(8,128)(2,1)S(1)} %get-tuple-element.6), channel_id=1, source_target_pairs={{0,12},{4,0},{8,4},{12,8},{1,13},{5,1},{9,5},{13,9},{2,14},{6,2},{... | collective-permute-start | bytes 2162696 | tf_op jit(solution)/shard_map/ppermute | solution.py:99
  130.7 14.6 %collective-permute-start.14 = (bf16[352,1024]{1,0:T(8,128)(2,1)S(1)}, bf16[352,1024]{1,0:T(8,128)(2,1)S(1)}, u32[]{:S(2)}, u32[]{:S(2)}) collective-permute-start(bf16[352,1024]{1,0:T(8,128)(2,1)S(1)} %get-tuple-element.7), channel_id=1, source_target_pairs={{0,4},{4,8},{8,12},{12,0},{1,5},{5,9},{9,13},{13,1},{2,6},{6,10},{... | collective-permute-start | bytes 2162696 | tf_op jit(solution)/shard_map/ppermute | solution.py:99
  130.7 44.8 %copy-start.10 = (s32[88,2]{0,1:T(2,128)S(1)}, s32[88,2]{0,1:T(2,128)}, u32[]{:S(2)}) copy-start(s32[88,2]{0,1:T(2,128)} %param.15) | copy-start | bytes 2116
  130.7 45.1 %copy-start.9 = (s32[176]{0:T(256)S(1)}, s32[176]{0:T(256)}, u32[]{:S(2)}) copy-start(s32[176]{0:T(256)} %copy-done.8) | copy-start | bytes 2116
  130.7 27.9 %collective-permute-start.13 = (bf16[352,1024]{1,0:T(8,128)(2,1)S(1)}, bf16[352,1024]{1,0:T(8,128)(2,1)S(1)}, u32[]{:S(2)}, u32[]{:S(2)}) collective-permute-start(bf16[352,1024]{1,0:T(8,128)(2,1)S(1)} %get-tuple-element.8), channel_id=1, source_target_pairs={{0,8},{4,12},{8,0},{12,4},{1,9},{5,13},{9,1},{13,5},{2,10},{6,14},... | collective-permute-start | bytes 2162696 | tf_op jit(solution)/shard_map/ppermute | solution.py:99
  161.4 36.9 %all-to-all-start.2 = ((bf16[16,22,1024]{2,1,0:T(8,128)(2,1)}), bf16[16,22,1024]{2,1,0:T(8,128)(2,1)S(1)}, u32[]{:S(2)}, u32[]{:S(2)}) async-start(bf16[16,22,1024]{2,1,0:T(8,128)(2,1)} %reshape.240), calls=%async_computation.2 | async-start | bytes 1572864 | tf_op jit(solution)/shard_map/all_to_all | solution.py:103
  178.6 20.4 %copy-start.12 = (f32[1024]{0:T(1024)S(1)}, f32[1024]{0:T(1024)}, u32[]{:S(2)}) copy-start(f32[1024]{0:T(1024)} %param.19) | copy-start | bytes 12292
  199.0 0.8 copy-start.3

commit v4 on v3

--- a/solution.py
+++ b/solution.py
@@ -48,22 +48,30 @@
     n_tx = lax.axis_size("tx")
     ty = lax.axis_index("ty")
     tx = lax.axis_index("tx")
-    near = [out_proj] + [
-        lax.ppermute(out_proj, "tx", shift_pairs(n_tx, s)) for s in range(1, n_tx)
-    ]
+    core = lax.axis_index("expert") % 2
+    half = width // 2
+    my_cols = lax.dynamic_slice_in_dim(out_proj, core * half, half, axis=1)
+    near = [my_cols] + [lax.ppermute(my_cols, "tx", shift_pairs(n_tx, s)) for s in range(1, n_tx)]
     near = jnp.stack(near)
-    full_proj = [near] + [lax.ppermute(near, "ty", shift_pairs(n_ty, s)) for s in range(1, n_ty)]
-    full_proj = jnp.stack(full_proj)
+    my_half = [near] + [lax.ppermute(near, "ty", shift_pairs(n_ty, s)) for s in range(1, n_ty)]
+    my_half = jnp.stack(my_half)
+    other_half = lax.ppermute(my_half, "expert", [(i, i ^ 1) for i in range(n_expert)])
     own_heads = lax.all_to_all(attn_heads, TENSOR_AXES, 1, 0, tiled=True)
     own_heads = own_heads.reshape(n_ty, n_tx, -1, row_count)
     from_y = (ty - jnp.arange(n_ty)) % n_ty
     from_x = (tx - jnp.arange(n_tx)) % n_tx
     own_heads = jnp.take(jnp.take(own_heads, from_y, axis=0), from_x, axis=1)
-    projected = lax.dot_general(
-        own_heads, full_proj, (((0, 1, 2), (0, 1, 2)), ((), ())), preferred_element_type=jnp.float32
+    contract = (((0, 1, 2), (0, 1, 2)), ((), ()))
+    proj_mine = lax.dot_general(own_heads, my_half, contract, preferred_element_type=jnp.float32)
+    proj_other = lax.dot_general(own_heads, other_half, contract, preferred_element_type=jnp.float32)
+    projected = jnp.where(
+        core == 0,
+        jnp.concatenate([proj_mine, proj_other], axis=1),
+        jnp.concatenate([proj_other, proj_mine], axis=1),
     )
 
     stacked = jnp.concatenate([w_gate, w_upward, w_downward], axis=0)
+    stacked, near = lax.optimization_barrier((stacked, near))
     pieces = [stacked] + [
         lax.ppermute(stacked, "tx", shift_pairs(n_tx, s)) for s in range(1, n_tx)
     ]
@@ -85,9 +93,10 @@
     repeated = jnp.repeat(normed, 2, axis=0)
     send_slots = jnp.dot(placing, repeated, preferred_element_type=jnp.float32).astype(jnp.bfloat16)
     send_slots = send_slots.reshape(n_expert, capacity, width)
+    received = lax.all_to_all(send_slots, "expert", split_axis=0, concat_axis=0, tiled=True)
+    received, *pieces = lax.optimization_barrier((received, *pieces))
     weights = jnp.concatenate(pieces, axis=1)
     gate_rows, up_rows, down_rows = weights[0], weights[1], weights[2]
-    received = lax.all_to_all(send_slots, "expert", split_axis=0, concat_axis=0, tiled=True)
     slot_total = n_expert * capacity
     rows_in = received.reshape(slot_total, width)
     all_rows = [rows_in] + [lax.ppermute(rows_in, "ty", shift_pairs(n_ty, s)) for s in range(1, n_ty)]

time: 204 us -> 221 us (1.083); the launches traced: 200 us -> 221 us
  waiting for transfers between devices: 113 us -> 140 us
  starting transfers between devices: 50.1 us -> 44.6 us
  local copies, waits for them, and re-layouts: 12.7 us -> 15.7 us
  other arithmetic: 6.96 us -> 4.27 us
    ppermute x3, waiting for transfers between devices: 1.37 us -> 29.1 us  [per_device(): lax.ppermute(rows_in, 'ty', shift_pairs(n_ty, s))]
    ppermute x3, waiting for transfers between devices: 25.1 us -> 45.8 us  [per_device(): lax.ppermute(stacked, 'tx', shift_pairs(n_tx, s))]
    all_to_all x1, waiting for transfers between devices: 19.5 us -> 0.01 us  [per_device(): lax.all_to_all(send_slots, 'expert', split_axis=0, concat_axis=0, tiled=T...]
    ppermute x3, waiting for transfers between devices: 21 us -> 11.7 us  [per_device(): lax.ppermute(near, 'ty', shift_pairs(n_ty, s))]
    ppermute x3, waiting for transfers between devices: 26.6 us -> 34 us  [per_device(): back = lax.ppermute(partial[s], 'ty', shift_pairs(n_ty, -s))]
    all_to_all x1, starting transfers between devices: 14.2 us -> 7.21 us  [per_device(): lax.all_to_all(expert_out, 'expert', split_axis=0, concat_axis=0, tiled=T...]
    ppermute x3 -> x4, starting transfers between devices: 5.1 us -> 7.28 us  [the longest x3 5.63 us: per_device(): lax.ppermute(my_cols, 'tx', shift_pairs(n_tx, s))]
    unnamed x34 -> x41, local copies, waits for them, and re-layouts: 3.07 us -> 4.72 us
  transfers between devices with their start and end apart: 18 -> 19, of which waited for: 10 -> 11; matrix products, arithmetic and copies ran while one was open for 5% -> 4% of each run, Pallas kernels for 0% -> 0%
where the time goes in v4:
time: 221 us
  waiting for transfers between devices  140 us (63%)
  starting transfers between devices  44.6 us (20%)
  local copies, waits for them, and re-layouts  15.7 us (7%)
  matrix products  14.7 us (7%)
  other arithmetic  4.27 us (2%)
    ppermute x3, waiting for transfers between devices, per_device(): lax.ppermute(stacked, 'tx', shift_pairs(n_tx, s))  45.8 us
    ppermute x3, waiting for transfers between devices, per_device(): back = lax.ppermute(partial[s], 'ty', shift_pairs(n_ty, -s))  34 us
    ppermute x3, waiting for transfers between devices, per_device(): lax.ppermute(rows_in, 'ty', shift_pairs(n_ty, s))  29.1 us
    all_to_all x1, waiting for transfers between devices, per_device(): lax.all_to_all(expert_out, 'expert', split_axis=0, concat_axis=0, tiled=T...  19.4 us
    ppermute x3, waiting for transfers between devices, per_device(): lax.ppermute(near, 'ty', shift_pairs(n_ty, s))  11.7 us
    all_to_all x1, starting transfers between devices, per_device(): lax.all_to_all(send_slots, 'expert', split_axis=0, concat_axis=0, tiled=T...  8.85 us
    dot_general x1, matrix products, expert_block(): return jnp.dot(hid, down_rows, preferred_element_type=jnp.float32)  8.59 us
    all_to_all x1, starting transfers between devices, per_device(): lax.all_to_all(expert_out, 'expert', split_axis=0, concat_axis=0, tiled=T...  7.21 us
  transfers between devices with their start and end apart: 19, of which 11 were waited for; matrix products, arithmetic and copies ran while one was open for 4% of the time, Pallas kernels for 0%

profile of v4, /device:TPU:1, one launch (start us, length us, event | category | flops | bytes accessed | tf_op | source)
XLA Modules:
  0.0 220.9 jit_solution(9262504705853349591)
XLA Ops:
  0.7 0.9 copy-done
  1.5 2.0 collective-permute-start
  3.6 2.5 %collective-permute-start.1 = (bf16[64,512]{1,0:T(8,128)(2,1)S(1)}, bf16[64,512]{1,0:T(8,128)(2,1)S(1)}, u32[]{:S(2)}, u32[]{:S(2)}) collective-permute-start(bf16[64,512]{1,0:T(8,128)(2,1)S(1)} %constant_dynamic-slice_fusion), channel_id=1, source_target_pairs={{0,2},{1,3},{2,0},{3,1},{4,6},{5,7},{6,4},{7,5},{8,10},{9,11},{10,... | collective-permute-start | bytes 196616 | tf_op jit(solution)/shard_map/ppermute | solution.py:54
  6.0 1.2 collective-permute-start.2
  7.2 1.4 all_to_all.18
  8.6 0.8 copy.26
  9.4 4.3 %all-to-all-start = ((bf16[64,16,88]{2,0,1:T(8,128)(2,1)}), bf16[64,16,88]{2,0,1:T(8,128)(2,1)S(1)}, u32[]{:S(2)}, u32[]{:S(2)}) async-start(bf16[64,16,88]{2,0,1:T(8,128)(2,1)} %copy.26), calls=%async_computation | async-start | bytes 524288 | tf_op jit(solution)/shard_map/all_to_all | solution.py:59
  13.7 0.8 copy.31
  14.5 0.1 reshape.234
  14.7 0.6 reduce-window.6
  15.3 0.2 slice_reduce_fusion
  15.6 1.4 collective-permute-start.3
  17.0 2.4 %collective-permute-start.4 = (bf16[4,64,512]{2,1,0:T(8,128)(2,1)S(1)}, bf16[4,64,512]{2,1,0:T(8,128)(2,1)S(1)}, u32[]{:S(2)}, u32[]{:S(2)}) collective-permute-start(bf16[4,64,512]{2,1,0:T(8,128)(2,1)S(1)} %get-tuple-element.24), channel_id=1, source_target_pairs={{0,8},{4,12},{8,0},{12,4},{1,9},{5,13},{9,1},{13,5},{2,10},{6,14},... | collective-permute-start | bytes 786440 | tf_op jit(solution)/shard_map/ppermute | solution.py:56
  19.4 1.2 collective-permute-start.5
  20.6 6.0 %collective-permute-done.3 = bf16[4,64,512]{2,1,0:T(8,128)(2,1)S(1)} collective-permute-done((bf16[4,64,512]{2,1,0:T(8,128)(2,1)S(1)}, bf16[4,64,512]{2,1,0:T(8,128)(2,1)S(1)}, u32[]{:S(2)}, u32[]{:S(2)}) %collective-permute-start.3) | collective-permute-done | bytes 262176 | tf_op jit(solution)/shard_map/ppermute | solution.py:56
  26.6 5.7 %collective-permute-done.4 = bf16[4,64,512]{2,1,0:T(8,128)(2,1)S(1)} collective-permute-done((bf16[4,64,512]{2,1,0:T(8,128)(2,1)S(1)}, bf16[4,64,512]{2,1,0:T(8,128)(2,1)S(1)}, u32[]{:S(2)}, u32[]{:S(2)}) %collective-permute-start.4) | collective-permute-done | bytes 262176 | tf_op jit(solution)/shard_map/ppermute | solution.py:56
  32.3 0.1 pad_maximum_fusion.1
  32.5 1.6 collective-permute-start.6
  34.2 0.6 gather_fusion
  34.9 0.6 gather_fusion.1
  35.6 0.4 convolution_bitcast_fusion.1
  35.9 0.5 collective-permute-done.6
  36.4 0.4 convolution_bitcast_fusion
  36.8 0.2 fusion.20
  37.1 0.2 broadcast_in_dim.40
  37.3 0.1 reshape.237
  37.5 0.3 convolution_convert_fusion.1
  37.8 1.1 reshape.238
  38.9 8.9 %all-to-all-start.1 = ((bf16[16,22,1024]{2,1,0:T(8,128)(2,1)}), bf16[16,22,1024]{2,1,0:T(8,128)(2,1)S(1)}, u32[]{:S(2)}, u32[]{:S(2)}) async-start(bf16[16,22,1024]{2,1,0:T(8,128)(2,1)} %reshape.238), calls=%async_computation.1 | async-start | bytes 1572864 | tf_op jit(solution)/shard_map/all_to_all | solution.py:96
  47.8 0.1 pad_maximum_fusion
  47.9 0.9 collective-permute-start.7
  48.8 2.2 collective-permute-start.8
  51.0 1.2 collective-permute-start.9
  52.2 22.3 %collective-permute-done.7 = bf16[3,176,1024]{2,1,0:T(8,128)(2,1)S(1)} collective-permute-done((bf16[3,176,1024]{2,1,0:T(8,128)(2,1)S(1)}, bf16[3,176,1024]{2,1,0:T(8,128)(2,1)S(1)}, u32[]{:S(2)}, u32[]{:S(2)}) %collective-permute-start.7) | collective-permute-done | bytes 1081376 | tf_op jit(solution)/shard_map/ppermute | solution.py:76
  74.5 23.5 %collective-permute-done.8 = bf16[3,176,1024]{2,1,0:T(8,128)(2,1)S(1)} collective-permute-done((bf16[3,176,1024]{2,1,0:T(8,128)(2,1)S(1)}, bf16[3,176,1024]{2,1,0:T(8,128)(2,1)S(1)}, u32[]{:S(2)}, u32[]{:S(2)}) %collective-permute-start.8) | collective-permute-done | bytes 1081376 | tf_op jit(solution)/shard_map/ppermute | solution.py:76
  98.0 1.0 copy-done.4
  99.0 0.2 reshape.239
  99.2 0.4 collective-permute-start.10
  99.6 2.1 collective-permute-start.11
  101.8 1.0 collective-permute-start.12
  103.0 1.3 constant_dynamic-update-slice_fusion.4
  104.4 13.2 %collective-permute-done.10 = bf16[352,1024]{1,0:T(8,128)(2,1)S(1)} collective-permute-done((bf16[352,1024]{1,0:T(8,128)(2,1)S(1)}, bf16[352,1024]{1,0:T(8,128)(2,1)S(1)}, u32[]{:S(2)}, u32[]{:S(2)}) %collective-permute-start.10) | collective-permute-done | bytes 720928 | tf_op jit(solution)/shard_map/ppermute | solution.py:102
  117.6 15.0 %collective-permute-done.11 = bf16[352,1024]{1,0:T(8,128)(2,1)S(1)} collective-permute-done((bf16[352,1024]{1,0:T(8,128)(2,1)S(1)}, bf16[352,1024]{1,0:T(8,128)(2,1)S(1)}, u32[]{:S(2)}, u32[]{:S(2)}) %collective-permute-start.11) | collective-permute-done | bytes 720928 | tf_op jit(solution)/shard_map/ppermute | solution.py:102
  132.6 1.0 collective-permute-done.12
  133.7 1.6 copy-done.11
  135.3 4.3 %fusion.15 = f32[1408,704]{0,1:T(8,128)} fusion(bf16[1408,1024]{1,0:T(8,128)(2,1)S(1)} %constant_dynamic-update-slice_fusion, bf16[3,704,1024]{2,1,0:T(8,128)(2,1)S(1)} %constant_dynamic-update-slice_fusion.4), kind=kOutput, calls=%fused_computation.22 | convolution fusion | flops 2030043136 | bytes 8290304 | tf_op jit(solution)/shard_map/dot_general | solution.py:20
  139.7 8.6 %convolution_convert_fusion = bf16[1408,1024]{1,0:T(8,128)(2,1)S(1)} fusion(f32[1408,704]{0,1:T(8,128)} %fusion.15, bf16[3,704,1024]{2,1,0:T(8,128)(2,1)} %copy-done.10, bf16[1408,1024]{1,0:T(8,128)(2,1)} %copy-done.11), kind=kOutput, calls=%fused_computation.13 | convolution fusion | flops 4071440384 | bytes 12615680 | tf_op jit(solution)/shard_map/dot_general | solution.py:27
  148.3 0.2 fusion.48
  148.5 3.5 %collective-permute-start.13 = (bf16[352,1024]{1,0:T(8,128)(2,1)S(1)}, bf16[352,1024]{1,0:T(8,128)(2,1)S(1)}, u32[]{:S(2)}, u32[]{:S(2)}) collective-permute-start(bf16[352,1024]{1,0:T(8,128)(2,1)S(1)} %get-tuple-element.20), channel_id=1, source_target_pairs={{0,12},{4,0},{8,4},{12,8},{1,13},{5,1},{9,5},{13,9},{2,14},{6,2},{... | collective-permute-start | bytes 2162696 | tf_op jit(solution)/shard_map/ppermute | solution.py:108
  152.1 0.6 collective-permute-start.15
  152.6 29.6 %collective-permute-done.13 = bf16[352,1024]{1,0:T(8,128)(2,1)S(1)} collective-permute-done((bf16[352,1024]{1,0:T(8,128)(2,1)S(1)}, bf16[352,1024]{1,0:T(8,128)(2,1)S(1)}, u32[]{:S(2)}, u32[]{:S(2)}) %collective-permute-start.13) | collective-permute-done | bytes 720928 | tf_op jit(solution)/shard_map/ppermute | solution.py:108
  182.3 4.4 %collective-permute-done.15 = bf16[352,1024]{1,0:T(8,128)(2,1)S(1)} collective-permute-done((bf16[352,1024]{1,0:T(8,128)(2,1)S(1)}, bf16[352,1024]{1,0:T(8,128)(2,1)S(1)}, u32[]{:S(2)}, u32[]{:S(2)}) %collective-permute-start.15) | collective-permute-done | bytes 720928 | tf_op jit(solution)/shard_map/ppermute | solution.py:108
  186.6 1.7 add_convert_fusion
  188.3 1.1 reshape.240
  189.4 7.2 %all-to-all-start.2 = ((bf16[16,22,1024]{2,1,0:T(8,128)(2,1)}), bf16[16,22,1024]{2,1,0:T(8,128)(2,1)S(1)}, u32[]{:S(2)}, u32[]{:S(2)}) async-start(bf16[16,22,1024]{2,1,0:T(8,128)(2,1)} %reshape.240), calls=%async_computation.2 | async-start | bytes 1572864 | tf_op jit(solution)/shard_map/all_to_all | solution.py:112
  196.7 0.1 reshape.259
  197.1 0.3 fusion.49
  197.4 2.3 %gather_fusion.2 = f32[176]{0:T(256)S(1)} fusion(f32[88,16]{0,1:T(8,128)S(1)} %fusion.32, s32[176]{0:T(256)S(1)} %reshape.259), kind=kCustom, calls=%fused_computation.2 | custom fusion | bytes 2816 | tf_op jit(solution)/shard_map/jit(take_along_axis)/gather | solution.py:83
  199.7 0.1 reshape.262
  199.9 19.4 %all-to-all-done.2 = bf16[16,22,1024]{2,1,0:T(8,128)(2,1)S(1)} async-done(((bf16[16,22,1024]{2,1,0:T(8,128)(2,1)}), bf16[16,22,1024]{2,1,0:T(8,128)(2,1)S(1)}, u32[]{:S(2)}, u32[]{:S(2)}) %all-to-all-start.2) | async-done | bytes 720928 | tf_op jit(solution)/shard_map/all_to_all | solution.py:112
  219.3 0.2 reshape.272
  219.5 0.4 fusion.16
  219.9 0.1 fusion.17
  220.1 0.8 fusion.19
  (76 shorter events, 1.6 us)
Async XLA Ops:
  0.6 0.9 copy-start
  1.5 13.9 %collective-permute-start = (bf16[64,512]{1,0:T(8,128)(2,1)S(1)}, bf16[64,512]{1,0:T(8,128)(2,1)S(1)}, u32[]{:S(2)}, u32[]{:S(2)}) collective-permute-start(bf16[64,512]{1,0:T(8,128)(2,1)S(1)} %constant_dynamic-slice_fusion), channel_id=1, source_target_pairs={{0,1},{1,2},{2,3},{3,0},{4,5},{5,6},{6,7},{7,4},{8,9},{9,10},{10,1... | collective-permute-start | bytes 196616 | tf_op jit(solution)/shard_map/ppermute | solution.py:54
  3.6 11.9 %collective-permute-start.1 = (bf16[64,512]{1,0:T(8,128)(2,1)S(1)}, bf16[64,512]{1,0:T(8,128)(2,1)S(1)}, u32[]{:S(2)}, u32[]{:S(2)}) collective-permute-start(bf16[64,512]{1,0:T(8,128)(2,1)S(1)} %constant_dynamic-slice_fusion), channel_id=1, source_target_pairs={{0,2},{1,3},{2,0},{3,1},{4,6},{5,7},{6,4},{7,5},{8,10},{9,11},{10,... | collective-permute-start | bytes 196616 | tf_op jit(solution)/shard_map/ppermute | solution.py:54
  6.0 9.5 %collective-permute-start.2 = (bf16[64,512]{1,0:T(8,128)(2,1)S(1)}, bf16[64,512]{1,0:T(8,128)(2,1)S(1)}, u32[]{:S(2)}, u32[]{:S(2)}) collective-permute-start(bf16[64,512]{1,0:T(8,128)(2,1)S(1)} %constant_dynamic-slice_fusion), channel_id=1, source_target_pairs={{0,3},{1,0},{2,1},{3,2},{4,7},{5,4},{6,5},{7,6},{8,11},{9,8},{10,9... | collective-permute-start | bytes 196616 | tf_op jit(solution)/shard_map/ppermute | solution.py:54
  9.4 24.9 %all-to-all-start = ((bf16[64,16,88]{2,0,1:T(8,128)(2,1)}), bf16[64,16,88]{2,0,1:T(8,128)(2,1)S(1)}, u32[]{:S(2)}, u32[]{:S(2)}) async-start(bf16[64,16,88]{2,0,1:T(8,128)(2,1)} %copy.26), calls=%async_computation | async-start | bytes 524288 | tf_op jit(solution)/shard_map/all_to_all | solution.py:59
  15.6 11.0 %collective-permute-start.3 = (bf16[4,64,512]{2,1,0:T(8,128)(2,1)S(1)}, bf16[4,64,512]{2,1,0:T(8,128)(2,1)S(1)}, u32[]{:S(2)}, u32[]{:S(2)}) collective-permute-start(bf16[4,64,512]{2,1,0:T(8,128)(2,1)S(1)} %get-tuple-element.24), channel_id=1, source_target_pairs={{0,4},{4,8},{8,12},{12,0},{1,5},{5,9},{9,13},{13,1},{2,6},{6,10},{... | collective-permute-start | bytes 786440 | tf_op jit(solution)/shard_map/ppermute | solution.py:56
  17.0 15.3 %collective-permute-start.4 = (bf16[4,64,512]{2,1,0:T(8,128)(2,1)S(1)}, bf16[4,64,512]{2,1,0:T(8,128)(2,1)S(1)}, u32[]{:S(2)}, u32[]{:S(2)}) collective-permute-start(bf16[4,64,512]{2,1,0:T(8,128)(2,1)S(1)} %get-tuple-element.24), channel_id=1, source_target_pairs={{0,8},{4,12},{8,0},{12,4},{1,9},{5,13},{9,1},{13,5},{2,10},{6,14},... | collective-permute-start | bytes 786440 | tf_op jit(solution)/shard_map/ppermute | solution.py:56
  19.4 12.9 %collective-permute-start.5 = (bf16[4,64,512]{2,1,0:T(8,128)(2,1)S(1)}, bf16[4,64,512]{2,1,0:T(8,128)(2,1)S(1)}, u32[]{:S(2)}, u32[]{:S(2)}) collective-permute-start(bf16[4,64,512]{2,1,0:T(8,128)(2,1)S(1)} %get-tuple-element.24), channel_id=1, source_target_pairs={{0,12},{4,0},{8,4},{12,8},{1,13},{5,1},{9,5},{13,9},{2,14},{6,2},{... | collective-permute-start | bytes 786440 | tf_op jit(solution)/shard_map/ppermute | solution.py:56
  32.3 4.5 %copy-start.12 = (bf16[88,1024]{1,0:T(8,128)(2,1)S(1)}, bf16[88,1024]{1,0:T(8,128)(2,1)}, u32[]{:S(2)}) copy-start(bf16[88,1024]{1,0:T(8,128)(2,1)} %param.10) | copy-start | bytes 540676
  32.4 4.5 %copy-start.15 = (f32[1024]{0:T(1024)S(1)}, f32[1024]{0:T(1024)}, u32[]{:S(2)}) copy-start(f32[1024]{0:T(1024)} %param.13) | copy-start | bytes 12292
  32.5 3.9 %collective-permute-start.6 = (bf16[4,4,64,512]{3,2,1,0:T(8,128)(2,1)S(1)}, bf16[4,4,64,512]{3,2,1,0:T(8,128)(2,1)S(1)}, u32[]{:S(2)}, u32[]{:S(2)}) collective-permute-start(bf16[4,4,64,512]{3,2,1,0:T(8,128)(2,1)S(1)} %pad_maximum_fusion.1), channel_id=1, source_target_pairs={{0,16},{16,0},{32,48},{48,32},{64,80},{80,64},{96,112},{112,96},{1... | collective-permute-start | bytes 3145736 | tf_op jit(solution)/shard_map/ppermute | solution.py:58
  37.0 10.8 %copy-start.7 = (bf16[1,176,1024]{2,1,0:T(8,128)(2,1)S(1)}, bf16[1,176,1024]{2,1,0:T(8,128)(2,1)}, u32[]{:S(2)}) copy-start(bf16[1,176,1024]{2,1,0:T(8,128)(2,1)} %param.18) | copy-start | bytes 1081348
  37.0 10.8 %copy-start.8 = (bf16[1,176,1024]{2,1,0:T(8,128)(2,1)S(1)}, bf16[1,176,1024]{2,1,0:T(8,128)(2,1)}, u32[]{:S(2)}) copy-start(bf16[1,176,1024]{2,1,0:T(8,128)(2,1)} %param.17) | copy-start | bytes 1081348
  37.0 10.8 %copy-start.9 = (bf16[1,176,1024]{2,1,0:T(8,128)(2,1)S(1)}, bf16[1,176,1024]{2,1,0:T(8,128)(2,1)}, u32[]{:S(2)}) copy-start(bf16[1,176,1024]{2,1,0:T(8,128)(2,1)} %param.16) | copy-start | bytes 1081348
  38.9 60.1 %all-to-all-start.1 = ((bf16[16,22,1024]{2,1,0:T(8,128)(2,1)}), bf16[16,22,1024]{2,1,0:T(8,128)(2,1)S(1)}, u32[]{:S(2)}, u32[]{:S(2)}) async-start(bf16[16,22,1024]{2,1,0:T(8,128)(2,1)} %reshape.238), calls=%async_computation.1 | async-start | bytes 1572864 | tf_op jit(solution)/shard_map/all_to_all | solution.py:96
  47.9 26.6 %collective-permute-start.7 = (bf16[3,176,1024]{2,1,0:T(8,128)(2,1)S(1)}, bf16[3,176,1024]{2,1,0:T(8,128)(2,1)S(1)}, u32[]{:S(2)}, u32[]{:S(2)}) collective-permute-start(bf16[3,176,1024]{2,1,0:T(8,128)(2,1)S(1)} %pad_maximum_fusion), channel_id=1, source_target_pairs={{0,1},{1,2},{2,3},{3,0},{4,5},{5,6},{6,7},{7,4},{8,9},{9,10},{10,1... | collective-permute-start | bytes 3244040 | tf_op jit(solution)/shard_map/ppermute | solution.py:76
  48.8 49.2 %collective-permute-start.8 = (bf16[3,176,1024]{2,1,0:T(8,128)(2,1)S(1)}, bf16[3,176,1024]{2,1,0:T(8,128)(2,1)S(1)}, u32[]{:S(2)}, u32[]{:S(2)}) collective-permute-start(bf16[3,176,1024]{2,1,0:T(8,128)(2,1)S(1)} %pad_maximum_fusion), channel_id=1, source_target_pairs={{0,2},{1,3},{2,0},{3,1},{4,6},{5,7},{6,4},{7,5},{8,10},{9,11},{10,... | collective-permute-start | bytes 3244040 | tf_op jit(solution)/shard_map/ppermute | solution.py:76
  51.0 48.0 %collective-permute-start.9 = (bf16[3,176,1024]{2,1,0:T(8,128)(2,1)S(1)}, bf16[3,176,1024]{2,1,0:T(8,128)(2,1)}, u32[]{:S(2)}, u32[]{:S(2)}) collective-permute-start(bf16[3,176,1024]{2,1,0:T(8,128)(2,1)S(1)} %pad_maximum_fusion), channel_id=1, source_target_pairs={{0,3},{1,0},{2,1},{3,2},{4,7},{5,4},{6,5},{7,6},{8,11},{9,8},{10,9... | collective-permute-start | bytes 3244040 | tf_op jit(solution)/shard_map/ppermute | solution.py:76
  74.5 23.5 %copy-start.2 = (bf16[3,176,1024]{2,1,0:T(8,128)(2,1)}, bf16[3,176,1024]{2,1,0:T(8,128)(2,1)S(1)}, u32[]{:S(2)}) copy-start(bf16[3,176,1024]{2,1,0:T(8,128)(2,1)S(1)} %collective-permute-done.7) | copy-start | bytes 3244036
  98.0 1.0 copy-start.4
  99.2 3.6 %copy-start.3 = (bf16[3,176,1024]{2,1,0:T(8,128)(2,1)S(1)}, bf16[3,176,1024]{2,1,0:T(8,128)(2,1)}, u32[]{:S(2)}) copy-start(bf16[3,176,1024]{2,1,0:T(8,128)(2,1)} %copy-done.2) | copy-start | bytes 3244036
  99.2 3.7 %copy-start.5 = (bf16[3,176,1024]{2,1,0:T(8,128)(2,1)S(1)}, bf16[3,176,1024]{2,1,0:T(8,128)(2,1)}, u32[]{:S(2)}) copy-start(bf16[3,176,1024]{2,1,0:T(8,128)(2,1)} %copy-done.4) | copy-start | bytes 3244036
  99.2 18.3 %collective-permute-start.10 = (bf16[352,1024]{1,0:T(8,128)(2,1)S(1)}, bf16[352,1024]{1,0:T(8,128)(2,1)S(1)}, u32[]{:S(2)}, u32[]{:S(2)}) collective-permute-start(bf16[352,1024]{1,0:T(8,128)(2,1)S(1)} %reshape.239), channel_id=1, source_target_pairs={{0,4},{4,8},{8,12},{12,0},{1,5},{5,9},{9,13},{13,1},{2,6},{6,10},{... | collective-permute-start | bytes 2162696 | tf_op jit(solution)/shard_map/ppermute | solution.py:102
  99.6 32.9 %collective-permute-start.11 = (bf16[352,1024]{1,0:T(8,128)(2,1)S(1)}, bf16[352,1024]{1,0:T(8,128)(2,1)S(1)}, u32[]{:S(2)}, u32[]{:S(2)}) collective-permute-start(bf16[352,1024]{1,0:T(8,128)(2,1)S(1)} %reshape.239), channel_id=1, source_target_pairs={{0,8},{4,12},{8,0},{12,4},{1,9},{5,13},{9,1},{13,5},{2,10},{6,14},... | collective-permute-start | bytes 2162696 | tf_op jit(solution)/shard_map/ppermute | solution.py:102
  101.8 31.8 %collective-permute-start.12 = (bf16[352,1024]{1,0:T(8,128)(2,1)S(1)}, bf16[352,1024]{1,0:T(8,128)(2,1)S(1)}, u32[]{:S(2)}, u32[]{:S(2)}) collective-permute-start(bf16[352,1024]{1,0:T(8,128)(2,1)S(1)} %reshape.239), channel_id=1, source_target_pairs={{0,12},{4,0},{8,4},{12,8},{1,13},{5,1},{9,5},{13,9},{2,14},{6,2},{... | collective-permute-start | bytes 2162696 | tf_op jit(solution)/shard_map/ppermute | solution.py:102
  104.3 29.3 %copy-start.10 = (bf16[3,704,1024]{2,1,0:T(8,128)(2,1)}, bf16[3,704,1024]{2,1,0:T(8,128)(2,1)S(1)}, u32[]{:S(2)}) copy-start(bf16[3,704,1024]{2,1,0:T(8,128)(2,1)S(1)} %constant_dynamic-update-slice_fusion.4) | copy-start | bytes 12976132
  133.7 1.7 copy-start.11
  148.3 34.0 %copy-start.1 = (bf16[1408,1024]{1,0:T(8,128)(2,1)}, bf16[1408,1024]{1,0:T(8,128)(2,1)S(1)}, u32[]{:S(2)}) copy-start(bf16[1408,1024]{1,0:T(8,128)(2,1)S(1)} %convolution_convert_fusion) | copy-start | bytes 8650756
  148.5 33.8 %collective-permute-start.13 = (bf16[352,1024]{1,0:T(8,128)(2,1)S(1)}, bf16[352,1024]{1,0:T(8,128)(2,1)S(1)}, u32[]{:S(2)}, u32[]{:S(2)}) collective-permute-start(bf16[352,1024]{1,0:T(8,128)(2,1)S(1)} %get-tuple-element.20), channel_id=1, source_target_pairs={{0,12},{4,0},{8,4},{12,8},{1,13},{5,1},{9,5},{13,9},{2,14},{6,2},{... | collective-permute-start | bytes 2162696 | tf_op jit(solution)/shard_map/ppermute | solution.py:108
  152.0 30.3 %collective-permute-start.14 = (bf16[352,1024]{1,0:T(8,128)(2,1)S(1)}, bf16[352,1024]{1,0:T(8,128)(2,1)S(1)}, u32[]{:S(2)}, u32[]{:S(2)}) collective-permute-start(bf16[352,1024]{1,0:T(8,128)(2,1)S(1)} %get-tuple-element.22), channel_id=1, source_target_pairs={{0,8},{4,12},{8,0},{12,4},{1,9},{5,13},{9,1},{13,5},{2,10},{6,14},... | collective-permute-start | bytes 2162696 | tf_op jit(solution)/shard_map/ppermute | solution.py:108
  152.1 44.5 %copy-start.14 = (s32[88,2]{0,1:T(2,128)S(1)}, s32[88,2]{0,1:T(2,128)}, u32[]{:S(2)}) copy-start(s32[88,2]{0,1:T(2,128)} %param.15) | copy-start | bytes 2116
  152.1 45.0 %copy-start.13 = (f32[1024,16]{0,1:T(8,128)S(1)}, f32[1024,16]{0,1:T(8,128)}, u32[]{:S(2)}) copy-start(f32[1024,16]{0,1:T(8,128)} %param.14) | copy-start | bytes 196612
  152.1 34.5 %collective-permute-start.15 = (bf16[352,1024]{1,0:T(8,128)(2,1)S(1)}, bf16[352,1024]{1,0:T(8,128)(2,1)S(1)}, u32[]{:S(2)}, u32[]{:S(2)}) collective-permute-start(bf16[352,1024]{1,0:T(8,128)(2,1)S(1)} %get-tuple-element.21), channel_id=1, source_target_pairs={{0,4},{4,8},{8,12},{12,0},{1,5},{5,9},{9,13},{13,1},{2,6},{6,10},{... | collective-permute-start | bytes 2162696 | tf_op jit(solution)/shard_map/ppermute | solution.py:108
  189.4 29.9 %all-to-all-start.2 = ((bf16[16,22,1024]{2,1,0:T(8,128)(2,1)}), bf16[16,22,1024]{2,1,0:T(8,128)(2,1)S(1)}, u32[]{:S(2)}, u32[]{:S(2)}) async-start(bf16[16,22,1024]{2,1,0:T(8,128)(2,1)} %reshape.240), calls=%async_computation.2 | async-start | bytes 1572864 | tf_op jit(solution)/shard_map/all_to_all | solution.py:112
  199.7 20.4 %copy-start.16 = (f32[1024]{0:T(1024)S(1)}, f32[1024]{0:T(1024)}, u32[]{:S(2)}) copy-start(f32[1024]{0:T(1024)} %param.19) | copy-start | bytes 12292
  220.0 0.8 copy-start.6

commit v5 on v4

--- a/solution.py
+++ b/solution.py
@@ -71,7 +71,6 @@
     )
 
     stacked = jnp.concatenate([w_gate, w_upward, w_downward], axis=0)
-    stacked, near = lax.optimization_barrier((stacked, near))
     pieces = [stacked] + [
         lax.ppermute(stacked, "tx", shift_pairs(n_tx, s)) for s in range(1, n_tx)
     ]
@@ -94,7 +93,6 @@
     send_slots = jnp.dot(placing, repeated, preferred_element_type=jnp.float32).astype(jnp.bfloat16)
     send_slots = send_slots.reshape(n_expert, capacity, width)
     received = lax.all_to_all(send_slots, "expert", split_axis=0, concat_axis=0, tiled=True)
-    received, *pieces = lax.optimization_barrier((received, *pieces))
     weights = jnp.concatenate(pieces, axis=1)
     gate_rows, up_rows, down_rows = weights[0], weights[1], weights[2]
     slot_total = n_expert * capacity

time: 221 us -> 189 us (0.86)
  waiting for transfers between devices: 140 us -> 112 us
  starting transfers between devices: 44.6 us -> 41.6 us
  local copies, waits for them, and re-layouts: 15.7 us -> 13.3 us
    ppermute x3, waiting for transfers between devices: 29.1 us -> 4.12 us  [per_device(): lax.ppermute(rows_in, 'ty', shift_pairs(n_ty, s))]
    ppermute x3, waiting for transfers between devices: 45.8 us -> 23.5 us  [per_device(): lax.ppermute(stacked, 'tx', shift_pairs(n_tx, s))]
    all_to_all x1, waiting for transfers between devices: 0.01 us -> 18.3 us  [per_device(): lax.all_to_all(send_slots, 'expert', split_axis=0, concat_axis=0, tiled=T...]
    all_to_all x1, starting transfers between devices: 7.21 us -> 4.59 us  [per_device(): lax.all_to_all(expert_out, 'expert', split_axis=0, concat_axis=0, tiled=T...]
    unnamed x41 -> x32, local copies, waits for them, and re-layouts: 4.72 us -> 3.56 us
  transfers between devices with their start and end apart: 19 -> 19, of which waited for: 11 -> 12; matrix products, arithmetic and copies ran while one was open for 4% -> 6% of each run, Pallas kernels for 0% -> 0%
where the time goes in v5:
time: 189 us
  waiting for transfers between devices  112 us (59%)
  starting transfers between devices  41.6 us (22%)
  matrix products  14.7 us (8%)
  local copies, waits for them, and re-layouts  13.3 us (7%)
  other arithmetic  6.33 us (3%)
    ppermute x3, waiting for transfers between devices, per_device(): back = lax.ppermute(partial[s], 'ty', shift_pairs(n_ty, -s))  34.3 us
    ppermute x3, waiting for transfers between devices, per_device(): lax.ppermute(stacked, 'tx', shift_pairs(n_tx, s))  23.5 us
    all_to_all x1, waiting for transfers between devices, per_device(): lax.all_to_all(expert_out, 'expert', split_axis=0, concat_axis=0, tiled=T...  19.4 us
    all_to_all x1, waiting for transfers between devices, per_device(): lax.all_to_all(send_slots, 'expert', split_axis=0, concat_axis=0, tiled=T...  18.3 us
    ppermute x3, waiting for transfers between devices, per_device(): lax.ppermute(near, 'ty', shift_pairs(n_ty, s))  11.7 us
    all_to_all x1, starting transfers between devices, per_device(): lax.all_to_all(send_slots, 'expert', split_axis=0, concat_axis=0, tiled=T...  8.85 us
    dot_general x1, matrix products, expert_block(): return jnp.dot(hid, down_rows, preferred_element_type=jnp.float32)  8.6 us
    ppermute x3, starting transfers between devices, per_device(): lax.ppermute(my_cols, 'tx', shift_pairs(n_tx, s))  5.63 us
  transfers between devices with their start and end apart: 19, of which 12 were waited for; matrix products, arithmetic and copies ran while one was open for 6% of the time, Pallas kernels for 0%

profile of v5, /device:TPU:1, one launch (start us, length us, event | category | flops | bytes accessed | tf_op | source)
XLA Modules:
  0.0 188.8 jit_solution(5358903560013502727)
XLA Ops:
  0.7 0.9 copy-done
  1.5 2.0 %collective-permute-start = (bf16[64,512]{1,0:T(8,128)(2,1)S(1)}, bf16[64,512]{1,0:T(8,128)(2,1)S(1)}, u32[]{:S(2)}, u32[]{:S(2)}) collective-permute-start(bf16[64,512]{1,0:T(8,128)(2,1)S(1)} %constant_dynamic-slice_fusion), channel_id=1, source_target_pairs={{0,1},{1,2},{2,3},{3,0},{4,5},{5,6},{6,7},{7,4},{8,9},{9,10},{10,1... | collective-permute-start | bytes 196616 | tf_op jit(solution)/shard_map/ppermute | solution.py:54
  3.6 2.5 %collective-permute-start.1 = (bf16[64,512]{1,0:T(8,128)(2,1)S(1)}, bf16[64,512]{1,0:T(8,128)(2,1)S(1)}, u32[]{:S(2)}, u32[]{:S(2)}) collective-permute-start(bf16[64,512]{1,0:T(8,128)(2,1)S(1)} %constant_dynamic-slice_fusion), channel_id=1, source_target_pairs={{0,2},{1,3},{2,0},{3,1},{4,6},{5,7},{6,4},{7,5},{8,10},{9,11},{10,... | collective-permute-start | bytes 196616 | tf_op jit(solution)/shard_map/ppermute | solution.py:54
  6.0 1.2 collective-permute-start.2
  7.2 1.4 all_to_all.18
  8.6 0.8 copy.26
  9.4 4.3 %all-to-all-start = ((bf16[64,16,88]{2,0,1:T(8,128)(2,1)}), bf16[64,16,88]{2,0,1:T(8,128)(2,1)S(1)}, u32[]{:S(2)}, u32[]{:S(2)}) async-start(bf16[64,16,88]{2,0,1:T(8,128)(2,1)} %copy.26), calls=%async_computation | async-start | bytes 524288 | tf_op jit(solution)/shard_map/all_to_all | solution.py:59
  13.7 0.8 copy.31
  14.5 0.1 reshape.234
  14.7 0.6 reduce-window.6
  15.3 0.2 slice_reduce_fusion
  15.6 1.4 collective-permute-start.3
  17.0 2.4 %collective-permute-start.4 = (bf16[4,64,512]{2,1,0:T(8,128)(2,1)S(1)}, bf16[4,64,512]{2,1,0:T(8,128)(2,1)S(1)}, u32[]{:S(2)}, u32[]{:S(2)}) collective-permute-start(bf16[4,64,512]{2,1,0:T(8,128)(2,1)S(1)} %get-tuple-element.12), channel_id=1, source_target_pairs={{0,8},{4,12},{8,0},{12,4},{1,9},{5,13},{9,1},{13,5},{2,10},{6,14},... | collective-permute-start | bytes 786440 | tf_op jit(solution)/shard_map/ppermute | solution.py:56
  19.4 1.2 collective-permute-start.5
  20.7 6.0 %collective-permute-done.3 = bf16[4,64,512]{2,1,0:T(8,128)(2,1)S(1)} collective-permute-done((bf16[4,64,512]{2,1,0:T(8,128)(2,1)S(1)}, bf16[4,64,512]{2,1,0:T(8,128)(2,1)S(1)}, u32[]{:S(2)}, u32[]{:S(2)}) %collective-permute-start.3) | collective-permute-done | bytes 262176 | tf_op jit(solution)/shard_map/ppermute | solution.py:56
  26.6 5.7 %collective-permute-done.4 = bf16[4,64,512]{2,1,0:T(8,128)(2,1)S(1)} collective-permute-done((bf16[4,64,512]{2,1,0:T(8,128)(2,1)S(1)}, bf16[4,64,512]{2,1,0:T(8,128)(2,1)S(1)}, u32[]{:S(2)}, u32[]{:S(2)}) %collective-permute-start.4) | collective-permute-done | bytes 262176 | tf_op jit(solution)/shard_map/ppermute | solution.py:56
  32.3 0.1 pad_maximum_fusion.1
  32.5 1.6 collective-permute-start.6
  34.3 0.6 gather_fusion
  35.0 0.6 gather_fusion.1
  35.6 0.4 convolution_bitcast_fusion.1
  36.0 0.5 collective-permute-done.6
  36.4 0.4 convolution_bitcast_fusion
  36.8 0.2 fusion.20
  37.1 0.2 broadcast_in_dim.40
  37.3 0.1 reshape.237
  37.5 0.4 convolution_convert_fusion.1
  37.8 1.1 reshape.238
  38.9 8.8 %all-to-all-start.1 = ((bf16[16,22,1024]{2,1,0:T(8,128)(2,1)}), bf16[16,22,1024]{2,1,0:T(8,128)(2,1)S(1)}, u32[]{:S(2)}, u32[]{:S(2)}) async-start(bf16[16,22,1024]{2,1,0:T(8,128)(2,1)} %reshape.238), calls=%async_computation.1 | async-start | bytes 1572864 | tf_op jit(solution)/shard_map/all_to_all | solution.py:95
  47.9 0.9 collective-permute-start.10
  48.8 2.2 %collective-permute-start.11 = (bf16[3,176,1024]{2,1,0:T(8,128)(2,1)S(1)}, bf16[3,176,1024]{2,1,0:T(8,128)(2,1)}, u32[]{:S(2)}, u32[]{:S(2)}) collective-permute-start(bf16[3,176,1024]{2,1,0:T(8,128)(2,1)S(1)} %constant_dynamic-update-slice_fusion.4), channel_id=1, source_target_pairs={{0,2},{1,3},{2,0},{3,1},{4,6},{5,7},{6,4},{7,5},{8,10},{9,11},{10,... | collective-permute-start | bytes 3244040 | tf_op jit(solution)/shard_map/ppermute | solution.py:75
  51.0 1.2 collective-permute-start.12
  52.2 18.3 %all-to-all-done.1 = bf16[16,22,1024]{2,1,0:T(8,128)(2,1)S(1)} async-done(((bf16[16,22,1024]{2,1,0:T(8,128)(2,1)}), bf16[16,22,1024]{2,1,0:T(8,128)(2,1)S(1)}, u32[]{:S(2)}, u32[]{:S(2)}) %all-to-all-start.1) | async-done | bytes 720928 | tf_op jit(solution)/shard_map/all_to_all | solution.py:95
  70.5 0.2 reshape.239
  70.7 0.5 collective-permute-start.7
  71.2 2.1 %collective-permute-start.8 = (bf16[352,1024]{1,0:T(8,128)(2,1)S(1)}, bf16[352,1024]{1,0:T(8,128)(2,1)S(1)}, u32[]{:S(2)}, u32[]{:S(2)}) collective-permute-start(bf16[352,1024]{1,0:T(8,128)(2,1)S(1)} %reshape.239), channel_id=1, source_target_pairs={{0,8},{4,12},{8,0},{12,4},{1,9},{5,13},{9,1},{13,5},{2,10},{6,14},... | collective-permute-start | bytes 2162696 | tf_op jit(solution)/shard_map/ppermute | solution.py:100
  73.3 1.3 collective-permute-done.10
  74.6 1.3 collective-permute-start.9
  76.0 22.2 %collective-permute-done.11 = bf16[3,176,1024]{2,1,0:T(8,128)(2,1)} collective-permute-done((bf16[3,176,1024]{2,1,0:T(8,128)(2,1)S(1)}, bf16[3,176,1024]{2,1,0:T(8,128)(2,1)}, u32[]{:S(2)}, u32[]{:S(2)}) %collective-permute-start.11) | collective-permute-done | bytes 1081376 | tf_op jit(solution)/shard_map/ppermute | solution.py:75
  98.1 2.2 %pad_maximum_fusion = bf16[3,704,1024]{2,1,0:T(8,128)(2,1)S(1)} fusion(bf16[3,176,1024]{2,1,0:T(8,128)(2,1)} %collective-permute-done.12, bf16[3,176,1024]{2,1,0:T(8,128)(2,1)} %collective-permute-done.11, bf16[3,176,1024]{2,1,0:T(8,128)(2,1)} %collective-permute-done.10, bf16[3,176,1024]{2,1,0:T(8,128)(2,1)S(1)} %constant_dynamic-update-slice_fusion.4), kind=kLoop, calls=%fused_computation.4 | loop fusion | flops 17301504 | bytes 8650752 | tf_op jit(solution)/shard_map/concatenate | solution.py:96
  100.4 3.3 %collective-permute-done.7 = bf16[352,1024]{1,0:T(8,128)(2,1)S(1)} collective-permute-done((bf16[352,1024]{1,0:T(8,128)(2,1)S(1)}, bf16[352,1024]{1,0:T(8,128)(2,1)S(1)}, u32[]{:S(2)}, u32[]{:S(2)}) %collective-permute-start.7) | collective-permute-done | bytes 720928 | tf_op jit(solution)/shard_map/ppermute | solution.py:100
  103.8 0.8 collective-permute-done.9
  104.7 1.6 copy-done.7
  106.3 4.4 %fusion.15 = f32[1408,704]{0,1:T(8,128)} fusion(bf16[1408,1024]{1,0:T(8,128)(2,1)S(1)} %constant_dynamic-update-slice_fusion, bf16[3,704,1024]{2,1,0:T(8,128)(2,1)S(1)} %pad_maximum_fusion), kind=kOutput, calls=%fused_computation.23 | convolution fusion | flops 2030043136 | bytes 8290304 | tf_op jit(solution)/shard_map/dot_general | solution.py:20
  110.7 8.6 %convolution_convert_fusion = bf16[1408,1024]{1,0:T(8,128)(2,1)S(1)} fusion(f32[1408,704]{0,1:T(8,128)} %fusion.15, bf16[3,704,1024]{2,1,0:T(8,128)(2,1)} %copy-done.1, bf16[1408,1024]{1,0:T(8,128)(2,1)} %copy-done.7), kind=kOutput, calls=%fused_computation.14 | convolution fusion | flops 4071440384 | bytes 12615680 | tf_op jit(solution)/shard_map/dot_general | solution.py:27
  119.4 0.2 fusion.48
  119.5 2.6 %collective-permute-start.13 = (bf16[352,1024]{1,0:T(8,128)(2,1)S(1)}, bf16[352,1024]{1,0:T(8,128)(2,1)S(1)}, u32[]{:S(2)}, u32[]{:S(2)}) collective-permute-start(bf16[352,1024]{1,0:T(8,128)(2,1)S(1)} %get-tuple-element.8), channel_id=1, source_target_pairs={{0,12},{4,0},{8,4},{12,8},{1,13},{5,1},{9,5},{13,9},{2,14},{6,2},{... | collective-permute-start | bytes 2162696 | tf_op jit(solution)/shard_map/ppermute | solution.py:106
  122.2 0.4 collective-permute-start.14
  122.6 0.3 collective-permute-start.15
  122.8 14.6 %collective-permute-done.13 = bf16[352,1024]{1,0:T(8,128)(2,1)S(1)} collective-permute-done((bf16[352,1024]{1,0:T(8,128)(2,1)S(1)}, bf16[352,1024]{1,0:T(8,128)(2,1)S(1)}, u32[]{:S(2)}, u32[]{:S(2)}) %collective-permute-start.13) | collective-permute-done | bytes 720928 | tf_op jit(solution)/shard_map/ppermute | solution.py:106
  137.4 3.2 %collective-permute-done.14 = bf16[352,1024]{1,0:T(8,128)(2,1)S(1)} collective-permute-done((bf16[352,1024]{1,0:T(8,128)(2,1)S(1)}, bf16[352,1024]{1,0:T(8,128)(2,1)S(1)}, u32[]{:S(2)}, u32[]{:S(2)}) %collective-permute-start.14) | collective-permute-done | bytes 720928 | tf_op jit(solution)/shard_map/ppermute | solution.py:106
  140.6 16.5 %collective-permute-done.15 = bf16[352,1024]{1,0:T(8,128)(2,1)S(1)} collective-permute-done((bf16[352,1024]{1,0:T(8,128)(2,1)S(1)}, bf16[352,1024]{1,0:T(8,128)(2,1)S(1)}, u32[]{:S(2)}, u32[]{:S(2)}) %collective-permute-start.15) | collective-permute-done | bytes 720928 | tf_op jit(solution)/shard_map/ppermute | solution.py:106
  157.2 1.7 add_convert_fusion
  158.8 1.1 reshape.240
  159.9 4.6 %all-to-all-start.2 = ((bf16[16,22,1024]{2,1,0:T(8,128)(2,1)}), bf16[16,22,1024]{2,1,0:T(8,128)(2,1)S(1)}, u32[]{:S(2)}, u32[]{:S(2)}) async-start(bf16[16,22,1024]{2,1,0:T(8,128)(2,1)} %reshape.240), calls=%async_computation.2 | async-start | bytes 1572864 | tf_op jit(solution)/shard_map/all_to_all | solution.py:110
  164.6 0.1 reshape.259
  165.0 0.3 fusion.49
  165.3 2.3 %gather_fusion.2 = f32[176]{0:T(256)S(1)} fusion(f32[88,16]{0,1:T(8,128)S(1)} %fusion.32, s32[176]{0:T(256)S(1)} %reshape.259), kind=kCustom, calls=%fused_computation.2 | custom fusion | bytes 2816 | tf_op jit(solution)/shard_map/jit(take_along_axis)/gather | solution.py:82
  167.6 0.1 reshape.262
  167.9 19.4 %all-to-all-done.2 = bf16[16,22,1024]{2,1,0:T(8,128)(2,1)S(1)} async-done(((bf16[16,22,1024]{2,1,0:T(8,128)(2,1)}), bf16[16,22,1024]{2,1,0:T(8,128)(2,1)S(1)}, u32[]{:S(2)}, u32[]{:S(2)}) %all-to-all-start.2) | async-done | bytes 720928 | tf_op jit(solution)/shard_map/all_to_all | solution.py:110
  187.2 0.2 reshape.272
  187.5 0.4 fusion.16
  187.8 0.1 fusion.17
  188.0 0.8 fusion.19
  (67 shorter events, 1.3 us)
Async XLA Ops:
  0.6 0.9 copy-start
  1.5 13.9 %collective-permute-start = (bf16[64,512]{1,0:T(8,128)(2,1)S(1)}, bf16[64,512]{1,0:T(8,128)(2,1)S(1)}, u32[]{:S(2)}, u32[]{:S(2)}) collective-permute-start(bf16[64,512]{1,0:T(8,128)(2,1)S(1)} %constant_dynamic-slice_fusion), channel_id=1, source_target_pairs={{0,1},{1,2},{2,3},{3,0},{4,5},{5,6},{6,7},{7,4},{8,9},{9,10},{10,1... | collective-permute-start | bytes 196616 | tf_op jit(solution)/shard_map/ppermute | solution.py:54
  3.6 11.9 %collective-permute-start.1 = (bf16[64,512]{1,0:T(8,128)(2,1)S(1)}, bf16[64,512]{1,0:T(8,128)(2,1)S(1)}, u32[]{:S(2)}, u32[]{:S(2)}) collective-permute-start(bf16[64,512]{1,0:T(8,128)(2,1)S(1)} %constant_dynamic-slice_fusion), channel_id=1, source_target_pairs={{0,2},{1,3},{2,0},{3,1},{4,6},{5,7},{6,4},{7,5},{8,10},{9,11},{10,... | collective-permute-start | bytes 196616 | tf_op jit(solution)/shard_map/ppermute | solution.py:54
  6.0 9.5 %collective-permute-start.2 = (bf16[64,512]{1,0:T(8,128)(2,1)S(1)}, bf16[64,512]{1,0:T(8,128)(2,1)S(1)}, u32[]{:S(2)}, u32[]{:S(2)}) collective-permute-start(bf16[64,512]{1,0:T(8,128)(2,1)S(1)} %constant_dynamic-slice_fusion), channel_id=1, source_target_pairs={{0,3},{1,0},{2,1},{3,2},{4,7},{5,4},{6,5},{7,6},{8,11},{9,8},{10,9... | collective-permute-start | bytes 196616 | tf_op jit(solution)/shard_map/ppermute | solution.py:54
  9.4 24.9 %all-to-all-start = ((bf16[64,16,88]{2,0,1:T(8,128)(2,1)}), bf16[64,16,88]{2,0,1:T(8,128)(2,1)S(1)}, u32[]{:S(2)}, u32[]{:S(2)}) async-start(bf16[64,16,88]{2,0,1:T(8,128)(2,1)} %copy.26), calls=%async_computation | async-start | bytes 524288 | tf_op jit(solution)/shard_map/all_to_all | solution.py:59
  15.6 11.0 %collective-permute-start.3 = (bf16[4,64,512]{2,1,0:T(8,128)(2,1)S(1)}, bf16[4,64,512]{2,1,0:T(8,128)(2,1)S(1)}, u32[]{:S(2)}, u32[]{:S(2)}) collective-permute-start(bf16[4,64,512]{2,1,0:T(8,128)(2,1)S(1)} %get-tuple-element.12), channel_id=1, source_target_pairs={{0,4},{4,8},{8,12},{12,0},{1,5},{5,9},{9,13},{13,1},{2,6},{6,10},{... | collective-permute-start | bytes 786440 | tf_op jit(solution)/shard_map/ppermute | solution.py:56
  17.0 15.3 %collective-permute-start.4 = (bf16[4,64,512]{2,1,0:T(8,128)(2,1)S(1)}, bf16[4,64,512]{2,1,0:T(8,128)(2,1)S(1)}, u32[]{:S(2)}, u32[]{:S(2)}) collective-permute-start(bf16[4,64,512]{2,1,0:T(8,128)(2,1)S(1)} %get-tuple-element.12), channel_id=1, source_target_pairs={{0,8},{4,12},{8,0},{12,4},{1,9},{5,13},{9,1},{13,5},{2,10},{6,14},... | collective-permute-start | bytes 786440 | tf_op jit(solution)/shard_map/ppermute | solution.py:56
  19.4 12.9 %collective-permute-start.5 = (bf16[4,64,512]{2,1,0:T(8,128)(2,1)S(1)}, bf16[4,64,512]{2,1,0:T(8,128)(2,1)S(1)}, u32[]{:S(2)}, u32[]{:S(2)}) collective-permute-start(bf16[4,64,512]{2,1,0:T(8,128)(2,1)S(1)} %get-tuple-element.12), channel_id=1, source_target_pairs={{0,12},{4,0},{8,4},{12,8},{1,13},{5,1},{9,5},{13,9},{2,14},{6,2},{... | collective-permute-start | bytes 786440 | tf_op jit(solution)/shard_map/ppermute | solution.py:56
  32.3 4.5 %copy-start.8 = (bf16[88,1024]{1,0:T(8,128)(2,1)S(1)}, bf16[88,1024]{1,0:T(8,128)(2,1)}, u32[]{:S(2)}) copy-start(bf16[88,1024]{1,0:T(8,128)(2,1)} %param.10) | copy-start | bytes 540676
  32.5 4.5 %copy-start.11 = (f32[1024]{0:T(1024)S(1)}, f32[1024]{0:T(1024)}, u32[]{:S(2)}) copy-start(f32[1024]{0:T(1024)} %param.13) | copy-start | bytes 12292
  32.5 3.9 %collective-permute-start.6 = (bf16[4,4,64,512]{3,2,1,0:T(8,128)(2,1)S(1)}, bf16[4,4,64,512]{3,2,1,0:T(8,128)(2,1)S(1)}, u32[]{:S(2)}, u32[]{:S(2)}) collective-permute-start(bf16[4,4,64,512]{3,2,1,0:T(8,128)(2,1)S(1)} %pad_maximum_fusion.1), channel_id=1, source_target_pairs={{0,16},{16,0},{32,48},{48,32},{64,80},{80,64},{96,112},{112,96},{1... | collective-permute-start | bytes 3145736 | tf_op jit(solution)/shard_map/ppermute | solution.py:58
  37.0 10.8 %copy-start.4 = (bf16[1,176,1024]{2,1,0:T(8,128)(2,1)S(1)}, bf16[1,176,1024]{2,1,0:T(8,128)(2,1)}, u32[]{:S(2)}) copy-start(bf16[1,176,1024]{2,1,0:T(8,128)(2,1)} %param.16) | copy-start | bytes 1081348
  37.3 10.5 %copy-start.5 = (bf16[1,176,1024]{2,1,0:T(8,128)(2,1)S(1)}, bf16[1,176,1024]{2,1,0:T(8,128)(2,1)}, u32[]{:S(2)}) copy-start(bf16[1,176,1024]{2,1,0:T(8,128)(2,1)} %param.17) | copy-start | bytes 1081348
  37.5 10.4 %copy-start.6 = (bf16[1,176,1024]{2,1,0:T(8,128)(2,1)S(1)}, bf16[1,176,1024]{2,1,0:T(8,128)(2,1)}, u32[]{:S(2)}) copy-start(bf16[1,176,1024]{2,1,0:T(8,128)(2,1)} %param.18) | copy-start | bytes 1081348
  38.9 31.6 %all-to-all-start.1 = ((bf16[16,22,1024]{2,1,0:T(8,128)(2,1)}), bf16[16,22,1024]{2,1,0:T(8,128)(2,1)S(1)}, u32[]{:S(2)}, u32[]{:S(2)}) async-start(bf16[16,22,1024]{2,1,0:T(8,128)(2,1)} %reshape.238), calls=%async_computation.1 | async-start | bytes 1572864 | tf_op jit(solution)/shard_map/all_to_all | solution.py:95
  47.9 26.7 %collective-permute-start.10 = (bf16[3,176,1024]{2,1,0:T(8,128)(2,1)S(1)}, bf16[3,176,1024]{2,1,0:T(8,128)(2,1)}, u32[]{:S(2)}, u32[]{:S(2)}) collective-permute-start(bf16[3,176,1024]{2,1,0:T(8,128)(2,1)S(1)} %constant_dynamic-update-slice_fusion.4), channel_id=1, source_target_pairs={{0,1},{1,2},{2,3},{3,0},{4,5},{5,6},{6,7},{7,4},{8,9},{9,10},{10,1... | collective-permute-start | bytes 3244040 | tf_op jit(solution)/shard_map/ppermute | solution.py:75
  48.8 49.3 %collective-permute-start.11 = (bf16[3,176,1024]{2,1,0:T(8,128)(2,1)S(1)}, bf16[3,176,1024]{2,1,0:T(8,128)(2,1)}, u32[]{:S(2)}, u32[]{:S(2)}) collective-permute-start(bf16[3,176,1024]{2,1,0:T(8,128)(2,1)S(1)} %constant_dynamic-update-slice_fusion.4), channel_id=1, source_target_pairs={{0,2},{1,3},{2,0},{3,1},{4,6},{5,7},{6,4},{7,5},{8,10},{9,11},{10,... | collective-permute-start | bytes 3244040 | tf_op jit(solution)/shard_map/ppermute | solution.py:75
  51.0 47.1 %collective-permute-start.12 = (bf16[3,176,1024]{2,1,0:T(8,128)(2,1)S(1)}, bf16[3,176,1024]{2,1,0:T(8,128)(2,1)}, u32[]{:S(2)}, u32[]{:S(2)}) collective-permute-start(bf16[3,176,1024]{2,1,0:T(8,128)(2,1)S(1)} %constant_dynamic-update-slice_fusion.4), channel_id=1, source_target_pairs={{0,3},{1,0},{2,1},{3,2},{4,7},{5,4},{6,5},{7,6},{8,11},{9,8},{10,9... | collective-permute-start | bytes 3244040 | tf_op jit(solution)/shard_map/ppermute | solution.py:75
  70.7 33.0 %collective-permute-start.7 = (bf16[352,1024]{1,0:T(8,128)(2,1)S(1)}, bf16[352,1024]{1,0:T(8,128)(2,1)S(1)}, u32[]{:S(2)}, u32[]{:S(2)}) collective-permute-start(bf16[352,1024]{1,0:T(8,128)(2,1)S(1)} %reshape.239), channel_id=1, source_target_pairs={{0,4},{4,8},{8,12},{12,0},{1,5},{5,9},{9,13},{13,1},{2,6},{6,10},{... | collective-permute-start | bytes 2162696 | tf_op jit(solution)/shard_map/ppermute | solution.py:100
  71.2 32.6 %collective-permute-start.8 = (bf16[352,1024]{1,0:T(8,128)(2,1)S(1)}, bf16[352,1024]{1,0:T(8,128)(2,1)S(1)}, u32[]{:S(2)}, u32[]{:S(2)}) collective-permute-start(bf16[352,1024]{1,0:T(8,128)(2,1)S(1)} %reshape.239), channel_id=1, source_target_pairs={{0,8},{4,12},{8,0},{12,4},{1,9},{5,13},{9,1},{13,5},{2,10},{6,14},... | collective-permute-start | bytes 2162696 | tf_op jit(solution)/shard_map/ppermute | solution.py:100
  74.6 30.0 %collective-permute-start.9 = (bf16[352,1024]{1,0:T(8,128)(2,1)S(1)}, bf16[352,1024]{1,0:T(8,128)(2,1)S(1)}, u32[]{:S(2)}, u32[]{:S(2)}) collective-permute-start(bf16[352,1024]{1,0:T(8,128)(2,1)S(1)} %reshape.239), channel_id=1, source_target_pairs={{0,12},{4,0},{8,4},{12,8},{1,13},{5,1},{9,5},{13,9},{2,14},{6,2},{... | collective-permute-start | bytes 2162696 | tf_op jit(solution)/shard_map/ppermute | solution.py:100
  100.3 4.4 %copy-start.1 = (bf16[3,704,1024]{2,1,0:T(8,128)(2,1)}, bf16[3,704,1024]{2,1,0:T(8,128)(2,1)S(1)}, u32[]{:S(2)}) copy-start(bf16[3,704,1024]{2,1,0:T(8,128)(2,1)S(1)} %pad_maximum_fusion) | copy-start | bytes 12976132
  104.7 1.7 copy-start.7
  119.3 21.3 %copy-start.2 = (bf16[1408,1024]{1,0:T(8,128)(2,1)}, bf16[1408,1024]{1,0:T(8,128)(2,1)S(1)}, u32[]{:S(2)}) copy-start(bf16[1408,1024]{1,0:T(8,128)(2,1)S(1)} %convolution_convert_fusion) | copy-start | bytes 8650756
  119.5 17.9 %collective-permute-start.13 = (bf16[352,1024]{1,0:T(8,128)(2,1)S(1)}, bf16[352,1024]{1,0:T(8,128)(2,1)S(1)}, u32[]{:S(2)}, u32[]{:S(2)}) collective-permute-start(bf16[352,1024]{1,0:T(8,128)(2,1)S(1)} %get-tuple-element.8), channel_id=1, source_target_pairs={{0,12},{4,0},{8,4},{12,8},{1,13},{5,1},{9,5},{13,9},{2,14},{6,2},{... | collective-permute-start | bytes 2162696 | tf_op jit(solution)/shard_map/ppermute | solution.py:106
  122.2 18.5 %collective-permute-start.14 = (bf16[352,1024]{1,0:T(8,128)(2,1)S(1)}, bf16[352,1024]{1,0:T(8,128)(2,1)S(1)}, u32[]{:S(2)}, u32[]{:S(2)}) collective-permute-start(bf16[352,1024]{1,0:T(8,128)(2,1)S(1)} %get-tuple-element.10), channel_id=1, source_target_pairs={{0,8},{4,12},{8,0},{12,4},{1,9},{5,13},{9,1},{13,5},{2,10},{6,14},... | collective-permute-start | bytes 2162696 | tf_op jit(solution)/shard_map/ppermute | solution.py:106
  122.5 42.0 %copy-start.10 = (s32[88,2]{0,1:T(2,128)S(1)}, s32[88,2]{0,1:T(2,128)}, u32[]{:S(2)}) copy-start(s32[88,2]{0,1:T(2,128)} %param.15) | copy-start | bytes 2116
  122.5 42.5 %copy-start.9 = (f32[1024,16]{0,1:T(8,128)S(1)}, f32[1024,16]{0,1:T(8,128)}, u32[]{:S(2)}) copy-start(f32[1024,16]{0,1:T(8,128)} %param.14) | copy-start | bytes 196612
  122.6 34.6 %collective-permute-start.15 = (bf16[352,1024]{1,0:T(8,128)(2,1)S(1)}, bf16[352,1024]{1,0:T(8,128)(2,1)S(1)}, u32[]{:S(2)}, u32[]{:S(2)}) collective-permute-start(bf16[352,1024]{1,0:T(8,128)(2,1)S(1)} %get-tuple-element.9), channel_id=1, source_target_pairs={{0,4},{4,8},{8,12},{12,0},{1,5},{5,9},{9,13},{13,1},{2,6},{6,10},{... | collective-permute-start | bytes 2162696 | tf_op jit(solution)/shard_map/ppermute | solution.py:106
  159.9 27.3 %all-to-all-start.2 = ((bf16[16,22,1024]{2,1,0:T(8,128)(2,1)}), bf16[16,22,1024]{2,1,0:T(8,128)(2,1)S(1)}, u32[]{:S(2)}, u32[]{:S(2)}) async-start(bf16[16,22,1024]{2,1,0:T(8,128)(2,1)} %reshape.240), calls=%async_computation.2 | async-start | bytes 1572864 | tf_op jit(solution)/shard_map/all_to_all | solution.py:110
  167.6 20.4 %copy-start.12 = (f32[1024]{0:T(1024)S(1)}, f32[1024]{0:T(1024)}, u32[]{:S(2)}) copy-start(f32[1024]{0:T(1024)} %param.19) | copy-start | bytes 12292
  188.0 0.8 copy-start.3

commit v6 on v5

--- a/solution.py
+++ b/solution.py
@@ -92,23 +92,29 @@
     repeated = jnp.repeat(normed, 2, axis=0)
     send_slots = jnp.dot(placing, repeated, preferred_element_type=jnp.float32).astype(jnp.bfloat16)
     send_slots = send_slots.reshape(n_expert, capacity, width)
-    received = lax.all_to_all(send_slots, "expert", split_axis=0, concat_axis=0, tiled=True)
+    slot_total = n_expert * capacity
+    n_chunks = 2
+    chunk = capacity // n_chunks
     weights = jnp.concatenate(pieces, axis=1)
     gate_rows, up_rows, down_rows = weights[0], weights[1], weights[2]
-    slot_total = n_expert * capacity
-    rows_in = received.reshape(slot_total, width)
-    all_rows = [rows_in] + [lax.ppermute(rows_in, "ty", shift_pairs(n_ty, s)) for s in range(1, n_ty)]
-    all_rows = jnp.concatenate(all_rows, axis=0)
-    partial = expert_block(all_rows, gate_rows, up_rows, down_rows).astype(jnp.bfloat16)
-    partial = partial.reshape(n_ty, slot_total, width)
-    expert_sum = partial[0].astype(jnp.float32)
-    for s in range(1, n_ty):
-        back = lax.ppermute(partial[s], "ty", shift_pairs(n_ty, -s))
-        expert_sum = expert_sum + back.astype(jnp.float32)
-    expert_sum = expert_sum.astype(jnp.bfloat16)
-    expert_out = expert_sum.reshape(n_expert, capacity, width)
-    returned = lax.all_to_all(expert_out, "expert", split_axis=0, concat_axis=0, tiled=True)
-    returned = returned.reshape(slot_total, width)
+    returned = []
+    for c in range(n_chunks):
+        part = send_slots[:, c * chunk:(c + 1) * chunk]
+        received = lax.all_to_all(part, "expert", split_axis=0, concat_axis=0, tiled=True)
+        rows_in = received.reshape(n_expert * chunk, width)
+        all_rows = [rows_in] + [
+            lax.ppermute(rows_in, "ty", shift_pairs(n_ty, s)) for s in range(1, n_ty)
+        ]
+        all_rows = jnp.concatenate(all_rows, axis=0)
+        partial = expert_block(all_rows, gate_rows, up_rows, down_rows).astype(jnp.bfloat16)
+        partial = partial.reshape(n_ty, n_expert * chunk, width)
+        expert_sum = partial[0].astype(jnp.float32)
+        for s in range(1, n_ty):
+            back = lax.ppermute(partial[s], "ty", shift_pairs(n_ty, -s))
+            expert_sum = expert_sum + back.astype(jnp.float32)
+        expert_out = expert_sum.astype(jnp.bfloat16).reshape(n_expert, chunk, width)
+        returned.append(lax.all_to_all(expert_out, "expert", split_axis=0, concat_axis=0, tiled=True))
+    returned = jnp.concatenate(returned, axis=1).reshape(slot_total, width)
     per_route = lax.dot_general(
         placing, returned, (((0,), (0,)), ((), ())), preferred_element_type=jnp.float32
     )

time: 189 us -> 223 us (1.18)
  blocking collectives: 0 us -> 25.8 us
  waiting for transfers between devices: 112 us -> 86.9 us
  starting transfers between devices: 41.6 us -> 52.5 us
  matrix products: 14.7 us -> 24.3 us
  local copies, waits for them, and re-layouts: 13.3 us -> 20.1 us
  other arithmetic: 6.33 us -> 10.1 us
    ppermute x3, waiting for transfers between devices: 0.01 us -> 36.1 us  [per_device(): lax.ppermute(my_cols, 'tx', shift_pairs(n_tx, s))]
    ppermute x3 -> x6, waiting for transfers between devices: 34.3 us -> 3.39 us  [per_device(): back = lax.ppermute(partial[s], 'ty', shift_pairs(n_ty, -s))]
    all_to_all x0 -> x1, blocking collectives: none -> 25.8 us  [per_device(): lax.all_to_all(part, 'expert', split_axis=0, concat_axis=0, tiled=True)]
    ppermute x3, waiting for transfers between devices: 23.5 us -> 0.01 us  [per_device(): lax.ppermute(stacked, 'tx', shift_pairs(n_tx, s))]
    all_to_all x1, waiting for transfers between devices: 18.3 us -> 9.16 us  [per_device(): lax.all_to_all(part, 'expert', split_axis=0, concat_axis=0, tiled=True)]
    all_to_all x1 -> x2, starting transfers between devices: 4.59 us -> 12.6 us  [per_device(): lax.all_to_all(expert_out, 'expert', split_axis=0, concat_axis=0, tiled=T...]
    all_to_all x1 -> x2, waiting for transfers between devices: 19.4 us -> 25.1 us  [per_device(): lax.all_to_all(expert_out, 'expert', split_axis=0, concat_axis=0, tiled=T...]
    all_to_all x1, starting transfers between devices: 8.85 us -> 3.47 us  [per_device(): lax.all_to_all(part, 'expert', split_axis=0, concat_axis=0, tiled=True)]
  transfers between devices with their start and end apart: 19 -> 26, of which waited for: 12 -> 10; matrix products, arithmetic and copies ran while one was open for 6% -> 22% of each run, Pallas kernels for 0% -> 0%
where the time goes in v6:
time: 223 us; the launch traced here: 221 us
  waiting for transfers between devices  86.9 us (39%)
  starting transfers between devices  52.5 us (24%)
  blocking collectives  25.8 us (12%)
  matrix products  24.3 us (11%)
  local copies, waits for them, and re-layouts  20.1 us (9%)
  other arithmetic  10.1 us (5%)
    ppermute x3, waiting for transfers between devices, per_device(): lax.ppermute(my_cols, 'tx', shift_pairs(n_tx, s))  36.1 us
    all_to_all x1, blocking collectives, per_device(): lax.all_to_all(part, 'expert', split_axis=0, concat_axis=0, tiled=True)  25.8 us
    all_to_all x2, waiting for transfers between devices, per_device(): lax.all_to_all(expert_out, 'expert', split_axis=0, concat_axis=0, tiled=T...  25.1 us
    dot_general x2, matrix products, expert_block(): return jnp.dot(hid, down_rows, preferred_element_type=jnp.float32)  13.2 us
    all_to_all x2, starting transfers between devices, per_device(): lax.all_to_all(expert_out, 'expert', split_axis=0, concat_axis=0, tiled=T...  12.6 us
    ppermute x3, waiting for transfers between devices, per_device(): lax.ppermute(near, 'ty', shift_pairs(n_ty, s))  9.74 us
    all_to_all x1, waiting for transfers between devices, per_device(): lax.all_to_all(part, 'expert', split_axis=0, concat_axis=0, tiled=True)  9.16 us
    dot_general x2, matrix products, expert_block(): lax.dot_general(inputs, gate_rows, (((1,), (1,)), ((), ())), preferred_el...  8.14 us
  transfers between devices with their start and end apart: 26, of which 10 were waited for; matrix products, arithmetic and copies ran while one was open for 22% of the time, Pallas kernels for 0%

profile of v6, /device:TPU:1, one launch (start us, length us, event | category | flops | bytes accessed | tf_op | source)
XLA Modules:
  0.0 220.9 jit_solution(12511355447670644458)
XLA Ops:
  0.7 1.1 constant_dynamic-update-slice_fusion.6
  1.7 1.0 constant_dynamic-update-slice_fusion.5
  2.8 3.4 %collective-permute-start.12 = (bf16[3,176,1024]{2,1,0:T(8,128)(2,1)S(1)}, bf16[3,176,1024]{2,1,0:T(8,128)(2,1)}, u32[]{:S(2)}, u32[]{:S(2)}) collective-permute-start(bf16[3,176,1024]{2,1,0:T(8,128)(2,1)S(1)} %constant_dynamic-update-slice_fusion.4), channel_id=1, source_target_pairs={{0,3},{1,0},{2,1},{3,2},{4,7},{5,4},{6,5},{7,6},{8,11},{9,8},{10,9... | collective-permute-start | bytes 3244040 | tf_op jit(solution)/shard_map/ppermute | solution.py:75
  6.2 0.5 collective-permute-start.11
  6.7 0.8 collective-permute-start.2
  7.5 1.8 collective-permute-start.1
  9.3 0.8 collective-permute-start
  10.1 0.5 all_to_all.24
  10.6 0.8 copy.26
  11.4 5.9 %all-to-all-start = ((bf16[64,16,88]{2,0,1:T(8,128)(2,1)}), bf16[64,16,88]{2,0,1:T(8,128)(2,1)S(1)}, u32[]{:S(2)}, u32[]{:S(2)}) async-start(bf16[64,16,88]{2,0,1:T(8,128)(2,1)} %copy.26), calls=%async_computation | async-start | bytes 524288 | tf_op jit(solution)/shard_map/all_to_all | solution.py:59
  17.6 0.6 reduce-window.6
  18.4 36.1 %collective-permute-done.2 = bf16[64,512]{1,0:T(8,128)(2,1)S(1)} collective-permute-done((bf16[64,512]{1,0:T(8,128)(2,1)S(1)}, bf16[64,512]{1,0:T(8,128)(2,1)S(1)}, u32[]{:S(2)}, u32[]{:S(2)}) %collective-permute-start.2) | collective-permute-done | bytes 65568 | tf_op jit(solution)/shard_map/ppermute | solution.py:54
  54.6 2.3 %collective-permute-start.5 = (bf16[4,64,512]{2,1,0:T(8,128)(2,1)S(1)}, bf16[4,64,512]{2,1,0:T(8,128)(2,1)S(1)}, u32[]{:S(2)}, u32[]{:S(2)}) collective-permute-start(bf16[4,64,512]{2,1,0:T(8,128)(2,1)S(1)} %get-tuple-element.17), channel_id=1, source_target_pairs={{0,12},{4,0},{8,4},{12,8},{1,13},{5,1},{9,5},{13,9},{2,14},{6,2},{... | collective-permute-start | bytes 786440 | tf_op jit(solution)/shard_map/ppermute | solution.py:56
  56.9 0.3 collective-permute-start.4
  57.3 0.7 collective-permute-start.3
  58.0 3.9 %collective-permute-done.5 = bf16[4,64,512]{2,1,0:T(8,128)(2,1)S(1)} collective-permute-done((bf16[4,64,512]{2,1,0:T(8,128)(2,1)S(1)}, bf16[4,64,512]{2,1,0:T(8,128)(2,1)S(1)}, u32[]{:S(2)}, u32[]{:S(2)}) %collective-permute-start.5) | collective-permute-done | bytes 262176 | tf_op jit(solution)/shard_map/ppermute | solution.py:56
  62.0 2.3 %collective-permute-start.10 = (bf16[3,176,1024]{2,1,0:T(8,128)(2,1)S(1)}, bf16[3,176,1024]{2,1,0:T(8,128)(2,1)}, u32[]{:S(2)}, u32[]{:S(2)}) collective-permute-start(bf16[3,176,1024]{2,1,0:T(8,128)(2,1)S(1)} %constant_dynamic-update-slice_fusion.4), channel_id=1, source_target_pairs={{0,1},{1,2},{2,3},{3,0},{4,5},{5,6},{6,7},{7,4},{8,9},{9,10},{10,1... | collective-permute-start | bytes 3244040 | tf_op jit(solution)/shard_map/ppermute | solution.py:75
  64.3 5.8 %collective-permute-done.3 = bf16[4,64,512]{2,1,0:T(8,128)(2,1)} collective-permute-done((bf16[4,64,512]{2,1,0:T(8,128)(2,1)S(1)}, bf16[4,64,512]{2,1,0:T(8,128)(2,1)}, u32[]{:S(2)}, u32[]{:S(2)}) %collective-permute-start.3) | collective-permute-done | bytes 262176 | tf_op jit(solution)/shard_map/ppermute | solution.py:56
  70.1 1.1 pad_maximum_fusion.1
  71.1 2.9 %collective-permute-start.6 = (bf16[4,4,64,512]{3,2,1,0:T(8,128)(2,1)S(1)}, bf16[4,4,64,512]{3,2,1,0:T(8,128)(2,1)}, u32[]{:S(2)}, u32[]{:S(2)}) collective-permute-start(bf16[4,4,64,512]{3,2,1,0:T(8,128)(2,1)S(1)} %pad_maximum_fusion.1), channel_id=1, source_target_pairs={{0,16},{16,0},{32,48},{48,32},{64,80},{80,64},{96,112},{112,96},{1... | collective-permute-start | bytes 3145736 | tf_op jit(solution)/shard_map/ppermute | solution.py:58
  74.2 0.6 gather_fusion
  74.9 0.6 gather_fusion.1
  75.5 0.4 convolution_bitcast_fusion.1
  75.9 0.6 collective-permute-done.6
  76.5 1.6 convolution_bitcast_fusion
  78.7 0.3 convolution_convert_fusion.2
  79.3 1.0 fusion.60
  80.3 25.8 %all_to_all.36 = bf16[16,11,1024]{2,1,0:T(8,128)(2,1)S(1)} all-to-all(bf16[16,11,1024]{2,1,0:T(8,128)(2,1)S(1)} %get-tuple-element.15), channel_id=1, replica_groups=mesh['expert'=16,'ty'=4,'tx'=4] {'expert'}, dimensions={0} | all-to-all | bytes 720896 | tf_op jit(solution)/shard_map/all_to_all | solution.py:103
  106.1 3.5 %all-to-all-start.1 = ((bf16[16,11,1024]{2,1,0:T(8,128)(2,1)}), bf16[16,11,1024]{2,1,0:T(8,128)(2,1)S(1)}, u32[]{:S(2)}, u32[]{:S(2)}) async-start(bf16[16,11,1024]{2,1,0:T(8,128)(2,1)} %get-tuple-element.14), calls=%async_computation.1 | async-start | bytes 1048576 | tf_op jit(solution)/shard_map/all_to_all | solution.py:103
  110.1 3.7 %pad_maximum_fusion = bf16[3,704,1024]{2,1,0:T(8,128)(2,1)} fusion(bf16[3,176,1024]{2,1,0:T(8,128)(2,1)} %collective-permute-done.12, bf16[3,176,1024]{2,1,0:T(8,128)(2,1)} %collective-permute-done.11, bf16[3,176,1024]{2,1,0:T(8,128)(2,1)} %collective-permute-done.10, bf16[3,176,1024]{2,1,0:T(8,128)(2,1)S(1)} %constant_dynamic-update-slice_fusion.4), kind=kLoop, calls=%fused_computation.3 | loop fusion | flops 17301504 | bytes 8650752 | tf_op jit(solution)/shard_map/concatenate | solution.py:98
  113.8 3.3 %collective-permute-start.17 = (bf16[176,1024]{1,0:T(8,128)(2,1)S(1)}, bf16[176,1024]{1,0:T(8,128)(2,1)S(1)}, u32[]{:S(2)}, u32[]{:S(2)}) collective-permute-start(bf16[176,1024]{1,0:T(8,128)(2,1)S(1)} %reshape.256), channel_id=1, source_target_pairs={{0,8},{4,12},{8,0},{12,4},{1,9},{5,13},{9,1},{13,5},{2,10},{6,14},... | collective-permute-start | bytes 1081352 | tf_op jit(solution)/shard_map/ppermute | solution.py:106
  117.1 9.2 %all-to-all-done.1 = bf16[16,11,1024]{2,1,0:T(8,128)(2,1)S(1)} async-done(((bf16[16,11,1024]{2,1,0:T(8,128)(2,1)}), bf16[16,11,1024]{2,1,0:T(8,128)(2,1)S(1)}, u32[]{:S(2)}, u32[]{:S(2)}) %all-to-all-start.1) | async-done | bytes 360480 | tf_op jit(solution)/shard_map/all_to_all | solution.py:103
  126.5 3.3 %collective-permute-start.8 = (bf16[176,1024]{1,0:T(8,128)(2,1)S(1)}, bf16[176,1024]{1,0:T(8,128)(2,1)S(1)}, u32[]{:S(2)}, u32[]{:S(2)}) collective-permute-start(bf16[176,1024]{1,0:T(8,128)(2,1)S(1)} %reshape.254), channel_id=1, source_target_pairs={{0,8},{4,12},{8,0},{12,4},{1,9},{5,13},{9,1},{13,5},{2,10},{6,14},... | collective-permute-start | bytes 1081352 | tf_op jit(solution)/shard_map/ppermute | solution.py:106
  129.9 0.8 constant_dynamic-update-slice_fusion.3
  130.7 2.8 %collective-permute-done.18 = bf16[176,1024]{1,0:T(8,128)(2,1)S(1)} collective-permute-done((bf16[176,1024]{1,0:T(8,128)(2,1)S(1)}, bf16[176,1024]{1,0:T(8,128)(2,1)S(1)}, u32[]{:S(2)}, u32[]{:S(2)}) %collective-permute-start.18) | collective-permute-done | bytes 360480 | tf_op jit(solution)/shard_map/ppermute | solution.py:106
  133.5 1.2 copy-done.7
  134.7 4.0 %fusion.18 = f32[704,704]{1,0:T(8,128)} fusion(bf16[704,1024]{1,0:T(8,128)(2,1)S(1)} %constant_dynamic-update-slice_fusion.7, bf16[3,704,1024]{2,1,0:T(8,128)(2,1)} %pad_maximum_fusion), kind=kOutput, calls=%fused_computation.31 | convolution fusion | flops 1015021568 | bytes 4866048 | tf_op jit(solution)/shard_map/dot_general | solution.py:20
  138.7 6.0 %convolution_convert_fusion = bf16[704,1024]{1,0:T(8,128)(2,1)S(1)} fusion(bf16[3,704,1024]{2,1,0:T(8,128)(2,1)} %pad_maximum_fusion, f32[704,704]{1,0:T(8,128)} %fusion.18, bf16[704,1024]{1,0:T(8,128)(2,1)} %copy-done.7), kind=kOutput, calls=%fused_computation.24 | convolution fusion | flops 2035720192 | bytes 7929856 | tf_op jit(solution)/shard_map/dot_general | solution.py:27
  144.8 1.0 fusion.59
  145.8 0.3 collective-permute-start.21
  146.0 3.8 %collective-permute-start.20 = (bf16[176,1024]{1,0:T(8,128)(2,1)}, bf16[176,1024]{1,0:T(8,128)(2,1)}, u32[]{:S(2)}, u32[]{:S(2)}) collective-permute-start(bf16[176,1024]{1,0:T(8,128)(2,1)} %get-tuple-element.13), channel_id=1, source_target_pairs={{0,8},{4,12},{8,0},{12,4},{1,9},{5,13},{9,1},{13,5},{2,10},{6,14},... | collective-permute-start | bytes 1081352 | tf_op jit(solution)/shard_map/ppermute | solution.py:113
  149.8 1.0 constant_dynamic-update-slice_fusion.2
  150.9 1.0 constant_dynamic-update-slice_fusion
  151.9 1.1 copy-done.6
  153.0 4.1 %fusion.19 = f32[704,704]{1,0:T(8,128)} fusion(bf16[704,1024]{1,0:T(8,128)(2,1)S(1)} %constant_dynamic-update-slice_fusion, bf16[3,704,1024]{2,1,0:T(8,128)(2,1)} %pad_maximum_fusion), kind=kOutput, calls=%fused_computation.32 | convolution fusion | flops 1015021568 | bytes 4866048 | tf_op jit(solution)/shard_map/dot_general | solution.py:20
  157.1 7.2 %convolution_convert_fusion.1 = bf16[704,1024]{1,0:T(8,128)(2,1)} fusion(bf16[3,704,1024]{2,1,0:T(8,128)(2,1)} %pad_maximum_fusion, f32[704,704]{1,0:T(8,128)} %fusion.19, bf16[704,1024]{1,0:T(8,128)(2,1)} %copy-done.6), kind=kOutput, calls=%fused_computation.25 | convolution fusion | flops 2035720192 | bytes 7929856 | tf_op jit(solution)/shard_map/dot_general | solution.py:27
  164.3 2.2 %fusion.58 = (bf16[176,1024]{1,0:T(8,128)(2,1)}, bf16[176,1024]{1,0:T(8,128)(2,1)}, bf16[176,1024]{1,0:T(8,128)(2,1)}) fusion(bf16[704,1024]{1,0:T(8,128)(2,1)} %convolution_convert_fusion.1), kind=kLoop, calls=%fused_computation.134 | loop fusion | bytes 2162688 | tf_op jit(solution)/shard_map/slice | solution.py:113
  166.5 1.5 collective-permute-start.15
  168.0 0.5 collective-permute-start.14
  168.4 1.9 collective-permute-start.13
  170.4 1.3 add_convert_fusion
  171.7 0.9 reshape.257
  172.7 9.1 %all-to-all-start.4 = ((bf16[16,11,1024]{2,1,0:T(8,128)(2,1)}), bf16[16,11,1024]{2,1,0:T(8,128)(2,1)S(1)}, u32[]{:S(2)}, u32[]{:S(2)}) async-start(bf16[16,11,1024]{2,1,0:T(8,128)(2,1)} %reshape.257), calls=%async_computation.4 | async-start | bytes 1048576 | tf_op jit(solution)/shard_map/all_to_all | solution.py:116
  182.0 0.3 fusion.61
  182.3 2.1 collective-permute-done.14
  184.4 1.3 collective-permute-done.13
  185.7 1.4 add_convert_fusion.1
  187.1 0.9 reshape.255
  188.0 10.9 %all-to-all-done.4 = bf16[16,11,1024]{2,1,0:T(8,128)(2,1)S(1)} async-done(((bf16[16,11,1024]{2,1,0:T(8,128)(2,1)}), bf16[16,11,1024]{2,1,0:T(8,128)(2,1)S(1)}, u32[]{:S(2)}, u32[]{:S(2)}) %all-to-all-start.4) | async-done | bytes 360480 | tf_op jit(solution)/shard_map/all_to_all | solution.py:116
  199.0 3.5 %all-to-all-start.2 = ((bf16[16,11,1024]{2,1,0:T(8,128)(2,1)}), bf16[16,11,1024]{2,1,0:T(8,128)(2,1)S(1)}, u32[]{:S(2)}, u32[]{:S(2)}) async-start(bf16[16,11,1024]{2,1,0:T(8,128)(2,1)} %reshape.255), calls=%async_computation.2 | async-start | bytes 1048576 | tf_op jit(solution)/shard_map/all_to_all | solution.py:116
  202.5 2.3 %gather_fusion.2 = f32[176]{0:T(256)S(1)} fusion(f32[88,16]{0,1:T(8,128)S(1)} %fusion.38, s32[176]{0:T(256)S(1)} %reshape.276), kind=kCustom, calls=%fused_computation.2 | custom fusion | bytes 2816 | tf_op jit(solution)/shard_map/jit(take_along_axis)/gather | solution.py:82
  205.0 14.1 %all-to-all-done.2 = bf16[16,11,1024]{2,1,0:T(8,128)(2,1)S(1)} async-done(((bf16[16,11,1024]{2,1,0:T(8,128)(2,1)}), bf16[16,11,1024]{2,1,0:T(8,128)(2,1)S(1)}, u32[]{:S(2)}, u32[]{:S(2)}) %all-to-all-start.2) | async-done | bytes 360480 | tf_op jit(solution)/shard_map/all_to_all | solution.py:116
  219.6 0.4 fusion.22
  220.2 0.8 fusion.25
  (92 shorter events, 3.6 us)
Async XLA Ops:
  0.6 6.1 %copy-start = (bf16[64,1024]{1,0:T(8,128)(2,1)S(1)}, bf16[64,1024]{1,0:T(8,128)(2,1)}, u32[]{:S(2)}) copy-start(bf16[64,1024]{1,0:T(8,128)(2,1)} %param.12) | copy-start | bytes 393220
  0.6 2.1 copy-start.2
  0.7 9.5 %copy-start.3 = (bf16[64,1408]{1,0:T(8,128)(2,1)S(1)}, bf16[64,1408]{1,0:T(8,128)(2,1)}, u32[]{:S(2)}) copy-start(bf16[64,1408]{1,0:T(8,128)(2,1)} %param.11) | copy-start | bytes 540676
  2.8 14.6 %copy-start.9 = (s32[88,2]{0,1:T(2,128)S(1)}, s32[88,2]{0,1:T(2,128)}, u32[]{:S(2)}) copy-start(s32[88,2]{0,1:T(2,128)} %param.15) | copy-start | bytes 2116
  2.8 107.3 %collective-permute-start.12 = (bf16[3,176,1024]{2,1,0:T(8,128)(2,1)S(1)}, bf16[3,176,1024]{2,1,0:T(8,128)(2,1)}, u32[]{:S(2)}, u32[]{:S(2)}) collective-permute-start(bf16[3,176,1024]{2,1,0:T(8,128)(2,1)S(1)} %constant_dynamic-update-slice_fusion.4), channel_id=1, source_target_pairs={{0,3},{1,0},{2,1},{3,2},{4,7},{5,4},{6,5},{7,6},{8,11},{9,8},{10,9... | collective-permute-start | bytes 3244040 | tf_op jit(solution)/shard_map/ppermute | solution.py:75
  6.2 103.9 %collective-permute-start.11 = (bf16[3,176,1024]{2,1,0:T(8,128)(2,1)S(1)}, bf16[3,176,1024]{2,1,0:T(8,128)(2,1)}, u32[]{:S(2)}, u32[]{:S(2)}) collective-permute-start(bf16[3,176,1024]{2,1,0:T(8,128)(2,1)S(1)} %constant_dynamic-update-slice_fusion.4), channel_id=1, source_target_pairs={{0,2},{1,3},{2,0},{3,1},{4,6},{5,7},{6,4},{7,5},{8,10},{9,11},{10,... | collective-permute-start | bytes 3244040 | tf_op jit(solution)/shard_map/ppermute | solution.py:75
  6.7 47.9 %collective-permute-start.2 = (bf16[64,512]{1,0:T(8,128)(2,1)S(1)}, bf16[64,512]{1,0:T(8,128)(2,1)S(1)}, u32[]{:S(2)}, u32[]{:S(2)}) collective-permute-start(bf16[64,512]{1,0:T(8,128)(2,1)S(1)} %constant_dynamic-slice_fusion), channel_id=1, source_target_pairs={{0,3},{1,0},{2,1},{3,2},{4,7},{5,4},{6,5},{7,6},{8,11},{9,8},{10,9... | collective-permute-start | bytes 196616 | tf_op jit(solution)/shard_map/ppermute | solution.py:54
  7.5 47.1 %collective-permute-start.1 = (bf16[64,512]{1,0:T(8,128)(2,1)S(1)}, bf16[64,512]{1,0:T(8,128)(2,1)S(1)}, u32[]{:S(2)}, u32[]{:S(2)}) collective-permute-start(bf16[64,512]{1,0:T(8,128)(2,1)S(1)} %constant_dynamic-slice_fusion), channel_id=1, source_target_pairs={{0,2},{1,3},{2,0},{3,1},{4,6},{5,7},{6,4},{7,5},{8,10},{9,11},{10,... | collective-permute-start | bytes 196616 | tf_op jit(solution)/shard_map/ppermute | solution.py:54
  9.3 45.2 %collective-permute-start = (bf16[64,512]{1,0:T(8,128)(2,1)S(1)}, bf16[64,512]{1,0:T(8,128)(2,1)S(1)}, u32[]{:S(2)}, u32[]{:S(2)}) collective-permute-start(bf16[64,512]{1,0:T(8,128)(2,1)S(1)} %constant_dynamic-slice_fusion), channel_id=1, source_target_pairs={{0,1},{1,2},{2,3},{3,0},{4,5},{5,6},{6,7},{7,4},{8,9},{9,10},{10,1... | collective-permute-start | bytes 196616 | tf_op jit(solution)/shard_map/ppermute | solution.py:54
  11.4 62.8 %all-to-all-start = ((bf16[64,16,88]{2,0,1:T(8,128)(2,1)}), bf16[64,16,88]{2,0,1:T(8,128)(2,1)S(1)}, u32[]{:S(2)}, u32[]{:S(2)}) async-start(bf16[64,16,88]{2,0,1:T(8,128)(2,1)} %copy.26), calls=%async_computation | async-start | bytes 524288 | tf_op jit(solution)/shard_map/all_to_all | solution.py:59
  54.6 7.3 %collective-permute-start.5 = (bf16[4,64,512]{2,1,0:T(8,128)(2,1)S(1)}, bf16[4,64,512]{2,1,0:T(8,128)(2,1)S(1)}, u32[]{:S(2)}, u32[]{:S(2)}) collective-permute-start(bf16[4,64,512]{2,1,0:T(8,128)(2,1)S(1)} %get-tuple-element.17), channel_id=1, source_target_pairs={{0,12},{4,0},{8,4},{12,8},{1,13},{5,1},{9,5},{13,9},{2,14},{6,2},{... | collective-permute-start | bytes 786440 | tf_op jit(solution)/shard_map/ppermute | solution.py:56
  56.9 7.3 %collective-permute-start.4 = (bf16[4,64,512]{2,1,0:T(8,128)(2,1)S(1)}, bf16[4,64,512]{2,1,0:T(8,128)(2,1)S(1)}, u32[]{:S(2)}, u32[]{:S(2)}) collective-permute-start(bf16[4,64,512]{2,1,0:T(8,128)(2,1)S(1)} %get-tuple-element.17), channel_id=1, source_target_pairs={{0,8},{4,12},{8,0},{12,4},{1,9},{5,13},{9,1},{13,5},{2,10},{6,14},... | collective-permute-start | bytes 786440 | tf_op jit(solution)/shard_map/ppermute | solution.py:56
  57.3 12.8 %collective-permute-start.3 = (bf16[4,64,512]{2,1,0:T(8,128)(2,1)S(1)}, bf16[4,64,512]{2,1,0:T(8,128)(2,1)}, u32[]{:S(2)}, u32[]{:S(2)}) collective-permute-start(bf16[4,64,512]{2,1,0:T(8,128)(2,1)S(1)} %get-tuple-element.17), channel_id=1, source_target_pairs={{0,4},{4,8},{8,12},{12,0},{1,5},{5,9},{9,13},{13,1},{2,6},{6,10},{... | collective-permute-start | bytes 786440 | tf_op jit(solution)/shard_map/ppermute | solution.py:56
  62.0 48.1 %collective-permute-start.10 = (bf16[3,176,1024]{2,1,0:T(8,128)(2,1)S(1)}, bf16[3,176,1024]{2,1,0:T(8,128)(2,1)}, u32[]{:S(2)}, u32[]{:S(2)}) collective-permute-start(bf16[3,176,1024]{2,1,0:T(8,128)(2,1)S(1)} %constant_dynamic-update-slice_fusion.4), channel_id=1, source_target_pairs={{0,1},{1,2},{2,3},{3,0},{4,5},{5,6},{6,7},{7,4},{8,9},{9,10},{10,1... | collective-permute-start | bytes 3244040 | tf_op jit(solution)/shard_map/ppermute | solution.py:75
  71.1 5.3 %collective-permute-start.6 = (bf16[4,4,64,512]{3,2,1,0:T(8,128)(2,1)S(1)}, bf16[4,4,64,512]{3,2,1,0:T(8,128)(2,1)}, u32[]{:S(2)}, u32[]{:S(2)}) collective-permute-start(bf16[4,4,64,512]{3,2,1,0:T(8,128)(2,1)S(1)} %pad_maximum_fusion.1), channel_id=1, source_target_pairs={{0,16},{16,0},{32,48},{48,32},{64,80},{80,64},{96,112},{112,96},{1... | collective-permute-start | bytes 3145736 | tf_op jit(solution)/shard_map/ppermute | solution.py:58
  75.5 2.6 %copy-start.4 = (bf16[88,1024]{1,0:T(8,128)(2,1)S(1)}, bf16[88,1024]{1,0:T(8,128)(2,1)}, u32[]{:S(2)}) copy-start(bf16[88,1024]{1,0:T(8,128)(2,1)} %param.10) | copy-start | bytes 540676
  75.9 2.4 %copy-start.10 = (f32[1024]{0:T(1024)S(1)}, f32[1024]{0:T(1024)}, u32[]{:S(2)}) copy-start(f32[1024]{0:T(1024)} %param.13) | copy-start | bytes 12292
  106.1 20.2 %all-to-all-start.1 = ((bf16[16,11,1024]{2,1,0:T(8,128)(2,1)}), bf16[16,11,1024]{2,1,0:T(8,128)(2,1)S(1)}, u32[]{:S(2)}, u32[]{:S(2)}) async-start(bf16[16,11,1024]{2,1,0:T(8,128)(2,1)} %get-tuple-element.14), calls=%async_computation.1 | async-start | bytes 1048576 | tf_op jit(solution)/shard_map/all_to_all | solution.py:103
  110.0 20.6 %collective-permute-start.16 = (bf16[176,1024]{1,0:T(8,128)(2,1)S(1)}, bf16[176,1024]{1,0:T(8,128)(2,1)S(1)}, u32[]{:S(2)}, u32[]{:S(2)}) collective-permute-start(bf16[176,1024]{1,0:T(8,128)(2,1)S(1)} %reshape.256), channel_id=1, source_target_pairs={{0,4},{4,8},{8,12},{12,0},{1,5},{5,9},{9,13},{13,1},{2,6},{6,10},{... | collective-permute-start | bytes 1081352 | tf_op jit(solution)/shard_map/ppermute | solution.py:106
  113.8 16.9 %collective-permute-start.17 = (bf16[176,1024]{1,0:T(8,128)(2,1)S(1)}, bf16[176,1024]{1,0:T(8,128)(2,1)S(1)}, u32[]{:S(2)}, u32[]{:S(2)}) collective-permute-start(bf16[176,1024]{1,0:T(8,128)(2,1)S(1)} %reshape.256), channel_id=1, source_target_pairs={{0,8},{4,12},{8,0},{12,4},{1,9},{5,13},{9,1},{13,5},{2,10},{6,14},... | collective-permute-start | bytes 1081352 | tf_op jit(solution)/shard_map/ppermute | solution.py:106
  117.1 16.4 %collective-permute-start.18 = (bf16[176,1024]{1,0:T(8,128)(2,1)S(1)}, bf16[176,1024]{1,0:T(8,128)(2,1)S(1)}, u32[]{:S(2)}, u32[]{:S(2)}) collective-permute-start(bf16[176,1024]{1,0:T(8,128)(2,1)S(1)} %reshape.256), channel_id=1, source_target_pairs={{0,12},{4,0},{8,4},{12,8},{1,13},{5,1},{9,5},{13,9},{2,14},{6,2},{... | collective-permute-start | bytes 1081352 | tf_op jit(solution)/shard_map/ppermute | solution.py:106
  126.4 23.4 %collective-permute-start.7 = (bf16[176,1024]{1,0:T(8,128)(2,1)S(1)}, bf16[176,1024]{1,0:T(8,128)(2,1)}, u32[]{:S(2)}, u32[]{:S(2)}) collective-permute-start(bf16[176,1024]{1,0:T(8,128)(2,1)S(1)} %reshape.254), channel_id=1, source_target_pairs={{0,4},{4,8},{8,12},{12,0},{1,5},{5,9},{9,13},{13,1},{2,6},{6,10},{... | collective-permute-start | bytes 1081352 | tf_op jit(solution)/shard_map/ppermute | solution.py:106
  126.5 24.3 %collective-permute-start.8 = (bf16[176,1024]{1,0:T(8,128)(2,1)S(1)}, bf16[176,1024]{1,0:T(8,128)(2,1)S(1)}, u32[]{:S(2)}, u32[]{:S(2)}) collective-permute-start(bf16[176,1024]{1,0:T(8,128)(2,1)S(1)} %reshape.254), channel_id=1, source_target_pairs={{0,8},{4,12},{8,0},{12,4},{1,9},{5,13},{9,1},{13,5},{2,10},{6,14},... | collective-permute-start | bytes 1081352 | tf_op jit(solution)/shard_map/ppermute | solution.py:106
  130.6 20.2 %collective-permute-start.9 = (bf16[176,1024]{1,0:T(8,128)(2,1)S(1)}, bf16[176,1024]{1,0:T(8,128)(2,1)}, u32[]{:S(2)}, u32[]{:S(2)}) collective-permute-start(bf16[176,1024]{1,0:T(8,128)(2,1)S(1)} %reshape.254), channel_id=1, source_target_pairs={{0,12},{4,0},{8,4},{12,8},{1,13},{5,1},{9,5},{13,9},{2,14},{6,2},{... | collective-permute-start | bytes 1081352 | tf_op jit(solution)/shard_map/ppermute | solution.py:106
  133.5 1.2 copy-start.7
  144.8 5.0 %copy-start.5 = (bf16[704,1024]{1,0:T(8,128)(2,1)S(1)}, bf16[704,1024]{1,0:T(8,128)(2,1)}, u32[]{:S(2)}) copy-start(bf16[704,1024]{1,0:T(8,128)(2,1)} %constant_dynamic-update-slice_fusion.3) | copy-start | bytes 4325380
  145.8 22.7 %collective-permute-start.21 = (bf16[176,1024]{1,0:T(8,128)(2,1)}, bf16[176,1024]{1,0:T(8,128)(2,1)S(1)}, u32[]{:S(2)}, u32[]{:S(2)}) collective-permute-start(bf16[176,1024]{1,0:T(8,128)(2,1)} %get-tuple-element.12), channel_id=1, source_target_pairs={{0,4},{4,8},{8,12},{12,0},{1,5},{5,9},{9,13},{13,1},{2,6},{6,10},{... | collective-permute-start | bytes 1081352 | tf_op jit(solution)/shard_map/ppermute | solution.py:113
  146.0 24.3 %collective-permute-start.20 = (bf16[176,1024]{1,0:T(8,128)(2,1)}, bf16[176,1024]{1,0:T(8,128)(2,1)}, u32[]{:S(2)}, u32[]{:S(2)}) collective-permute-start(bf16[176,1024]{1,0:T(8,128)(2,1)} %get-tuple-element.13), channel_id=1, source_target_pairs={{0,8},{4,12},{8,0},{12,4},{1,9},{5,13},{9,1},{13,5},{2,10},{6,14},... | collective-permute-start | bytes 1081352 | tf_op jit(solution)/shard_map/ppermute | solution.py:113
  149.8 20.6 %collective-permute-start.19 = (bf16[176,1024]{1,0:T(8,128)(2,1)}, bf16[176,1024]{1,0:T(8,128)(2,1)}, u32[]{:S(2)}, u32[]{:S(2)}) collective-permute-start(bf16[176,1024]{1,0:T(8,128)(2,1)} %get-tuple-element.11), channel_id=1, source_target_pairs={{0,12},{4,0},{8,4},{12,8},{1,13},{5,1},{9,5},{13,9},{2,14},{6,2},{... | collective-permute-start | bytes 1081352 | tf_op jit(solution)/shard_map/ppermute | solution.py:113
  151.9 1.1 copy-start.6
  166.5 15.8 %collective-permute-start.15 = (bf16[176,1024]{1,0:T(8,128)(2,1)}, bf16[176,1024]{1,0:T(8,128)(2,1)S(1)}, u32[]{:S(2)}, u32[]{:S(2)}) collective-permute-start(bf16[176,1024]{1,0:T(8,128)(2,1)} %get-tuple-element.9), channel_id=1, source_target_pairs={{0,4},{4,8},{8,12},{12,0},{1,5},{5,9},{9,13},{13,1},{2,6},{6,10},{... | collective-permute-start | bytes 1081352 | tf_op jit(solution)/shard_map/ppermute | solution.py:113
  168.0 16.4 %collective-permute-start.14 = (bf16[176,1024]{1,0:T(8,128)(2,1)}, bf16[176,1024]{1,0:T(8,128)(2,1)}, u32[]{:S(2)}, u32[]{:S(2)}) collective-permute-start(bf16[176,1024]{1,0:T(8,128)(2,1)} %get-tuple-element.10), channel_id=1, source_target_pairs={{0,8},{4,12},{8,0},{12,4},{1,9},{5,13},{9,1},{13,5},{2,10},{6,14},... | collective-permute-start | bytes 1081352 | tf_op jit(solution)/shard_map/ppermute | solution.py:113
  168.4 17.2 %collective-permute-start.13 = (bf16[176,1024]{1,0:T(8,128)(2,1)}, bf16[176,1024]{1,0:T(8,128)(2,1)}, u32[]{:S(2)}, u32[]{:S(2)}) collective-permute-start(bf16[176,1024]{1,0:T(8,128)(2,1)} %get-tuple-element.8), channel_id=1, source_target_pairs={{0,12},{4,0},{8,4},{12,8},{1,13},{5,1},{9,5},{13,9},{2,14},{6,2},{... | collective-permute-start | bytes 1081352 | tf_op jit(solution)/shard_map/ppermute | solution.py:113
  171.7 10.3 %copy-start.8 = (f32[1024,16]{0,1:T(8,128)S(1)}, f32[1024,16]{0,1:T(8,128)}, u32[]{:S(2)}) copy-start(f32[1024,16]{0,1:T(8,128)} %param.14) | copy-start | bytes 196612
  172.7 26.3 %all-to-all-start.4 = ((bf16[16,11,1024]{2,1,0:T(8,128)(2,1)}), bf16[16,11,1024]{2,1,0:T(8,128)(2,1)S(1)}, u32[]{:S(2)}, u32[]{:S(2)}) async-start(bf16[16,11,1024]{2,1,0:T(8,128)(2,1)} %reshape.257), calls=%async_computation.4 | async-start | bytes 1048576 | tf_op jit(solution)/shard_map/all_to_all | solution.py:116
  199.0 20.2 %all-to-all-start.2 = ((bf16[16,11,1024]{2,1,0:T(8,128)(2,1)}), bf16[16,11,1024]{2,1,0:T(8,128)(2,1)S(1)}, u32[]{:S(2)}, u32[]{:S(2)}) async-start(bf16[16,11,1024]{2,1,0:T(8,128)(2,1)} %reshape.255), calls=%async_computation.2 | async-start | bytes 1048576 | tf_op jit(solution)/shard_map/all_to_all | solution.py:116
  219.4 0.8 copy-start.11
  220.1 0.8 copy-start.1

commit v7 on v5

--- a/solution.py
+++ b/solution.py
@@ -51,17 +51,15 @@
     core = lax.axis_index("expert") % 2
     half = width // 2
     my_cols = lax.dynamic_slice_in_dim(out_proj, core * half, half, axis=1)
-    near = [my_cols] + [lax.ppermute(my_cols, "tx", shift_pairs(n_tx, s)) for s in range(1, n_tx)]
-    near = jnp.stack(near)
-    my_half = [near] + [lax.ppermute(near, "ty", shift_pairs(n_ty, s)) for s in range(1, n_ty)]
-    my_half = jnp.stack(my_half)
+    n_tensor = n_ty * n_tx
+    heads_for = attn_heads.reshape(-1, n_tensor, row_count).transpose(1, 0, 2)
+    proj_for = jnp.broadcast_to(my_cols, (n_tensor, *my_cols.shape))
+    mail = jnp.concatenate([heads_for, proj_for], axis=2)
+    mail = lax.all_to_all(mail, TENSOR_AXES, 0, 0, tiled=True)
+    own_heads = mail[:, :, :row_count]
+    my_half = mail[:, :, row_count:]
     other_half = lax.ppermute(my_half, "expert", [(i, i ^ 1) for i in range(n_expert)])
-    own_heads = lax.all_to_all(attn_heads, TENSOR_AXES, 1, 0, tiled=True)
-    own_heads = own_heads.reshape(n_ty, n_tx, -1, row_count)
-    from_y = (ty - jnp.arange(n_ty)) % n_ty
-    from_x = (tx - jnp.arange(n_tx)) % n_tx
-    own_heads = jnp.take(jnp.take(own_heads, from_y, axis=0), from_x, axis=1)
-    contract = (((0, 1, 2), (0, 1, 2)), ((), ()))
+    contract = (((0, 1), (0, 1)), ((), ()))
     proj_mine = lax.dot_general(own_heads, my_half, contract, preferred_element_type=jnp.float32)
     proj_other = lax.dot_general(own_heads, other_half, contract, preferred_element_type=jnp.float32)
     projected = jnp.where(

time: 189 us -> 198 us (1.048)
  the two profiles are of different devices: /device:TPU:1 before, /device:TPU:7 now
where the time goes in v7:
time: 198 us; the launch traced here: 197 us
  waiting for transfers between devices  122 us (62%)
  starting transfers between devices  34.5 us (17%)
  matrix products  14.8 us (7%)
  local copies, waits for them, and re-layouts  13.6 us (7%)
  other arithmetic  11.6 us (6%)
    ppermute x3, waiting for transfers between devices, per_device(): back = lax.ppermute(partial[s], 'ty', shift_pairs(n_ty, -s))  29.8 us
    ppermute x3, waiting for transfers between devices, per_device(): lax.ppermute(stacked, 'tx', shift_pairs(n_tx, s))  27.4 us
    all_to_all x1, waiting for transfers between devices, per_device(): lax.all_to_all(expert_out, 'expert', split_axis=0, concat_axis=0, tiled=T...  19.4 us
    all_to_all x1, waiting for transfers between devices, per_device(): mail = lax.all_to_all(mail, TENSOR_AXES, 0, 0, tiled=True)  16.6 us
    all_to_all x1, waiting for transfers between devices, per_device(): lax.all_to_all(send_slots, 'expert', split_axis=0, concat_axis=0, tiled=T...  16 us
    ppermute x3, waiting for transfers between devices, per_device(): lax.ppermute(rows_in, 'ty', shift_pairs(n_ty, s))  12.3 us
    dot_general x1, matrix products, expert_block(): return jnp.dot(hid, down_rows, preferred_element_type=jnp.float32)  8.6 us
    all_to_all x1, starting transfers between devices, per_device(): lax.all_to_all(send_slots, 'expert', split_axis=0, concat_axis=0, tiled=T...  8.6 us
  transfers between devices with their start and end apart: 13, of which 9 were waited for; matrix products, arithmetic and copies ran while one was open for 7% of the time, Pallas kernels for 0%

profile of v7, /device:TPU:7, one launch (start us, length us, event | category | flops | bytes accessed | tf_op | source)
XLA Modules:
  0.0 197.3 jit_solution(568202395534566074)
XLA Ops:
  0.7 1.4 reshape.120
  2.2 0.1 broadcast_in_dim.8
  2.3 1.8 pad_maximum_fusion.1
  4.1 6.9 %all-to-all-start = ((bf16[16,64,600]{2,1,0:T(8,128)(2,1)}), bf16[16,64,600]{2,1,0:T(8,128)(2,1)S(1)}, u32[]{:S(2)}, u32[]{:S(2)}) async-start(bf16[16,64,600]{2,1,0:T(8,128)(2,1)} %pad_maximum_fusion.1), calls=%async_computation | async-start | bytes 2621440 | tf_op jit(solution)/shard_map/all_to_all | solution.py:58
  11.0 0.1 copy.26
  11.1 0.1 reshape.122
  11.2 16.6 %all-to-all-done = bf16[16,64,600]{2,1,0:T(8,128)(2,1)S(1)} async-done(((bf16[16,64,600]{2,1,0:T(8,128)(2,1)}), bf16[16,64,600]{2,1,0:T(8,128)(2,1)S(1)}, u32[]{:S(2)}, u32[]{:S(2)}) %all-to-all-start) | async-done | bytes 1228832 | tf_op jit(solution)/shard_map/all_to_all | solution.py:58
  27.9 0.5 slice.55
  28.4 1.8 collective-permute-start
  30.1 0.6 copy_bitcast_fusion.1
  30.7 1.3 reduce-window.6
  32.0 0.7 slice_reduce_fusion
  32.7 1.3 reduce-window.9
  34.0 0.7 slice.43
  34.8 0.1 bitcast_bitcast_fusion
  34.8 0.7 fusion.31
  35.5 0.7 multiply_add_fusion
  36.2 0.6 convolution_bitcast_fusion.1
  36.8 0.3 convolution_bitcast_fusion
  37.1 0.2 fusion.20
  37.3 0.1 fusion.22
  37.4 0.2 broadcast_in_dim.10
  37.6 0.1 reshape.125
  37.7 0.3 convolution_convert_fusion.1
  38.1 1.1 reshape.126
  39.2 8.6 %all-to-all-start.1 = ((bf16[16,22,1024]{2,1,0:T(8,128)(2,1)}), bf16[16,22,1024]{2,1,0:T(8,128)(2,1)S(1)}, u32[]{:S(2)}, u32[]{:S(2)}) async-start(bf16[16,22,1024]{2,1,0:T(8,128)(2,1)} %reshape.126), calls=%async_computation.1 | async-start | bytes 1572864 | tf_op jit(solution)/shard_map/all_to_all | solution.py:93
  47.8 1.0 constant_dynamic-update-slice_fusion.5
  48.8 1.0 constant_dynamic-update-slice_fusion.4
  49.8 0.7 collective-permute-start.6
  50.5 4.0 %collective-permute-start.5 = (bf16[3,176,1024]{2,1,0:T(8,128)(2,1)S(1)}, bf16[3,176,1024]{2,1,0:T(8,128)(2,1)}, u32[]{:S(2)}, u32[]{:S(2)}) collective-permute-start(bf16[3,176,1024]{2,1,0:T(8,128)(2,1)S(1)} %constant_dynamic-update-slice_fusion.4), channel_id=1, source_target_pairs={{0,2},{1,3},{2,0},{3,1},{4,6},{5,7},{6,4},{7,5},{8,10},{9,11},{10,... | collective-permute-start | bytes 3244040 | tf_op jit(solution)/shard_map/ppermute | solution.py:73
  54.5 16.0 %all-to-all-done.1 = bf16[16,22,1024]{2,1,0:T(8,128)(2,1)S(1)} async-done(((bf16[16,22,1024]{2,1,0:T(8,128)(2,1)}), bf16[16,22,1024]{2,1,0:T(8,128)(2,1)S(1)}, u32[]{:S(2)}, u32[]{:S(2)}) %all-to-all-start.1) | async-done | bytes 720928 | tf_op jit(solution)/shard_map/all_to_all | solution.py:93
  70.5 0.2 reshape.127
  70.7 1.1 collective-permute-start.1
  71.8 1.8 collective-permute-start.2
  73.6 4.0 %collective-permute-done.6 = bf16[3,176,1024]{2,1,0:T(8,128)(2,1)} collective-permute-done((bf16[3,176,1024]{2,1,0:T(8,128)(2,1)S(1)}, bf16[3,176,1024]{2,1,0:T(8,128)(2,1)}, u32[]{:S(2)}, u32[]{:S(2)}) %collective-permute-start.6) | collective-permute-done | bytes 1081376 | tf_op jit(solution)/shard_map/ppermute | solution.py:73
  77.6 0.6 collective-permute-start.3
  78.2 23.5 %collective-permute-done.5 = bf16[3,176,1024]{2,1,0:T(8,128)(2,1)} collective-permute-done((bf16[3,176,1024]{2,1,0:T(8,128)(2,1)S(1)}, bf16[3,176,1024]{2,1,0:T(8,128)(2,1)}, u32[]{:S(2)}, u32[]{:S(2)}) %collective-permute-start.5) | collective-permute-done | bytes 1081376 | tf_op jit(solution)/shard_map/ppermute | solution.py:73
  101.6 2.2 %pad_maximum_fusion = bf16[3,704,1024]{2,1,0:T(8,128)(2,1)S(1)} fusion(bf16[3,176,1024]{2,1,0:T(8,128)(2,1)} %collective-permute-done.6, bf16[3,176,1024]{2,1,0:T(8,128)(2,1)} %collective-permute-done.5, bf16[3,176,1024]{2,1,0:T(8,128)(2,1)} %collective-permute-done.4, bf16[3,176,1024]{2,1,0:T(8,128)(2,1)S(1)} %constant_dynamic-update-slice_fusion.4), kind=kLoop, calls=%fused_computation.2 | loop fusion | flops 17301504 | bytes 8650752 | tf_op jit(solution)/shard_map/concatenate | solution.py:94
  104.0 12.3 %collective-permute-done.3 = bf16[352,1024]{1,0:T(8,128)(2,1)S(1)} collective-permute-done((bf16[352,1024]{1,0:T(8,128)(2,1)S(1)}, bf16[352,1024]{1,0:T(8,128)(2,1)S(1)}, u32[]{:S(2)}, u32[]{:S(2)}) %collective-permute-start.3) | collective-permute-done | bytes 720928 | tf_op jit(solution)/shard_map/ppermute | solution.py:98
  116.4 1.7 copy-done.5
  118.0 4.4 %fusion.15 = f32[1408,704]{0,1:T(8,128)} fusion(bf16[1408,1024]{1,0:T(8,128)(2,1)S(1)} %constant_dynamic-update-slice_fusion, bf16[3,704,1024]{2,1,0:T(8,128)(2,1)S(1)} %pad_maximum_fusion), kind=kOutput, calls=%fused_computation.21 | convolution fusion | flops 2030043136 | bytes 8290304 | tf_op jit(solution)/shard_map/dot_general | solution.py:20
  122.4 8.6 %convolution_convert_fusion = bf16[1408,1024]{1,0:T(8,128)(2,1)S(1)} fusion(f32[1408,704]{0,1:T(8,128)} %fusion.15, bf16[3,704,1024]{2,1,0:T(8,128)(2,1)} %copy-done.1, bf16[1408,1024]{1,0:T(8,128)(2,1)} %copy-done.5), kind=kOutput, calls=%fused_computation.12 | convolution fusion | flops 4071440384 | bytes 12615680 | tf_op jit(solution)/shard_map/dot_general | solution.py:27
  131.0 0.2 fusion.42
  131.2 0.1 collective-permute-start.7
  131.3 1.5 collective-permute-start.9
  132.8 1.5 collective-permute-start.8
  134.3 13.2 %collective-permute-done.7 = bf16[352,1024]{1,0:T(8,128)(2,1)S(1)} collective-permute-done((bf16[352,1024]{1,0:T(8,128)(2,1)S(1)}, bf16[352,1024]{1,0:T(8,128)(2,1)S(1)}, u32[]{:S(2)}, u32[]{:S(2)}) %collective-permute-start.7) | collective-permute-done | bytes 720928 | tf_op jit(solution)/shard_map/ppermute | solution.py:104
  147.5 1.4 collective-permute-done.9
  148.9 15.3 %collective-permute-done.8 = bf16[352,1024]{1,0:T(8,128)(2,1)S(1)} collective-permute-done((bf16[352,1024]{1,0:T(8,128)(2,1)S(1)}, bf16[352,1024]{1,0:T(8,128)(2,1)S(1)}, u32[]{:S(2)}, u32[]{:S(2)}) %collective-permute-start.8) | collective-permute-done | bytes 720928 | tf_op jit(solution)/shard_map/ppermute | solution.py:104
  164.1 1.7 add_convert_fusion
  165.8 1.1 reshape.128
  166.9 6.1 %all-to-all-start.2 = ((bf16[16,22,1024]{2,1,0:T(8,128)(2,1)}), bf16[16,22,1024]{2,1,0:T(8,128)(2,1)S(1)}, u32[]{:S(2)}, u32[]{:S(2)}) async-start(bf16[16,22,1024]{2,1,0:T(8,128)(2,1)} %reshape.128), calls=%async_computation.2 | async-start | bytes 1572864 | tf_op jit(solution)/shard_map/all_to_all | solution.py:108
  173.0 0.1 copy.24
  173.1 0.1 reshape.131
  173.2 0.1 iota_compare_fusion.2
  173.3 0.1 eq.63
  173.5 0.3 fusion.43
  173.8 2.3 %gather_fusion = f32[176]{0:T(256)S(1)} fusion(f32[88,16]{0,1:T(8,128)S(1)} %fusion.32, s32[176]{0:T(256)S(1)} %reshape.131), kind=kCustom, calls=%fused_computation | custom fusion | bytes 2816 | tf_op jit(solution)/shard_map/jit(take_along_axis)/gather | solution.py:80
  176.1 0.1 reshape.134
  176.3 19.4 %all-to-all-done.2 = bf16[16,22,1024]{2,1,0:T(8,128)(2,1)S(1)} async-done(((bf16[16,22,1024]{2,1,0:T(8,128)(2,1)}), bf16[16,22,1024]{2,1,0:T(8,128)(2,1)S(1)}, u32[]{:S(2)}, u32[]{:S(2)}) %all-to-all-start.2) | async-done | bytes 720928 | tf_op jit(solution)/shard_map/all_to_all | solution.py:108
  195.7 0.2 reshape.144
  195.9 0.4 fusion.16
  196.3 0.1 fusion.17
  196.5 0.8 fusion.19
  (46 shorter events, 0.5 us)
Async XLA Ops:
  0.6 1.6 copy-start
  2.3 8.7 %copy-start.9 = (s32[88,2]{0,1:T(2,128)S(1)}, s32[88,2]{0,1:T(2,128)}, u32[]{:S(2)}) copy-start(s32[88,2]{0,1:T(2,128)} %param.15) | copy-start | bytes 2116
  4.1 23.8 %all-to-all-start = ((bf16[16,64,600]{2,1,0:T(8,128)(2,1)}), bf16[16,64,600]{2,1,0:T(8,128)(2,1)S(1)}, u32[]{:S(2)}, u32[]{:S(2)}) async-start(bf16[16,64,600]{2,1,0:T(8,128)(2,1)} %pad_maximum_fusion.1), calls=%async_computation | async-start | bytes 2621440 | tf_op jit(solution)/shard_map/all_to_all | solution.py:58
  11.2 18.9 %copy-start.8 = (s32[176]{0:T(256)}, s32[176]{0:T(256)S(1)}, u32[]{:S(2)}) copy-start(s32[176]{0:T(256)S(1)} %reshape.122) | copy-start | bytes 2116
  28.4 8.4 %collective-permute-start = (bf16[16,64,512]{2,1,0:T(8,128)(2,1)S(1)}, bf16[16,64,512]{2,1,0:T(8,128)(2,1)S(1)}, u32[]{:S(2)}, u32[]{:S(2)}) collective-permute-start(bf16[16,64,512]{2,1,0:T(8,128)(2,1)S(1)} %slice.55), channel_id=1, source_target_pairs={{0,16},{16,0},{32,48},{48,32},{64,80},{80,64},{96,112},{112,96},{1... | collective-permute-start | bytes 3145736 | tf_op jit(solution)/shard_map/ppermute | solution.py:61
  34.0 3.1 %copy-start.6 = (bf16[88,1024]{1,0:T(8,128)(2,1)S(1)}, bf16[88,1024]{1,0:T(8,128)(2,1)}, u32[]{:S(2)}) copy-start(bf16[88,1024]{1,0:T(8,128)(2,1)} %param.10) | copy-start | bytes 540676
  34.0 3.2 %copy-start.11 = (f32[1024]{0:T(1024)S(1)}, f32[1024]{0:T(1024)}, u32[]{:S(2)}) copy-start(f32[1024]{0:T(1024)} %param.13) | copy-start | bytes 12292
  37.3 10.5 %copy-start.4 = (bf16[1,176,1024]{2,1,0:T(8,128)(2,1)S(1)}, bf16[1,176,1024]{2,1,0:T(8,128)(2,1)}, u32[]{:S(2)}) copy-start(bf16[1,176,1024]{2,1,0:T(8,128)(2,1)} %param.16) | copy-start | bytes 1081348
  39.2 31.3 %all-to-all-start.1 = ((bf16[16,22,1024]{2,1,0:T(8,128)(2,1)}), bf16[16,22,1024]{2,1,0:T(8,128)(2,1)S(1)}, u32[]{:S(2)}, u32[]{:S(2)}) async-start(bf16[16,22,1024]{2,1,0:T(8,128)(2,1)} %reshape.126), calls=%async_computation.1 | async-start | bytes 1572864 | tf_op jit(solution)/shard_map/all_to_all | solution.py:93
  49.8 27.7 %collective-permute-start.6 = (bf16[3,176,1024]{2,1,0:T(8,128)(2,1)S(1)}, bf16[3,176,1024]{2,1,0:T(8,128)(2,1)}, u32[]{:S(2)}, u32[]{:S(2)}) collective-permute-start(bf16[3,176,1024]{2,1,0:T(8,128)(2,1)S(1)} %constant_dynamic-update-slice_fusion.4), channel_id=1, source_target_pairs={{0,3},{1,0},{2,1},{3,2},{4,7},{5,4},{6,5},{7,6},{8,11},{9,8},{10,9... | collective-permute-start | bytes 3244040 | tf_op jit(solution)/shard_map/ppermute | solution.py:73
  50.5 51.1 %collective-permute-start.5 = (bf16[3,176,1024]{2,1,0:T(8,128)(2,1)S(1)}, bf16[3,176,1024]{2,1,0:T(8,128)(2,1)}, u32[]{:S(2)}, u32[]{:S(2)}) collective-permute-start(bf16[3,176,1024]{2,1,0:T(8,128)(2,1)S(1)} %constant_dynamic-update-slice_fusion.4), channel_id=1, source_target_pairs={{0,2},{1,3},{2,0},{3,1},{4,6},{5,7},{6,4},{7,5},{8,10},{9,11},{10,... | collective-permute-start | bytes 3244040 | tf_op jit(solution)/shard_map/ppermute | solution.py:73
  54.5 47.1 %collective-permute-start.4 = (bf16[3,176,1024]{2,1,0:T(8,128)(2,1)S(1)}, bf16[3,176,1024]{2,1,0:T(8,128)(2,1)}, u32[]{:S(2)}, u32[]{:S(2)}) collective-permute-start(bf16[3,176,1024]{2,1,0:T(8,128)(2,1)S(1)} %constant_dynamic-update-slice_fusion.4), channel_id=1, source_target_pairs={{0,1},{1,2},{2,3},{3,0},{4,5},{5,6},{6,7},{7,4},{8,9},{9,10},{10,1... | collective-permute-start | bytes 3244040 | tf_op jit(solution)/shard_map/ppermute | solution.py:73
  70.7 33.2 %collective-permute-start.1 = (bf16[352,1024]{1,0:T(8,128)(2,1)S(1)}, bf16[352,1024]{1,0:T(8,128)(2,1)S(1)}, u32[]{:S(2)}, u32[]{:S(2)}) collective-permute-start(bf16[352,1024]{1,0:T(8,128)(2,1)S(1)} %reshape.127), channel_id=1, source_target_pairs={{0,4},{4,8},{8,12},{12,0},{1,5},{5,9},{9,13},{13,1},{2,6},{6,10},{... | collective-permute-start | bytes 2162696 | tf_op jit(solution)/shard_map/ppermute | solution.py:98
  71.8 32.2 %collective-permute-start.2 = (bf16[352,1024]{1,0:T(8,128)(2,1)S(1)}, bf16[352,1024]{1,0:T(8,128)(2,1)S(1)}, u32[]{:S(2)}, u32[]{:S(2)}) collective-permute-start(bf16[352,1024]{1,0:T(8,128)(2,1)S(1)} %reshape.127), channel_id=1, source_target_pairs={{0,8},{4,12},{8,0},{12,4},{1,9},{5,13},{9,1},{13,5},{2,10},{6,14},... | collective-permute-start | bytes 2162696 | tf_op jit(solution)/shard_map/ppermute | solution.py:98
  77.6 38.7 %collective-permute-start.3 = (bf16[352,1024]{1,0:T(8,128)(2,1)S(1)}, bf16[352,1024]{1,0:T(8,128)(2,1)S(1)}, u32[]{:S(2)}, u32[]{:S(2)}) collective-permute-start(bf16[352,1024]{1,0:T(8,128)(2,1)S(1)} %reshape.127), channel_id=1, source_target_pairs={{0,12},{4,0},{8,4},{12,8},{1,13},{5,1},{9,5},{13,9},{2,14},{6,2},{... | collective-permute-start | bytes 2162696 | tf_op jit(solution)/shard_map/ppermute | solution.py:98
  103.8 12.5 %copy-start.1 = (bf16[3,704,1024]{2,1,0:T(8,128)(2,1)}, bf16[3,704,1024]{2,1,0:T(8,128)(2,1)S(1)}, u32[]{:S(2)}) copy-start(bf16[3,704,1024]{2,1,0:T(8,128)(2,1)S(1)} %pad_maximum_fusion) | copy-start | bytes 12976132
  116.4 1.7 copy-start.5
  131.0 17.8 %copy-start.2 = (bf16[1408,1024]{1,0:T(8,128)(2,1)}, bf16[1408,1024]{1,0:T(8,128)(2,1)S(1)}, u32[]{:S(2)}) copy-start(bf16[1408,1024]{1,0:T(8,128)(2,1)S(1)} %convolution_convert_fusion) | copy-start | bytes 8650756
  131.2 16.2 %collective-permute-start.7 = (bf16[352,1024]{1,0:T(8,128)(2,1)S(1)}, bf16[352,1024]{1,0:T(8,128)(2,1)S(1)}, u32[]{:S(2)}, u32[]{:S(2)}) collective-permute-start(bf16[352,1024]{1,0:T(8,128)(2,1)S(1)} %get-tuple-element.8), channel_id=1, source_target_pairs={{0,12},{4,0},{8,4},{12,8},{1,13},{5,1},{9,5},{13,9},{2,14},{6,2},{... | collective-permute-start | bytes 2162696 | tf_op jit(solution)/shard_map/ppermute | solution.py:104
  131.3 17.5 %collective-permute-start.9 = (bf16[352,1024]{1,0:T(8,128)(2,1)S(1)}, bf16[352,1024]{1,0:T(8,128)(2,1)S(1)}, u32[]{:S(2)}, u32[]{:S(2)}) collective-permute-start(bf16[352,1024]{1,0:T(8,128)(2,1)S(1)} %get-tuple-element.9), channel_id=1, source_target_pairs={{0,4},{4,8},{8,12},{12,0},{1,5},{5,9},{9,13},{13,1},{2,6},{6,10},{... | collective-permute-start | bytes 2162696 | tf_op jit(solution)/shard_map/ppermute | solution.py:104
  132.8 40.2 %copy-start.10 = (s32[88,2]{0,1:T(2,128)S(1)}, s32[88,2]{0,1:T(2,128)}, u32[]{:S(2)}) copy-start(s32[88,2]{0,1:T(2,128)} %param.15) | copy-start | bytes 2116
  132.8 40.7 %copy-start.7 = (f32[1024,16]{0,1:T(8,128)S(1)}, f32[1024,16]{0,1:T(8,128)}, u32[]{:S(2)}) copy-start(f32[1024,16]{0,1:T(8,128)} %param.14) | copy-start | bytes 196612
  132.8 31.4 %collective-permute-start.8 = (bf16[352,1024]{1,0:T(8,128)(2,1)S(1)}, bf16[352,1024]{1,0:T(8,128)(2,1)S(1)}, u32[]{:S(2)}, u32[]{:S(2)}) collective-permute-start(bf16[352,1024]{1,0:T(8,128)(2,1)S(1)} %get-tuple-element.10), channel_id=1, source_target_pairs={{0,8},{4,12},{8,0},{12,4},{1,9},{5,13},{9,1},{13,5},{2,10},{6,14},... | collective-permute-start | bytes 2162696 | tf_op jit(solution)/shard_map/ppermute | solution.py:104
  166.9 28.9 %all-to-all-start.2 = ((bf16[16,22,1024]{2,1,0:T(8,128)(2,1)}), bf16[16,22,1024]{2,1,0:T(8,128)(2,1)S(1)}, u32[]{:S(2)}, u32[]{:S(2)}) async-start(bf16[16,22,1024]{2,1,0:T(8,128)(2,1)} %reshape.128), calls=%async_computation.2 | async-start | bytes 1572864 | tf_op jit(solution)/shard_map/all_to_all | solution.py:108
  176.1 20.4 %copy-start.12 = (f32[1024]{0:T(1024)S(1)}, f32[1024]{0:T(1024)}, u32[]{:S(2)}) copy-start(f32[1024]{0:T(1024)} %param.19) | copy-start | bytes 12292
  196.5 0.8 copy-start.3

commit v8 on v5

--- a/solution.py
+++ b/solution.py
@@ -6,7 +6,8 @@
 from jax.sharding import Mesh
 from jax.sharding import PartitionSpec as P
 
-ROWS_AXES = ("expert", "ty", "tx")
+EXPERT_AXES = ("ez", "ec")
+ROWS_AXES = ("ez", "ec", "ty", "tx")
 TENSOR_AXES = ("ty", "tx")
 
 
@@ -41,21 +42,23 @@
 ):
     row_count = residual_in.shape[0]
     width = residual_in.shape[1]
-    n_expert = lax.axis_size("expert")
+    n_ez = lax.axis_size("ez")
+    n_ec = lax.axis_size("ec")
+    n_expert = n_ez * n_ec
     capacity = 4 * row_count // n_expert
 
     n_ty = lax.axis_size("ty")
     n_tx = lax.axis_size("tx")
     ty = lax.axis_index("ty")
     tx = lax.axis_index("tx")
-    core = lax.axis_index("expert") % 2
+    core = lax.axis_index("ec")
     half = width // 2
     my_cols = lax.dynamic_slice_in_dim(out_proj, core * half, half, axis=1)
     near = [my_cols] + [lax.ppermute(my_cols, "tx", shift_pairs(n_tx, s)) for s in range(1, n_tx)]
     near = jnp.stack(near)
     my_half = [near] + [lax.ppermute(near, "ty", shift_pairs(n_ty, s)) for s in range(1, n_ty)]
     my_half = jnp.stack(my_half)
-    other_half = lax.ppermute(my_half, "expert", [(i, i ^ 1) for i in range(n_expert)])
+    other_half = lax.ppermute(my_half, "ec", [(i, i ^ 1) for i in range(n_ec)])
     own_heads = lax.all_to_all(attn_heads, TENSOR_AXES, 1, 0, tiled=True)
     own_heads = own_heads.reshape(n_ty, n_tx, -1, row_count)
     from_y = (ty - jnp.arange(n_ty)) % n_ty
@@ -92,7 +95,9 @@
     repeated = jnp.repeat(normed, 2, axis=0)
     send_slots = jnp.dot(placing, repeated, preferred_element_type=jnp.float32).astype(jnp.bfloat16)
     send_slots = send_slots.reshape(n_expert, capacity, width)
-    received = lax.all_to_all(send_slots, "expert", split_axis=0, concat_axis=0, tiled=True)
+    send_slots = send_slots.reshape(n_ez, n_ec, capacity, width)
+    received = lax.all_to_all(send_slots, "ez", split_axis=0, concat_axis=0, tiled=True)
+    received = lax.all_to_all(received, "ec", split_axis=1, concat_axis=1, tiled=True)
     weights = jnp.concatenate(pieces, axis=1)
     gate_rows, up_rows, down_rows = weights[0], weights[1], weights[2]
     slot_total = n_expert * capacity
@@ -106,8 +111,9 @@
         back = lax.ppermute(partial[s], "ty", shift_pairs(n_ty, -s))
         expert_sum = expert_sum + back.astype(jnp.float32)
     expert_sum = expert_sum.astype(jnp.bfloat16)
-    expert_out = expert_sum.reshape(n_expert, capacity, width)
-    returned = lax.all_to_all(expert_out, "expert", split_axis=0, concat_axis=0, tiled=True)
+    expert_out = expert_sum.reshape(n_ez, n_ec, capacity, width)
+    returned = lax.all_to_all(expert_out, "ec", split_axis=1, concat_axis=1, tiled=True)
+    returned = lax.all_to_all(returned, "ez", split_axis=0, concat_axis=0, tiled=True)
     returned = returned.reshape(slot_total, width)
     per_route = lax.dot_general(
         placing, returned, (((0,), (0,)), ((), ())), preferred_element_type=jnp.float32
@@ -133,18 +139,19 @@
 def solution(mesh):
     n_expert = mesh.shape["expert"]
     n_ty, n_tx = split_tensor(mesh.shape["tensor"])
-    grid = Mesh(mesh.devices.reshape(n_expert, n_ty, n_tx), ROWS_AXES)
+    n_ec = 2 if n_expert % 2 == 0 else 1
+    grid = Mesh(mesh.devices.reshape(n_expert // n_ec, n_ec, n_ty, n_tx), ROWS_AXES)
     rows = P(ROWS_AXES, None)
     placed = (
         rows,
-        P(TENSOR_AXES, "expert"),
+        P(TENSOR_AXES, EXPERT_AXES),
         P(TENSOR_AXES, None),
         P(),
         P(),
         rows,
-        P("expert", TENSOR_AXES, None),
-        P("expert", TENSOR_AXES, None),
-        P("expert", TENSOR_AXES, None),
+        P(EXPERT_AXES, TENSOR_AXES, None),
+        P(EXPERT_AXES, TENSOR_AXES, None),
+        P(EXPERT_AXES, TENSOR_AXES, None),
         P(),
     )
     return jax.shard_map(

time: 189 us -> 199 us (1.053); the launches traced: 189 us -> 196 us
  blocking collectives: 0 us -> 13 us
  waiting for transfers between devices: 112 us -> 107 us
  starting transfers between devices: 41.6 us -> 37.4 us
  local copies, waits for them, and re-layouts: 13.3 us -> 15.9 us
    all_to_all x0 -> x2, blocking collectives: none -> 13 us  [the longest x1 8.6 us: per_device(): lax.all_to_all(expert_out, 'ec', split_axis=1, concat_axis=1, tiled=True)]
    ppermute x3, waiting for transfers between devices: 34.3 us -> 28.6 us  [per_device(): back = lax.ppermute(partial[s], 'ty', shift_pairs(n_ty, -s))]
    ppermute x3, waiting for transfers between devices: 4.12 us -> 6.75 us  [per_device(): lax.ppermute(rows_in, 'ty', shift_pairs(n_ty, s))]
    all_to_all x0 -> x4, local copies, waits for them, and re-layouts: none -> 2.42 us  [the longest x1 1.6 us: per_device(): lax.all_to_all(expert_out, 'ec', split_axis=1, concat_axis=1, tiled=True)]
  transfers between devices with their start and end apart: 19 -> 19, of which waited for: 12 -> 9; matrix products, arithmetic and copies ran while one was open for 6% -> 6% of each run, Pallas kernels for 0% -> 0%
where the time goes in v8:
time: 199 us; the launch traced here: 196 us
  waiting for transfers between devices  107 us (54%)
  starting transfers between devices  37.4 us (19%)
  local copies, waits for them, and re-layouts  15.9 us (8%)
  matrix products  14.7 us (7%)
  blocking collectives  13 us (7%)
  other arithmetic  6.34 us (3%)
    ppermute x3, waiting for transfers between devices, per_device(): back = lax.ppermute(partial[s], 'ty', shift_pairs(n_ty, -s))  28.6 us
    ppermute x3, waiting for transfers between devices, per_device(): lax.ppermute(stacked, 'tx', shift_pairs(n_tx, s))  21.6 us
    all_to_all x1, waiting for transfers between devices, per_device(): lax.all_to_all(send_slots, 'ez', split_axis=0, concat_axis=0, tiled=True)  18.9 us
    all_to_all x1, waiting for transfers between devices, per_device(): lax.all_to_all(returned, 'ez', split_axis=0, concat_axis=0, tiled=True)  18.7 us
    ppermute x3, waiting for transfers between devices, per_device(): lax.ppermute(near, 'ty', shift_pairs(n_ty, s))  11.9 us
    dot_general x1, matrix products, expert_block(): return jnp.dot(hid, down_rows, preferred_element_type=jnp.float32)  8.61 us
    all_to_all x1, blocking collectives, per_device(): lax.all_to_all(expert_out, 'ec', split_axis=1, concat_axis=1, tiled=True)  8.6 us
    all_to_all x1, starting transfers between devices, per_device(): lax.all_to_all(send_slots, 'ez', split_axis=0, concat_axis=0, tiled=True)  8.18 us
  transfers between devices with their start and end apart: 19, of which 9 were waited for; matrix products, arithmetic and copies ran while one was open for 6% of the time, Pallas kernels for 0%

profile of v8, /device:TPU:1, one launch (start us, length us, event | category | flops | bytes accessed | tf_op | source)
XLA Modules:
  0.0 195.7 jit_solution(5087119504112750196)
XLA Ops:
  0.7 0.9 copy-done
  1.5 3.6 %collective-permute-start.1 = (bf16[64,512]{1,0:T(8,128)(2,1)S(1)}, bf16[64,512]{1,0:T(8,128)(2,1)S(1)}, u32[]{:S(2)}, u32[]{:S(2)}) collective-permute-start(bf16[64,512]{1,0:T(8,128)(2,1)S(1)} %constant_dynamic-slice_fusion), channel_id=1, source_target_pairs={{0,2},{1,3},{2,0},{3,1},{4,6},{5,7},{6,4},{7,5},{8,10},{9,11},{10,... | collective-permute-start | bytes 196616 | tf_op jit(solution)/shard_map/ppermute | solution.py:57
  5.1 0.3 collective-permute-start
  5.4 2.4 %collective-permute-start.2 = (bf16[64,512]{1,0:T(8,128)(2,1)S(1)}, bf16[64,512]{1,0:T(8,128)(2,1)S(1)}, u32[]{:S(2)}, u32[]{:S(2)}) collective-permute-start(bf16[64,512]{1,0:T(8,128)(2,1)S(1)} %constant_dynamic-slice_fusion), channel_id=1, source_target_pairs={{0,3},{1,0},{2,1},{3,2},{4,7},{5,4},{6,5},{7,6},{8,11},{9,8},{10,9... | collective-permute-start | bytes 196616 | tf_op jit(solution)/shard_map/ppermute | solution.py:57
  7.8 1.4 all_to_all.24
  9.2 0.8 copy.45
  10.0 4.3 %all-to-all-start = ((bf16[64,16,88]{2,0,1:T(8,128)(2,1)}), bf16[64,16,88]{2,0,1:T(8,128)(2,1)S(1)}, u32[]{:S(2)}, u32[]{:S(2)}) async-start(bf16[64,16,88]{2,0,1:T(8,128)(2,1)} %copy.45), calls=%async_computation | async-start | bytes 524288 | tf_op jit(solution)/shard_map/all_to_all | solution.py:62
  14.3 0.8 copy.50
  15.3 0.6 reduce-window.6
  15.9 0.2 slice_reduce_fusion
  16.2 2.9 %collective-permute-start.4 = (bf16[4,64,512]{2,1,0:T(8,128)(2,1)S(1)}, bf16[4,64,512]{2,1,0:T(8,128)(2,1)S(1)}, u32[]{:S(2)}, u32[]{:S(2)}) collective-permute-start(bf16[4,64,512]{2,1,0:T(8,128)(2,1)S(1)} %get-tuple-element.12), channel_id=1, source_target_pairs={{0,8},{4,12},{8,0},{12,4},{1,9},{5,13},{9,1},{13,5},{2,10},{6,14},... | collective-permute-start | bytes 786440 | tf_op jit(solution)/shard_map/ppermute | solution.py:59
  19.1 0.3 collective-permute-start.3
  19.4 2.4 %collective-permute-start.5 = (bf16[4,64,512]{2,1,0:T(8,128)(2,1)S(1)}, bf16[4,64,512]{2,1,0:T(8,128)(2,1)S(1)}, u32[]{:S(2)}, u32[]{:S(2)}) collective-permute-start(bf16[4,64,512]{2,1,0:T(8,128)(2,1)S(1)} %get-tuple-element.12), channel_id=1, source_target_pairs={{0,12},{4,0},{8,4},{12,8},{1,13},{5,1},{9,5},{13,9},{2,14},{6,2},{... | collective-permute-start | bytes 786440 | tf_op jit(solution)/shard_map/ppermute | solution.py:59
  21.8 5.3 %collective-permute-done.4 = bf16[4,64,512]{2,1,0:T(8,128)(2,1)S(1)} collective-permute-done((bf16[4,64,512]{2,1,0:T(8,128)(2,1)S(1)}, bf16[4,64,512]{2,1,0:T(8,128)(2,1)S(1)}, u32[]{:S(2)}, u32[]{:S(2)}) %collective-permute-start.4) | collective-permute-done | bytes 262176 | tf_op jit(solution)/shard_map/ppermute | solution.py:59
  27.2 6.6 %collective-permute-done.3 = bf16[4,64,512]{2,1,0:T(8,128)(2,1)S(1)} collective-permute-done((bf16[4,64,512]{2,1,0:T(8,128)(2,1)S(1)}, bf16[4,64,512]{2,1,0:T(8,128)(2,1)S(1)}, u32[]{:S(2)}, u32[]{:S(2)}) %collective-permute-start.3) | collective-permute-done | bytes 262176 | tf_op jit(solution)/shard_map/ppermute | solution.py:59
  33.9 0.5 collective-permute-start.6
  34.6 0.6 gather_fusion
  35.3 0.6 gather_fusion.1
  35.9 0.4 convolution_bitcast_fusion.1
  36.3 0.5 collective-permute-done.6
  36.7 0.4 convolution_bitcast_fusion
  37.1 0.2 fusion.20
  37.4 0.2 broadcast_in_dim.40
  37.6 0.1 reshape.234
  37.8 0.3 convolution_convert_fusion.1
  38.1 0.2 reshape_reshape.3
  38.3 1.6 copy.53
  40.0 8.2 %all-to-all-start.1 = ((bf16[8,2,22,1024]{3,1,2,0:T(2,128)(2,1)}), bf16[8,2,22,1024]{3,1,2,0:T(2,128)(2,1)S(1)}, u32[]{:S(2)}, u32[]{:S(2)}) async-start(bf16[8,2,22,1024]{3,1,2,0:T(2,128)(2,1)} %copy.53), calls=%async_computation.1 | async-start | bytes 1441792 | tf_op jit(solution)/shard_map/all_to_all | solution.py:99
  48.3 1.9 collective-permute-start.12
  50.2 0.8 collective-permute-start.11
  51.0 0.4 collective-permute-start.10
  51.4 18.9 %all-to-all-done.1 = bf16[8,2,22,1024]{3,1,2,0:T(2,128)(2,1)S(1)} async-done(((bf16[8,2,22,1024]{3,1,2,0:T(2,128)(2,1)}), bf16[8,2,22,1024]{3,1,2,0:T(2,128)(2,1)S(1)}, u32[]{:S(2)}, u32[]{:S(2)}) %all-to-all-start.1) | async-done | bytes 720928 | tf_op jit(solution)/shard_map/all_to_all | solution.py:99
  70.3 0.2 copy.54
  70.5 4.4 %all_to_all.36 = bf16[8,2,22,1024]{3,0,2,1:T(8,128)(2,1)S(1)} all-to-all(bf16[8,2,22,1024]{3,0,2,1:T(8,128)(2,1)S(1)} %copy.54), channel_id=1, replica_groups=mesh['ez'=8,'ec'=2,'ty'=4,'tx'=4] {'ec'}, dimensions={1} | all-to-all | bytes 1441792 | tf_op jit(solution)/shard_map/all_to_all | solution.py:100
  75.0 0.4 copy.55
  75.4 0.2 reshape.235
  75.6 0.8 collective-permute-start.7
  76.4 2.2 %collective-permute-start.8 = (bf16[352,1024]{1,0:T(8,128)(2,1)S(1)}, bf16[352,1024]{1,0:T(8,128)(2,1)S(1)}, u32[]{:S(2)}, u32[]{:S(2)}) collective-permute-start(bf16[352,1024]{1,0:T(8,128)(2,1)S(1)} %reshape.235), channel_id=1, source_target_pairs={{0,8},{4,12},{8,0},{12,4},{1,9},{5,13},{9,1},{13,5},{2,10},{6,14},... | collective-permute-start | bytes 2162696 | tf_op jit(solution)/shard_map/ppermute | solution.py:105
  78.5 0.7 collective-permute-start.9
  79.2 21.6 %collective-permute-done.10 = bf16[3,176,1024]{2,1,0:T(8,128)(2,1)} collective-permute-done((bf16[3,176,1024]{2,1,0:T(8,128)(2,1)S(1)}, bf16[3,176,1024]{2,1,0:T(8,128)(2,1)}, u32[]{:S(2)}, u32[]{:S(2)}) %collective-permute-start.10) | collective-permute-done | bytes 1081376 | tf_op jit(solution)/shard_map/ppermute | solution.py:78
  100.8 2.2 %pad_maximum_fusion = bf16[3,704,1024]{2,1,0:T(8,128)(2,1)S(1)} fusion(bf16[3,176,1024]{2,1,0:T(8,128)(2,1)} %collective-permute-done.12, bf16[3,176,1024]{2,1,0:T(8,128)(2,1)} %collective-permute-done.11, bf16[3,176,1024]{2,1,0:T(8,128)(2,1)} %collective-permute-done.10, bf16[3,176,1024]{2,1,0:T(8,128)(2,1)S(1)} %constant_dynamic-update-slice_fusion.4), kind=kLoop, calls=%fused_computation.4 | loop fusion | flops 17301504 | bytes 8650752 | tf_op jit(solution)/shard_map/concatenate | solution.py:101
  103.1 6.7 %collective-permute-done.8 = bf16[352,1024]{1,0:T(8,128)(2,1)S(1)} collective-permute-done((bf16[352,1024]{1,0:T(8,128)(2,1)S(1)}, bf16[352,1024]{1,0:T(8,128)(2,1)S(1)}, u32[]{:S(2)}, u32[]{:S(2)}) %collective-permute-start.8) | collective-permute-done | bytes 720928 | tf_op jit(solution)/shard_map/ppermute | solution.py:105
  110.0 1.6 copy-done.7
  111.6 4.4 %fusion.15 = f32[1408,704]{0,1:T(8,128)} fusion(bf16[1408,1024]{1,0:T(8,128)(2,1)S(1)} %constant_dynamic-update-slice_fusion, bf16[3,704,1024]{2,1,0:T(8,128)(2,1)S(1)} %pad_maximum_fusion), kind=kOutput, calls=%fused_computation.23 | convolution fusion | flops 2030043136 | bytes 8290304 | tf_op jit(solution)/shard_map/dot_general | solution.py:21
  116.0 8.6 %convolution_convert_fusion = bf16[1408,1024]{1,0:T(8,128)(2,1)S(1)} fusion(f32[1408,704]{0,1:T(8,128)} %fusion.15, bf16[3,704,1024]{2,1,0:T(8,128)(2,1)} %copy-done.1, bf16[1408,1024]{1,0:T(8,128)(2,1)} %copy-done.7), kind=kOutput, calls=%fused_computation.14 | convolution fusion | flops 4071440384 | bytes 12615680 | tf_op jit(solution)/shard_map/dot_general | solution.py:28
  124.7 0.2 fusion.48
  124.9 1.5 collective-permute-start.15
  126.4 0.8 collective-permute-start.14
  127.2 13.7 %collective-permute-done.13 = bf16[352,1024]{1,0:T(8,128)(2,1)S(1)} collective-permute-done((bf16[352,1024]{1,0:T(8,128)(2,1)S(1)}, bf16[352,1024]{1,0:T(8,128)(2,1)S(1)}, u32[]{:S(2)}, u32[]{:S(2)}) %collective-permute-start.13) | collective-permute-done | bytes 720928 | tf_op jit(solution)/shard_map/ppermute | solution.py:111
  140.9 14.9 %collective-permute-done.14 = bf16[352,1024]{1,0:T(8,128)(2,1)S(1)} collective-permute-done((bf16[352,1024]{1,0:T(8,128)(2,1)S(1)}, bf16[352,1024]{1,0:T(8,128)(2,1)S(1)}, u32[]{:S(2)}, u32[]{:S(2)}) %collective-permute-start.14) | collective-permute-done | bytes 720928 | tf_op jit(solution)/shard_map/ppermute | solution.py:111
  155.8 1.7 add_convert_fusion
  157.5 0.2 reshape.236
  157.7 0.4 copy.56
  158.1 8.6 %all_to_all.37 = bf16[8,2,22,1024]{3,0,2,1:T(8,128)(2,1)S(1)} all-to-all(bf16[8,2,22,1024]{3,0,2,1:T(8,128)(2,1)S(1)} %copy.56), channel_id=1, replica_groups=mesh['ez'=8,'ec'=2,'ty'=4,'tx'=4] {'ec'}, dimensions={1} | all-to-all | bytes 1441792 | tf_op jit(solution)/shard_map/all_to_all | solution.py:115
  166.7 1.6 copy.57
  168.3 3.5 %all-to-all-start.4 = ((bf16[8,2,22,1024]{3,1,2,0:T(2,128)(2,1)}), bf16[8,2,22,1024]{3,1,2,0:T(2,128)(2,1)S(1)}, u32[]{:S(2)}, u32[]{:S(2)}) async-start(bf16[8,2,22,1024]{3,1,2,0:T(2,128)(2,1)} %copy.57), calls=%async_computation.4 | async-start | bytes 1441792 | tf_op jit(solution)/shard_map/all_to_all | solution.py:116
  172.3 0.3 fusion.49
  172.7 2.3 %gather_fusion.2 = f32[176]{0:T(256)S(1)} fusion(f32[88,16]{0,1:T(8,128)S(1)} %fusion.32, s32[176]{0:T(256)S(1)} %reshape.255), kind=kCustom, calls=%fused_computation.2 | custom fusion | bytes 2816 | tf_op jit(solution)/shard_map/jit(take_along_axis)/gather | solution.py:85
  175.2 18.7 %all-to-all-done.4 = bf16[8,2,22,1024]{3,1,2,0:T(2,128)(2,1)S(1)} async-done(((bf16[8,2,22,1024]{3,1,2,0:T(2,128)(2,1)}), bf16[8,2,22,1024]{3,1,2,0:T(2,128)(2,1)S(1)}, u32[]{:S(2)}, u32[]{:S(2)}) %all-to-all-start.4) | async-done | bytes 720928 | tf_op jit(solution)/shard_map/all_to_all | solution.py:116
  193.9 0.2 copy.58
  194.2 0.2 reshape.268
  194.4 0.4 fusion.16
  194.7 0.2 fusion.17
  194.9 0.8 fusion.19
  (75 shorter events, 2.0 us)
Async XLA Ops:
  0.6 0.9 copy-start
  1.5 14.5 %collective-permute-start.1 = (bf16[64,512]{1,0:T(8,128)(2,1)S(1)}, bf16[64,512]{1,0:T(8,128)(2,1)S(1)}, u32[]{:S(2)}, u32[]{:S(2)}) collective-permute-start(bf16[64,512]{1,0:T(8,128)(2,1)S(1)} %constant_dynamic-slice_fusion), channel_id=1, source_target_pairs={{0,2},{1,3},{2,0},{3,1},{4,6},{5,7},{6,4},{7,5},{8,10},{9,11},{10,... | collective-permute-start | bytes 196616 | tf_op jit(solution)/shard_map/ppermute | solution.py:57
  5.1 11.0 %collective-permute-start = (bf16[64,512]{1,0:T(8,128)(2,1)S(1)}, bf16[64,512]{1,0:T(8,128)(2,1)S(1)}, u32[]{:S(2)}, u32[]{:S(2)}) collective-permute-start(bf16[64,512]{1,0:T(8,128)(2,1)S(1)} %constant_dynamic-slice_fusion), channel_id=1, source_target_pairs={{0,1},{1,2},{2,3},{3,0},{4,5},{5,6},{6,7},{7,4},{8,9},{9,10},{10,1... | collective-permute-start | bytes 196616 | tf_op jit(solution)/shard_map/ppermute | solution.py:57
  5.4 10.7 %collective-permute-start.2 = (bf16[64,512]{1,0:T(8,128)(2,1)S(1)}, bf16[64,512]{1,0:T(8,128)(2,1)S(1)}, u32[]{:S(2)}, u32[]{:S(2)}) collective-permute-start(bf16[64,512]{1,0:T(8,128)(2,1)S(1)} %constant_dynamic-slice_fusion), channel_id=1, source_target_pairs={{0,3},{1,0},{2,1},{3,2},{4,7},{5,4},{6,5},{7,6},{8,11},{9,8},{10,9... | collective-permute-start | bytes 196616 | tf_op jit(solution)/shard_map/ppermute | solution.py:57
  10.0 24.6 %all-to-all-start = ((bf16[64,16,88]{2,0,1:T(8,128)(2,1)}), bf16[64,16,88]{2,0,1:T(8,128)(2,1)S(1)}, u32[]{:S(2)}, u32[]{:S(2)}) async-start(bf16[64,16,88]{2,0,1:T(8,128)(2,1)} %copy.45), calls=%async_computation | async-start | bytes 524288 | tf_op jit(solution)/shard_map/all_to_all | solution.py:62
  16.2 11.0 %collective-permute-start.4 = (bf16[4,64,512]{2,1,0:T(8,128)(2,1)S(1)}, bf16[4,64,512]{2,1,0:T(8,128)(2,1)S(1)}, u32[]{:S(2)}, u32[]{:S(2)}) collective-permute-start(bf16[4,64,512]{2,1,0:T(8,128)(2,1)S(1)} %get-tuple-element.12), channel_id=1, source_target_pairs={{0,8},{4,12},{8,0},{12,4},{1,9},{5,13},{9,1},{13,5},{2,10},{6,14},... | collective-permute-start | bytes 786440 | tf_op jit(solution)/shard_map/ppermute | solution.py:59
  19.1 14.7 %collective-permute-start.3 = (bf16[4,64,512]{2,1,0:T(8,128)(2,1)S(1)}, bf16[4,64,512]{2,1,0:T(8,128)(2,1)S(1)}, u32[]{:S(2)}, u32[]{:S(2)}) collective-permute-start(bf16[4,64,512]{2,1,0:T(8,128)(2,1)S(1)} %get-tuple-element.12), channel_id=1, source_target_pairs={{0,4},{4,8},{8,12},{12,0},{1,5},{5,9},{9,13},{13,1},{2,6},{6,10},{... | collective-permute-start | bytes 786440 | tf_op jit(solution)/shard_map/ppermute | solution.py:59
  19.4 14.4 %collective-permute-start.5 = (bf16[4,64,512]{2,1,0:T(8,128)(2,1)S(1)}, bf16[4,64,512]{2,1,0:T(8,128)(2,1)S(1)}, u32[]{:S(2)}, u32[]{:S(2)}) collective-permute-start(bf16[4,64,512]{2,1,0:T(8,128)(2,1)S(1)} %get-tuple-element.12), channel_id=1, source_target_pairs={{0,12},{4,0},{8,4},{12,8},{1,13},{5,1},{9,5},{13,9},{2,14},{6,2},{... | collective-permute-start | bytes 786440 | tf_op jit(solution)/shard_map/ppermute | solution.py:59
  33.8 3.3 %copy-start.8 = (bf16[88,1024]{1,0:T(8,128)(2,1)S(1)}, bf16[88,1024]{1,0:T(8,128)(2,1)}, u32[]{:S(2)}) copy-start(bf16[88,1024]{1,0:T(8,128)(2,1)} %param.10) | copy-start | bytes 540676
  33.9 3.3 %copy-start.11 = (f32[1024]{0:T(1024)S(1)}, f32[1024]{0:T(1024)}, u32[]{:S(2)}) copy-start(f32[1024]{0:T(1024)} %param.13) | copy-start | bytes 12292
  33.9 2.8 %collective-permute-start.6 = (bf16[4,4,64,512]{3,2,1,0:T(8,128)(2,1)S(1)}, bf16[4,4,64,512]{3,2,1,0:T(8,128)(2,1)S(1)}, u32[]{:S(2)}, u32[]{:S(2)}) collective-permute-start(bf16[4,4,64,512]{3,2,1,0:T(8,128)(2,1)S(1)} %pad_maximum_fusion.1), channel_id=1, source_target_pairs={{0,16},{16,0},{1,17},{17,1},{2,18},{18,2},{3,19},{19,3},{4,20},{20... | collective-permute-start | bytes 3145736 | tf_op jit(solution)/shard_map/ppermute | solution.py:61
  37.7 10.4 %copy-start.4 = (bf16[1,176,1024]{2,1,0:T(8,128)(2,1)S(1)}, bf16[1,176,1024]{2,1,0:T(8,128)(2,1)}, u32[]{:S(2)}) copy-start(bf16[1,176,1024]{2,1,0:T(8,128)(2,1)} %param.16) | copy-start | bytes 1081348
  37.8 10.4 %copy-start.5 = (bf16[1,176,1024]{2,1,0:T(8,128)(2,1)S(1)}, bf16[1,176,1024]{2,1,0:T(8,128)(2,1)}, u32[]{:S(2)}) copy-start(bf16[1,176,1024]{2,1,0:T(8,128)(2,1)} %param.17) | copy-start | bytes 1081348
  38.1 10.1 %copy-start.6 = (bf16[1,176,1024]{2,1,0:T(8,128)(2,1)S(1)}, bf16[1,176,1024]{2,1,0:T(8,128)(2,1)}, u32[]{:S(2)}) copy-start(bf16[1,176,1024]{2,1,0:T(8,128)(2,1)} %param.18) | copy-start | bytes 1081348
  40.0 30.4 %all-to-all-start.1 = ((bf16[8,2,22,1024]{3,1,2,0:T(2,128)(2,1)}), bf16[8,2,22,1024]{3,1,2,0:T(2,128)(2,1)S(1)}, u32[]{:S(2)}, u32[]{:S(2)}) async-start(bf16[8,2,22,1024]{3,1,2,0:T(2,128)(2,1)} %copy.53), calls=%async_computation.1 | async-start | bytes 1441792 | tf_op jit(solution)/shard_map/all_to_all | solution.py:99
  48.3 30.3 %collective-permute-start.12 = (bf16[3,176,1024]{2,1,0:T(8,128)(2,1)S(1)}, bf16[3,176,1024]{2,1,0:T(8,128)(2,1)}, u32[]{:S(2)}, u32[]{:S(2)}) collective-permute-start(bf16[3,176,1024]{2,1,0:T(8,128)(2,1)S(1)} %constant_dynamic-update-slice_fusion.4), channel_id=1, source_target_pairs={{0,3},{1,0},{2,1},{3,2},{4,7},{5,4},{6,5},{7,6},{8,11},{9,8},{10,9... | collective-permute-start | bytes 3244040 | tf_op jit(solution)/shard_map/ppermute | solution.py:78
  50.2 29.0 %collective-permute-start.11 = (bf16[3,176,1024]{2,1,0:T(8,128)(2,1)S(1)}, bf16[3,176,1024]{2,1,0:T(8,128)(2,1)}, u32[]{:S(2)}, u32[]{:S(2)}) collective-permute-start(bf16[3,176,1024]{2,1,0:T(8,128)(2,1)S(1)} %constant_dynamic-update-slice_fusion.4), channel_id=1, source_target_pairs={{0,2},{1,3},{2,0},{3,1},{4,6},{5,7},{6,4},{7,5},{8,10},{9,11},{10,... | collective-permute-start | bytes 3244040 | tf_op jit(solution)/shard_map/ppermute | solution.py:78
  51.0 49.8 %collective-permute-start.10 = (bf16[3,176,1024]{2,1,0:T(8,128)(2,1)S(1)}, bf16[3,176,1024]{2,1,0:T(8,128)(2,1)}, u32[]{:S(2)}, u32[]{:S(2)}) collective-permute-start(bf16[3,176,1024]{2,1,0:T(8,128)(2,1)S(1)} %constant_dynamic-update-slice_fusion.4), channel_id=1, source_target_pairs={{0,1},{1,2},{2,3},{3,0},{4,5},{5,6},{6,7},{7,4},{8,9},{9,10},{10,1... | collective-permute-start | bytes 3244040 | tf_op jit(solution)/shard_map/ppermute | solution.py:78
  75.6 27.5 %collective-permute-start.7 = (bf16[352,1024]{1,0:T(8,128)(2,1)S(1)}, bf16[352,1024]{1,0:T(8,128)(2,1)S(1)}, u32[]{:S(2)}, u32[]{:S(2)}) collective-permute-start(bf16[352,1024]{1,0:T(8,128)(2,1)S(1)} %reshape.235), channel_id=1, source_target_pairs={{0,4},{4,8},{8,12},{12,0},{1,5},{5,9},{9,13},{13,1},{2,6},{6,10},{... | collective-permute-start | bytes 2162696 | tf_op jit(solution)/shard_map/ppermute | solution.py:105
  76.4 33.5 %collective-permute-start.8 = (bf16[352,1024]{1,0:T(8,128)(2,1)S(1)}, bf16[352,1024]{1,0:T(8,128)(2,1)S(1)}, u32[]{:S(2)}, u32[]{:S(2)}) collective-permute-start(bf16[352,1024]{1,0:T(8,128)(2,1)S(1)} %reshape.235), channel_id=1, source_target_pairs={{0,8},{4,12},{8,0},{12,4},{1,9},{5,13},{9,1},{13,5},{2,10},{6,14},... | collective-permute-start | bytes 2162696 | tf_op jit(solution)/shard_map/ppermute | solution.py:105
  78.5 31.4 %collective-permute-start.9 = (bf16[352,1024]{1,0:T(8,128)(2,1)S(1)}, bf16[352,1024]{1,0:T(8,128)(2,1)S(1)}, u32[]{:S(2)}, u32[]{:S(2)}) collective-permute-start(bf16[352,1024]{1,0:T(8,128)(2,1)S(1)} %reshape.235), channel_id=1, source_target_pairs={{0,12},{4,0},{8,4},{12,8},{1,13},{5,1},{9,5},{13,9},{2,14},{6,2},{... | collective-permute-start | bytes 2162696 | tf_op jit(solution)/shard_map/ppermute | solution.py:105
  103.0 7.0 %copy-start.1 = (bf16[3,704,1024]{2,1,0:T(8,128)(2,1)}, bf16[3,704,1024]{2,1,0:T(8,128)(2,1)S(1)}, u32[]{:S(2)}) copy-start(bf16[3,704,1024]{2,1,0:T(8,128)(2,1)S(1)} %pad_maximum_fusion) | copy-start | bytes 12976132
  110.0 1.7 copy-start.7
  124.6 16.2 %copy-start.2 = (bf16[1408,1024]{1,0:T(8,128)(2,1)}, bf16[1408,1024]{1,0:T(8,128)(2,1)S(1)}, u32[]{:S(2)}) copy-start(bf16[1408,1024]{1,0:T(8,128)(2,1)S(1)} %convolution_convert_fusion) | copy-start | bytes 8650756
  124.8 16.0 %collective-permute-start.13 = (bf16[352,1024]{1,0:T(8,128)(2,1)S(1)}, bf16[352,1024]{1,0:T(8,128)(2,1)S(1)}, u32[]{:S(2)}, u32[]{:S(2)}) collective-permute-start(bf16[352,1024]{1,0:T(8,128)(2,1)S(1)} %get-tuple-element.8), channel_id=1, source_target_pairs={{0,12},{4,0},{8,4},{12,8},{1,13},{5,1},{9,5},{13,9},{2,14},{6,2},{... | collective-permute-start | bytes 2162696 | tf_op jit(solution)/shard_map/ppermute | solution.py:111
  124.9 15.9 %collective-permute-start.15 = (bf16[352,1024]{1,0:T(8,128)(2,1)S(1)}, bf16[352,1024]{1,0:T(8,128)(2,1)S(1)}, u32[]{:S(2)}, u32[]{:S(2)}) collective-permute-start(bf16[352,1024]{1,0:T(8,128)(2,1)S(1)} %get-tuple-element.9), channel_id=1, source_target_pairs={{0,4},{4,8},{8,12},{12,0},{1,5},{5,9},{9,13},{13,1},{2,6},{6,10},{... | collective-permute-start | bytes 2162696 | tf_op jit(solution)/shard_map/ppermute | solution.py:111
  126.4 29.4 %collective-permute-start.14 = (bf16[352,1024]{1,0:T(8,128)(2,1)S(1)}, bf16[352,1024]{1,0:T(8,128)(2,1)S(1)}, u32[]{:S(2)}, u32[]{:S(2)}) collective-permute-start(bf16[352,1024]{1,0:T(8,128)(2,1)S(1)} %get-tuple-element.10), channel_id=1, source_target_pairs={{0,8},{4,12},{8,0},{12,4},{1,9},{5,13},{9,1},{13,5},{2,10},{6,14},... | collective-permute-start | bytes 2162696 | tf_op jit(solution)/shard_map/ppermute | solution.py:111
  157.7 14.2 %copy-start.10 = (s32[88,2]{0,1:T(2,128)S(1)}, s32[88,2]{0,1:T(2,128)}, u32[]{:S(2)}) copy-start(s32[88,2]{0,1:T(2,128)} %param.15) | copy-start | bytes 2116
  157.7 14.7 %copy-start.9 = (f32[1024,16]{0,1:T(8,128)S(1)}, f32[1024,16]{0,1:T(8,128)}, u32[]{:S(2)}) copy-start(f32[1024,16]{0,1:T(8,128)} %param.14) | copy-start | bytes 196612
  168.3 25.6 %all-to-all-start.4 = ((bf16[8,2,22,1024]{3,1,2,0:T(2,128)(2,1)}), bf16[8,2,22,1024]{3,1,2,0:T(2,128)(2,1)S(1)}, u32[]{:S(2)}, u32[]{:S(2)}) async-start(bf16[8,2,22,1024]{3,1,2,0:T(2,128)(2,1)} %copy.57), calls=%async_computation.4 | async-start | bytes 1441792 | tf_op jit(solution)/shard_map/all_to_all | solution.py:116
  174.9 20.0 %copy-start.12 = (f32[1024]{0:T(1024)S(1)}, f32[1024]{0:T(1024)}, u32[]{:S(2)}) copy-start(f32[1024]{0:T(1024)} %param.19) | copy-start | bytes 12292
  194.9 0.8 copy-start.3

commit v9 on v5

--- a/solution.py
+++ b/solution.py
@@ -72,7 +72,7 @@
 
     stacked = jnp.concatenate([w_gate, w_upward, w_downward], axis=0)
     pieces = [stacked] + [
-        lax.ppermute(stacked, "tx", shift_pairs(n_tx, s)) for s in range(1, n_tx)
+        lax.ppermute(stacked, "ty", shift_pairs(n_ty, s)) for s in range(1, n_ty)
     ]
 
     hidden_one = (residual_in.astype(jnp.float32) + projected).astype(jnp.bfloat16)
@@ -97,13 +97,13 @@
     gate_rows, up_rows, down_rows = weights[0], weights[1], weights[2]
     slot_total = n_expert * capacity
     rows_in = received.reshape(slot_total, width)
-    all_rows = [rows_in] + [lax.ppermute(rows_in, "ty", shift_pairs(n_ty, s)) for s in range(1, n_ty)]
+    all_rows = [rows_in] + [lax.ppermute(rows_in, "tx", shift_pairs(n_tx, s)) for s in range(1, n_tx)]
     all_rows = jnp.concatenate(all_rows, axis=0)
     partial = expert_block(all_rows, gate_rows, up_rows, down_rows).astype(jnp.bfloat16)
-    partial = partial.reshape(n_ty, slot_total, width)
+    partial = partial.reshape(n_tx, slot_total, width)
     expert_sum = partial[0].astype(jnp.float32)
-    for s in range(1, n_ty):
-        back = lax.ppermute(partial[s], "ty", shift_pairs(n_ty, -s))
+    for s in range(1, n_tx):
+        back = lax.ppermute(partial[s], "tx", shift_pairs(n_tx, -s))
         expert_sum = expert_sum + back.astype(jnp.float32)
     expert_sum = expert_sum.astype(jnp.bfloat16)
     expert_out = expert_sum.reshape(n_expert, capacity, width)

time: 189 us -> 189 us (level)
  waiting for transfers between devices: 112 us -> 108 us
  starting transfers between devices: 41.6 us -> 44.2 us
    ppermute x9, waiting for transfers between devices: 61.9 us -> 58 us  [the longest x3 32 us: per_device(): back = lax.ppermute(partial[s], 'tx', shift_pairs(n_tx, -s))]
    all_to_all x1, starting transfers between devices: 4.59 us -> 8.35 us  [per_device(): lax.all_to_all(expert_out, 'expert', split_axis=0, concat_axis=0, tiled=T...]
  transfers between devices with their start and end apart: 19 -> 19, of which waited for: 12 -> 11; matrix products, arithmetic and copies ran while one was open for 6% -> 6% of each run, Pallas kernels for 0% -> 0%
where the time goes in v9:
time: 189 us; the launch traced here: 188 us
  waiting for transfers between devices  108 us (57%)
  starting transfers between devices  44.2 us (23%)
  matrix products  14.7 us (8%)
  local copies, waits for them, and re-layouts  13.3 us (7%)
  other arithmetic  6.33 us (3%)
    ppermute x3, waiting for transfers between devices, per_device(): back = lax.ppermute(partial[s], 'tx', shift_pairs(n_tx, -s))  32 us
    ppermute x3, waiting for transfers between devices, per_device(): lax.ppermute(stacked, 'ty', shift_pairs(n_ty, s))  22.4 us
    all_to_all x1, waiting for transfers between devices, per_device(): lax.all_to_all(expert_out, 'expert', split_axis=0, concat_axis=0, tiled=T...  19.4 us
    all_to_all x1, waiting for transfers between devices, per_device(): lax.all_to_all(send_slots, 'expert', split_axis=0, concat_axis=0, tiled=T...  18.9 us
    ppermute x3, waiting for transfers between devices, per_device(): lax.ppermute(near, 'ty', shift_pairs(n_ty, s))  11.7 us
    all_to_all x1, starting transfers between devices, per_device(): lax.all_to_all(send_slots, 'expert', split_axis=0, concat_axis=0, tiled=T...  8.85 us
    dot_general x1, matrix products, expert_block(): return jnp.dot(hid, down_rows, preferred_element_type=jnp.float32)  8.6 us
    all_to_all x1, starting transfers between devices, per_device(): lax.all_to_all(expert_out, 'expert', split_axis=0, concat_axis=0, tiled=T...  8.35 us
  transfers between devices with their start and end apart: 19, of which 11 were waited for; matrix products, arithmetic and copies ran while one was open for 6% of the time, Pallas kernels for 0%

profile of v9, /device:TPU:1, one launch (start us, length us, event | category | flops | bytes accessed | tf_op | source)
XLA Modules:
  0.0 188.1 jit_solution(9514466397145070177)
XLA Ops:
  0.7 0.9 copy-done
  1.5 2.0 %collective-permute-start = (bf16[64,512]{1,0:T(8,128)(2,1)S(1)}, bf16[64,512]{1,0:T(8,128)(2,1)S(1)}, u32[]{:S(2)}, u32[]{:S(2)}) collective-permute-start(bf16[64,512]{1,0:T(8,128)(2,1)S(1)} %constant_dynamic-slice_fusion), channel_id=1, source_target_pairs={{0,1},{1,2},{2,3},{3,0},{4,5},{5,6},{6,7},{7,4},{8,9},{9,10},{10,1... | collective-permute-start | bytes 196616 | tf_op jit(solution)/shard_map/ppermute | solution.py:54
  3.6 2.5 %collective-permute-start.1 = (bf16[64,512]{1,0:T(8,128)(2,1)S(1)}, bf16[64,512]{1,0:T(8,128)(2,1)S(1)}, u32[]{:S(2)}, u32[]{:S(2)}) collective-permute-start(bf16[64,512]{1,0:T(8,128)(2,1)S(1)} %constant_dynamic-slice_fusion), channel_id=1, source_target_pairs={{0,2},{1,3},{2,0},{3,1},{4,6},{5,7},{6,4},{7,5},{8,10},{9,11},{10,... | collective-permute-start | bytes 196616 | tf_op jit(solution)/shard_map/ppermute | solution.py:54
  6.0 1.2 collective-permute-start.2
  7.2 1.4 all_to_all.18
  8.6 0.8 copy.26
  9.4 4.3 %all-to-all-start = ((bf16[64,16,88]{2,0,1:T(8,128)(2,1)}), bf16[64,16,88]{2,0,1:T(8,128)(2,1)S(1)}, u32[]{:S(2)}, u32[]{:S(2)}) async-start(bf16[64,16,88]{2,0,1:T(8,128)(2,1)} %copy.26), calls=%async_computation | async-start | bytes 524288 | tf_op jit(solution)/shard_map/all_to_all | solution.py:59
  13.7 0.8 copy.31
  14.5 0.1 reshape.234
  14.7 0.6 reduce-window.6
  15.3 0.2 slice_reduce_fusion
  15.6 1.4 collective-permute-start.3
  17.0 2.4 %collective-permute-start.4 = (bf16[4,64,512]{2,1,0:T(8,128)(2,1)S(1)}, bf16[4,64,512]{2,1,0:T(8,128)(2,1)S(1)}, u32[]{:S(2)}, u32[]{:S(2)}) collective-permute-start(bf16[4,64,512]{2,1,0:T(8,128)(2,1)S(1)} %get-tuple-element.12), channel_id=1, source_target_pairs={{0,8},{4,12},{8,0},{12,4},{1,9},{5,13},{9,1},{13,5},{2,10},{6,14},... | collective-permute-start | bytes 786440 | tf_op jit(solution)/shard_map/ppermute | solution.py:56
  19.4 1.2 collective-permute-start.5
  20.7 6.0 %collective-permute-done.3 = bf16[4,64,512]{2,1,0:T(8,128)(2,1)S(1)} collective-permute-done((bf16[4,64,512]{2,1,0:T(8,128)(2,1)S(1)}, bf16[4,64,512]{2,1,0:T(8,128)(2,1)S(1)}, u32[]{:S(2)}, u32[]{:S(2)}) %collective-permute-start.3) | collective-permute-done | bytes 262176 | tf_op jit(solution)/shard_map/ppermute | solution.py:56
  26.6 5.7 %collective-permute-done.4 = bf16[4,64,512]{2,1,0:T(8,128)(2,1)S(1)} collective-permute-done((bf16[4,64,512]{2,1,0:T(8,128)(2,1)S(1)}, bf16[4,64,512]{2,1,0:T(8,128)(2,1)S(1)}, u32[]{:S(2)}, u32[]{:S(2)}) %collective-permute-start.4) | collective-permute-done | bytes 262176 | tf_op jit(solution)/shard_map/ppermute | solution.py:56
  32.3 0.1 pad_maximum_fusion.1
  32.5 1.6 collective-permute-start.6
  34.3 0.6 gather_fusion
  35.0 0.6 gather_fusion.1
  35.6 0.4 convolution_bitcast_fusion.1
  36.0 0.5 collective-permute-done.6
  36.4 0.4 convolution_bitcast_fusion
  36.8 0.2 fusion.20
  37.0 0.1 fusion.22
  37.1 0.2 broadcast_in_dim.40
  37.3 0.1 reshape.237
  37.5 0.4 convolution_convert_fusion.1
  37.8 1.1 reshape.238
  38.9 8.8 %all-to-all-start.1 = ((bf16[16,22,1024]{2,1,0:T(8,128)(2,1)}), bf16[16,22,1024]{2,1,0:T(8,128)(2,1)S(1)}, u32[]{:S(2)}, u32[]{:S(2)}) async-start(bf16[16,22,1024]{2,1,0:T(8,128)(2,1)} %reshape.238), calls=%async_computation.1 | async-start | bytes 1572864 | tf_op jit(solution)/shard_map/all_to_all | solution.py:95
  47.9 0.5 collective-permute-start.10
  48.4 2.1 %collective-permute-start.11 = (bf16[3,176,1024]{2,1,0:T(8,128)(2,1)S(1)}, bf16[3,176,1024]{2,1,0:T(8,128)(2,1)}, u32[]{:S(2)}, u32[]{:S(2)}) collective-permute-start(bf16[3,176,1024]{2,1,0:T(8,128)(2,1)S(1)} %constant_dynamic-update-slice_fusion.4), channel_id=1, source_target_pairs={{0,8},{4,12},{8,0},{12,4},{1,9},{5,13},{9,1},{13,5},{2,10},{6,14},... | collective-permute-start | bytes 3244040 | tf_op jit(solution)/shard_map/ppermute | solution.py:75
  50.5 1.1 collective-permute-start.12
  51.6 18.9 %all-to-all-done.1 = bf16[16,22,1024]{2,1,0:T(8,128)(2,1)S(1)} async-done(((bf16[16,22,1024]{2,1,0:T(8,128)(2,1)}), bf16[16,22,1024]{2,1,0:T(8,128)(2,1)S(1)}, u32[]{:S(2)}, u32[]{:S(2)}) %all-to-all-start.1) | async-done | bytes 720928 | tf_op jit(solution)/shard_map/all_to_all | solution.py:95
  70.5 0.2 reshape.239
  70.7 0.9 collective-permute-start.7
  71.6 2.2 %collective-permute-start.8 = (bf16[352,1024]{1,0:T(8,128)(2,1)S(1)}, bf16[352,1024]{1,0:T(8,128)(2,1)S(1)}, u32[]{:S(2)}, u32[]{:S(2)}) collective-permute-start(bf16[352,1024]{1,0:T(8,128)(2,1)S(1)} %reshape.239), channel_id=1, source_target_pairs={{0,2},{1,3},{2,0},{3,1},{4,6},{5,7},{6,4},{7,5},{8,10},{9,11},{10,... | collective-permute-start | bytes 2162696 | tf_op jit(solution)/shard_map/ppermute | solution.py:100
  73.8 1.0 collective-permute-done.10
  74.8 1.9 %collective-permute-start.9 = (bf16[352,1024]{1,0:T(8,128)(2,1)S(1)}, bf16[352,1024]{1,0:T(8,128)(2,1)S(1)}, u32[]{:S(2)}, u32[]{:S(2)}) collective-permute-start(bf16[352,1024]{1,0:T(8,128)(2,1)S(1)} %reshape.239), channel_id=1, source_target_pairs={{0,3},{1,0},{2,1},{3,2},{4,7},{5,4},{6,5},{7,6},{8,11},{9,8},{10,9... | collective-permute-start | bytes 2162696 | tf_op jit(solution)/shard_map/ppermute | solution.py:100
  76.7 21.0 %collective-permute-done.11 = bf16[3,176,1024]{2,1,0:T(8,128)(2,1)} collective-permute-done((bf16[3,176,1024]{2,1,0:T(8,128)(2,1)S(1)}, bf16[3,176,1024]{2,1,0:T(8,128)(2,1)}, u32[]{:S(2)}, u32[]{:S(2)}) %collective-permute-start.11) | collective-permute-done | bytes 1081376 | tf_op jit(solution)/shard_map/ppermute | solution.py:75
  97.7 0.5 collective-permute-done.12
  98.1 2.2 %pad_maximum_fusion = bf16[3,704,1024]{2,1,0:T(8,128)(2,1)S(1)} fusion(bf16[3,176,1024]{2,1,0:T(8,128)(2,1)} %collective-permute-done.12, bf16[3,176,1024]{2,1,0:T(8,128)(2,1)} %collective-permute-done.11, bf16[3,176,1024]{2,1,0:T(8,128)(2,1)} %collective-permute-done.10, bf16[3,176,1024]{2,1,0:T(8,128)(2,1)S(1)} %constant_dynamic-update-slice_fusion.4), kind=kLoop, calls=%fused_computation.4 | loop fusion | flops 17301504 | bytes 8650752 | tf_op jit(solution)/shard_map/concatenate | solution.py:96
  100.4 3.6 %collective-permute-done.8 = bf16[352,1024]{1,0:T(8,128)(2,1)S(1)} collective-permute-done((bf16[352,1024]{1,0:T(8,128)(2,1)S(1)}, bf16[352,1024]{1,0:T(8,128)(2,1)S(1)}, u32[]{:S(2)}, u32[]{:S(2)}) %collective-permute-start.8) | collective-permute-done | bytes 720928 | tf_op jit(solution)/shard_map/ppermute | solution.py:100
  104.2 1.6 copy-done.7
  105.9 4.4 %fusion.15 = f32[1408,704]{0,1:T(8,128)} fusion(bf16[1408,1024]{1,0:T(8,128)(2,1)S(1)} %constant_dynamic-update-slice_fusion, bf16[3,704,1024]{2,1,0:T(8,128)(2,1)S(1)} %pad_maximum_fusion), kind=kOutput, calls=%fused_computation.23 | convolution fusion | flops 2030043136 | bytes 8290304 | tf_op jit(solution)/shard_map/dot_general | solution.py:20
  110.2 8.6 %convolution_convert_fusion = bf16[1408,1024]{1,0:T(8,128)(2,1)S(1)} fusion(f32[1408,704]{0,1:T(8,128)} %fusion.15, bf16[3,704,1024]{2,1,0:T(8,128)(2,1)} %copy-done.1, bf16[1408,1024]{1,0:T(8,128)(2,1)} %copy-done.7), kind=kOutput, calls=%fused_computation.14 | convolution fusion | flops 4071440384 | bytes 12615680 | tf_op jit(solution)/shard_map/dot_general | solution.py:27
  118.9 0.2 fusion.48
  119.1 0.8 collective-permute-start.14
  120.0 0.8 collective-permute-start.15
  120.8 10.2 %collective-permute-done.13 = bf16[352,1024]{1,0:T(8,128)(2,1)S(1)} collective-permute-done((bf16[352,1024]{1,0:T(8,128)(2,1)S(1)}, bf16[352,1024]{1,0:T(8,128)(2,1)S(1)}, u32[]{:S(2)}, u32[]{:S(2)}) %collective-permute-start.13) | collective-permute-done | bytes 720928 | tf_op jit(solution)/shard_map/ppermute | solution.py:106
  131.0 21.8 %collective-permute-done.15 = bf16[352,1024]{1,0:T(8,128)(2,1)S(1)} collective-permute-done((bf16[352,1024]{1,0:T(8,128)(2,1)S(1)}, bf16[352,1024]{1,0:T(8,128)(2,1)S(1)}, u32[]{:S(2)}, u32[]{:S(2)}) %collective-permute-start.15) | collective-permute-done | bytes 720928 | tf_op jit(solution)/shard_map/ppermute | solution.py:106
  152.8 1.7 add_convert_fusion
  154.4 1.1 reshape.240
  155.5 8.4 %all-to-all-start.2 = ((bf16[16,22,1024]{2,1,0:T(8,128)(2,1)}), bf16[16,22,1024]{2,1,0:T(8,128)(2,1)S(1)}, u32[]{:S(2)}, u32[]{:S(2)}) async-start(bf16[16,22,1024]{2,1,0:T(8,128)(2,1)} %reshape.240), calls=%async_computation.2 | async-start | bytes 1572864 | tf_op jit(solution)/shard_map/all_to_all | solution.py:110
  164.0 0.1 reshape.259
  164.1 0.1 iota_compare_fusion.2
  164.4 0.3 fusion.49
  164.7 2.3 %gather_fusion.2 = f32[176]{0:T(256)S(1)} fusion(f32[88,16]{0,1:T(8,128)S(1)} %fusion.32, s32[176]{0:T(256)S(1)} %reshape.259), kind=kCustom, calls=%fused_computation.2 | custom fusion | bytes 2816 | tf_op jit(solution)/shard_map/jit(take_along_axis)/gather | solution.py:82
  167.0 0.1 reshape.262
  167.2 19.4 %all-to-all-done.2 = bf16[16,22,1024]{2,1,0:T(8,128)(2,1)S(1)} async-done(((bf16[16,22,1024]{2,1,0:T(8,128)(2,1)}), bf16[16,22,1024]{2,1,0:T(8,128)(2,1)S(1)}, u32[]{:S(2)}, u32[]{:S(2)}) %all-to-all-start.2) | async-done | bytes 720928 | tf_op jit(solution)/shard_map/all_to_all | solution.py:110
  186.6 0.2 reshape.272
  186.8 0.4 fusion.16
  187.2 0.1 fusion.17
  187.4 0.8 fusion.19
  (67 shorter events, 1.2 us)
Async XLA Ops:
  0.6 0.9 copy-start
  1.5 13.9 %collective-permute-start = (bf16[64,512]{1,0:T(8,128)(2,1)S(1)}, bf16[64,512]{1,0:T(8,128)(2,1)S(1)}, u32[]{:S(2)}, u32[]{:S(2)}) collective-permute-start(bf16[64,512]{1,0:T(8,128)(2,1)S(1)} %constant_dynamic-slice_fusion), channel_id=1, source_target_pairs={{0,1},{1,2},{2,3},{3,0},{4,5},{5,6},{6,7},{7,4},{8,9},{9,10},{10,1... | collective-permute-start | bytes 196616 | tf_op jit(solution)/shard_map/ppermute | solution.py:54
  3.6 11.9 %collective-permute-start.1 = (bf16[64,512]{1,0:T(8,128)(2,1)S(1)}, bf16[64,512]{1,0:T(8,128)(2,1)S(1)}, u32[]{:S(2)}, u32[]{:S(2)}) collective-permute-start(bf16[64,512]{1,0:T(8,128)(2,1)S(1)} %constant_dynamic-slice_fusion), channel_id=1, source_target_pairs={{0,2},{1,3},{2,0},{3,1},{4,6},{5,7},{6,4},{7,5},{8,10},{9,11},{10,... | collective-permute-start | bytes 196616 | tf_op jit(solution)/shard_map/ppermute | solution.py:54
  6.0 9.5 %collective-permute-start.2 = (bf16[64,512]{1,0:T(8,128)(2,1)S(1)}, bf16[64,512]{1,0:T(8,128)(2,1)S(1)}, u32[]{:S(2)}, u32[]{:S(2)}) collective-permute-start(bf16[64,512]{1,0:T(8,128)(2,1)S(1)} %constant_dynamic-slice_fusion), channel_id=1, source_target_pairs={{0,3},{1,0},{2,1},{3,2},{4,7},{5,4},{6,5},{7,6},{8,11},{9,8},{10,9... | collective-permute-start | bytes 196616 | tf_op jit(solution)/shard_map/ppermute | solution.py:54
  9.4 24.9 %all-to-all-start = ((bf16[64,16,88]{2,0,1:T(8,128)(2,1)}), bf16[64,16,88]{2,0,1:T(8,128)(2,1)S(1)}, u32[]{:S(2)}, u32[]{:S(2)}) async-start(bf16[64,16,88]{2,0,1:T(8,128)(2,1)} %copy.26), calls=%async_computation | async-start | bytes 524288 | tf_op jit(solution)/shard_map/all_to_all | solution.py:59
  15.6 11.0 %collective-permute-start.3 = (bf16[4,64,512]{2,1,0:T(8,128)(2,1)S(1)}, bf16[4,64,512]{2,1,0:T(8,128)(2,1)S(1)}, u32[]{:S(2)}, u32[]{:S(2)}) collective-permute-start(bf16[4,64,512]{2,1,0:T(8,128)(2,1)S(1)} %get-tuple-element.12), channel_id=1, source_target_pairs={{0,4},{4,8},{8,12},{12,0},{1,5},{5,9},{9,13},{13,1},{2,6},{6,10},{... | collective-permute-start | bytes 786440 | tf_op jit(solution)/shard_map/ppermute | solution.py:56
  17.0 15.3 %collective-permute-start.4 = (bf16[4,64,512]{2,1,0:T(8,128)(2,1)S(1)}, bf16[4,64,512]{2,1,0:T(8,128)(2,1)S(1)}, u32[]{:S(2)}, u32[]{:S(2)}) collective-permute-start(bf16[4,64,512]{2,1,0:T(8,128)(2,1)S(1)} %get-tuple-element.12), channel_id=1, source_target_pairs={{0,8},{4,12},{8,0},{12,4},{1,9},{5,13},{9,1},{13,5},{2,10},{6,14},... | collective-permute-start | bytes 786440 | tf_op jit(solution)/shard_map/ppermute | solution.py:56
  19.4 12.9 %collective-permute-start.5 = (bf16[4,64,512]{2,1,0:T(8,128)(2,1)S(1)}, bf16[4,64,512]{2,1,0:T(8,128)(2,1)S(1)}, u32[]{:S(2)}, u32[]{:S(2)}) collective-permute-start(bf16[4,64,512]{2,1,0:T(8,128)(2,1)S(1)} %get-tuple-element.12), channel_id=1, source_target_pairs={{0,12},{4,0},{8,4},{12,8},{1,13},{5,1},{9,5},{13,9},{2,14},{6,2},{... | collective-permute-start | bytes 786440 | tf_op jit(solution)/shard_map/ppermute | solution.py:56
  32.3 4.5 %copy-start.8 = (bf16[88,1024]{1,0:T(8,128)(2,1)S(1)}, bf16[88,1024]{1,0:T(8,128)(2,1)}, u32[]{:S(2)}) copy-start(bf16[88,1024]{1,0:T(8,128)(2,1)} %param.10) | copy-start | bytes 540676
  32.5 4.5 %copy-start.11 = (f32[1024]{0:T(1024)S(1)}, f32[1024]{0:T(1024)}, u32[]{:S(2)}) copy-start(f32[1024]{0:T(1024)} %param.13) | copy-start | bytes 12292
  32.5 3.9 %collective-permute-start.6 = (bf16[4,4,64,512]{3,2,1,0:T(8,128)(2,1)S(1)}, bf16[4,4,64,512]{3,2,1,0:T(8,128)(2,1)S(1)}, u32[]{:S(2)}, u32[]{:S(2)}) collective-permute-start(bf16[4,4,64,512]{3,2,1,0:T(8,128)(2,1)S(1)} %pad_maximum_fusion.1), channel_id=1, source_target_pairs={{0,16},{16,0},{32,48},{48,32},{64,80},{80,64},{96,112},{112,96},{1... | collective-permute-start | bytes 3145736 | tf_op jit(solution)/shard_map/ppermute | solution.py:58
  37.0 10.8 %copy-start.4 = (bf16[1,176,1024]{2,1,0:T(8,128)(2,1)S(1)}, bf16[1,176,1024]{2,1,0:T(8,128)(2,1)}, u32[]{:S(2)}) copy-start(bf16[1,176,1024]{2,1,0:T(8,128)(2,1)} %param.16) | copy-start | bytes 1081348
  37.3 10.5 %copy-start.5 = (bf16[1,176,1024]{2,1,0:T(8,128)(2,1)S(1)}, bf16[1,176,1024]{2,1,0:T(8,128)(2,1)}, u32[]{:S(2)}) copy-start(bf16[1,176,1024]{2,1,0:T(8,128)(2,1)} %param.17) | copy-start | bytes 1081348
  37.5 10.4 %copy-start.6 = (bf16[1,176,1024]{2,1,0:T(8,128)(2,1)S(1)}, bf16[1,176,1024]{2,1,0:T(8,128)(2,1)}, u32[]{:S(2)}) copy-start(bf16[1,176,1024]{2,1,0:T(8,128)(2,1)} %param.18) | copy-start | bytes 1081348
  38.9 31.6 %all-to-all-start.1 = ((bf16[16,22,1024]{2,1,0:T(8,128)(2,1)}), bf16[16,22,1024]{2,1,0:T(8,128)(2,1)S(1)}, u32[]{:S(2)}, u32[]{:S(2)}) async-start(bf16[16,22,1024]{2,1,0:T(8,128)(2,1)} %reshape.238), calls=%async_computation.1 | async-start | bytes 1572864 | tf_op jit(solution)/shard_map/all_to_all | solution.py:95
  47.9 26.9 %collective-permute-start.10 = (bf16[3,176,1024]{2,1,0:T(8,128)(2,1)S(1)}, bf16[3,176,1024]{2,1,0:T(8,128)(2,1)}, u32[]{:S(2)}, u32[]{:S(2)}) collective-permute-start(bf16[3,176,1024]{2,1,0:T(8,128)(2,1)S(1)} %constant_dynamic-update-slice_fusion.4), channel_id=1, source_target_pairs={{0,4},{4,8},{8,12},{12,0},{1,5},{5,9},{9,13},{13,1},{2,6},{6,10},{... | collective-permute-start | bytes 3244040 | tf_op jit(solution)/shard_map/ppermute | solution.py:75
  48.4 49.3 %collective-permute-start.11 = (bf16[3,176,1024]{2,1,0:T(8,128)(2,1)S(1)}, bf16[3,176,1024]{2,1,0:T(8,128)(2,1)}, u32[]{:S(2)}, u32[]{:S(2)}) collective-permute-start(bf16[3,176,1024]{2,1,0:T(8,128)(2,1)S(1)} %constant_dynamic-update-slice_fusion.4), channel_id=1, source_target_pairs={{0,8},{4,12},{8,0},{12,4},{1,9},{5,13},{9,1},{13,5},{2,10},{6,14},... | collective-permute-start | bytes 3244040 | tf_op jit(solution)/shard_map/ppermute | solution.py:75
  50.5 47.6 %collective-permute-start.12 = (bf16[3,176,1024]{2,1,0:T(8,128)(2,1)S(1)}, bf16[3,176,1024]{2,1,0:T(8,128)(2,1)}, u32[]{:S(2)}, u32[]{:S(2)}) collective-permute-start(bf16[3,176,1024]{2,1,0:T(8,128)(2,1)S(1)} %constant_dynamic-update-slice_fusion.4), channel_id=1, source_target_pairs={{0,12},{4,0},{8,4},{12,8},{1,13},{5,1},{9,5},{13,9},{2,14},{6,2},{... | collective-permute-start | bytes 3244040 | tf_op jit(solution)/shard_map/ppermute | solution.py:75
  70.7 29.7 %collective-permute-start.7 = (bf16[352,1024]{1,0:T(8,128)(2,1)S(1)}, bf16[352,1024]{1,0:T(8,128)(2,1)S(1)}, u32[]{:S(2)}, u32[]{:S(2)}) collective-permute-start(bf16[352,1024]{1,0:T(8,128)(2,1)S(1)} %reshape.239), channel_id=1, source_target_pairs={{0,1},{1,2},{2,3},{3,0},{4,5},{5,6},{6,7},{7,4},{8,9},{9,10},{10,1... | collective-permute-start | bytes 2162696 | tf_op jit(solution)/shard_map/ppermute | solution.py:100
  71.6 32.5 %collective-permute-start.8 = (bf16[352,1024]{1,0:T(8,128)(2,1)S(1)}, bf16[352,1024]{1,0:T(8,128)(2,1)S(1)}, u32[]{:S(2)}, u32[]{:S(2)}) collective-permute-start(bf16[352,1024]{1,0:T(8,128)(2,1)S(1)} %reshape.239), channel_id=1, source_target_pairs={{0,2},{1,3},{2,0},{3,1},{4,6},{5,7},{6,4},{7,5},{8,10},{9,11},{10,... | collective-permute-start | bytes 2162696 | tf_op jit(solution)/shard_map/ppermute | solution.py:100
  74.8 29.4 %collective-permute-start.9 = (bf16[352,1024]{1,0:T(8,128)(2,1)S(1)}, bf16[352,1024]{1,0:T(8,128)(2,1)S(1)}, u32[]{:S(2)}, u32[]{:S(2)}) collective-permute-start(bf16[352,1024]{1,0:T(8,128)(2,1)S(1)} %reshape.239), channel_id=1, source_target_pairs={{0,3},{1,0},{2,1},{3,2},{4,7},{5,4},{6,5},{7,6},{8,11},{9,8},{10,9... | collective-permute-start | bytes 2162696 | tf_op jit(solution)/shard_map/ppermute | solution.py:100
  100.3 3.9 %copy-start.1 = (bf16[3,704,1024]{2,1,0:T(8,128)(2,1)}, bf16[3,704,1024]{2,1,0:T(8,128)(2,1)S(1)}, u32[]{:S(2)}) copy-start(bf16[3,704,1024]{2,1,0:T(8,128)(2,1)S(1)} %pad_maximum_fusion) | copy-start | bytes 12976132
  104.2 1.7 copy-start.7
  118.9 12.1 %copy-start.2 = (bf16[1408,1024]{1,0:T(8,128)(2,1)}, bf16[1408,1024]{1,0:T(8,128)(2,1)S(1)}, u32[]{:S(2)}) copy-start(bf16[1408,1024]{1,0:T(8,128)(2,1)S(1)} %convolution_convert_fusion) | copy-start | bytes 8650756
  119.1 11.9 %collective-permute-start.13 = (bf16[352,1024]{1,0:T(8,128)(2,1)S(1)}, bf16[352,1024]{1,0:T(8,128)(2,1)S(1)}, u32[]{:S(2)}, u32[]{:S(2)}) collective-permute-start(bf16[352,1024]{1,0:T(8,128)(2,1)S(1)} %get-tuple-element.8), channel_id=1, source_target_pairs={{0,3},{1,0},{2,1},{3,2},{4,7},{5,4},{6,5},{7,6},{8,11},{9,8},{10,9... | collective-permute-start | bytes 2162696 | tf_op jit(solution)/shard_map/ppermute | solution.py:106
  119.1 11.8 %collective-permute-start.14 = (bf16[352,1024]{1,0:T(8,128)(2,1)S(1)}, bf16[352,1024]{1,0:T(8,128)(2,1)S(1)}, u32[]{:S(2)}, u32[]{:S(2)}) collective-permute-start(bf16[352,1024]{1,0:T(8,128)(2,1)S(1)} %get-tuple-element.10), channel_id=1, source_target_pairs={{0,2},{1,3},{2,0},{3,1},{4,6},{5,7},{6,4},{7,5},{8,10},{9,11},{10,... | collective-permute-start | bytes 2162696 | tf_op jit(solution)/shard_map/ppermute | solution.py:106
  120.0 43.9 %copy-start.10 = (s32[88,2]{0,1:T(2,128)S(1)}, s32[88,2]{0,1:T(2,128)}, u32[]{:S(2)}) copy-start(s32[88,2]{0,1:T(2,128)} %param.15) | copy-start | bytes 2116
  120.0 44.4 %copy-start.9 = (f32[1024,16]{0,1:T(8,128)S(1)}, f32[1024,16]{0,1:T(8,128)}, u32[]{:S(2)}) copy-start(f32[1024,16]{0,1:T(8,128)} %param.14) | copy-start | bytes 196612
  120.0 32.8 %collective-permute-start.15 = (bf16[352,1024]{1,0:T(8,128)(2,1)S(1)}, bf16[352,1024]{1,0:T(8,128)(2,1)S(1)}, u32[]{:S(2)}, u32[]{:S(2)}) collective-permute-start(bf16[352,1024]{1,0:T(8,128)(2,1)S(1)} %get-tuple-element.9), channel_id=1, source_target_pairs={{0,1},{1,2},{2,3},{3,0},{4,5},{5,6},{6,7},{7,4},{8,9},{9,10},{10,1... | collective-permute-start | bytes 2162696 | tf_op jit(solution)/shard_map/ppermute | solution.py:106
  155.5 31.1 %all-to-all-start.2 = ((bf16[16,22,1024]{2,1,0:T(8,128)(2,1)}), bf16[16,22,1024]{2,1,0:T(8,128)(2,1)S(1)}, u32[]{:S(2)}, u32[]{:S(2)}) async-start(bf16[16,22,1024]{2,1,0:T(8,128)(2,1)} %reshape.240), calls=%async_computation.2 | async-start | bytes 1572864 | tf_op jit(solution)/shard_map/all_to_all | solution.py:110
  167.0 20.4 %copy-start.12 = (f32[1024]{0:T(1024)S(1)}, f32[1024]{0:T(1024)}, u32[]{:S(2)}) copy-start(f32[1024]{0:T(1024)} %param.19) | copy-start | bytes 12292
  187.3 0.8 copy-start.3

commit v10 on v9

--- a/solution.py
+++ b/solution.py
@@ -97,13 +97,14 @@
     gate_rows, up_rows, down_rows = weights[0], weights[1], weights[2]
     slot_total = n_expert * capacity
     rows_in = received.reshape(slot_total, width)
-    all_rows = [rows_in] + [lax.ppermute(rows_in, "tx", shift_pairs(n_tx, s)) for s in range(1, n_tx)]
-    all_rows = jnp.concatenate(all_rows, axis=0)
-    partial = expert_block(all_rows, gate_rows, up_rows, down_rows).astype(jnp.bfloat16)
-    partial = partial.reshape(n_tx, slot_total, width)
-    expert_sum = partial[0].astype(jnp.float32)
+    peer_rows = [lax.ppermute(rows_in, "tx", shift_pairs(n_tx, s)) for s in range(1, n_tx)]
+    own = expert_block(rows_in, gate_rows, up_rows, down_rows).astype(jnp.bfloat16)
+    peer_rows = jnp.concatenate(peer_rows, axis=0)
+    partial = expert_block(peer_rows, gate_rows, up_rows, down_rows).astype(jnp.bfloat16)
+    partial = partial.reshape(n_tx - 1, slot_total, width)
+    expert_sum = own.astype(jnp.float32)
     for s in range(1, n_tx):
-        back = lax.ppermute(partial[s], "tx", shift_pairs(n_tx, -s))
+        back = lax.ppermute(partial[s - 1], "tx", shift_pairs(n_tx, -s))
         expert_sum = expert_sum + back.astype(jnp.float32)
     expert_sum = expert_sum.astype(jnp.bfloat16)
     expert_out = expert_sum.reshape(n_expert, capacity, width)

time: 189 us -> 188 us (level)
  waiting for transfers between devices: 108 us -> 100 us
  matrix products: 14.7 us -> 21.4 us
    ppermute x3, waiting for transfers between devices: 32 us -> 24 us  [per_device(): back = lax.ppermute(partial[s - 1], 'tx', shift_pairs(n_tx, -s))]
    dot_general x1 -> x2, matrix products: 8.6 us -> 12.9 us  [expert_block(): return jnp.dot(hid, down_rows, preferred_element_type=jnp.float32)]
    dot_general x0 -> x1, matrix products: none -> 3.13 us  [expert_block(): lax.dot_general(inputs, up_rows, (((1,), (1,)), ((), ())), preferred_elem...]
  transfers between devices with their start and end apart: 19 -> 19, of which waited for: 11 -> 11; matrix products, arithmetic and copies ran while one was open for 6% -> 10% of each run, Pallas kernels for 0% -> 0%
where the time goes in v10:
time: 188 us
  waiting for transfers between devices  100 us (53%)
  starting transfers between devices  44.4 us (24%)
  matrix products  21.4 us (11%)
  local copies, waits for them, and re-layouts  14.2 us (8%)
  other arithmetic  6.35 us (3%)
    ppermute x3, waiting for transfers between devices, per_device(): back = lax.ppermute(partial[s - 1], 'tx', shift_pairs(n_tx, -s))  24 us
    ppermute x3, waiting for transfers between devices, per_device(): lax.ppermute(stacked, 'ty', shift_pairs(n_ty, s))  22.4 us
    all_to_all x1, waiting for transfers between devices, per_device(): lax.all_to_all(expert_out, 'expert', split_axis=0, concat_axis=0, tiled=T...  19.4 us
    all_to_all x1, waiting for transfers between devices, per_device(): lax.all_to_all(send_slots, 'expert', split_axis=0, concat_axis=0, tiled=T...  18.9 us
    dot_general x2, matrix products, expert_block(): return jnp.dot(hid, down_rows, preferred_element_type=jnp.float32)  12.9 us
    ppermute x3, waiting for transfers between devices, per_device(): lax.ppermute(near, 'ty', shift_pairs(n_ty, s))  11.7 us
    all_to_all x1, starting transfers between devices, per_device(): lax.all_to_all(send_slots, 'expert', split_axis=0, concat_axis=0, tiled=T...  8.85 us
    all_to_all x1, starting transfers between devices, per_device(): lax.all_to_all(expert_out, 'expert', split_axis=0, concat_axis=0, tiled=T...  8.56 us
  transfers between devices with their start and end apart: 19, of which 11 were waited for; matrix products, arithmetic and copies ran while one was open for 10% of the time, Pallas kernels for 0%

profile of v10, /device:TPU:1, one launch (start us, length us, event | category | flops | bytes accessed | tf_op | source)
XLA Modules:
  0.0 188.0 jit_solution(4182121107653642446)
XLA Ops:
  0.7 0.9 copy-done
  1.5 2.0 %collective-permute-start = (bf16[64,512]{1,0:T(8,128)(2,1)S(1)}, bf16[64,512]{1,0:T(8,128)(2,1)S(1)}, u32[]{:S(2)}, u32[]{:S(2)}) collective-permute-start(bf16[64,512]{1,0:T(8,128)(2,1)S(1)} %constant_dynamic-slice_fusion), channel_id=1, source_target_pairs={{0,1},{1,2},{2,3},{3,0},{4,5},{5,6},{6,7},{7,4},{8,9},{9,10},{10,1... | collective-permute-start | bytes 196616 | tf_op jit(solution)/shard_map/ppermute | solution.py:54
  3.6 2.5 %collective-permute-start.1 = (bf16[64,512]{1,0:T(8,128)(2,1)S(1)}, bf16[64,512]{1,0:T(8,128)(2,1)S(1)}, u32[]{:S(2)}, u32[]{:S(2)}) collective-permute-start(bf16[64,512]{1,0:T(8,128)(2,1)S(1)} %constant_dynamic-slice_fusion), channel_id=1, source_target_pairs={{0,2},{1,3},{2,0},{3,1},{4,6},{5,7},{6,4},{7,5},{8,10},{9,11},{10,... | collective-permute-start | bytes 196616 | tf_op jit(solution)/shard_map/ppermute | solution.py:54
  6.0 1.2 collective-permute-start.2
  7.2 1.4 all_to_all.18
  8.6 0.8 copy.26
  9.4 4.3 %all-to-all-start = ((bf16[64,16,88]{2,0,1:T(8,128)(2,1)}), bf16[64,16,88]{2,0,1:T(8,128)(2,1)S(1)}, u32[]{:S(2)}, u32[]{:S(2)}) async-start(bf16[64,16,88]{2,0,1:T(8,128)(2,1)} %copy.26), calls=%async_computation | async-start | bytes 524288 | tf_op jit(solution)/shard_map/all_to_all | solution.py:59
  13.8 0.8 copy.31
  14.5 0.1 reshape.232
  14.7 0.6 reduce-window.6
  15.3 0.2 slice_reduce_fusion
  15.6 1.4 collective-permute-start.3
  17.0 2.4 %collective-permute-start.4 = (bf16[4,64,512]{2,1,0:T(8,128)(2,1)S(1)}, bf16[4,64,512]{2,1,0:T(8,128)(2,1)S(1)}, u32[]{:S(2)}, u32[]{:S(2)}) collective-permute-start(bf16[4,64,512]{2,1,0:T(8,128)(2,1)S(1)} %get-tuple-element.12), channel_id=1, source_target_pairs={{0,8},{4,12},{8,0},{12,4},{1,9},{5,13},{9,1},{13,5},{2,10},{6,14},... | collective-permute-start | bytes 786440 | tf_op jit(solution)/shard_map/ppermute | solution.py:56
  19.4 1.2 collective-permute-start.5
  20.7 6.0 %collective-permute-done.3 = bf16[4,64,512]{2,1,0:T(8,128)(2,1)S(1)} collective-permute-done((bf16[4,64,512]{2,1,0:T(8,128)(2,1)S(1)}, bf16[4,64,512]{2,1,0:T(8,128)(2,1)S(1)}, u32[]{:S(2)}, u32[]{:S(2)}) %collective-permute-start.3) | collective-permute-done | bytes 262176 | tf_op jit(solution)/shard_map/ppermute | solution.py:56
  26.6 5.7 %collective-permute-done.4 = bf16[4,64,512]{2,1,0:T(8,128)(2,1)S(1)} collective-permute-done((bf16[4,64,512]{2,1,0:T(8,128)(2,1)S(1)}, bf16[4,64,512]{2,1,0:T(8,128)(2,1)S(1)}, u32[]{:S(2)}, u32[]{:S(2)}) %collective-permute-start.4) | collective-permute-done | bytes 262176 | tf_op jit(solution)/shard_map/ppermute | solution.py:56
  32.3 0.1 pad_maximum_fusion.1
  32.5 1.6 collective-permute-start.6
  34.3 0.6 gather_fusion
  35.0 0.6 gather_fusion.1
  35.6 0.4 convolution_bitcast_fusion.1
  36.0 0.4 collective-permute-done.6
  36.4 0.4 convolution_bitcast_fusion
  36.8 0.2 fusion.35
  37.1 0.2 broadcast_in_dim.40
  37.3 0.1 reshape.235
  37.4 0.3 convolution_convert_fusion.2
  37.8 1.1 reshape.236
  38.9 8.9 %all-to-all-start.1 = ((bf16[16,22,1024]{2,1,0:T(8,128)(2,1)}), bf16[16,22,1024]{2,1,0:T(8,128)(2,1)S(1)}, u32[]{:S(2)}, u32[]{:S(2)}) async-start(bf16[16,22,1024]{2,1,0:T(8,128)(2,1)} %reshape.236), calls=%async_computation.1 | async-start | bytes 1572864 | tf_op jit(solution)/shard_map/all_to_all | solution.py:95
  47.9 0.5 collective-permute-start.7
  48.4 2.1 %collective-permute-start.8 = (bf16[3,176,1024]{2,1,0:T(8,128)(2,1)S(1)}, bf16[3,176,1024]{2,1,0:T(8,128)(2,1)}, u32[]{:S(2)}, u32[]{:S(2)}) collective-permute-start(bf16[3,176,1024]{2,1,0:T(8,128)(2,1)S(1)} %constant_dynamic-update-slice_fusion), channel_id=1, source_target_pairs={{0,8},{4,12},{8,0},{12,4},{1,9},{5,13},{9,1},{13,5},{2,10},{6,14},... | collective-permute-start | bytes 3244040 | tf_op jit(solution)/shard_map/ppermute | solution.py:75
  50.5 1.1 collective-permute-start.9
  51.6 18.9 %all-to-all-done.1 = bf16[16,22,1024]{2,1,0:T(8,128)(2,1)S(1)} async-done(((bf16[16,22,1024]{2,1,0:T(8,128)(2,1)}), bf16[16,22,1024]{2,1,0:T(8,128)(2,1)S(1)}, u32[]{:S(2)}, u32[]{:S(2)}) %all-to-all-start.1) | async-done | bytes 720928 | tf_op jit(solution)/shard_map/all_to_all | solution.py:95
  70.5 0.2 reshape.237
  70.7 0.9 collective-permute-start.10
  71.6 2.2 %collective-permute-start.11 = (bf16[352,1024]{1,0:T(8,128)(2,1)S(1)}, bf16[352,1024]{1,0:T(8,128)(2,1)S(1)}, u32[]{:S(2)}, u32[]{:S(2)}) collective-permute-start(bf16[352,1024]{1,0:T(8,128)(2,1)S(1)} %reshape.237), channel_id=1, source_target_pairs={{0,2},{1,3},{2,0},{3,1},{4,6},{5,7},{6,4},{7,5},{8,10},{9,11},{10,... | collective-permute-start | bytes 2162696 | tf_op jit(solution)/shard_map/ppermute | solution.py:100
  73.8 1.0 collective-permute-done.7
  74.8 1.9 %collective-permute-start.12 = (bf16[352,1024]{1,0:T(8,128)(2,1)S(1)}, bf16[352,1024]{1,0:T(8,128)(2,1)S(1)}, u32[]{:S(2)}, u32[]{:S(2)}) collective-permute-start(bf16[352,1024]{1,0:T(8,128)(2,1)S(1)} %reshape.237), channel_id=1, source_target_pairs={{0,3},{1,0},{2,1},{3,2},{4,7},{5,4},{6,5},{7,6},{8,11},{9,8},{10,9... | collective-permute-start | bytes 2162696 | tf_op jit(solution)/shard_map/ppermute | solution.py:100
  76.7 21.0 %collective-permute-done.8 = bf16[3,176,1024]{2,1,0:T(8,128)(2,1)} collective-permute-done((bf16[3,176,1024]{2,1,0:T(8,128)(2,1)S(1)}, bf16[3,176,1024]{2,1,0:T(8,128)(2,1)}, u32[]{:S(2)}, u32[]{:S(2)}) %collective-permute-start.8) | collective-permute-done | bytes 1081376 | tf_op jit(solution)/shard_map/ppermute | solution.py:75
  97.7 0.5 collective-permute-done.9
  98.1 2.2 %pad_maximum_fusion = bf16[3,704,1024]{2,1,0:T(8,128)(2,1)S(1)} fusion(bf16[3,176,1024]{2,1,0:T(8,128)(2,1)} %collective-permute-done.9, bf16[3,176,1024]{2,1,0:T(8,128)(2,1)} %collective-permute-done.8, bf16[3,176,1024]{2,1,0:T(8,128)(2,1)} %collective-permute-done.7, bf16[3,176,1024]{2,1,0:T(8,128)(2,1)S(1)} %constant_dynamic-update-slice_fusion), kind=kLoop, calls=%fused_computation.4 | loop fusion | flops 17301504 | bytes 8650752 | tf_op jit(solution)/shard_map/concatenate | solution.py:96
  100.4 3.7 %collective-permute-done.11 = bf16[352,1024]{1,0:T(8,128)(2,1)S(1)} collective-permute-done((bf16[352,1024]{1,0:T(8,128)(2,1)S(1)}, bf16[352,1024]{1,0:T(8,128)(2,1)S(1)}, u32[]{:S(2)}, u32[]{:S(2)}) %collective-permute-start.11) | collective-permute-done | bytes 720928 | tf_op jit(solution)/shard_map/ppermute | solution.py:100
  104.2 1.4 copy-done.6
  105.6 3.6 %fusion.14 = f32[1056,704]{1,0:T(8,128)} fusion(bf16[1056,1024]{1,0:T(8,128)(2,1)S(1)} %constant_dynamic-update-slice_fusion.3, bf16[3,704,1024]{2,1,0:T(8,128)(2,1)S(1)} %pad_maximum_fusion), kind=kOutput, calls=%fused_computation.27 | convolution fusion | flops 1522532352 | bytes 6578176 | tf_op jit(solution)/shard_map/dot_general | solution.py:20
  109.2 8.0 %convolution_convert_fusion = bf16[1056,1024]{1,0:T(8,128)(2,1)S(1)} fusion(f32[1056,704]{1,0:T(8,128)} %fusion.14, bf16[3,704,1024]{2,1,0:T(8,128)(2,1)} %copy-done.1, bf16[1056,1024]{1,0:T(8,128)(2,1)} %copy-done.6), kind=kOutput, calls=%fused_computation.5 | convolution fusion | flops 3053580288 | bytes 10452992 | tf_op jit(solution)/shard_map/dot_general | solution.py:27
  117.3 1.4 fusion.67
  118.7 0.8 collective-permute-start.14
  119.5 0.9 collective-permute-start.15
  120.3 3.1 %fusion.17 = f32[352,704]{1,0:T(8,128)} fusion(bf16[352,1024]{1,0:T(8,128)(2,1)S(1)} %reshape.237, bf16[3,704,1024]{2,1,0:T(8,128)(2,1)} %copy-done.1), kind=kOutput, calls=%fused_computation.30 | convolution fusion | flops 507510784 | bytes 3153920 | tf_op jit(solution)/shard_map/dot_general | solution.py:23
  123.5 4.9 %convolution_convert_fusion.1 = bf16[352,1024]{1,0:T(8,128)(2,1)} fusion(bf16[3,704,1024]{2,1,0:T(8,128)(2,1)} %copy-done.1, f32[352,704]{1,0:T(8,128)} %fusion.17, bf16[352,1024]{1,0:T(8,128)(2,1)S(1)} %reshape.237), kind=kOutput, calls=%fused_computation.24 | convolution fusion | flops 1017860096 | bytes 5406720 | tf_op jit(solution)/shard_map/dot_general | solution.py:27
  128.4 2.4 %collective-permute-done.13 = bf16[352,1024]{1,0:T(8,128)(2,1)S(1)} collective-permute-done((bf16[352,1024]{1,0:T(8,128)(2,1)}, bf16[352,1024]{1,0:T(8,128)(2,1)S(1)}, u32[]{:S(2)}, u32[]{:S(2)}) %collective-permute-start.13) | collective-permute-done | bytes 720928 | tf_op jit(solution)/shard_map/ppermute | solution.py:107
  130.7 21.6 %collective-permute-done.15 = bf16[352,1024]{1,0:T(8,128)(2,1)S(1)} collective-permute-done((bf16[352,1024]{1,0:T(8,128)(2,1)}, bf16[352,1024]{1,0:T(8,128)(2,1)S(1)}, u32[]{:S(2)}, u32[]{:S(2)}) %collective-permute-start.15) | collective-permute-done | bytes 720928 | tf_op jit(solution)/shard_map/ppermute | solution.py:107
  152.4 1.7 add_convert_fusion
  154.1 1.1 reshape.238
  155.1 8.6 %all-to-all-start.2 = ((bf16[16,22,1024]{2,1,0:T(8,128)(2,1)}), bf16[16,22,1024]{2,1,0:T(8,128)(2,1)S(1)}, u32[]{:S(2)}, u32[]{:S(2)}) async-start(bf16[16,22,1024]{2,1,0:T(8,128)(2,1)} %reshape.238), calls=%async_computation.2 | async-start | bytes 1572864 | tf_op jit(solution)/shard_map/all_to_all | solution.py:111
  163.8 0.1 reshape.257
  164.2 0.3 fusion.68
  164.5 2.3 %gather_fusion.2 = f32[176]{0:T(256)S(1)} fusion(f32[88,16]{0,1:T(8,128)S(1)} %fusion.47, s32[176]{0:T(256)S(1)} %reshape.257), kind=kCustom, calls=%fused_computation.2 | custom fusion | bytes 2816 | tf_op jit(solution)/shard_map/jit(take_along_axis)/gather | solution.py:82
  166.8 0.1 reshape.260
  167.1 19.4 %all-to-all-done.2 = bf16[16,22,1024]{2,1,0:T(8,128)(2,1)S(1)} async-done(((bf16[16,22,1024]{2,1,0:T(8,128)(2,1)}), bf16[16,22,1024]{2,1,0:T(8,128)(2,1)S(1)}, u32[]{:S(2)}, u32[]{:S(2)}) %all-to-all-start.2) | async-done | bytes 720928 | tf_op jit(solution)/shard_map/all_to_all | solution.py:111
  186.4 0.2 reshape.270
  186.6 0.4 fusion.18
  187.0 0.2 fusion.32
  187.2 0.8 fusion.34
  (66 shorter events, 1.3 us)
Async XLA Ops:
  0.6 0.9 copy-start
  1.5 13.9 %collective-permute-start = (bf16[64,512]{1,0:T(8,128)(2,1)S(1)}, bf16[64,512]{1,0:T(8,128)(2,1)S(1)}, u32[]{:S(2)}, u32[]{:S(2)}) collective-permute-start(bf16[64,512]{1,0:T(8,128)(2,1)S(1)} %constant_dynamic-slice_fusion), channel_id=1, source_target_pairs={{0,1},{1,2},{2,3},{3,0},{4,5},{5,6},{6,7},{7,4},{8,9},{9,10},{10,1... | collective-permute-start | bytes 196616 | tf_op jit(solution)/shard_map/ppermute | solution.py:54
  3.6 11.9 %collective-permute-start.1 = (bf16[64,512]{1,0:T(8,128)(2,1)S(1)}, bf16[64,512]{1,0:T(8,128)(2,1)S(1)}, u32[]{:S(2)}, u32[]{:S(2)}) collective-permute-start(bf16[64,512]{1,0:T(8,128)(2,1)S(1)} %constant_dynamic-slice_fusion), channel_id=1, source_target_pairs={{0,2},{1,3},{2,0},{3,1},{4,6},{5,7},{6,4},{7,5},{8,10},{9,11},{10,... | collective-permute-start | bytes 196616 | tf_op jit(solution)/shard_map/ppermute | solution.py:54
  6.0 9.5 %collective-permute-start.2 = (bf16[64,512]{1,0:T(8,128)(2,1)S(1)}, bf16[64,512]{1,0:T(8,128)(2,1)S(1)}, u32[]{:S(2)}, u32[]{:S(2)}) collective-permute-start(bf16[64,512]{1,0:T(8,128)(2,1)S(1)} %constant_dynamic-slice_fusion), channel_id=1, source_target_pairs={{0,3},{1,0},{2,1},{3,2},{4,7},{5,4},{6,5},{7,6},{8,11},{9,8},{10,9... | collective-permute-start | bytes 196616 | tf_op jit(solution)/shard_map/ppermute | solution.py:54
  9.4 24.9 %all-to-all-start = ((bf16[64,16,88]{2,0,1:T(8,128)(2,1)}), bf16[64,16,88]{2,0,1:T(8,128)(2,1)S(1)}, u32[]{:S(2)}, u32[]{:S(2)}) async-start(bf16[64,16,88]{2,0,1:T(8,128)(2,1)} %copy.26), calls=%async_computation | async-start | bytes 524288 | tf_op jit(solution)/shard_map/all_to_all | solution.py:59
  15.6 11.0 %collective-permute-start.3 = (bf16[4,64,512]{2,1,0:T(8,128)(2,1)S(1)}, bf16[4,64,512]{2,1,0:T(8,128)(2,1)S(1)}, u32[]{:S(2)}, u32[]{:S(2)}) collective-permute-start(bf16[4,64,512]{2,1,0:T(8,128)(2,1)S(1)} %get-tuple-element.12), channel_id=1, source_target_pairs={{0,4},{4,8},{8,12},{12,0},{1,5},{5,9},{9,13},{13,1},{2,6},{6,10},{... | collective-permute-start | bytes 786440 | tf_op jit(solution)/shard_map/ppermute | solution.py:56
  17.0 15.3 %collective-permute-start.4 = (bf16[4,64,512]{2,1,0:T(8,128)(2,1)S(1)}, bf16[4,64,512]{2,1,0:T(8,128)(2,1)S(1)}, u32[]{:S(2)}, u32[]{:S(2)}) collective-permute-start(bf16[4,64,512]{2,1,0:T(8,128)(2,1)S(1)} %get-tuple-element.12), channel_id=1, source_target_pairs={{0,8},{4,12},{8,0},{12,4},{1,9},{5,13},{9,1},{13,5},{2,10},{6,14},... | collective-permute-start | bytes 786440 | tf_op jit(solution)/shard_map/ppermute | solution.py:56
  19.4 12.9 %collective-permute-start.5 = (bf16[4,64,512]{2,1,0:T(8,128)(2,1)S(1)}, bf16[4,64,512]{2,1,0:T(8,128)(2,1)S(1)}, u32[]{:S(2)}, u32[]{:S(2)}) collective-permute-start(bf16[4,64,512]{2,1,0:T(8,128)(2,1)S(1)} %get-tuple-element.12), channel_id=1, source_target_pairs={{0,12},{4,0},{8,4},{12,8},{1,13},{5,1},{9,5},{13,9},{2,14},{6,2},{... | collective-permute-start | bytes 786440 | tf_op jit(solution)/shard_map/ppermute | solution.py:56
  32.5 3.9 %collective-permute-start.6 = (bf16[4,4,64,512]{3,2,1,0:T(8,128)(2,1)S(1)}, bf16[4,4,64,512]{3,2,1,0:T(8,128)(2,1)S(1)}, u32[]{:S(2)}, u32[]{:S(2)}) collective-permute-start(bf16[4,4,64,512]{3,2,1,0:T(8,128)(2,1)S(1)} %pad_maximum_fusion.1), channel_id=1, source_target_pairs={{0,16},{16,0},{32,48},{48,32},{64,80},{80,64},{96,112},{112,96},{1... | collective-permute-start | bytes 3145736 | tf_op jit(solution)/shard_map/ppermute | solution.py:58
  34.2 2.5 %copy-start.7 = (bf16[88,1024]{1,0:T(8,128)(2,1)S(1)}, bf16[88,1024]{1,0:T(8,128)(2,1)}, u32[]{:S(2)}) copy-start(bf16[88,1024]{1,0:T(8,128)(2,1)} %param.10) | copy-start | bytes 540676
  35.0 2.0 %copy-start.10 = (f32[1024]{0:T(1024)S(1)}, f32[1024]{0:T(1024)}, u32[]{:S(2)}) copy-start(f32[1024]{0:T(1024)} %param.13) | copy-start | bytes 12292
  37.4 10.3 %copy-start.3 = (bf16[1,176,1024]{2,1,0:T(8,128)(2,1)S(1)}, bf16[1,176,1024]{2,1,0:T(8,128)(2,1)}, u32[]{:S(2)}) copy-start(bf16[1,176,1024]{2,1,0:T(8,128)(2,1)} %param.16) | copy-start | bytes 1081348
  37.8 10.0 %copy-start.4 = (bf16[1,176,1024]{2,1,0:T(8,128)(2,1)S(1)}, bf16[1,176,1024]{2,1,0:T(8,128)(2,1)}, u32[]{:S(2)}) copy-start(bf16[1,176,1024]{2,1,0:T(8,128)(2,1)} %param.17) | copy-start | bytes 1081348
  37.8 10.1 %copy-start.5 = (bf16[1,176,1024]{2,1,0:T(8,128)(2,1)S(1)}, bf16[1,176,1024]{2,1,0:T(8,128)(2,1)}, u32[]{:S(2)}) copy-start(bf16[1,176,1024]{2,1,0:T(8,128)(2,1)} %param.18) | copy-start | bytes 1081348
  38.9 31.6 %all-to-all-start.1 = ((bf16[16,22,1024]{2,1,0:T(8,128)(2,1)}), bf16[16,22,1024]{2,1,0:T(8,128)(2,1)S(1)}, u32[]{:S(2)}, u32[]{:S(2)}) async-start(bf16[16,22,1024]{2,1,0:T(8,128)(2,1)} %reshape.236), calls=%async_computation.1 | async-start | bytes 1572864 | tf_op jit(solution)/shard_map/all_to_all | solution.py:95
  47.9 26.9 %collective-permute-start.7 = (bf16[3,176,1024]{2,1,0:T(8,128)(2,1)S(1)}, bf16[3,176,1024]{2,1,0:T(8,128)(2,1)}, u32[]{:S(2)}, u32[]{:S(2)}) collective-permute-start(bf16[3,176,1024]{2,1,0:T(8,128)(2,1)S(1)} %constant_dynamic-update-slice_fusion), channel_id=1, source_target_pairs={{0,4},{4,8},{8,12},{12,0},{1,5},{5,9},{9,13},{13,1},{2,6},{6,10},{... | collective-permute-start | bytes 3244040 | tf_op jit(solution)/shard_map/ppermute | solution.py:75
  48.4 49.3 %collective-permute-start.8 = (bf16[3,176,1024]{2,1,0:T(8,128)(2,1)S(1)}, bf16[3,176,1024]{2,1,0:T(8,128)(2,1)}, u32[]{:S(2)}, u32[]{:S(2)}) collective-permute-start(bf16[3,176,1024]{2,1,0:T(8,128)(2,1)S(1)} %constant_dynamic-update-slice_fusion), channel_id=1, source_target_pairs={{0,8},{4,12},{8,0},{12,4},{1,9},{5,13},{9,1},{13,5},{2,10},{6,14},... | collective-permute-start | bytes 3244040 | tf_op jit(solution)/shard_map/ppermute | solution.py:75
  50.5 47.6 %collective-permute-start.9 = (bf16[3,176,1024]{2,1,0:T(8,128)(2,1)S(1)}, bf16[3,176,1024]{2,1,0:T(8,128)(2,1)}, u32[]{:S(2)}, u32[]{:S(2)}) collective-permute-start(bf16[3,176,1024]{2,1,0:T(8,128)(2,1)S(1)} %constant_dynamic-update-slice_fusion), channel_id=1, source_target_pairs={{0,12},{4,0},{8,4},{12,8},{1,13},{5,1},{9,5},{13,9},{2,14},{6,2},{... | collective-permute-start | bytes 3244040 | tf_op jit(solution)/shard_map/ppermute | solution.py:75
  70.7 29.6 %collective-permute-start.10 = (bf16[352,1024]{1,0:T(8,128)(2,1)S(1)}, bf16[352,1024]{1,0:T(8,128)(2,1)S(1)}, u32[]{:S(2)}, u32[]{:S(2)}) collective-permute-start(bf16[352,1024]{1,0:T(8,128)(2,1)S(1)} %reshape.237), channel_id=1, source_target_pairs={{0,1},{1,2},{2,3},{3,0},{4,5},{5,6},{6,7},{7,4},{8,9},{9,10},{10,1... | collective-permute-start | bytes 2162696 | tf_op jit(solution)/shard_map/ppermute | solution.py:100
  71.6 32.5 %collective-permute-start.11 = (bf16[352,1024]{1,0:T(8,128)(2,1)S(1)}, bf16[352,1024]{1,0:T(8,128)(2,1)S(1)}, u32[]{:S(2)}, u32[]{:S(2)}) collective-permute-start(bf16[352,1024]{1,0:T(8,128)(2,1)S(1)} %reshape.237), channel_id=1, source_target_pairs={{0,2},{1,3},{2,0},{3,1},{4,6},{5,7},{6,4},{7,5},{8,10},{9,11},{10,... | collective-permute-start | bytes 2162696 | tf_op jit(solution)/shard_map/ppermute | solution.py:100
  74.8 29.4 %collective-permute-start.12 = (bf16[352,1024]{1,0:T(8,128)(2,1)S(1)}, bf16[352,1024]{1,0:T(8,128)(2,1)S(1)}, u32[]{:S(2)}, u32[]{:S(2)}) collective-permute-start(bf16[352,1024]{1,0:T(8,128)(2,1)S(1)} %reshape.237), channel_id=1, source_target_pairs={{0,3},{1,0},{2,1},{3,2},{4,7},{5,4},{6,5},{7,6},{8,11},{9,8},{10,9... | collective-permute-start | bytes 2162696 | tf_op jit(solution)/shard_map/ppermute | solution.py:100
  100.3 3.9 %copy-start.1 = (bf16[3,704,1024]{2,1,0:T(8,128)(2,1)}, bf16[3,704,1024]{2,1,0:T(8,128)(2,1)S(1)}, u32[]{:S(2)}) copy-start(bf16[3,704,1024]{2,1,0:T(8,128)(2,1)S(1)} %pad_maximum_fusion) | copy-start | bytes 12976132
  104.2 1.4 copy-start.6
  118.7 12.0 %collective-permute-start.13 = (bf16[352,1024]{1,0:T(8,128)(2,1)}, bf16[352,1024]{1,0:T(8,128)(2,1)S(1)}, u32[]{:S(2)}, u32[]{:S(2)}) collective-permute-start(bf16[352,1024]{1,0:T(8,128)(2,1)} %get-tuple-element.8), channel_id=1, source_target_pairs={{0,3},{1,0},{2,1},{3,2},{4,7},{5,4},{6,5},{7,6},{8,11},{9,8},{10,9... | collective-permute-start | bytes 2162696 | tf_op jit(solution)/shard_map/ppermute | solution.py:107
  118.7 12.0 %collective-permute-start.14 = (bf16[352,1024]{1,0:T(8,128)(2,1)}, bf16[352,1024]{1,0:T(8,128)(2,1)S(1)}, u32[]{:S(2)}, u32[]{:S(2)}) collective-permute-start(bf16[352,1024]{1,0:T(8,128)(2,1)} %get-tuple-element.10), channel_id=1, source_target_pairs={{0,2},{1,3},{2,0},{3,1},{4,6},{5,7},{6,4},{7,5},{8,10},{9,11},{10,... | collective-permute-start | bytes 2162696 | tf_op jit(solution)/shard_map/ppermute | solution.py:107
  119.5 32.9 %collective-permute-start.15 = (bf16[352,1024]{1,0:T(8,128)(2,1)}, bf16[352,1024]{1,0:T(8,128)(2,1)S(1)}, u32[]{:S(2)}, u32[]{:S(2)}) collective-permute-start(bf16[352,1024]{1,0:T(8,128)(2,1)} %get-tuple-element.9), channel_id=1, source_target_pairs={{0,1},{1,2},{2,3},{3,0},{4,5},{5,6},{6,7},{7,4},{8,9},{9,10},{10,1... | collective-permute-start | bytes 2162696 | tf_op jit(solution)/shard_map/ppermute | solution.py:107
  154.0 9.7 %copy-start.9 = (s32[88,2]{0,1:T(2,128)S(1)}, s32[88,2]{0,1:T(2,128)}, u32[]{:S(2)}) copy-start(s32[88,2]{0,1:T(2,128)} %param.15) | copy-start | bytes 2116
  154.1 10.1 %copy-start.8 = (f32[1024,16]{0,1:T(8,128)S(1)}, f32[1024,16]{0,1:T(8,128)}, u32[]{:S(2)}) copy-start(f32[1024,16]{0,1:T(8,128)} %param.14) | copy-start | bytes 196612
  155.1 31.3 %all-to-all-start.2 = ((bf16[16,22,1024]{2,1,0:T(8,128)(2,1)}), bf16[16,22,1024]{2,1,0:T(8,128)(2,1)S(1)}, u32[]{:S(2)}, u32[]{:S(2)}) async-start(bf16[16,22,1024]{2,1,0:T(8,128)(2,1)} %reshape.238), calls=%async_computation.2 | async-start | bytes 1572864 | tf_op jit(solution)/shard_map/all_to_all | solution.py:111
  166.8 20.4 %copy-start.11 = (f32[1024]{0:T(1024)S(1)}, f32[1024]{0:T(1024)}, u32[]{:S(2)}) copy-start(f32[1024]{0:T(1024)} %param.19) | copy-start | bytes 12292
  187.2 0.8 copy-start.2

commit v11 on v10

--- a/solution.py
+++ b/solution.py
@@ -51,16 +51,16 @@
     core = lax.axis_index("expert") % 2
     half = width // 2
     my_cols = lax.dynamic_slice_in_dim(out_proj, core * half, half, axis=1)
-    near = [my_cols] + [lax.ppermute(my_cols, "tx", shift_pairs(n_tx, s)) for s in range(1, n_tx)]
+    near = [my_cols] + [lax.ppermute(my_cols, "ty", shift_pairs(n_ty, s)) for s in range(1, n_ty)]
     near = jnp.stack(near)
-    my_half = [near] + [lax.ppermute(near, "ty", shift_pairs(n_ty, s)) for s in range(1, n_ty)]
+    my_half = [near] + [lax.ppermute(near, "tx", shift_pairs(n_tx, s)) for s in range(1, n_tx)]
     my_half = jnp.stack(my_half)
     other_half = lax.ppermute(my_half, "expert", [(i, i ^ 1) for i in range(n_expert)])
     own_heads = lax.all_to_all(attn_heads, TENSOR_AXES, 1, 0, tiled=True)
     own_heads = own_heads.reshape(n_ty, n_tx, -1, row_count)
     from_y = (ty - jnp.arange(n_ty)) % n_ty
     from_x = (tx - jnp.arange(n_tx)) % n_tx
-    own_heads = jnp.take(jnp.take(own_heads, from_y, axis=0), from_x, axis=1)
+    own_heads = jnp.take(jnp.take(own_heads, from_y, axis=0), from_x, axis=1).swapaxes(0, 1)
     contract = (((0, 1, 2), (0, 1, 2)), ((), ()))
     proj_mine = lax.dot_general(own_heads, my_half, contract, preferred_element_type=jnp.float32)
     proj_other = lax.dot_general(own_heads, other_half, contract, preferred_element_type=jnp.float32)
@@ -71,9 +71,7 @@
     )
 
     stacked = jnp.concatenate([w_gate, w_upward, w_downward], axis=0)
-    pieces = [stacked] + [
-        lax.ppermute(stacked, "ty", shift_pairs(n_ty, s)) for s in range(1, n_ty)
-    ]
+    gathered = lax.all_gather(stacked, "ty", axis=1, tiled=True)
 
     hidden_one = (residual_in.astype(jnp.float32) + projected).astype(jnp.bfloat16)
     normed = rms_scale(hidden_one, gain_first)
@@ -93,8 +91,7 @@
     send_slots = jnp.dot(placing, repeated, preferred_element_type=jnp.float32).astype(jnp.bfloat16)
     send_slots = send_slots.reshape(n_expert, capacity, width)
     received = lax.all_to_all(send_slots, "expert", split_axis=0, concat_axis=0, tiled=True)
-    weights = jnp.concatenate(pieces, axis=1)
-    gate_rows, up_rows, down_rows = weights[0], weights[1], weights[2]
+    gate_rows, up_rows, down_rows = gathered[0], gathered[1], gathered[2]
     slot_total = n_expert * capacity
     rows_in = received.reshape(slot_total, width)
     peer_rows = [lax.ppermute(rows_in, "tx", shift_pairs(n_tx, s)) for s in range(1, n_tx)]

time: 188 us -> 203 us (1.080)
  blocking collectives: 0 us -> 31.5 us
  starting transfers between devices: 44.4 us -> 26.1 us
  between operations: 1.14 us -> 14.4 us
  waiting for transfers between devices: 100 us -> 88.5 us
  matrix products: 21.4 us -> 23.5 us
  local copies, waits for them, and re-layouts: 14.2 us -> 12.1 us
    all_to_all x0 -> x1, blocking collectives: none -> 31.5 us  [per_device(): lax.all_to_all(send_slots, 'expert', split_axis=0, concat_axis=0, tiled=T...]
    ppermute x3, waiting for transfers between devices: 3.67 us -> 30 us  [per_device(): lax.ppermute(rows_in, 'tx', shift_pairs(n_tx, s))]
    ppermute x9 -> x6, waiting for transfers between devices: 34.1 us -> 12 us  [the longest x3 12 us: per_device(): lax.ppermute(near, 'tx', shift_pairs(n_tx, s))]
    all_to_all x1 -> x0, waiting for transfers between devices: 18.9 us -> none  [per_device(): lax.all_to_all(send_slots, 'expert', split_axis=0, concat_axis=0, tiled=T...]
    all_to_all x1 -> x0, starting transfers between devices: 8.85 us -> none  [per_device(): lax.all_to_all(send_slots, 'expert', split_axis=0, concat_axis=0, tiled=T...]
    dot_general x1 -> x2, matrix products: 3.62 us -> 8.92 us  [expert_block(): lax.dot_general(inputs, gate_rows, (((1,), (1,)), ((), ())), preferred_el...]
    all_to_all x1, starting transfers between devices: 8.56 us -> 3.89 us  [per_device(): lax.all_to_all(expert_out, 'expert', split_axis=0, concat_axis=0, tiled=T...]
    ppermute x9 -> x6, starting transfers between devices: 14.4 us -> 10.3 us  [the longest x3 5.88 us: per_device(): lax.ppermute(my_cols, 'ty', shift_pairs(n_ty, s))]
  transfers between devices with their start and end apart: 19 -> 16, of which waited for: 11 -> 10; matrix products, arithmetic and copies ran while one was open for 10% -> 10% of each run, Pallas kernels for 0% -> 0%
where the time goes in v11:
time: 203 us; the launch traced here: 202 us
  waiting for transfers between devices  88.5 us (44%)
  blocking collectives  31.5 us (16%)
  starting transfers between devices  26.1 us (13%)
  matrix products  23.5 us (12%)
  between operations  14.4 us (7%)
  local copies, waits for them, and re-layouts  12.1 us (6%)
  other arithmetic  6.44 us (3%)
    all_to_all x1, blocking collectives, per_device(): lax.all_to_all(send_slots, 'expert', split_axis=0, concat_axis=0, tiled=T...  31.5 us
    ppermute x3, waiting for transfers between devices, per_device(): lax.ppermute(rows_in, 'tx', shift_pairs(n_tx, s))  30 us
    ppermute x3, waiting for transfers between devices, per_device(): back = lax.ppermute(partial[s - 1], 'tx', shift_pairs(n_tx, -s))  26.6 us
    all_to_all x1, waiting for transfers between devices, per_device(): lax.all_to_all(expert_out, 'expert', split_axis=0, concat_axis=0, tiled=T...  19.4 us
    dot_general x2, matrix products, expert_block(): return jnp.dot(hid, down_rows, preferred_element_type=jnp.float32)  12.8 us
    ppermute x3, waiting for transfers between devices, per_device(): lax.ppermute(near, 'tx', shift_pairs(n_tx, s))  12 us
    dot_general x2, matrix products, expert_block(): lax.dot_general(inputs, gate_rows, (((1,), (1,)), ((), ())), preferred_el...  8.92 us
    ppermute x3, starting transfers between devices, per_device(): lax.ppermute(my_cols, 'ty', shift_pairs(n_ty, s))  5.88 us
  transfers between devices with their start and end apart: 16, of which 10 were waited for; matrix products, arithmetic and copies ran while one was open for 10% of the time, Pallas kernels for 0%

profile of v11, /device:TPU:1, one launch (start us, length us, event | category | flops | bytes accessed | tf_op | source)
XLA Modules:
  0.0 202.5 jit_solution(16371672117061425853)
XLA Ops:
  7.2 2.4 %pad_maximum_fusion = bf16[3,176,1024]{2,1,0:T(8,128)(2,1)} fusion(bf16[1,176,1024]{2,1,0:T(8,128)(2,1)} %param.18, bf16[1,176,1024]{2,1,0:T(8,128)(2,1)} %param.17, bf16[1,176,1024]{2,1,0:T(8,128)(2,1)} %param.16), kind=kLoop, calls=%fused_computation.41 | loop fusion | flops 1081344 | bytes 2162688 | tf_op jit(solution)/shard_map/concatenate | solution.py:73
  9.7 2.2 %collective-permute-start = (bf16[64,512]{1,0:T(8,128)(2,1)S(1)}, bf16[64,512]{1,0:T(8,128)(2,1)S(1)}, u32[]{:S(2)}, u32[]{:S(2)}) collective-permute-start(bf16[64,512]{1,0:T(8,128)(2,1)S(1)} %constant_dynamic-slice_fusion), channel_id=1, source_target_pairs={{0,4},{4,8},{8,12},{12,0},{1,5},{5,9},{9,13},{13,1},{2,6},{6,10},{... | collective-permute-start | bytes 196616 | tf_op jit(solution)/shard_map/ppermute | solution.py:54
  11.9 2.6 %collective-permute-start.1 = (bf16[64,512]{1,0:T(8,128)(2,1)S(1)}, bf16[64,512]{1,0:T(8,128)(2,1)S(1)}, u32[]{:S(2)}, u32[]{:S(2)}) collective-permute-start(bf16[64,512]{1,0:T(8,128)(2,1)S(1)} %constant_dynamic-slice_fusion), channel_id=1, source_target_pairs={{0,8},{4,12},{8,0},{12,4},{1,9},{5,13},{9,1},{13,5},{2,10},{6,14},... | collective-permute-start | bytes 196616 | tf_op jit(solution)/shard_map/ppermute | solution.py:54
  14.5 1.1 collective-permute-start.2
  15.6 0.5 all_to_all.18
  16.1 0.8 copy.23
  16.9 4.2 %all-to-all-start = ((bf16[64,16,88]{2,0,1:T(8,128)(2,1)}), bf16[64,16,88]{2,0,1:T(8,128)(2,1)S(1)}, u32[]{:S(2)}, u32[]{:S(2)}) async-start(bf16[64,16,88]{2,0,1:T(8,128)(2,1)} %copy.23), calls=%async_computation | async-start | bytes 524288 | tf_op jit(solution)/shard_map/all_to_all | solution.py:59
  21.2 0.1 copy.26
  21.3 0.1 reshape.232
  21.4 0.6 reduce-window.6
  22.0 0.2 slice_reduce_fusion
  22.3 2.9 %collective-permute-start.4 = (bf16[4,64,512]{2,1,0:T(8,128)(2,1)S(1)}, bf16[4,64,512]{2,1,0:T(8,128)(2,1)S(1)}, u32[]{:S(2)}, u32[]{:S(2)}) collective-permute-start(bf16[4,64,512]{2,1,0:T(8,128)(2,1)S(1)} %get-tuple-element.12), channel_id=1, source_target_pairs={{0,2},{1,3},{2,0},{3,1},{4,6},{5,7},{6,4},{7,5},{8,10},{9,11},{10,... | collective-permute-start | bytes 786440 | tf_op jit(solution)/shard_map/ppermute | solution.py:56
  25.3 0.9 collective-permute-start.5
  26.2 0.6 collective-permute-start.3
  26.8 4.8 %collective-permute-done.4 = bf16[4,64,512]{2,1,0:T(8,128)(2,1)S(1)} collective-permute-done((bf16[4,64,512]{2,1,0:T(8,128)(2,1)S(1)}, bf16[4,64,512]{2,1,0:T(8,128)(2,1)S(1)}, u32[]{:S(2)}, u32[]{:S(2)}) %collective-permute-start.4) | collective-permute-done | bytes 262176 | tf_op jit(solution)/shard_map/ppermute | solution.py:56
  31.6 5.8 %collective-permute-done.5 = bf16[4,64,512]{2,1,0:T(8,128)(2,1)S(1)} collective-permute-done((bf16[4,64,512]{2,1,0:T(8,128)(2,1)S(1)}, bf16[4,64,512]{2,1,0:T(8,128)(2,1)S(1)}, u32[]{:S(2)}, u32[]{:S(2)}) %collective-permute-start.5) | collective-permute-done | bytes 262176 | tf_op jit(solution)/shard_map/ppermute | solution.py:56
  37.5 1.4 collective-permute-done.3
  38.8 0.1 pad_maximum_fusion.1
  39.0 1.2 collective-permute-start.6
  40.3 0.6 gather_fusion
  41.0 0.6 gather_fusion.1
  41.6 0.4 convolution_bitcast_fusion.1
  42.0 0.4 collective-permute-done.6
  42.4 0.4 convolution_bitcast_fusion
  42.8 0.2 fusion.29
  43.0 0.1 fusion.31
  43.1 0.2 broadcast_in_dim.40
  43.3 0.1 reshape.235
  43.5 0.3 convolution_convert_fusion.2
  43.8 0.2 reshape.236
  44.0 31.5 %all_to_all.26 = bf16[16,22,1024]{2,1,0:T(8,128)(2,1)S(1)} all-to-all(bf16[16,22,1024]{2,1,0:T(8,128)(2,1)S(1)} %reshape.236), channel_id=1, replica_groups=mesh['expert'=16,'ty'=4,'tx'=4] {'expert'}, dimensions={0} | all-to-all | bytes 1441792 | tf_op jit(solution)/shard_map/all_to_all | solution.py:93
  75.5 0.2 reshape.237
  75.7 0.6 collective-permute-start.7
  76.3 2.2 %collective-permute-start.8 = (bf16[352,1024]{1,0:T(8,128)(2,1)S(1)}, bf16[352,1024]{1,0:T(8,128)(2,1)S(1)}, u32[]{:S(2)}, u32[]{:S(2)}) collective-permute-start(bf16[352,1024]{1,0:T(8,128)(2,1)S(1)} %reshape.237), channel_id=1, source_target_pairs={{0,2},{1,3},{2,0},{3,1},{4,6},{5,7},{6,4},{7,5},{8,10},{9,11},{10,... | collective-permute-start | bytes 2162696 | tf_op jit(solution)/shard_map/ppermute | solution.py:97
  78.5 1.1 collective-permute-start.9
  79.6 15.4 %collective-permute-done.7 = bf16[352,1024]{1,0:T(8,128)(2,1)S(1)} collective-permute-done((bf16[352,1024]{1,0:T(8,128)(2,1)S(1)}, bf16[352,1024]{1,0:T(8,128)(2,1)S(1)}, u32[]{:S(2)}, u32[]{:S(2)}) %collective-permute-start.7) | collective-permute-done | bytes 720928 | tf_op jit(solution)/shard_map/ppermute | solution.py:97
  95.1 0.9 constant_dynamic-update-slice_fusion.2
  96.0 14.6 %collective-permute-done.8 = bf16[352,1024]{1,0:T(8,128)(2,1)S(1)} collective-permute-done((bf16[352,1024]{1,0:T(8,128)(2,1)S(1)}, bf16[352,1024]{1,0:T(8,128)(2,1)S(1)}, u32[]{:S(2)}, u32[]{:S(2)}) %collective-permute-start.8) | collective-permute-done | bytes 720928 | tf_op jit(solution)/shard_map/ppermute | solution.py:97
  110.6 1.0 constant_dynamic-update-slice_fusion.1
  111.5 1.0 constant_dynamic-update-slice_fusion
  112.5 5.6 %fusion.15 = f32[1056,704]{1,0:T(8,128)} fusion(bf16[1056,1024]{1,0:T(8,128)(2,1)} %constant_dynamic-update-slice_fusion, bf16[3,704,1024]{2,1,0:T(8,128)(2,1)} %all-gather.2.cloned.1.call-done), kind=kOutput, calls=%fused_computation.28 | convolution fusion | flops 1522532352 | bytes 6578176 | tf_op jit(solution)/shard_map/dot_general | solution.py:20
  118.1 8.0 %convolution_convert_fusion = bf16[1056,1024]{1,0:T(8,128)(2,1)S(1)} fusion(f32[1056,704]{1,0:T(8,128)} %fusion.15, bf16[3,704,1024]{2,1,0:T(8,128)(2,1)} %all-gather.2.cloned.1.call-done, bf16[1056,1024]{1,0:T(8,128)(2,1)} %constant_dynamic-update-slice_fusion), kind=kOutput, calls=%fused_computation.4 | convolution fusion | flops 3053580288 | bytes 10452992 | tf_op jit(solution)/shard_map/dot_general | solution.py:27
  126.2 1.4 fusion.57
  127.6 2.0 collective-permute-start.10
  129.5 0.6 collective-permute-start.11
  130.1 3.3 %fusion.25 = f32[352,704]{1,0:T(8,128)} fusion(bf16[352,1024]{1,0:T(8,128)(2,1)S(1)} %reshape.237, bf16[3,704,1024]{2,1,0:T(8,128)(2,1)} %all-gather.2.cloned.1.call-done), kind=kOutput, calls=%fused_computation.40 | convolution fusion | flops 509493248 | bytes 3153920 | tf_op jit(solution)/shard_map/dot_general | solution.py:20
  133.4 4.7 %convolution_convert_fusion.1 = bf16[352,1024]{1,0:T(8,128)(2,1)} fusion(bf16[3,704,1024]{2,1,0:T(8,128)(2,1)} %all-gather.2.cloned.1.call-done, f32[352,704]{1,0:T(8,128)} %fusion.25, bf16[352,1024]{1,0:T(8,128)(2,1)S(1)} %reshape.237), kind=kOutput, calls=%fused_computation.23 | convolution fusion | flops 1015877632 | bytes 5406720 | tf_op jit(solution)/shard_map/dot_general | solution.py:27
  138.2 7.0 %collective-permute-done.10 = bf16[352,1024]{1,0:T(8,128)(2,1)S(1)} collective-permute-done((bf16[352,1024]{1,0:T(8,128)(2,1)}, bf16[352,1024]{1,0:T(8,128)(2,1)S(1)}, u32[]{:S(2)}, u32[]{:S(2)}) %collective-permute-start.10) | collective-permute-done | bytes 720928 | tf_op jit(solution)/shard_map/ppermute | solution.py:104
  145.2 3.1 %collective-permute-done.11 = bf16[352,1024]{1,0:T(8,128)(2,1)S(1)} collective-permute-done((bf16[352,1024]{1,0:T(8,128)(2,1)}, bf16[352,1024]{1,0:T(8,128)(2,1)S(1)}, u32[]{:S(2)}, u32[]{:S(2)}) %collective-permute-start.11) | collective-permute-done | bytes 720928 | tf_op jit(solution)/shard_map/ppermute | solution.py:104
  148.3 16.5 %collective-permute-done.12 = bf16[352,1024]{1,0:T(8,128)(2,1)S(1)} collective-permute-done((bf16[352,1024]{1,0:T(8,128)(2,1)}, bf16[352,1024]{1,0:T(8,128)(2,1)S(1)}, u32[]{:S(2)}, u32[]{:S(2)}) %collective-permute-start.12) | collective-permute-done | bytes 720928 | tf_op jit(solution)/shard_map/ppermute | solution.py:104
  164.8 1.6 add_convert_fusion
  166.3 1.1 reshape.238
  167.4 3.9 %all-to-all-start.2 = ((bf16[16,22,1024]{2,1,0:T(8,128)(2,1)}), bf16[16,22,1024]{2,1,0:T(8,128)(2,1)S(1)}, u32[]{:S(2)}, u32[]{:S(2)}) async-start(bf16[16,22,1024]{2,1,0:T(8,128)(2,1)} %reshape.238), calls=%async_computation.2 | async-start | bytes 1572864 | tf_op jit(solution)/shard_map/all_to_all | solution.py:108
  171.3 0.1 copy.24
  171.4 0.1 reshape.257
  171.6 0.1 iota_compare_fusion.2
  171.8 0.3 fusion.58
  172.1 2.3 %gather_fusion.2 = f32[176]{0:T(256)S(1)} fusion(f32[88,16]{0,1:T(8,128)S(1)} %fusion.39, s32[176]{0:T(256)S(1)} %reshape.257), kind=kCustom, calls=%fused_computation.2 | custom fusion | bytes 2816 | tf_op jit(solution)/shard_map/jit(take_along_axis)/gather | solution.py:80
  174.4 0.1 reshape.260
  174.7 19.4 %all-to-all-done.2 = bf16[16,22,1024]{2,1,0:T(8,128)(2,1)S(1)} async-done(((bf16[16,22,1024]{2,1,0:T(8,128)(2,1)}), bf16[16,22,1024]{2,1,0:T(8,128)(2,1)S(1)}, u32[]{:S(2)}, u32[]{:S(2)}) %all-to-all-start.2) | async-done | bytes 720928 | tf_op jit(solution)/shard_map/all_to_all | solution.py:108
  194.1 0.2 reshape.270
  194.3 0.4 fusion.18
  194.7 0.2 fusion.26
  194.9 0.8 fusion.28
  (51 shorter events, 0.8 us)
Async XLA Ops:
  7.2 2.5 %copy-start = (bf16[64,1024]{1,0:T(8,128)(2,1)S(1)}, bf16[64,1024]{1,0:T(8,128)(2,1)}, u32[]{:S(2)}) copy-start(bf16[64,1024]{1,0:T(8,128)(2,1)} %param.12) | copy-start | bytes 393220
  7.2 8.4 %copy-start.2 = (bf16[64,1408]{1,0:T(8,128)(2,1)S(1)}, bf16[64,1408]{1,0:T(8,128)(2,1)}, u32[]{:S(2)}) copy-start(bf16[64,1408]{1,0:T(8,128)(2,1)} %param.11) | copy-start | bytes 540676
  7.2 14.0 %copy-start.5 = (s32[88,2]{0,1:T(2,128)S(1)}, s32[88,2]{0,1:T(2,128)}, u32[]{:S(2)}) copy-start(s32[88,2]{0,1:T(2,128)} %param.15) | copy-start | bytes 2116
  7.2 105.3 %all-gather.2.cloned.1.call-start = ((), (), s32[]{:S(2)}) async-start(), calls=%async_computation.3 | async-start | bytes 5406720 | tf_op jit(solution)/shard_map/all_gather | solution.py:74
  9.7 12.5 %collective-permute-start = (bf16[64,512]{1,0:T(8,128)(2,1)S(1)}, bf16[64,512]{1,0:T(8,128)(2,1)S(1)}, u32[]{:S(2)}, u32[]{:S(2)}) collective-permute-start(bf16[64,512]{1,0:T(8,128)(2,1)S(1)} %constant_dynamic-slice_fusion), channel_id=1, source_target_pairs={{0,4},{4,8},{8,12},{12,0},{1,5},{5,9},{9,13},{13,1},{2,6},{6,10},{... | collective-permute-start | bytes 196616 | tf_op jit(solution)/shard_map/ppermute | solution.py:54
  11.9 10.4 %collective-permute-start.1 = (bf16[64,512]{1,0:T(8,128)(2,1)S(1)}, bf16[64,512]{1,0:T(8,128)(2,1)S(1)}, u32[]{:S(2)}, u32[]{:S(2)}) collective-permute-start(bf16[64,512]{1,0:T(8,128)(2,1)S(1)} %constant_dynamic-slice_fusion), channel_id=1, source_target_pairs={{0,8},{4,12},{8,0},{12,4},{1,9},{5,13},{9,1},{13,5},{2,10},{6,14},... | collective-permute-start | bytes 196616 | tf_op jit(solution)/shard_map/ppermute | solution.py:54
  14.5 7.7 %collective-permute-start.2 = (bf16[64,512]{1,0:T(8,128)(2,1)S(1)}, bf16[64,512]{1,0:T(8,128)(2,1)S(1)}, u32[]{:S(2)}, u32[]{:S(2)}) collective-permute-start(bf16[64,512]{1,0:T(8,128)(2,1)S(1)} %constant_dynamic-slice_fusion), channel_id=1, source_target_pairs={{0,12},{4,0},{8,4},{12,8},{1,13},{5,1},{9,5},{13,9},{2,14},{6,2},{... | collective-permute-start | bytes 196616 | tf_op jit(solution)/shard_map/ppermute | solution.py:54
  16.9 23.4 %all-to-all-start = ((bf16[64,16,88]{2,0,1:T(8,128)(2,1)}), bf16[64,16,88]{2,0,1:T(8,128)(2,1)S(1)}, u32[]{:S(2)}, u32[]{:S(2)}) async-start(bf16[64,16,88]{2,0,1:T(8,128)(2,1)} %copy.23), calls=%async_computation | async-start | bytes 524288 | tf_op jit(solution)/shard_map/all_to_all | solution.py:59
  22.3 9.3 %collective-permute-start.4 = (bf16[4,64,512]{2,1,0:T(8,128)(2,1)S(1)}, bf16[4,64,512]{2,1,0:T(8,128)(2,1)S(1)}, u32[]{:S(2)}, u32[]{:S(2)}) collective-permute-start(bf16[4,64,512]{2,1,0:T(8,128)(2,1)S(1)} %get-tuple-element.12), channel_id=1, source_target_pairs={{0,2},{1,3},{2,0},{3,1},{4,6},{5,7},{6,4},{7,5},{8,10},{9,11},{10,... | collective-permute-start | bytes 786440 | tf_op jit(solution)/shard_map/ppermute | solution.py:56
  25.3 12.2 %collective-permute-start.5 = (bf16[4,64,512]{2,1,0:T(8,128)(2,1)S(1)}, bf16[4,64,512]{2,1,0:T(8,128)(2,1)S(1)}, u32[]{:S(2)}, u32[]{:S(2)}) collective-permute-start(bf16[4,64,512]{2,1,0:T(8,128)(2,1)S(1)} %get-tuple-element.12), channel_id=1, source_target_pairs={{0,3},{1,0},{2,1},{3,2},{4,7},{5,4},{6,5},{7,6},{8,11},{9,8},{10,9... | collective-permute-start | bytes 786440 | tf_op jit(solution)/shard_map/ppermute | solution.py:56
  26.2 12.7 %collective-permute-start.3 = (bf16[4,64,512]{2,1,0:T(8,128)(2,1)S(1)}, bf16[4,64,512]{2,1,0:T(8,128)(2,1)S(1)}, u32[]{:S(2)}, u32[]{:S(2)}) collective-permute-start(bf16[4,64,512]{2,1,0:T(8,128)(2,1)S(1)} %get-tuple-element.12), channel_id=1, source_target_pairs={{0,1},{1,2},{2,3},{3,0},{4,5},{5,6},{6,7},{7,4},{8,9},{9,10},{10,1... | collective-permute-start | bytes 786440 | tf_op jit(solution)/shard_map/ppermute | solution.py:56
  39.0 3.4 %collective-permute-start.6 = (bf16[4,4,64,512]{3,2,1,0:T(8,128)(2,1)S(1)}, bf16[4,4,64,512]{3,2,1,0:T(8,128)(2,1)S(1)}, u32[]{:S(2)}, u32[]{:S(2)}) collective-permute-start(bf16[4,4,64,512]{3,2,1,0:T(8,128)(2,1)S(1)} %pad_maximum_fusion.1), channel_id=1, source_target_pairs={{0,16},{16,0},{32,48},{48,32},{64,80},{80,64},{96,112},{112,96},{1... | collective-permute-start | bytes 3145736 | tf_op jit(solution)/shard_map/ppermute | solution.py:58
  40.3 2.6 %copy-start.3 = (bf16[88,1024]{1,0:T(8,128)(2,1)S(1)}, bf16[88,1024]{1,0:T(8,128)(2,1)}, u32[]{:S(2)}) copy-start(bf16[88,1024]{1,0:T(8,128)(2,1)} %param.10) | copy-start | bytes 540676
  41.0 2.0 %copy-start.6 = (f32[1024]{0:T(1024)S(1)}, f32[1024]{0:T(1024)}, u32[]{:S(2)}) copy-start(f32[1024]{0:T(1024)} %param.13) | copy-start | bytes 12292
  75.7 19.4 %collective-permute-start.7 = (bf16[352,1024]{1,0:T(8,128)(2,1)S(1)}, bf16[352,1024]{1,0:T(8,128)(2,1)S(1)}, u32[]{:S(2)}, u32[]{:S(2)}) collective-permute-start(bf16[352,1024]{1,0:T(8,128)(2,1)S(1)} %reshape.237), channel_id=1, source_target_pairs={{0,1},{1,2},{2,3},{3,0},{4,5},{5,6},{6,7},{7,4},{8,9},{9,10},{10,1... | collective-permute-start | bytes 2162696 | tf_op jit(solution)/shard_map/ppermute | solution.py:97
  76.3 34.3 %collective-permute-start.8 = (bf16[352,1024]{1,0:T(8,128)(2,1)S(1)}, bf16[352,1024]{1,0:T(8,128)(2,1)S(1)}, u32[]{:S(2)}, u32[]{:S(2)}) collective-permute-start(bf16[352,1024]{1,0:T(8,128)(2,1)S(1)} %reshape.237), channel_id=1, source_target_pairs={{0,2},{1,3},{2,0},{3,1},{4,6},{5,7},{6,4},{7,5},{8,10},{9,11},{10,... | collective-permute-start | bytes 2162696 | tf_op jit(solution)/shard_map/ppermute | solution.py:97
  78.5 33.0 %collective-permute-start.9 = (bf16[352,1024]{1,0:T(8,128)(2,1)S(1)}, bf16[352,1024]{1,0:T(8,128)(2,1)S(1)}, u32[]{:S(2)}, u32[]{:S(2)}) collective-permute-start(bf16[352,1024]{1,0:T(8,128)(2,1)S(1)} %reshape.237), channel_id=1, source_target_pairs={{0,3},{1,0},{2,1},{3,2},{4,7},{5,4},{6,5},{7,6},{8,11},{9,8},{10,9... | collective-permute-start | bytes 2162696 | tf_op jit(solution)/shard_map/ppermute | solution.py:97
  127.6 17.6 %collective-permute-start.10 = (bf16[352,1024]{1,0:T(8,128)(2,1)}, bf16[352,1024]{1,0:T(8,128)(2,1)S(1)}, u32[]{:S(2)}, u32[]{:S(2)}) collective-permute-start(bf16[352,1024]{1,0:T(8,128)(2,1)} %get-tuple-element.8), channel_id=1, source_target_pairs={{0,3},{1,0},{2,1},{3,2},{4,7},{5,4},{6,5},{7,6},{8,11},{9,8},{10,9... | collective-permute-start | bytes 2162696 | tf_op jit(solution)/shard_map/ppermute | solution.py:104
  129.5 18.7 %collective-permute-start.11 = (bf16[352,1024]{1,0:T(8,128)(2,1)}, bf16[352,1024]{1,0:T(8,128)(2,1)S(1)}, u32[]{:S(2)}, u32[]{:S(2)}) collective-permute-start(bf16[352,1024]{1,0:T(8,128)(2,1)} %get-tuple-element.10), channel_id=1, source_target_pairs={{0,2},{1,3},{2,0},{3,1},{4,6},{5,7},{6,4},{7,5},{8,10},{9,11},{10,... | collective-permute-start | bytes 2162696 | tf_op jit(solution)/shard_map/ppermute | solution.py:104
  130.1 34.6 %collective-permute-start.12 = (bf16[352,1024]{1,0:T(8,128)(2,1)}, bf16[352,1024]{1,0:T(8,128)(2,1)S(1)}, u32[]{:S(2)}, u32[]{:S(2)}) collective-permute-start(bf16[352,1024]{1,0:T(8,128)(2,1)} %get-tuple-element.9), channel_id=1, source_target_pairs={{0,1},{1,2},{2,3},{3,0},{4,5},{5,6},{6,7},{7,4},{8,9},{9,10},{10,1... | collective-permute-start | bytes 2162696 | tf_op jit(solution)/shard_map/ppermute | solution.py:104
  166.3 5.5 %copy-start.4 = (f32[1024,16]{0,1:T(8,128)S(1)}, f32[1024,16]{0,1:T(8,128)}, u32[]{:S(2)}) copy-start(f32[1024,16]{0,1:T(8,128)} %param.14) | copy-start | bytes 196612
  167.4 26.7 %all-to-all-start.2 = ((bf16[16,22,1024]{2,1,0:T(8,128)(2,1)}), bf16[16,22,1024]{2,1,0:T(8,128)(2,1)S(1)}, u32[]{:S(2)}, u32[]{:S(2)}) async-start(bf16[16,22,1024]{2,1,0:T(8,128)(2,1)} %reshape.238), calls=%async_computation.2 | async-start | bytes 1572864 | tf_op jit(solution)/shard_map/all_to_all | solution.py:108
  174.4 20.4 %copy-start.7 = (f32[1024]{0:T(1024)S(1)}, f32[1024]{0:T(1024)}, u32[]{:S(2)}) copy-start(f32[1024]{0:T(1024)} %param.19) | copy-start | bytes 12292
  194.8 0.8 copy-start.1
Sparse Core Ops, SparseCore 0:
  9.8 56.0 all-gather.1

commit v12 on v10

--- a/solution.py
+++ b/solution.py
@@ -71,9 +71,22 @@
     )
 
     stacked = jnp.concatenate([w_gate, w_upward, w_downward], axis=0)
-    pieces = [stacked] + [
-        lax.ppermute(stacked, "ty", shift_pairs(n_ty, s)) for s in range(1, n_ty)
-    ]
+    if n_ty == 4:
+        from_below = lax.ppermute(stacked, "ty", shift_pairs(n_ty, 1))
+        from_above = lax.ppermute(stacked, "ty", shift_pairs(n_ty, -1))
+        cut = stacked.shape[1] // 2
+        far = jnp.concatenate(
+            [
+                lax.ppermute(from_below[:, :cut], "ty", shift_pairs(n_ty, 1)),
+                lax.ppermute(from_above[:, cut:], "ty", shift_pairs(n_ty, -1)),
+            ],
+            axis=1,
+        )
+        pieces = [stacked, from_below, far, from_above]
+    else:
+        pieces = [stacked] + [
+            lax.ppermute(stacked, "ty", shift_pairs(n_ty, s)) for s in range(1, n_ty)
+        ]
 
     hidden_one = (residual_in.astype(jnp.float32) + projected).astype(jnp.bfloat16)
     normed = rms_scale(hidden_one, gain_first)

time: 188 us -> 206 us (1.096)
  local copies, waits for them, and re-layouts: 14.2 us -> 26.7 us
  waiting for transfers between devices: 100 us -> 104 us
  other arithmetic: 6.35 us -> 4.14 us
    all_to_all x1, waiting for transfers between devices: 18.9 us -> 0.01 us  [per_device(): lax.all_to_all(send_slots, 'expert', split_axis=0, concat_axis=0, tiled=T...]
    ppermute x3, waiting for transfers between devices: 3.67 us -> 18 us  [per_device(): lax.ppermute(rows_in, 'tx', shift_pairs(n_tx, s))]
    unnamed x29 -> x30, local copies, waits for them, and re-layouts: 3.29 us -> 10.4 us
    ppermute x3 -> x4, waiting for transfers between devices: 22.4 us -> 28.6 us  [the longest x1 24.1 us: per_device(): from_below = lax.ppermute(stacked, 'ty', shift_pairs(n_ty, 1))]
    ppermute x3, starting transfers between devices: 1.61 us -> 4.11 us  [per_device(): back = lax.ppermute(partial[s - 1], 'tx', shift_pairs(n_tx, -s))]
    ppermute x3, waiting for transfers between devices: 24 us -> 26.4 us  [per_device(): back = lax.ppermute(partial[s - 1], 'tx', shift_pairs(n_tx, -s))]
    concatenate x1 -> x0, other arithmetic: 2.19 us -> none  [per_device(): weights = jnp.concatenate(pieces, axis=1)]
    ppermute x3 -> x4, starting transfers between devices: 3.72 us -> 5.35 us  [the longest x1 2.67 us: per_device(): lax.ppermute(from_above[:, cut:], 'ty', shift_pairs(n_ty, -1))]
  transfers between devices with their start and end apart: 19 -> 20, of which waited for: 11 -> 11; matrix products, arithmetic and copies ran while one was open for 10% -> 14% of each run, Pallas kernels for 0% -> 0%
where the time goes in v12:
time: 206 us; the launch traced here: 205 us
  waiting for transfers between devices  104 us (50%)
  starting transfers between devices  46 us (22%)
  local copies, waits for them, and re-layouts  26.7 us (13%)
  matrix products  23.4 us (11%)
  other arithmetic  4.14 us (2%)
    ppermute x3, waiting for transfers between devices, per_device(): back = lax.ppermute(partial[s - 1], 'tx', shift_pairs(n_tx, -s))  26.4 us
    ppermute x1, waiting for transfers between devices, per_device(): from_below = lax.ppermute(stacked, 'ty', shift_pairs(n_ty, 1))  24.1 us
    all_to_all x1, waiting for transfers between devices, per_device(): lax.all_to_all(expert_out, 'expert', split_axis=0, concat_axis=0, tiled=T...  19.4 us
    ppermute x3, waiting for transfers between devices, per_device(): lax.ppermute(rows_in, 'tx', shift_pairs(n_tx, s))  18 us
    dot_general x2, matrix products, expert_block(): return jnp.dot(hid, down_rows, preferred_element_type=jnp.float32)  12.9 us
    ppermute x3, waiting for transfers between devices, per_device(): lax.ppermute(near, 'ty', shift_pairs(n_ty, s))  11.4 us
    unnamed x30, local copies, waits for them, and re-layouts  10.4 us
    all_to_all x1, starting transfers between devices, per_device(): lax.all_to_all(send_slots, 'expert', split_axis=0, concat_axis=0, tiled=T...  8.59 us
  transfers between devices with their start and end apart: 20, of which 11 were waited for; matrix products, arithmetic and copies ran while one was open for 14% of the time, Pallas kernels for 0%

profile of v12, /device:TPU:1, one launch (start us, length us, event | category | flops | bytes accessed | tf_op | source)
XLA Modules:
  0.0 205.1 jit_solution(1496271448307813308)
XLA Ops:
  0.7 0.9 copy-done
  1.5 2.0 collective-permute-start
  3.6 2.5 %collective-permute-start.1 = (bf16[64,512]{1,0:T(8,128)(2,1)S(1)}, bf16[64,512]{1,0:T(8,128)(2,1)S(1)}, u32[]{:S(2)}, u32[]{:S(2)}) collective-permute-start(bf16[64,512]{1,0:T(8,128)(2,1)S(1)} %constant_dynamic-slice_fusion), channel_id=1, source_target_pairs={{0,2},{1,3},{2,0},{3,1},{4,6},{5,7},{6,4},{7,5},{8,10},{9,11},{10,... | collective-permute-start | bytes 196616 | tf_op jit(solution)/shard_map/ppermute | solution.py:54
  6.0 1.2 collective-permute-start.2
  7.2 1.4 all_to_all.18
  8.6 0.8 copy.26
  9.4 4.3 %all-to-all-start = ((bf16[64,16,88]{2,0,1:T(8,128)(2,1)}), bf16[64,16,88]{2,0,1:T(8,128)(2,1)S(1)}, u32[]{:S(2)}, u32[]{:S(2)}) async-start(bf16[64,16,88]{2,0,1:T(8,128)(2,1)} %copy.26), calls=%async_computation | async-start | bytes 524288 | tf_op jit(solution)/shard_map/all_to_all | solution.py:59
  13.8 0.8 copy.31
  14.7 0.6 reduce-window.6
  15.7 1.4 collective-permute-start.3
  17.2 2.4 %collective-permute-start.4 = (bf16[4,64,512]{2,1,0:T(8,128)(2,1)S(1)}, bf16[4,64,512]{2,1,0:T(8,128)(2,1)S(1)}, u32[]{:S(2)}, u32[]{:S(2)}) collective-permute-start(bf16[4,64,512]{2,1,0:T(8,128)(2,1)S(1)} %get-tuple-element.18), channel_id=1, source_target_pairs={{0,8},{4,12},{8,0},{12,4},{1,9},{5,13},{9,1},{13,5},{2,10},{6,14},... | collective-permute-start | bytes 786440 | tf_op jit(solution)/shard_map/ppermute | solution.py:56
  19.6 1.2 collective-permute-start.5
  20.8 5.8 %collective-permute-done.3 = bf16[4,64,512]{2,1,0:T(8,128)(2,1)S(1)} collective-permute-done((bf16[4,64,512]{2,1,0:T(8,128)(2,1)S(1)}, bf16[4,64,512]{2,1,0:T(8,128)(2,1)S(1)}, u32[]{:S(2)}, u32[]{:S(2)}) %collective-permute-start.3) | collective-permute-done | bytes 262176 | tf_op jit(solution)/shard_map/ppermute | solution.py:56
  26.6 5.6 %collective-permute-done.4 = bf16[4,64,512]{2,1,0:T(8,128)(2,1)S(1)} collective-permute-done((bf16[4,64,512]{2,1,0:T(8,128)(2,1)S(1)}, bf16[4,64,512]{2,1,0:T(8,128)(2,1)S(1)}, u32[]{:S(2)}, u32[]{:S(2)}) %collective-permute-start.4) | collective-permute-done | bytes 262176 | tf_op jit(solution)/shard_map/ppermute | solution.py:56
  32.3 1.8 collective-permute-start.6
  34.1 0.9 constant_dynamic-update-slice_fusion.2
  35.1 1.0 constant_dynamic-update-slice_fusion.1
  36.1 0.6 gather_fusion
  36.8 0.6 gather_fusion.1
  37.4 0.4 convolution_bitcast_fusion.1
  37.8 0.4 convolution_bitcast_fusion
  38.8 0.3 convolution_convert_fusion.2
  39.2 1.1 reshape.236
  40.3 8.6 %all-to-all-start.1 = ((bf16[16,22,1024]{2,1,0:T(8,128)(2,1)}), bf16[16,22,1024]{2,1,0:T(8,128)(2,1)S(1)}, u32[]{:S(2)}, u32[]{:S(2)}) async-start(bf16[16,22,1024]{2,1,0:T(8,128)(2,1)} %reshape.236), calls=%async_computation.1 | async-start | bytes 1572864 | tf_op jit(solution)/shard_map/all_to_all | solution.py:108
  48.9 1.0 constant_dynamic-update-slice_fusion
  49.8 0.5 collective-permute-start.7
  50.4 2.1 %collective-permute-start.9 = (bf16[3,176,1024]{2,1,0:T(8,128)(2,1)}, bf16[3,176,1024]{2,1,0:T(8,128)(2,1)S(1)}, u32[]{:S(2)}, u32[]{:S(2)}) collective-permute-start(bf16[3,176,1024]{2,1,0:T(8,128)(2,1)} %get-tuple-element.11), channel_id=1, source_target_pairs={{0,12},{4,0},{8,4},{12,8},{1,13},{5,1},{9,5},{13,9},{2,14},{6,2},{... | collective-permute-start | bytes 3244040 | tf_op jit(solution)/shard_map/ppermute | solution.py:76
  52.5 24.1 %collective-permute-done.7 = bf16[3,176,1024]{2,1,0:T(8,128)(2,1)S(1)} collective-permute-done((bf16[3,176,1024]{2,1,0:T(8,128)(2,1)}, bf16[3,176,1024]{2,1,0:T(8,128)(2,1)S(1)}, u32[]{:S(2)}, u32[]{:S(2)}) %collective-permute-start.7) | collective-permute-done | bytes 1081376 | tf_op jit(solution)/shard_map/ppermute | solution.py:75
  76.6 0.8 slice.55
  77.4 0.8 slice.56
  78.3 2.7 %collective-permute-start.10 = (bf16[3,88,1024]{2,1,0:T(8,128)(2,1)}, bf16[3,88,1024]{2,1,0:T(8,128)(2,1)}, u32[]{:S(2)}, u32[]{:S(2)}) collective-permute-start(bf16[3,88,1024]{2,1,0:T(8,128)(2,1)} %slice.56), channel_id=1, source_target_pairs={{0,12},{4,0},{8,4},{12,8},{1,13},{5,1},{9,5},{13,9},{2,14},{6,2},{... | collective-permute-start | bytes 1622024 | tf_op jit(solution)/shard_map/ppermute | solution.py:81
  80.9 1.1 reshape.237
  82.0 0.9 collective-permute-start.11
  82.9 2.1 %collective-permute-start.12 = (bf16[352,1024]{1,0:T(8,128)(2,1)}, bf16[352,1024]{1,0:T(8,128)(2,1)S(1)}, u32[]{:S(2)}, u32[]{:S(2)}) collective-permute-start(bf16[352,1024]{1,0:T(8,128)(2,1)} %reshape.237), channel_id=1, source_target_pairs={{0,2},{1,3},{2,0},{3,1},{4,6},{5,7},{6,4},{7,5},{8,10},{9,11},{10,... | collective-permute-start | bytes 2162696 | tf_op jit(solution)/shard_map/ppermute | solution.py:113
  85.0 1.2 collective-permute-start.13
  86.2 1.1 constant_dynamic-update-slice_fusion.6
  87.2 4.6 %collective-permute-done.8 = bf16[3,88,1024]{2,1,0:T(8,128)(2,1)} collective-permute-done((bf16[3,88,1024]{2,1,0:T(8,128)(2,1)}, bf16[3,88,1024]{2,1,0:T(8,128)(2,1)}, u32[]{:S(2)}, u32[]{:S(2)}) %collective-permute-start.8) | collective-permute-done | bytes 540704 | tf_op jit(solution)/shard_map/ppermute | solution.py:80
  91.8 1.9 constant_dynamic-update-slice_fusion.5
  93.7 1.9 constant_dynamic-update-slice_fusion.4
  95.6 1.1 constant_dynamic-update-slice_fusion.3
  96.7 2.9 %collective-permute-done.11 = bf16[352,1024]{1,0:T(8,128)(2,1)S(1)} collective-permute-done((bf16[352,1024]{1,0:T(8,128)(2,1)}, bf16[352,1024]{1,0:T(8,128)(2,1)S(1)}, u32[]{:S(2)}, u32[]{:S(2)}) %collective-permute-start.11) | collective-permute-done | bytes 720928 | tf_op jit(solution)/shard_map/ppermute | solution.py:113
  99.6 0.9 constant_dynamic-update-slice_fusion.12
  100.5 14.8 %collective-permute-done.12 = bf16[352,1024]{1,0:T(8,128)(2,1)S(1)} collective-permute-done((bf16[352,1024]{1,0:T(8,128)(2,1)}, bf16[352,1024]{1,0:T(8,128)(2,1)S(1)}, u32[]{:S(2)}, u32[]{:S(2)}) %collective-permute-start.12) | collective-permute-done | bytes 720928 | tf_op jit(solution)/shard_map/ppermute | solution.py:113
  115.4 0.9 constant_dynamic-update-slice_fusion.11
  116.3 0.3 collective-permute-done.13
  116.6 0.9 constant_dynamic-update-slice_fusion.10
  117.5 5.6 %fusion.14 = f32[1056,704]{1,0:T(8,128)} fusion(bf16[1056,1024]{1,0:T(8,128)(2,1)} %constant_dynamic-update-slice_fusion.10, bf16[3,704,1024]{2,1,0:T(8,128)(2,1)} %constant_dynamic-update-slice_fusion.3), kind=kOutput, calls=%fused_computation.26 | convolution fusion | flops 1522532352 | bytes 6578176 | tf_op jit(solution)/shard_map/dot_general | solution.py:20
  123.1 8.0 %convolution_convert_fusion = bf16[1056,1024]{1,0:T(8,128)(2,1)S(1)} fusion(f32[1056,704]{1,0:T(8,128)} %fusion.14, bf16[3,704,1024]{2,1,0:T(8,128)(2,1)} %constant_dynamic-update-slice_fusion.3, bf16[1056,1024]{1,0:T(8,128)(2,1)} %constant_dynamic-update-slice_fusion.10), kind=kOutput, calls=%fused_computation.4 | convolution fusion | flops 3053580288 | bytes 10452992 | tf_op jit(solution)/shard_map/dot_general | solution.py:27
  131.1 1.4 fusion.67
  132.5 3.3 %collective-permute-start.14 = (bf16[352,1024]{1,0:T(8,128)(2,1)}, bf16[352,1024]{1,0:T(8,128)(2,1)S(1)}, u32[]{:S(2)}, u32[]{:S(2)}) collective-permute-start(bf16[352,1024]{1,0:T(8,128)(2,1)} %get-tuple-element.8), channel_id=1, source_target_pairs={{0,3},{1,0},{2,1},{3,2},{4,7},{5,4},{6,5},{7,6},{8,11},{9,8},{10,9... | collective-permute-start | bytes 2162696 | tf_op jit(solution)/shard_map/ppermute | solution.py:120
  135.8 0.8 collective-permute-start.15
  136.6 3.1 %fusion.17 = f32[352,704]{1,0:T(8,128)} fusion(bf16[352,1024]{1,0:T(8,128)(2,1)S(1)} %copy-done.1, bf16[3,704,1024]{2,1,0:T(8,128)(2,1)} %constant_dynamic-update-slice_fusion.3), kind=kOutput, calls=%fused_computation.29 | convolution fusion | flops 507510784 | bytes 3153920 | tf_op jit(solution)/shard_map/dot_general | solution.py:23
  139.8 4.9 %convolution_convert_fusion.1 = bf16[352,1024]{1,0:T(8,128)(2,1)} fusion(bf16[3,704,1024]{2,1,0:T(8,128)(2,1)} %constant_dynamic-update-slice_fusion.3, f32[352,704]{1,0:T(8,128)} %fusion.17, bf16[352,1024]{1,0:T(8,128)(2,1)S(1)} %copy-done.1), kind=kOutput, calls=%fused_computation.23 | convolution fusion | flops 1017860096 | bytes 5406720 | tf_op jit(solution)/shard_map/dot_general | solution.py:27
  144.6 8.1 %collective-permute-done.14 = bf16[352,1024]{1,0:T(8,128)(2,1)S(1)} collective-permute-done((bf16[352,1024]{1,0:T(8,128)(2,1)}, bf16[352,1024]{1,0:T(8,128)(2,1)S(1)}, u32[]{:S(2)}, u32[]{:S(2)}) %collective-permute-start.14) | collective-permute-done | bytes 720928 | tf_op jit(solution)/shard_map/ppermute | solution.py:120
  152.7 1.8 collective-permute-done.15
  154.5 16.5 %collective-permute-done.16 = bf16[352,1024]{1,0:T(8,128)(2,1)S(1)} collective-permute-done((bf16[352,1024]{1,0:T(8,128)(2,1)}, bf16[352,1024]{1,0:T(8,128)(2,1)S(1)}, u32[]{:S(2)}, u32[]{:S(2)}) %collective-permute-start.16) | collective-permute-done | bytes 720928 | tf_op jit(solution)/shard_map/ppermute | solution.py:120
  171.0 1.7 add_convert_fusion
  172.7 1.1 reshape.238
  173.8 7.0 %all-to-all-start.2 = ((bf16[16,22,1024]{2,1,0:T(8,128)(2,1)}), bf16[16,22,1024]{2,1,0:T(8,128)(2,1)S(1)}, u32[]{:S(2)}, u32[]{:S(2)}) async-start(bf16[16,22,1024]{2,1,0:T(8,128)(2,1)} %reshape.238), calls=%async_computation.2 | async-start | bytes 1572864 | tf_op jit(solution)/shard_map/all_to_all | solution.py:124
  181.3 0.3 fusion.68
  181.7 2.3 %gather_fusion.2 = f32[176]{0:T(256)S(1)} fusion(f32[88,16]{0,1:T(8,128)S(1)} %fusion.47, s32[176]{0:T(256)S(1)} %reshape.257), kind=kCustom, calls=%fused_computation.2 | custom fusion | bytes 2816 | tf_op jit(solution)/shard_map/jit(take_along_axis)/gather | solution.py:95
  184.2 19.4 %all-to-all-done.2 = bf16[16,22,1024]{2,1,0:T(8,128)(2,1)S(1)} async-done(((bf16[16,22,1024]{2,1,0:T(8,128)(2,1)}), bf16[16,22,1024]{2,1,0:T(8,128)(2,1)S(1)}, u32[]{:S(2)}, u32[]{:S(2)}) %all-to-all-start.2) | async-done | bytes 720928 | tf_op jit(solution)/shard_map/all_to_all | solution.py:124
  203.8 0.4 fusion.18
  204.3 0.8 fusion.34
  (71 shorter events, 2.6 us)
Async XLA Ops:
  0.6 0.9 copy-start
  1.5 14.1 %collective-permute-start = (bf16[64,512]{1,0:T(8,128)(2,1)S(1)}, bf16[64,512]{1,0:T(8,128)(2,1)S(1)}, u32[]{:S(2)}, u32[]{:S(2)}) collective-permute-start(bf16[64,512]{1,0:T(8,128)(2,1)S(1)} %constant_dynamic-slice_fusion), channel_id=1, source_target_pairs={{0,1},{1,2},{2,3},{3,0},{4,5},{5,6},{6,7},{7,4},{8,9},{9,10},{10,1... | collective-permute-start | bytes 196616 | tf_op jit(solution)/shard_map/ppermute | solution.py:54
  3.6 12.1 %collective-permute-start.1 = (bf16[64,512]{1,0:T(8,128)(2,1)S(1)}, bf16[64,512]{1,0:T(8,128)(2,1)S(1)}, u32[]{:S(2)}, u32[]{:S(2)}) collective-permute-start(bf16[64,512]{1,0:T(8,128)(2,1)S(1)} %constant_dynamic-slice_fusion), channel_id=1, source_target_pairs={{0,2},{1,3},{2,0},{3,1},{4,6},{5,7},{6,4},{7,5},{8,10},{9,11},{10,... | collective-permute-start | bytes 196616 | tf_op jit(solution)/shard_map/ppermute | solution.py:54
  6.0 9.6 %collective-permute-start.2 = (bf16[64,512]{1,0:T(8,128)(2,1)S(1)}, bf16[64,512]{1,0:T(8,128)(2,1)S(1)}, u32[]{:S(2)}, u32[]{:S(2)}) collective-permute-start(bf16[64,512]{1,0:T(8,128)(2,1)S(1)} %constant_dynamic-slice_fusion), channel_id=1, source_target_pairs={{0,3},{1,0},{2,1},{3,2},{4,7},{5,4},{6,5},{7,6},{8,11},{9,8},{10,9... | collective-permute-start | bytes 196616 | tf_op jit(solution)/shard_map/ppermute | solution.py:54
  8.6 25.5 %copy-start.3 = (bf16[1,176,1024]{2,1,0:T(8,128)(2,1)S(1)}, bf16[1,176,1024]{2,1,0:T(8,128)(2,1)}, u32[]{:S(2)}) copy-start(bf16[1,176,1024]{2,1,0:T(8,128)(2,1)} %param.16) | copy-start | bytes 1081348
  9.4 26.7 %all-to-all-start = ((bf16[64,16,88]{2,0,1:T(8,128)(2,1)}), bf16[64,16,88]{2,0,1:T(8,128)(2,1)S(1)}, u32[]{:S(2)}, u32[]{:S(2)}) async-start(bf16[64,16,88]{2,0,1:T(8,128)(2,1)} %copy.26), calls=%async_computation | async-start | bytes 524288 | tf_op jit(solution)/shard_map/all_to_all | solution.py:59
  13.7 21.4 %copy-start.4 = (bf16[1,176,1024]{2,1,0:T(8,128)(2,1)S(1)}, bf16[1,176,1024]{2,1,0:T(8,128)(2,1)}, u32[]{:S(2)}) copy-start(bf16[1,176,1024]{2,1,0:T(8,128)(2,1)} %param.17) | copy-start | bytes 1081348
  15.7 10.8 %collective-permute-start.3 = (bf16[4,64,512]{2,1,0:T(8,128)(2,1)S(1)}, bf16[4,64,512]{2,1,0:T(8,128)(2,1)S(1)}, u32[]{:S(2)}, u32[]{:S(2)}) collective-permute-start(bf16[4,64,512]{2,1,0:T(8,128)(2,1)S(1)} %get-tuple-element.18), channel_id=1, source_target_pairs={{0,4},{4,8},{8,12},{12,0},{1,5},{5,9},{9,13},{13,1},{2,6},{6,10},{... | collective-permute-start | bytes 786440 | tf_op jit(solution)/shard_map/ppermute | solution.py:56
  17.2 15.0 %collective-permute-start.4 = (bf16[4,64,512]{2,1,0:T(8,128)(2,1)S(1)}, bf16[4,64,512]{2,1,0:T(8,128)(2,1)S(1)}, u32[]{:S(2)}, u32[]{:S(2)}) collective-permute-start(bf16[4,64,512]{2,1,0:T(8,128)(2,1)S(1)} %get-tuple-element.18), channel_id=1, source_target_pairs={{0,8},{4,12},{8,0},{12,4},{1,9},{5,13},{9,1},{13,5},{2,10},{6,14},... | collective-permute-start | bytes 786440 | tf_op jit(solution)/shard_map/ppermute | solution.py:56
  19.6 12.6 %collective-permute-start.5 = (bf16[4,64,512]{2,1,0:T(8,128)(2,1)S(1)}, bf16[4,64,512]{2,1,0:T(8,128)(2,1)S(1)}, u32[]{:S(2)}, u32[]{:S(2)}) collective-permute-start(bf16[4,64,512]{2,1,0:T(8,128)(2,1)S(1)} %get-tuple-element.18), channel_id=1, source_target_pairs={{0,12},{4,0},{8,4},{12,8},{1,13},{5,1},{9,5},{13,9},{2,14},{6,2},{... | collective-permute-start | bytes 786440 | tf_op jit(solution)/shard_map/ppermute | solution.py:56
  32.3 5.4 %collective-permute-start.6 = (bf16[4,4,64,512]{3,2,1,0:T(8,128)(2,1)S(1)}, bf16[4,4,64,512]{3,2,1,0:T(8,128)(2,1)S(1)}, u32[]{:S(2)}, u32[]{:S(2)}) collective-permute-start(bf16[4,4,64,512]{3,2,1,0:T(8,128)(2,1)S(1)} %pad_maximum_fusion), channel_id=1, source_target_pairs={{0,16},{16,0},{32,48},{48,32},{64,80},{80,64},{96,112},{112,96},{1... | collective-permute-start | bytes 3145736 | tf_op jit(solution)/shard_map/ppermute | solution.py:58
  36.1 2.1 %copy-start.6 = (bf16[88,1024]{1,0:T(8,128)(2,1)S(1)}, bf16[88,1024]{1,0:T(8,128)(2,1)}, u32[]{:S(2)}) copy-start(bf16[88,1024]{1,0:T(8,128)(2,1)} %param.10) | copy-start | bytes 540676
  36.8 1.6 copy-start.9
  38.8 10.1 %copy-start.5 = (bf16[1,176,1024]{2,1,0:T(8,128)(2,1)S(1)}, bf16[1,176,1024]{2,1,0:T(8,128)(2,1)}, u32[]{:S(2)}) copy-start(bf16[1,176,1024]{2,1,0:T(8,128)(2,1)} %param.18) | copy-start | bytes 1081348
  40.3 40.7 %all-to-all-start.1 = ((bf16[16,22,1024]{2,1,0:T(8,128)(2,1)}), bf16[16,22,1024]{2,1,0:T(8,128)(2,1)S(1)}, u32[]{:S(2)}, u32[]{:S(2)}) async-start(bf16[16,22,1024]{2,1,0:T(8,128)(2,1)} %reshape.236), calls=%async_computation.1 | async-start | bytes 1572864 | tf_op jit(solution)/shard_map/all_to_all | solution.py:108
  49.8 26.7 %collective-permute-start.7 = (bf16[3,176,1024]{2,1,0:T(8,128)(2,1)}, bf16[3,176,1024]{2,1,0:T(8,128)(2,1)S(1)}, u32[]{:S(2)}, u32[]{:S(2)}) collective-permute-start(bf16[3,176,1024]{2,1,0:T(8,128)(2,1)} %get-tuple-element.11), channel_id=1, source_target_pairs={{0,4},{4,8},{8,12},{12,0},{1,5},{5,9},{9,13},{13,1},{2,6},{6,10},{... | collective-permute-start | bytes 3244040 | tf_op jit(solution)/shard_map/ppermute | solution.py:75
  50.4 27.1 %collective-permute-start.9 = (bf16[3,176,1024]{2,1,0:T(8,128)(2,1)}, bf16[3,176,1024]{2,1,0:T(8,128)(2,1)S(1)}, u32[]{:S(2)}, u32[]{:S(2)}) collective-permute-start(bf16[3,176,1024]{2,1,0:T(8,128)(2,1)} %get-tuple-element.11), channel_id=1, source_target_pairs={{0,12},{4,0},{8,4},{12,8},{1,13},{5,1},{9,5},{13,9},{2,14},{6,2},{... | collective-permute-start | bytes 3244040 | tf_op jit(solution)/shard_map/ppermute | solution.py:76
  77.4 14.4 %collective-permute-start.8 = (bf16[3,88,1024]{2,1,0:T(8,128)(2,1)}, bf16[3,88,1024]{2,1,0:T(8,128)(2,1)}, u32[]{:S(2)}, u32[]{:S(2)}) collective-permute-start(bf16[3,88,1024]{2,1,0:T(8,128)(2,1)} %slice.55), channel_id=1, source_target_pairs={{0,4},{4,8},{8,12},{12,0},{1,5},{5,9},{9,13},{13,1},{2,6},{6,10},{... | collective-permute-start | bytes 1622024 | tf_op jit(solution)/shard_map/ppermute | solution.py:80
  78.3 15.5 %collective-permute-start.10 = (bf16[3,88,1024]{2,1,0:T(8,128)(2,1)}, bf16[3,88,1024]{2,1,0:T(8,128)(2,1)}, u32[]{:S(2)}, u32[]{:S(2)}) collective-permute-start(bf16[3,88,1024]{2,1,0:T(8,128)(2,1)} %slice.56), channel_id=1, source_target_pairs={{0,12},{4,0},{8,4},{12,8},{1,13},{5,1},{9,5},{13,9},{2,14},{6,2},{... | collective-permute-start | bytes 1622024 | tf_op jit(solution)/shard_map/ppermute | solution.py:81
  82.0 17.6 %collective-permute-start.11 = (bf16[352,1024]{1,0:T(8,128)(2,1)}, bf16[352,1024]{1,0:T(8,128)(2,1)S(1)}, u32[]{:S(2)}, u32[]{:S(2)}) collective-permute-start(bf16[352,1024]{1,0:T(8,128)(2,1)} %reshape.237), channel_id=1, source_target_pairs={{0,1},{1,2},{2,3},{3,0},{4,5},{5,6},{6,7},{7,4},{8,9},{9,10},{10,1... | collective-permute-start | bytes 2162696 | tf_op jit(solution)/shard_map/ppermute | solution.py:113
  82.9 32.5 %collective-permute-start.12 = (bf16[352,1024]{1,0:T(8,128)(2,1)}, bf16[352,1024]{1,0:T(8,128)(2,1)S(1)}, u32[]{:S(2)}, u32[]{:S(2)}) collective-permute-start(bf16[352,1024]{1,0:T(8,128)(2,1)} %reshape.237), channel_id=1, source_target_pairs={{0,2},{1,3},{2,0},{3,1},{4,6},{5,7},{6,4},{7,5},{8,10},{9,11},{10,... | collective-permute-start | bytes 2162696 | tf_op jit(solution)/shard_map/ppermute | solution.py:113
  85.0 31.6 %collective-permute-start.13 = (bf16[352,1024]{1,0:T(8,128)(2,1)}, bf16[352,1024]{1,0:T(8,128)(2,1)S(1)}, u32[]{:S(2)}, u32[]{:S(2)}) collective-permute-start(bf16[352,1024]{1,0:T(8,128)(2,1)} %reshape.237), channel_id=1, source_target_pairs={{0,3},{1,0},{2,1},{3,2},{4,7},{5,4},{6,5},{7,6},{8,11},{9,8},{10,9... | collective-permute-start | bytes 2162696 | tf_op jit(solution)/shard_map/ppermute | solution.py:113
  131.1 5.5 %copy-start.1 = (bf16[352,1024]{1,0:T(8,128)(2,1)S(1)}, bf16[352,1024]{1,0:T(8,128)(2,1)}, u32[]{:S(2)}) copy-start(bf16[352,1024]{1,0:T(8,128)(2,1)} %reshape.237) | copy-start | bytes 2162692
  132.5 20.2 %collective-permute-start.14 = (bf16[352,1024]{1,0:T(8,128)(2,1)}, bf16[352,1024]{1,0:T(8,128)(2,1)S(1)}, u32[]{:S(2)}, u32[]{:S(2)}) collective-permute-start(bf16[352,1024]{1,0:T(8,128)(2,1)} %get-tuple-element.8), channel_id=1, source_target_pairs={{0,3},{1,0},{2,1},{3,2},{4,7},{5,4},{6,5},{7,6},{8,11},{9,8},{10,9... | collective-permute-start | bytes 2162696 | tf_op jit(solution)/shard_map/ppermute | solution.py:120
  135.8 18.7 %collective-permute-start.15 = (bf16[352,1024]{1,0:T(8,128)(2,1)}, bf16[352,1024]{1,0:T(8,128)(2,1)S(1)}, u32[]{:S(2)}, u32[]{:S(2)}) collective-permute-start(bf16[352,1024]{1,0:T(8,128)(2,1)} %get-tuple-element.10), channel_id=1, source_target_pairs={{0,2},{1,3},{2,0},{3,1},{4,6},{5,7},{6,4},{7,5},{8,10},{9,11},{10,... | collective-permute-start | bytes 2162696 | tf_op jit(solution)/shard_map/ppermute | solution.py:120
  136.6 34.4 %collective-permute-start.16 = (bf16[352,1024]{1,0:T(8,128)(2,1)}, bf16[352,1024]{1,0:T(8,128)(2,1)S(1)}, u32[]{:S(2)}, u32[]{:S(2)}) collective-permute-start(bf16[352,1024]{1,0:T(8,128)(2,1)} %get-tuple-element.9), channel_id=1, source_target_pairs={{0,1},{1,2},{2,3},{3,0},{4,5},{5,6},{6,7},{7,4},{8,9},{9,10},{10,1... | collective-permute-start | bytes 2162696 | tf_op jit(solution)/shard_map/ppermute | solution.py:120
  172.7 8.2 %copy-start.8 = (s32[88,2]{0,1:T(2,128)S(1)}, s32[88,2]{0,1:T(2,128)}, u32[]{:S(2)}) copy-start(s32[88,2]{0,1:T(2,128)} %param.15) | copy-start | bytes 2116
  172.7 8.6 %copy-start.7 = (f32[1024,16]{0,1:T(8,128)S(1)}, f32[1024,16]{0,1:T(8,128)}, u32[]{:S(2)}) copy-start(f32[1024,16]{0,1:T(8,128)} %param.14) | copy-start | bytes 196612
  173.8 29.8 %all-to-all-start.2 = ((bf16[16,22,1024]{2,1,0:T(8,128)(2,1)}), bf16[16,22,1024]{2,1,0:T(8,128)(2,1)S(1)}, u32[]{:S(2)}, u32[]{:S(2)}) async-start(bf16[16,22,1024]{2,1,0:T(8,128)(2,1)} %reshape.238), calls=%async_computation.2 | async-start | bytes 1572864 | tf_op jit(solution)/shard_map/all_to_all | solution.py:124
  183.9 20.4 %copy-start.10 = (f32[1024]{0:T(1024)S(1)}, f32[1024]{0:T(1024)}, u32[]{:S(2)}) copy-start(f32[1024]{0:T(1024)} %param.19) | copy-start | bytes 12292
  204.3 0.8 copy-start.2

commit v13 on v10

--- a/solution.py
+++ b/solution.py
@@ -97,7 +97,20 @@
     gate_rows, up_rows, down_rows = weights[0], weights[1], weights[2]
     slot_total = n_expert * capacity
     rows_in = received.reshape(slot_total, width)
-    peer_rows = [lax.ppermute(rows_in, "tx", shift_pairs(n_tx, s)) for s in range(1, n_tx)]
+    if n_tx == 4:
+        from_below = lax.ppermute(rows_in, "tx", shift_pairs(n_tx, 1))
+        from_above = lax.ppermute(rows_in, "tx", shift_pairs(n_tx, -1))
+        cut = slot_total // 2
+        far = jnp.concatenate(
+            [
+                lax.ppermute(from_below[:cut], "tx", shift_pairs(n_tx, 1)),
+                lax.ppermute(from_above[cut:], "tx", shift_pairs(n_tx, -1)),
+            ],
+            axis=0,
+        )
+        peer_rows = [from_below, far, from_above]
+    else:
+        peer_rows = [lax.ppermute(rows_in, "tx", shift_pairs(n_tx, s)) for s in range(1, n_tx)]
     own = expert_block(rows_in, gate_rows, up_rows, down_rows).astype(jnp.bfloat16)
     peer_rows = jnp.concatenate(peer_rows, axis=0)
     partial = expert_block(peer_rows, gate_rows, up_rows, down_rows).astype(jnp.bfloat16)

time: 188 us -> 188 us (level)
  waiting for transfers between devices: 100 us -> 98 us
    ppermute x3, waiting for transfers between devices: 22.4 us -> 6.37 us  [per_device(): lax.ppermute(stacked, 'ty', shift_pairs(n_ty, s))]
    ppermute x3 -> x4, waiting for transfers between devices: 3.67 us -> 15.2 us  [the longest x1 15.2 us: per_device(): from_below = lax.ppermute(rows_in, 'tx', shift_pairs(n_tx, 1))]
    ppermute x3, waiting for transfers between devices: 24 us -> 26 us  [per_device(): back = lax.ppermute(partial[s - 1], 'tx', shift_pairs(n_tx, -s))]
    unnamed x29 -> x30, local copies, waits for them, and re-layouts: 3.29 us -> 5.07 us
    ppermute x3 -> x4, starting transfers between devices: 5.01 us -> 5.75 us  [the longest x1 2.73 us: per_device(): lax.ppermute(from_above[cut:], 'tx', shift_pairs(n_tx, -1))]
  transfers between devices with their start and end apart: 19 -> 20, of which waited for: 11 -> 11; matrix products, arithmetic and copies ran while one was open for 10% -> 10% of each run, Pallas kernels for 0% -> 0%
where the time goes in v13:
time: 188 us
  waiting for transfers between devices  98 us (52%)
  starting transfers between devices  45 us (24%)
  matrix products  21.4 us (11%)
  local copies, waits for them, and re-layouts  16 us (9%)
  other arithmetic  6.35 us (3%)
    ppermute x3, waiting for transfers between devices, per_device(): back = lax.ppermute(partial[s - 1], 'tx', shift_pairs(n_tx, -s))  26 us
    all_to_all x1, waiting for transfers between devices, per_device(): lax.all_to_all(expert_out, 'expert', split_axis=0, concat_axis=0, tiled=T...  19.4 us
    all_to_all x1, waiting for transfers between devices, per_device(): lax.all_to_all(send_slots, 'expert', split_axis=0, concat_axis=0, tiled=T...  18.9 us
    ppermute x1, waiting for transfers between devices, per_device(): from_below = lax.ppermute(rows_in, 'tx', shift_pairs(n_tx, 1))  15.2 us
    dot_general x2, matrix products, expert_block(): return jnp.dot(hid, down_rows, preferred_element_type=jnp.float32)  12.9 us
    ppermute x3, waiting for transfers between devices, per_device(): lax.ppermute(near, 'ty', shift_pairs(n_ty, s))  11.7 us
    all_to_all x1, starting transfers between devices, per_device(): lax.all_to_all(send_slots, 'expert', split_axis=0, concat_axis=0, tiled=T...  8.85 us
    all_to_all x1, starting transfers between devices, per_device(): lax.all_to_all(expert_out, 'expert', split_axis=0, concat_axis=0, tiled=T...  7.04 us
  transfers between devices with their start and end apart: 20, of which 11 were waited for; matrix products, arithmetic and copies ran while one was open for 10% of the time, Pallas kernels for 0%

profile of v13, /device:TPU:1, one launch (start us, length us, event | category | flops | bytes accessed | tf_op | source)
XLA Modules:
  0.0 187.9 jit_solution(7481795257046638348)
XLA Ops:
  0.7 0.9 copy-done
  1.5 2.0 %collective-permute-start = (bf16[64,512]{1,0:T(8,128)(2,1)S(1)}, bf16[64,512]{1,0:T(8,128)(2,1)S(1)}, u32[]{:S(2)}, u32[]{:S(2)}) collective-permute-start(bf16[64,512]{1,0:T(8,128)(2,1)S(1)} %constant_dynamic-slice_fusion), channel_id=1, source_target_pairs={{0,1},{1,2},{2,3},{3,0},{4,5},{5,6},{6,7},{7,4},{8,9},{9,10},{10,1... | collective-permute-start | bytes 196616 | tf_op jit(solution)/shard_map/ppermute | solution.py:54
  3.6 2.5 %collective-permute-start.1 = (bf16[64,512]{1,0:T(8,128)(2,1)S(1)}, bf16[64,512]{1,0:T(8,128)(2,1)S(1)}, u32[]{:S(2)}, u32[]{:S(2)}) collective-permute-start(bf16[64,512]{1,0:T(8,128)(2,1)S(1)} %constant_dynamic-slice_fusion), channel_id=1, source_target_pairs={{0,2},{1,3},{2,0},{3,1},{4,6},{5,7},{6,4},{7,5},{8,10},{9,11},{10,... | collective-permute-start | bytes 196616 | tf_op jit(solution)/shard_map/ppermute | solution.py:54
  6.0 1.2 collective-permute-start.2
  7.2 1.4 all_to_all.18
  8.6 0.8 copy.26
  9.4 4.3 %all-to-all-start = ((bf16[64,16,88]{2,0,1:T(8,128)(2,1)}), bf16[64,16,88]{2,0,1:T(8,128)(2,1)S(1)}, u32[]{:S(2)}, u32[]{:S(2)}) async-start(bf16[64,16,88]{2,0,1:T(8,128)(2,1)} %copy.26), calls=%async_computation | async-start | bytes 524288 | tf_op jit(solution)/shard_map/all_to_all | solution.py:59
  13.7 0.8 copy.31
  14.7 0.6 reduce-window.6
  15.3 0.2 slice_reduce_fusion
  15.6 1.4 collective-permute-start.3
  17.0 2.4 %collective-permute-start.4 = (bf16[4,64,512]{2,1,0:T(8,128)(2,1)S(1)}, bf16[4,64,512]{2,1,0:T(8,128)(2,1)S(1)}, u32[]{:S(2)}, u32[]{:S(2)}) collective-permute-start(bf16[4,64,512]{2,1,0:T(8,128)(2,1)S(1)} %get-tuple-element.12), channel_id=1, source_target_pairs={{0,8},{4,12},{8,0},{12,4},{1,9},{5,13},{9,1},{13,5},{2,10},{6,14},... | collective-permute-start | bytes 786440 | tf_op jit(solution)/shard_map/ppermute | solution.py:56
  19.4 1.2 collective-permute-start.5
  20.7 6.0 %collective-permute-done.3 = bf16[4,64,512]{2,1,0:T(8,128)(2,1)S(1)} collective-permute-done((bf16[4,64,512]{2,1,0:T(8,128)(2,1)S(1)}, bf16[4,64,512]{2,1,0:T(8,128)(2,1)S(1)}, u32[]{:S(2)}, u32[]{:S(2)}) %collective-permute-start.3) | collective-permute-done | bytes 262176 | tf_op jit(solution)/shard_map/ppermute | solution.py:56
  26.6 5.7 %collective-permute-done.4 = bf16[4,64,512]{2,1,0:T(8,128)(2,1)S(1)} collective-permute-done((bf16[4,64,512]{2,1,0:T(8,128)(2,1)S(1)}, bf16[4,64,512]{2,1,0:T(8,128)(2,1)S(1)}, u32[]{:S(2)}, u32[]{:S(2)}) %collective-permute-start.4) | collective-permute-done | bytes 262176 | tf_op jit(solution)/shard_map/ppermute | solution.py:56
  32.5 1.6 collective-permute-start.6
  34.2 0.6 gather_fusion
  35.0 0.6 gather_fusion.1
  35.6 0.4 convolution_bitcast_fusion.1
  36.0 0.4 collective-permute-done.6
  36.4 0.4 convolution_bitcast_fusion
  36.8 0.2 fusion.35
  37.1 0.2 broadcast_in_dim.40
  37.3 0.1 reshape.235
  37.4 0.3 convolution_convert_fusion.2
  37.8 1.1 reshape.236
  38.9 8.9 %all-to-all-start.1 = ((bf16[16,22,1024]{2,1,0:T(8,128)(2,1)}), bf16[16,22,1024]{2,1,0:T(8,128)(2,1)S(1)}, u32[]{:S(2)}, u32[]{:S(2)}) async-start(bf16[16,22,1024]{2,1,0:T(8,128)(2,1)} %reshape.236), calls=%async_computation.1 | async-start | bytes 1572864 | tf_op jit(solution)/shard_map/all_to_all | solution.py:95
  47.9 0.5 collective-permute-start.7
  48.4 2.1 %collective-permute-start.8 = (bf16[3,176,1024]{2,1,0:T(8,128)(2,1)S(1)}, bf16[3,176,1024]{2,1,0:T(8,128)(2,1)}, u32[]{:S(2)}, u32[]{:S(2)}) collective-permute-start(bf16[3,176,1024]{2,1,0:T(8,128)(2,1)S(1)} %constant_dynamic-update-slice_fusion), channel_id=1, source_target_pairs={{0,8},{4,12},{8,0},{12,4},{1,9},{5,13},{9,1},{13,5},{2,10},{6,14},... | collective-permute-start | bytes 3244040 | tf_op jit(solution)/shard_map/ppermute | solution.py:75
  50.5 1.1 collective-permute-start.9
  51.6 18.9 %all-to-all-done.1 = bf16[16,22,1024]{2,1,0:T(8,128)(2,1)S(1)} async-done(((bf16[16,22,1024]{2,1,0:T(8,128)(2,1)}), bf16[16,22,1024]{2,1,0:T(8,128)(2,1)S(1)}, u32[]{:S(2)}, u32[]{:S(2)}) %all-to-all-start.1) | async-done | bytes 720928 | tf_op jit(solution)/shard_map/all_to_all | solution.py:95
  70.5 0.2 reshape.237
  70.7 0.9 collective-permute-start.10
  71.6 1.9 collective-permute-start.12
  73.4 15.2 %collective-permute-done.10 = bf16[352,1024]{1,0:T(8,128)(2,1)S(1)} collective-permute-done((bf16[352,1024]{1,0:T(8,128)(2,1)S(1)}, bf16[352,1024]{1,0:T(8,128)(2,1)S(1)}, u32[]{:S(2)}, u32[]{:S(2)}) %collective-permute-start.10) | collective-permute-done | bytes 720928 | tf_op jit(solution)/shard_map/ppermute | solution.py:101
  88.7 0.3 collective-permute-start.11
  89.0 2.7 %collective-permute-start.13 = (bf16[176,1024]{1,0:T(8,128)(2,1)S(1)}, bf16[176,1024]{1,0:T(8,128)(2,1)S(1)}, u32[]{:S(2)}, u32[]{:S(2)}) collective-permute-start(bf16[176,1024]{1,0:T(8,128)(2,1)S(1)} %slice.59), channel_id=1, source_target_pairs={{0,3},{1,0},{2,1},{3,2},{4,7},{5,4},{6,5},{7,6},{8,11},{9,8},{10,9... | collective-permute-start | bytes 1081352 | tf_op jit(solution)/shard_map/ppermute | solution.py:107
  91.7 5.9 %collective-permute-done.8 = bf16[3,176,1024]{2,1,0:T(8,128)(2,1)} collective-permute-done((bf16[3,176,1024]{2,1,0:T(8,128)(2,1)S(1)}, bf16[3,176,1024]{2,1,0:T(8,128)(2,1)}, u32[]{:S(2)}, u32[]{:S(2)}) %collective-permute-start.8) | collective-permute-done | bytes 1081376 | tf_op jit(solution)/shard_map/ppermute | solution.py:75
  97.7 0.5 collective-permute-done.9
  98.1 2.2 %pad_maximum_fusion = bf16[3,704,1024]{2,1,0:T(8,128)(2,1)S(1)} fusion(bf16[3,176,1024]{2,1,0:T(8,128)(2,1)} %collective-permute-done.9, bf16[3,176,1024]{2,1,0:T(8,128)(2,1)} %collective-permute-done.8, bf16[3,176,1024]{2,1,0:T(8,128)(2,1)} %collective-permute-done.7, bf16[3,176,1024]{2,1,0:T(8,128)(2,1)S(1)} %constant_dynamic-update-slice_fusion), kind=kLoop, calls=%fused_computation.4 | loop fusion | flops 17301504 | bytes 8650752 | tf_op jit(solution)/shard_map/concatenate | solution.py:96
  100.5 1.8 copy-done.1
  102.3 1.4 copy-done.6
  103.7 3.6 %fusion.14 = f32[1056,704]{1,0:T(8,128)} fusion(bf16[1056,1024]{1,0:T(8,128)(2,1)S(1)} %constant_dynamic-update-slice_fusion.3, bf16[3,704,1024]{2,1,0:T(8,128)(2,1)S(1)} %pad_maximum_fusion), kind=kOutput, calls=%fused_computation.27 | convolution fusion | flops 1522532352 | bytes 6578176 | tf_op jit(solution)/shard_map/dot_general | solution.py:20
  107.3 8.0 %convolution_convert_fusion = bf16[1056,1024]{1,0:T(8,128)(2,1)S(1)} fusion(f32[1056,704]{1,0:T(8,128)} %fusion.14, bf16[3,704,1024]{2,1,0:T(8,128)(2,1)} %copy-done.1, bf16[1056,1024]{1,0:T(8,128)(2,1)} %copy-done.6), kind=kOutput, calls=%fused_computation.5 | convolution fusion | flops 3053580288 | bytes 10452992 | tf_op jit(solution)/shard_map/dot_general | solution.py:27
  115.4 1.4 fusion.67
  116.8 1.8 collective-permute-start.14
  118.6 0.8 collective-permute-start.15
  119.4 0.4 collective-permute-start.16
  119.8 3.1 %fusion.17 = f32[352,704]{1,0:T(8,128)} fusion(bf16[352,1024]{1,0:T(8,128)(2,1)S(1)} %reshape.237, bf16[3,704,1024]{2,1,0:T(8,128)(2,1)} %copy-done.1), kind=kOutput, calls=%fused_computation.30 | convolution fusion | flops 507510784 | bytes 3153920 | tf_op jit(solution)/shard_map/dot_general | solution.py:23
  122.9 4.9 %convolution_convert_fusion.1 = bf16[352,1024]{1,0:T(8,128)(2,1)} fusion(bf16[3,704,1024]{2,1,0:T(8,128)(2,1)} %copy-done.1, f32[352,704]{1,0:T(8,128)} %fusion.17, bf16[352,1024]{1,0:T(8,128)(2,1)S(1)} %reshape.237), kind=kOutput, calls=%fused_computation.24 | convolution fusion | flops 1017860096 | bytes 5406720 | tf_op jit(solution)/shard_map/dot_general | solution.py:27
  127.8 5.6 %collective-permute-done.14 = bf16[352,1024]{1,0:T(8,128)(2,1)S(1)} collective-permute-done((bf16[352,1024]{1,0:T(8,128)(2,1)}, bf16[352,1024]{1,0:T(8,128)(2,1)S(1)}, u32[]{:S(2)}, u32[]{:S(2)}) %collective-permute-start.14) | collective-permute-done | bytes 720928 | tf_op jit(solution)/shard_map/ppermute | solution.py:120
  133.5 3.1 %collective-permute-done.15 = bf16[352,1024]{1,0:T(8,128)(2,1)S(1)} collective-permute-done((bf16[352,1024]{1,0:T(8,128)(2,1)}, bf16[352,1024]{1,0:T(8,128)(2,1)S(1)}, u32[]{:S(2)}, u32[]{:S(2)}) %collective-permute-start.15) | collective-permute-done | bytes 720928 | tf_op jit(solution)/shard_map/ppermute | solution.py:120
  136.6 17.3 %collective-permute-done.16 = bf16[352,1024]{1,0:T(8,128)(2,1)S(1)} collective-permute-done((bf16[352,1024]{1,0:T(8,128)(2,1)}, bf16[352,1024]{1,0:T(8,128)(2,1)S(1)}, u32[]{:S(2)}, u32[]{:S(2)}) %collective-permute-start.16) | collective-permute-done | bytes 720928 | tf_op jit(solution)/shard_map/ppermute | solution.py:120
  153.9 1.7 add_convert_fusion
  155.5 1.1 reshape.238
  156.6 7.0 %all-to-all-start.2 = ((bf16[16,22,1024]{2,1,0:T(8,128)(2,1)}), bf16[16,22,1024]{2,1,0:T(8,128)(2,1)S(1)}, u32[]{:S(2)}, u32[]{:S(2)}) async-start(bf16[16,22,1024]{2,1,0:T(8,128)(2,1)} %reshape.238), calls=%async_computation.2 | async-start | bytes 1572864 | tf_op jit(solution)/shard_map/all_to_all | solution.py:124
  163.8 0.1 reshape.257
  164.2 0.3 fusion.68
  164.5 2.3 %gather_fusion.2 = f32[176]{0:T(256)S(1)} fusion(f32[88,16]{0,1:T(8,128)S(1)} %fusion.47, s32[176]{0:T(256)S(1)} %reshape.257), kind=kCustom, calls=%fused_computation.2 | custom fusion | bytes 2816 | tf_op jit(solution)/shard_map/jit(take_along_axis)/gather | solution.py:82
  167.0 19.4 %all-to-all-done.2 = bf16[16,22,1024]{2,1,0:T(8,128)(2,1)S(1)} async-done(((bf16[16,22,1024]{2,1,0:T(8,128)(2,1)}), bf16[16,22,1024]{2,1,0:T(8,128)(2,1)S(1)}, u32[]{:S(2)}, u32[]{:S(2)}) %all-to-all-start.2) | async-done | bytes 720928 | tf_op jit(solution)/shard_map/all_to_all | solution.py:124
  186.4 0.2 reshape.270
  186.6 0.4 fusion.18
  187.0 0.2 fusion.32
  187.1 0.8 fusion.34
  (71 shorter events, 1.7 us)
Async XLA Ops:
  0.6 0.9 copy-start
  1.5 13.9 %collective-permute-start = (bf16[64,512]{1,0:T(8,128)(2,1)S(1)}, bf16[64,512]{1,0:T(8,128)(2,1)S(1)}, u32[]{:S(2)}, u32[]{:S(2)}) collective-permute-start(bf16[64,512]{1,0:T(8,128)(2,1)S(1)} %constant_dynamic-slice_fusion), channel_id=1, source_target_pairs={{0,1},{1,2},{2,3},{3,0},{4,5},{5,6},{6,7},{7,4},{8,9},{9,10},{10,1... | collective-permute-start | bytes 196616 | tf_op jit(solution)/shard_map/ppermute | solution.py:54
  3.6 11.9 %collective-permute-start.1 = (bf16[64,512]{1,0:T(8,128)(2,1)S(1)}, bf16[64,512]{1,0:T(8,128)(2,1)S(1)}, u32[]{:S(2)}, u32[]{:S(2)}) collective-permute-start(bf16[64,512]{1,0:T(8,128)(2,1)S(1)} %constant_dynamic-slice_fusion), channel_id=1, source_target_pairs={{0,2},{1,3},{2,0},{3,1},{4,6},{5,7},{6,4},{7,5},{8,10},{9,11},{10,... | collective-permute-start | bytes 196616 | tf_op jit(solution)/shard_map/ppermute | solution.py:54
  6.0 9.5 %collective-permute-start.2 = (bf16[64,512]{1,0:T(8,128)(2,1)S(1)}, bf16[64,512]{1,0:T(8,128)(2,1)S(1)}, u32[]{:S(2)}, u32[]{:S(2)}) collective-permute-start(bf16[64,512]{1,0:T(8,128)(2,1)S(1)} %constant_dynamic-slice_fusion), channel_id=1, source_target_pairs={{0,3},{1,0},{2,1},{3,2},{4,7},{5,4},{6,5},{7,6},{8,11},{9,8},{10,9... | collective-permute-start | bytes 196616 | tf_op jit(solution)/shard_map/ppermute | solution.py:54
  9.4 24.9 %all-to-all-start = ((bf16[64,16,88]{2,0,1:T(8,128)(2,1)}), bf16[64,16,88]{2,0,1:T(8,128)(2,1)S(1)}, u32[]{:S(2)}, u32[]{:S(2)}) async-start(bf16[64,16,88]{2,0,1:T(8,128)(2,1)} %copy.26), calls=%async_computation | async-start | bytes 524288 | tf_op jit(solution)/shard_map/all_to_all | solution.py:59
  15.6 11.0 %collective-permute-start.3 = (bf16[4,64,512]{2,1,0:T(8,128)(2,1)S(1)}, bf16[4,64,512]{2,1,0:T(8,128)(2,1)S(1)}, u32[]{:S(2)}, u32[]{:S(2)}) collective-permute-start(bf16[4,64,512]{2,1,0:T(8,128)(2,1)S(1)} %get-tuple-element.12), channel_id=1, source_target_pairs={{0,4},{4,8},{8,12},{12,0},{1,5},{5,9},{9,13},{13,1},{2,6},{6,10},{... | collective-permute-start | bytes 786440 | tf_op jit(solution)/shard_map/ppermute | solution.py:56
  17.0 15.3 %collective-permute-start.4 = (bf16[4,64,512]{2,1,0:T(8,128)(2,1)S(1)}, bf16[4,64,512]{2,1,0:T(8,128)(2,1)S(1)}, u32[]{:S(2)}, u32[]{:S(2)}) collective-permute-start(bf16[4,64,512]{2,1,0:T(8,128)(2,1)S(1)} %get-tuple-element.12), channel_id=1, source_target_pairs={{0,8},{4,12},{8,0},{12,4},{1,9},{5,13},{9,1},{13,5},{2,10},{6,14},... | collective-permute-start | bytes 786440 | tf_op jit(solution)/shard_map/ppermute | solution.py:56
  19.4 12.9 %collective-permute-start.5 = (bf16[4,64,512]{2,1,0:T(8,128)(2,1)S(1)}, bf16[4,64,512]{2,1,0:T(8,128)(2,1)S(1)}, u32[]{:S(2)}, u32[]{:S(2)}) collective-permute-start(bf16[4,64,512]{2,1,0:T(8,128)(2,1)S(1)} %get-tuple-element.12), channel_id=1, source_target_pairs={{0,12},{4,0},{8,4},{12,8},{1,13},{5,1},{9,5},{13,9},{2,14},{6,2},{... | collective-permute-start | bytes 786440 | tf_op jit(solution)/shard_map/ppermute | solution.py:56
  32.5 3.9 %collective-permute-start.6 = (bf16[4,4,64,512]{3,2,1,0:T(8,128)(2,1)S(1)}, bf16[4,4,64,512]{3,2,1,0:T(8,128)(2,1)S(1)}, u32[]{:S(2)}, u32[]{:S(2)}) collective-permute-start(bf16[4,4,64,512]{3,2,1,0:T(8,128)(2,1)S(1)} %pad_maximum_fusion.1), channel_id=1, source_target_pairs={{0,16},{16,0},{32,48},{48,32},{64,80},{80,64},{96,112},{112,96},{1... | collective-permute-start | bytes 3145736 | tf_op jit(solution)/shard_map/ppermute | solution.py:58
  34.2 2.5 %copy-start.7 = (bf16[88,1024]{1,0:T(8,128)(2,1)S(1)}, bf16[88,1024]{1,0:T(8,128)(2,1)}, u32[]{:S(2)}) copy-start(bf16[88,1024]{1,0:T(8,128)(2,1)} %param.10) | copy-start | bytes 540676
  35.0 2.0 %copy-start.10 = (f32[1024]{0:T(1024)S(1)}, f32[1024]{0:T(1024)}, u32[]{:S(2)}) copy-start(f32[1024]{0:T(1024)} %param.13) | copy-start | bytes 12292
  37.4 10.3 %copy-start.3 = (bf16[1,176,1024]{2,1,0:T(8,128)(2,1)S(1)}, bf16[1,176,1024]{2,1,0:T(8,128)(2,1)}, u32[]{:S(2)}) copy-start(bf16[1,176,1024]{2,1,0:T(8,128)(2,1)} %param.16) | copy-start | bytes 1081348
  37.8 10.0 %copy-start.4 = (bf16[1,176,1024]{2,1,0:T(8,128)(2,1)S(1)}, bf16[1,176,1024]{2,1,0:T(8,128)(2,1)}, u32[]{:S(2)}) copy-start(bf16[1,176,1024]{2,1,0:T(8,128)(2,1)} %param.17) | copy-start | bytes 1081348
  37.8 10.0 %copy-start.5 = (bf16[1,176,1024]{2,1,0:T(8,128)(2,1)S(1)}, bf16[1,176,1024]{2,1,0:T(8,128)(2,1)}, u32[]{:S(2)}) copy-start(bf16[1,176,1024]{2,1,0:T(8,128)(2,1)} %param.18) | copy-start | bytes 1081348
  38.9 31.6 %all-to-all-start.1 = ((bf16[16,22,1024]{2,1,0:T(8,128)(2,1)}), bf16[16,22,1024]{2,1,0:T(8,128)(2,1)S(1)}, u32[]{:S(2)}, u32[]{:S(2)}) async-start(bf16[16,22,1024]{2,1,0:T(8,128)(2,1)} %reshape.236), calls=%async_computation.1 | async-start | bytes 1572864 | tf_op jit(solution)/shard_map/all_to_all | solution.py:95
  47.9 43.9 %collective-permute-start.7 = (bf16[3,176,1024]{2,1,0:T(8,128)(2,1)S(1)}, bf16[3,176,1024]{2,1,0:T(8,128)(2,1)}, u32[]{:S(2)}, u32[]{:S(2)}) collective-permute-start(bf16[3,176,1024]{2,1,0:T(8,128)(2,1)S(1)} %constant_dynamic-update-slice_fusion), channel_id=1, source_target_pairs={{0,4},{4,8},{8,12},{12,0},{1,5},{5,9},{9,13},{13,1},{2,6},{6,10},{... | collective-permute-start | bytes 3244040 | tf_op jit(solution)/shard_map/ppermute | solution.py:75
  48.4 49.3 %collective-permute-start.8 = (bf16[3,176,1024]{2,1,0:T(8,128)(2,1)S(1)}, bf16[3,176,1024]{2,1,0:T(8,128)(2,1)}, u32[]{:S(2)}, u32[]{:S(2)}) collective-permute-start(bf16[3,176,1024]{2,1,0:T(8,128)(2,1)S(1)} %constant_dynamic-update-slice_fusion), channel_id=1, source_target_pairs={{0,8},{4,12},{8,0},{12,4},{1,9},{5,13},{9,1},{13,5},{2,10},{6,14},... | collective-permute-start | bytes 3244040 | tf_op jit(solution)/shard_map/ppermute | solution.py:75
  50.5 47.6 %collective-permute-start.9 = (bf16[3,176,1024]{2,1,0:T(8,128)(2,1)S(1)}, bf16[3,176,1024]{2,1,0:T(8,128)(2,1)}, u32[]{:S(2)}, u32[]{:S(2)}) collective-permute-start(bf16[3,176,1024]{2,1,0:T(8,128)(2,1)S(1)} %constant_dynamic-update-slice_fusion), channel_id=1, source_target_pairs={{0,12},{4,0},{8,4},{12,8},{1,13},{5,1},{9,5},{13,9},{2,14},{6,2},{... | collective-permute-start | bytes 3244040 | tf_op jit(solution)/shard_map/ppermute | solution.py:75
  70.7 18.0 %collective-permute-start.10 = (bf16[352,1024]{1,0:T(8,128)(2,1)S(1)}, bf16[352,1024]{1,0:T(8,128)(2,1)S(1)}, u32[]{:S(2)}, u32[]{:S(2)}) collective-permute-start(bf16[352,1024]{1,0:T(8,128)(2,1)S(1)} %reshape.237), channel_id=1, source_target_pairs={{0,1},{1,2},{2,3},{3,0},{4,5},{5,6},{6,7},{7,4},{8,9},{9,10},{10,1... | collective-permute-start | bytes 2162696 | tf_op jit(solution)/shard_map/ppermute | solution.py:101
  71.6 17.4 %collective-permute-start.12 = (bf16[352,1024]{1,0:T(8,128)(2,1)S(1)}, bf16[352,1024]{1,0:T(8,128)(2,1)S(1)}, u32[]{:S(2)}, u32[]{:S(2)}) collective-permute-start(bf16[352,1024]{1,0:T(8,128)(2,1)S(1)} %reshape.237), channel_id=1, source_target_pairs={{0,3},{1,0},{2,1},{3,2},{4,7},{5,4},{6,5},{7,6},{8,11},{9,8},{10,9... | collective-permute-start | bytes 2162696 | tf_op jit(solution)/shard_map/ppermute | solution.py:102
  88.7 11.7 %collective-permute-start.11 = (bf16[176,1024]{1,0:T(8,128)(2,1)S(1)}, bf16[176,1024]{1,0:T(8,128)(2,1)S(1)}, u32[]{:S(2)}, u32[]{:S(2)}) collective-permute-start(bf16[176,1024]{1,0:T(8,128)(2,1)S(1)} %slice.58), channel_id=1, source_target_pairs={{0,1},{1,2},{2,3},{3,0},{4,5},{5,6},{6,7},{7,4},{8,9},{9,10},{10,1... | collective-permute-start | bytes 1081352 | tf_op jit(solution)/shard_map/ppermute | solution.py:106
  89.0 11.4 %collective-permute-start.13 = (bf16[176,1024]{1,0:T(8,128)(2,1)S(1)}, bf16[176,1024]{1,0:T(8,128)(2,1)S(1)}, u32[]{:S(2)}, u32[]{:S(2)}) collective-permute-start(bf16[176,1024]{1,0:T(8,128)(2,1)S(1)} %slice.59), channel_id=1, source_target_pairs={{0,3},{1,0},{2,1},{3,2},{4,7},{5,4},{6,5},{7,6},{8,11},{9,8},{10,9... | collective-permute-start | bytes 1081352 | tf_op jit(solution)/shard_map/ppermute | solution.py:107
  100.3 2.0 %copy-start.1 = (bf16[3,704,1024]{2,1,0:T(8,128)(2,1)}, bf16[3,704,1024]{2,1,0:T(8,128)(2,1)S(1)}, u32[]{:S(2)}) copy-start(bf16[3,704,1024]{2,1,0:T(8,128)(2,1)S(1)} %pad_maximum_fusion) | copy-start | bytes 12976132
  102.3 1.4 copy-start.6
  116.8 16.7 %collective-permute-start.14 = (bf16[352,1024]{1,0:T(8,128)(2,1)}, bf16[352,1024]{1,0:T(8,128)(2,1)S(1)}, u32[]{:S(2)}, u32[]{:S(2)}) collective-permute-start(bf16[352,1024]{1,0:T(8,128)(2,1)} %get-tuple-element.8), channel_id=1, source_target_pairs={{0,3},{1,0},{2,1},{3,2},{4,7},{5,4},{6,5},{7,6},{8,11},{9,8},{10,9... | collective-permute-start | bytes 2162696 | tf_op jit(solution)/shard_map/ppermute | solution.py:120
  118.6 17.9 %collective-permute-start.15 = (bf16[352,1024]{1,0:T(8,128)(2,1)}, bf16[352,1024]{1,0:T(8,128)(2,1)S(1)}, u32[]{:S(2)}, u32[]{:S(2)}) collective-permute-start(bf16[352,1024]{1,0:T(8,128)(2,1)} %get-tuple-element.10), channel_id=1, source_target_pairs={{0,2},{1,3},{2,0},{3,1},{4,6},{5,7},{6,4},{7,5},{8,10},{9,11},{10,... | collective-permute-start | bytes 2162696 | tf_op jit(solution)/shard_map/ppermute | solution.py:120
  119.4 34.5 %collective-permute-start.16 = (bf16[352,1024]{1,0:T(8,128)(2,1)}, bf16[352,1024]{1,0:T(8,128)(2,1)S(1)}, u32[]{:S(2)}, u32[]{:S(2)}) collective-permute-start(bf16[352,1024]{1,0:T(8,128)(2,1)} %get-tuple-element.9), channel_id=1, source_target_pairs={{0,1},{1,2},{2,3},{3,0},{4,5},{5,6},{6,7},{7,4},{8,9},{9,10},{10,1... | collective-permute-start | bytes 2162696 | tf_op jit(solution)/shard_map/ppermute | solution.py:120
  155.5 8.2 %copy-start.9 = (s32[88,2]{0,1:T(2,128)S(1)}, s32[88,2]{0,1:T(2,128)}, u32[]{:S(2)}) copy-start(s32[88,2]{0,1:T(2,128)} %param.15) | copy-start | bytes 2116
  155.5 8.6 %copy-start.8 = (f32[1024,16]{0,1:T(8,128)S(1)}, f32[1024,16]{0,1:T(8,128)}, u32[]{:S(2)}) copy-start(f32[1024,16]{0,1:T(8,128)} %param.14) | copy-start | bytes 196612
  156.6 29.8 %all-to-all-start.2 = ((bf16[16,22,1024]{2,1,0:T(8,128)(2,1)}), bf16[16,22,1024]{2,1,0:T(8,128)(2,1)S(1)}, u32[]{:S(2)}, u32[]{:S(2)}) async-start(bf16[16,22,1024]{2,1,0:T(8,128)(2,1)} %reshape.238), calls=%async_computation.2 | async-start | bytes 1572864 | tf_op jit(solution)/shard_map/all_to_all | solution.py:124
  166.8 20.4 %copy-start.11 = (f32[1024]{0:T(1024)S(1)}, f32[1024]{0:T(1024)}, u32[]{:S(2)}) copy-start(f32[1024]{0:T(1024)} %param.19) | copy-start | bytes 12292
  187.1 0.8 copy-start.2

commit v14 on v13

--- a/solution.py
+++ b/solution.py
@@ -116,9 +116,21 @@
     partial = expert_block(peer_rows, gate_rows, up_rows, down_rows).astype(jnp.bfloat16)
     partial = partial.reshape(n_tx - 1, slot_total, width)
     expert_sum = own.astype(jnp.float32)
-    for s in range(1, n_tx):
-        back = lax.ppermute(partial[s - 1], "tx", shift_pairs(n_tx, -s))
-        expert_sum = expert_sum + back.astype(jnp.float32)
+    if n_tx == 4:
+        cut = slot_total // 2
+        down_mail = jnp.concatenate([partial[0], partial[1][:cut]], axis=0)
+        up_mail = jnp.concatenate([partial[2], partial[1][cut:]], axis=0)
+        down_got = lax.ppermute(down_mail, "tx", shift_pairs(n_tx, -1))
+        up_got = lax.ppermute(up_mail, "tx", shift_pairs(n_tx, 1))
+        far_a = lax.ppermute(down_got[slot_total:], "tx", shift_pairs(n_tx, -1))
+        far_b = lax.ppermute(up_got[slot_total:], "tx", shift_pairs(n_tx, 1))
+        far = jnp.concatenate([far_a, far_b], axis=0)
+        for back in (down_got[:slot_total], up_got[:slot_total], far):
+            expert_sum = expert_sum + back.astype(jnp.float32)
+    else:
+        for s in range(1, n_tx):
+            back = lax.ppermute(partial[s - 1], "tx", shift_pairs(n_tx, -s))
+            expert_sum = expert_sum + back.astype(jnp.float32)
     expert_sum = expert_sum.astype(jnp.bfloat16)
     expert_out = expert_sum.reshape(n_expert, capacity, width)
     returned = lax.all_to_all(expert_out, "expert", split_axis=0, concat_axis=0, tiled=True)

time: 188 us -> 192 us (1.021); the launches traced: 188 us -> 190 us
  starting transfers between devices: 45 us -> 49.4 us
    ppermute x3 -> x4, starting transfers between devices: 2.99 us -> 5.64 us  [the longest x1 2.73 us: per_device(): far_a = lax.ppermute(down_got[slot_total:], 'tx', shift_pairs(n_tx, -1))]
    all_to_all x1, starting transfers between devices: 7.04 us -> 9.23 us  [per_device(): lax.all_to_all(expert_out, 'expert', split_axis=0, concat_axis=0, tiled=T...]
    ppermute x3 -> x4, waiting for transfers between devices: 26 us -> 25.7 us  [the longest x1 22.6 us: per_device(): up_got = lax.ppermute(up_mail, 'tx', shift_pairs(n_tx, 1))]
    unnamed x30 -> x32, local copies, waits for them, and re-layouts: 5.07 us -> 5.28 us
  transfers between devices with their start and end apart: 20 -> 21, of which waited for: 11 -> 10; matrix products, arithmetic and copies ran while one was open for 10% -> 7% of each run, Pallas kernels for 0% -> 0%
where the time goes in v14:
time: 192 us; the launch traced here: 190 us
  waiting for transfers between devices  98.6 us (51%)
  starting transfers between devices  49.4 us (26%)
  matrix products  20.8 us (11%)
  local copies, waits for them, and re-layouts  15 us (8%)
  other arithmetic  4.74 us (2%)
    ppermute x1, waiting for transfers between devices, per_device(): up_got = lax.ppermute(up_mail, 'tx', shift_pairs(n_tx, 1))  22.6 us
    all_to_all x1, waiting for transfers between devices, per_device(): lax.all_to_all(expert_out, 'expert', split_axis=0, concat_axis=0, tiled=T...  19.4 us
    all_to_all x1, waiting for transfers between devices, per_device(): lax.all_to_all(send_slots, 'expert', split_axis=0, concat_axis=0, tiled=T...  18.2 us
    ppermute x1, waiting for transfers between devices, per_device(): from_below = lax.ppermute(rows_in, 'tx', shift_pairs(n_tx, 1))  15.2 us
    dot_general x2, matrix products, expert_block(): return jnp.dot(hid, down_rows, preferred_element_type=jnp.float32)  12.3 us
    ppermute x3, waiting for transfers between devices, per_device(): lax.ppermute(near, 'ty', shift_pairs(n_ty, s))  12.3 us
    all_to_all x1, starting transfers between devices, per_device(): lax.all_to_all(expert_out, 'expert', split_axis=0, concat_axis=0, tiled=T...  9.23 us
    all_to_all x1, starting transfers between devices, per_device(): lax.all_to_all(send_slots, 'expert', split_axis=0, concat_axis=0, tiled=T...  8.85 us
  transfers between devices with their start and end apart: 21, of which 10 were waited for; matrix products, arithmetic and copies ran while one was open for 7% of the time, Pallas kernels for 0%

profile of v14, /device:TPU:1, one launch (start us, length us, event | category | flops | bytes accessed | tf_op | source)
XLA Modules:
  0.0 189.8 jit_solution(8896522923026116694)
XLA Ops:
  0.7 0.9 copy-done
  1.5 2.0 %collective-permute-start = (bf16[64,512]{1,0:T(8,128)(2,1)S(1)}, bf16[64,512]{1,0:T(8,128)(2,1)S(1)}, u32[]{:S(2)}, u32[]{:S(2)}) collective-permute-start(bf16[64,512]{1,0:T(8,128)(2,1)S(1)} %constant_dynamic-slice_fusion), channel_id=1, source_target_pairs={{0,1},{1,2},{2,3},{3,0},{4,5},{5,6},{6,7},{7,4},{8,9},{9,10},{10,1... | collective-permute-start | bytes 196616 | tf_op jit(solution)/shard_map/ppermute | solution.py:54
  3.6 2.5 %collective-permute-start.1 = (bf16[64,512]{1,0:T(8,128)(2,1)S(1)}, bf16[64,512]{1,0:T(8,128)(2,1)S(1)}, u32[]{:S(2)}, u32[]{:S(2)}) collective-permute-start(bf16[64,512]{1,0:T(8,128)(2,1)S(1)} %constant_dynamic-slice_fusion), channel_id=1, source_target_pairs={{0,2},{1,3},{2,0},{3,1},{4,6},{5,7},{6,4},{7,5},{8,10},{9,11},{10,... | collective-permute-start | bytes 196616 | tf_op jit(solution)/shard_map/ppermute | solution.py:54
  6.0 1.2 collective-permute-start.2
  7.2 1.4 all_to_all.18
  8.6 0.8 copy.26
  9.4 4.3 %all-to-all-start = ((bf16[64,16,88]{2,0,1:T(8,128)(2,1)}), bf16[64,16,88]{2,0,1:T(8,128)(2,1)S(1)}, u32[]{:S(2)}, u32[]{:S(2)}) async-start(bf16[64,16,88]{2,0,1:T(8,128)(2,1)} %copy.26), calls=%async_computation | async-start | bytes 524288 | tf_op jit(solution)/shard_map/all_to_all | solution.py:59
  13.9 0.1 reshape.233
  14.0 0.6 reduce-window.6
  14.6 0.2 slice_reduce_fusion
  14.9 1.4 collective-permute-start.3
  16.3 2.4 %collective-permute-start.4 = (bf16[4,64,512]{2,1,0:T(8,128)(2,1)S(1)}, bf16[4,64,512]{2,1,0:T(8,128)(2,1)S(1)}, u32[]{:S(2)}, u32[]{:S(2)}) collective-permute-start(bf16[4,64,512]{2,1,0:T(8,128)(2,1)S(1)} %get-tuple-element.9), channel_id=1, source_target_pairs={{0,8},{4,12},{8,0},{12,4},{1,9},{5,13},{9,1},{13,5},{2,10},{6,14},... | collective-permute-start | bytes 786440 | tf_op jit(solution)/shard_map/ppermute | solution.py:56
  18.7 1.2 collective-permute-start.5
  20.0 5.8 %collective-permute-done.3 = bf16[4,64,512]{2,1,0:T(8,128)(2,1)S(1)} collective-permute-done((bf16[4,64,512]{2,1,0:T(8,128)(2,1)S(1)}, bf16[4,64,512]{2,1,0:T(8,128)(2,1)S(1)}, u32[]{:S(2)}, u32[]{:S(2)}) %collective-permute-start.3) | collective-permute-done | bytes 262176 | tf_op jit(solution)/shard_map/ppermute | solution.py:56
  25.8 6.5 %collective-permute-done.4 = bf16[4,64,512]{2,1,0:T(8,128)(2,1)S(1)} collective-permute-done((bf16[4,64,512]{2,1,0:T(8,128)(2,1)S(1)}, bf16[4,64,512]{2,1,0:T(8,128)(2,1)S(1)}, u32[]{:S(2)}, u32[]{:S(2)}) %collective-permute-start.4) | collective-permute-done | bytes 262176 | tf_op jit(solution)/shard_map/ppermute | solution.py:56
  32.3 0.1 pad_maximum_fusion.2
  32.4 1.5 collective-permute-start.6
  34.1 0.6 gather_fusion
  34.8 0.6 gather_fusion.1
  35.4 0.4 convolution_bitcast_fusion.1
  35.8 0.4 collective-permute-done.6
  36.2 0.4 convolution_bitcast_fusion
  36.6 0.2 fusion.35
  36.9 0.2 broadcast_in_dim.40
  37.1 0.1 reshape.236
  37.3 0.3 convolution_convert_fusion.2
  37.6 1.1 reshape.237
  38.7 8.9 %all-to-all-start.1 = ((bf16[16,22,1024]{2,1,0:T(8,128)(2,1)}), bf16[16,22,1024]{2,1,0:T(8,128)(2,1)S(1)}, u32[]{:S(2)}, u32[]{:S(2)}) async-start(bf16[16,22,1024]{2,1,0:T(8,128)(2,1)} %reshape.237), calls=%async_computation.1 | async-start | bytes 1572864 | tf_op jit(solution)/shard_map/all_to_all | solution.py:95
  47.7 0.9 copy-done.5
  48.6 0.3 collective-permute-start.7
  48.9 2.0 %collective-permute-start.8 = (bf16[3,176,1024]{2,1,0:T(8,128)(2,1)S(1)}, bf16[3,176,1024]{2,1,0:T(8,128)(2,1)}, u32[]{:S(2)}, u32[]{:S(2)}) collective-permute-start(bf16[3,176,1024]{2,1,0:T(8,128)(2,1)S(1)} %constant_dynamic-update-slice_fusion), channel_id=1, source_target_pairs={{0,8},{4,12},{8,0},{12,4},{1,9},{5,13},{9,1},{13,5},{2,10},{6,14},... | collective-permute-start | bytes 3244040 | tf_op jit(solution)/shard_map/ppermute | solution.py:75
  50.9 1.2 collective-permute-start.9
  52.1 18.2 %all-to-all-done.1 = bf16[16,22,1024]{2,1,0:T(8,128)(2,1)S(1)} async-done(((bf16[16,22,1024]{2,1,0:T(8,128)(2,1)}), bf16[16,22,1024]{2,1,0:T(8,128)(2,1)S(1)}, u32[]{:S(2)}, u32[]{:S(2)}) %all-to-all-start.1) | async-done | bytes 720928 | tf_op jit(solution)/shard_map/all_to_all | solution.py:95
  70.3 0.2 reshape.238
  70.5 0.7 collective-permute-start.10
  71.2 2.0 %collective-permute-start.12 = (bf16[352,1024]{1,0:T(8,128)(2,1)S(1)}, bf16[352,1024]{1,0:T(8,128)(2,1)S(1)}, u32[]{:S(2)}, u32[]{:S(2)}) collective-permute-start(bf16[352,1024]{1,0:T(8,128)(2,1)S(1)} %reshape.238), channel_id=1, source_target_pairs={{0,3},{1,0},{2,1},{3,2},{4,7},{5,4},{6,5},{7,6},{8,11},{9,8},{10,9... | collective-permute-start | bytes 2162696 | tf_op jit(solution)/shard_map/ppermute | solution.py:102
  73.3 15.2 %collective-permute-done.10 = bf16[352,1024]{1,0:T(8,128)(2,1)S(1)} collective-permute-done((bf16[352,1024]{1,0:T(8,128)(2,1)S(1)}, bf16[352,1024]{1,0:T(8,128)(2,1)S(1)}, u32[]{:S(2)}, u32[]{:S(2)}) %collective-permute-start.10) | collective-permute-done | bytes 720928 | tf_op jit(solution)/shard_map/ppermute | solution.py:101
  88.5 0.3 collective-permute-start.11
  88.8 2.7 %collective-permute-start.13 = (bf16[176,1024]{1,0:T(8,128)(2,1)S(1)}, bf16[176,1024]{1,0:T(8,128)(2,1)S(1)}, u32[]{:S(2)}, u32[]{:S(2)}) collective-permute-start(bf16[176,1024]{1,0:T(8,128)(2,1)S(1)} %slice.79), channel_id=1, source_target_pairs={{0,3},{1,0},{2,1},{3,2},{4,7},{5,4},{6,5},{7,6},{8,11},{9,8},{10,9... | collective-permute-start | bytes 1081352 | tf_op jit(solution)/shard_map/ppermute | solution.py:107
  91.6 6.5 %collective-permute-done.8 = bf16[3,176,1024]{2,1,0:T(8,128)(2,1)} collective-permute-done((bf16[3,176,1024]{2,1,0:T(8,128)(2,1)S(1)}, bf16[3,176,1024]{2,1,0:T(8,128)(2,1)}, u32[]{:S(2)}, u32[]{:S(2)}) %collective-permute-start.8) | collective-permute-done | bytes 1081376 | tf_op jit(solution)/shard_map/ppermute | solution.py:75
  98.0 0.8 collective-permute-done.9
  98.8 2.2 %pad_maximum_fusion = bf16[3,704,1024]{2,1,0:T(8,128)(2,1)S(1)} fusion(bf16[3,176,1024]{2,1,0:T(8,128)(2,1)} %collective-permute-done.9, bf16[3,176,1024]{2,1,0:T(8,128)(2,1)} %collective-permute-done.8, bf16[3,176,1024]{2,1,0:T(8,128)(2,1)} %collective-permute-done.7, bf16[3,176,1024]{2,1,0:T(8,128)(2,1)S(1)} %constant_dynamic-update-slice_fusion), kind=kLoop, calls=%fused_computation.4 | loop fusion | flops 17301504 | bytes 8650752 | tf_op jit(solution)/shard_map/concatenate | solution.py:96
  101.2 1.8 copy-done.1
  103.0 1.4 copy-done.6
  104.4 3.6 %fusion.14 = f32[1056,704]{1,0:T(8,128)} fusion(bf16[1056,1024]{1,0:T(8,128)(2,1)S(1)} %constant_dynamic-update-slice_fusion.3, bf16[3,704,1024]{2,1,0:T(8,128)(2,1)S(1)} %pad_maximum_fusion), kind=kOutput, calls=%fused_computation.27 | convolution fusion | flops 1522532352 | bytes 6578176 | tf_op jit(solution)/shard_map/dot_general | solution.py:20
  108.0 8.0 %convolution_convert_fusion = bf16[1056,1024]{1,0:T(8,128)(2,1)S(1)} fusion(f32[1056,704]{1,0:T(8,128)} %fusion.14, bf16[3,704,1024]{2,1,0:T(8,128)(2,1)} %copy-done.1, bf16[1056,1024]{1,0:T(8,128)(2,1)} %copy-done.6), kind=kOutput, calls=%fused_computation.5 | convolution fusion | flops 3053580288 | bytes 10452992 | tf_op jit(solution)/shard_map/dot_general | solution.py:27
  116.2 0.7 collective-permute-start.15
  117.1 2.1 %collective-permute-start.14 = (bf16[528,1024]{1,0:T(8,128)(2,1)S(1)}, bf16[528,1024]{1,0:T(8,128)(2,1)S(1)}, u32[]{:S(2)}, u32[]{:S(2)}) collective-permute-start(bf16[528,1024]{1,0:T(8,128)(2,1)S(1)} %concatenate.35), channel_id=1, source_target_pairs={{0,3},{1,0},{2,1},{3,2},{4,7},{5,4},{6,5},{7,6},{8,11},{9,8},{10,9... | collective-permute-start | bytes 3244040 | tf_op jit(solution)/shard_map/ppermute | solution.py:123
  119.1 22.6 %collective-permute-done.15 = bf16[528,1024]{1,0:T(8,128)(2,1)S(1)} collective-permute-done((bf16[528,1024]{1,0:T(8,128)(2,1)S(1)}, bf16[528,1024]{1,0:T(8,128)(2,1)S(1)}, u32[]{:S(2)}, u32[]{:S(2)}) %collective-permute-start.15) | collective-permute-done | bytes 1081376 | tf_op jit(solution)/shard_map/ppermute | solution.py:124
  141.9 2.7 %collective-permute-start.16 = (bf16[176,1024]{1,0:T(8,128)(2,1)S(1)}, bf16[176,1024]{1,0:T(8,128)(2,1)}, u32[]{:S(2)}, u32[]{:S(2)}) collective-permute-start(bf16[176,1024]{1,0:T(8,128)(2,1)S(1)} %slice.84), channel_id=1, source_target_pairs={{0,3},{1,0},{2,1},{3,2},{4,7},{5,4},{6,5},{7,6},{8,11},{9,8},{10,9... | collective-permute-start | bytes 1081352 | tf_op jit(solution)/shard_map/ppermute | solution.py:125
  144.6 3.1 %fusion.17 = f32[352,704]{1,0:T(8,128)} fusion(bf16[352,1024]{1,0:T(8,128)(2,1)S(1)} %reshape.238, bf16[3,704,1024]{2,1,0:T(8,128)(2,1)} %copy-done.1), kind=kOutput, calls=%fused_computation.30 | convolution fusion | flops 507510784 | bytes 3153920 | tf_op jit(solution)/shard_map/dot_general | solution.py:23
  147.7 3.1 %collective-permute-done.17 = bf16[176,1024]{1,0:T(8,128)(2,1)S(1)} collective-permute-done((bf16[176,1024]{1,0:T(8,128)(2,1)S(1)}, bf16[176,1024]{1,0:T(8,128)(2,1)S(1)}, u32[]{:S(2)}, u32[]{:S(2)}) %collective-permute-start.17) | collective-permute-done | bytes 360480 | tf_op jit(solution)/shard_map/ppermute | solution.py:126
  150.9 4.3 %add_convert_fusion = bf16[352,1024]{1,0:T(8,128)(2,1)S(1)} fusion(bf16[528,1024]{1,0:T(8,128)(2,1)} %copy-done.8, bf16[528,1024]{1,0:T(8,128)(2,1)S(1)} %collective-permute-done.14, bf16[176,1024]{1,0:T(8,128)(2,1)S(1)} %collective-permute-done.17, bf16[176,1024]{1,0:T(8,128)(2,1)} %collective-permute-done.16, bf16[3,704,1024]{2,1,0:T(8,128)(2,1)} %copy-done.1, ...), kind=kOutput, calls=%fused_computation.23 | convolution fusion | flops 1021825024 | bytes 7569408 | tf_op jit(solution)/shard_map/dot_general | solution.py:27
  155.2 1.1 reshape.239
  156.3 9.2 %all-to-all-start.2 = ((bf16[16,22,1024]{2,1,0:T(8,128)(2,1)}), bf16[16,22,1024]{2,1,0:T(8,128)(2,1)S(1)}, u32[]{:S(2)}, u32[]{:S(2)}) async-start(bf16[16,22,1024]{2,1,0:T(8,128)(2,1)} %reshape.239), calls=%async_computation.2 | async-start | bytes 1572864 | tf_op jit(solution)/shard_map/all_to_all | solution.py:136
  165.6 0.1 reshape.258
  166.0 0.3 fusion.67
  166.3 2.3 %gather_fusion.2 = f32[176]{0:T(256)S(1)} fusion(f32[88,16]{0,1:T(8,128)S(1)} %fusion.47, s32[176]{0:T(256)S(1)} %reshape.258), kind=kCustom, calls=%fused_computation.2 | custom fusion | bytes 2816 | tf_op jit(solution)/shard_map/jit(take_along_axis)/gather | solution.py:82
  168.6 0.1 reshape.261
  168.8 19.4 %all-to-all-done.2 = bf16[16,22,1024]{2,1,0:T(8,128)(2,1)S(1)} async-done(((bf16[16,22,1024]{2,1,0:T(8,128)(2,1)}), bf16[16,22,1024]{2,1,0:T(8,128)(2,1)S(1)}, u32[]{:S(2)}, u32[]{:S(2)}) %all-to-all-start.2) | async-done | bytes 720928 | tf_op jit(solution)/shard_map/all_to_all | solution.py:136
  188.2 0.2 reshape.271
  188.4 0.4 fusion.18
  188.8 0.2 fusion.32
  189.0 0.8 fusion.34
  (79 shorter events, 1.8 us)
Async XLA Ops:
  0.6 0.9 copy-start
  0.6 13.1 %copy-start.10 = (s32[88,2]{0,1:T(2,128)S(1)}, s32[88,2]{0,1:T(2,128)}, u32[]{:S(2)}) copy-start(s32[88,2]{0,1:T(2,128)} %param.15) | copy-start | bytes 2116
  1.5 13.3 %collective-permute-start = (bf16[64,512]{1,0:T(8,128)(2,1)S(1)}, bf16[64,512]{1,0:T(8,128)(2,1)S(1)}, u32[]{:S(2)}, u32[]{:S(2)}) collective-permute-start(bf16[64,512]{1,0:T(8,128)(2,1)S(1)} %constant_dynamic-slice_fusion), channel_id=1, source_target_pairs={{0,1},{1,2},{2,3},{3,0},{4,5},{5,6},{6,7},{7,4},{8,9},{9,10},{10,1... | collective-permute-start | bytes 196616 | tf_op jit(solution)/shard_map/ppermute | solution.py:54
  3.6 11.3 %collective-permute-start.1 = (bf16[64,512]{1,0:T(8,128)(2,1)S(1)}, bf16[64,512]{1,0:T(8,128)(2,1)S(1)}, u32[]{:S(2)}, u32[]{:S(2)}) collective-permute-start(bf16[64,512]{1,0:T(8,128)(2,1)S(1)} %constant_dynamic-slice_fusion), channel_id=1, source_target_pairs={{0,2},{1,3},{2,0},{3,1},{4,6},{5,7},{6,4},{7,5},{8,10},{9,11},{10,... | collective-permute-start | bytes 196616 | tf_op jit(solution)/shard_map/ppermute | solution.py:54
  6.0 8.8 %collective-permute-start.2 = (bf16[64,512]{1,0:T(8,128)(2,1)S(1)}, bf16[64,512]{1,0:T(8,128)(2,1)S(1)}, u32[]{:S(2)}, u32[]{:S(2)}) collective-permute-start(bf16[64,512]{1,0:T(8,128)(2,1)S(1)} %constant_dynamic-slice_fusion), channel_id=1, source_target_pairs={{0,3},{1,0},{2,1},{3,2},{4,7},{5,4},{6,5},{7,6},{8,11},{9,8},{10,9... | collective-permute-start | bytes 196616 | tf_op jit(solution)/shard_map/ppermute | solution.py:54
  9.4 24.7 %all-to-all-start = ((bf16[64,16,88]{2,0,1:T(8,128)(2,1)}), bf16[64,16,88]{2,0,1:T(8,128)(2,1)S(1)}, u32[]{:S(2)}, u32[]{:S(2)}) async-start(bf16[64,16,88]{2,0,1:T(8,128)(2,1)} %copy.26), calls=%async_computation | async-start | bytes 524288 | tf_op jit(solution)/shard_map/all_to_all | solution.py:59
  14.9 10.9 %collective-permute-start.3 = (bf16[4,64,512]{2,1,0:T(8,128)(2,1)S(1)}, bf16[4,64,512]{2,1,0:T(8,128)(2,1)S(1)}, u32[]{:S(2)}, u32[]{:S(2)}) collective-permute-start(bf16[4,64,512]{2,1,0:T(8,128)(2,1)S(1)} %get-tuple-element.9), channel_id=1, source_target_pairs={{0,4},{4,8},{8,12},{12,0},{1,5},{5,9},{9,13},{13,1},{2,6},{6,10},{... | collective-permute-start | bytes 786440 | tf_op jit(solution)/shard_map/ppermute | solution.py:56
  16.3 16.0 %collective-permute-start.4 = (bf16[4,64,512]{2,1,0:T(8,128)(2,1)S(1)}, bf16[4,64,512]{2,1,0:T(8,128)(2,1)S(1)}, u32[]{:S(2)}, u32[]{:S(2)}) collective-permute-start(bf16[4,64,512]{2,1,0:T(8,128)(2,1)S(1)} %get-tuple-element.9), channel_id=1, source_target_pairs={{0,8},{4,12},{8,0},{12,4},{1,9},{5,13},{9,1},{13,5},{2,10},{6,14},... | collective-permute-start | bytes 786440 | tf_op jit(solution)/shard_map/ppermute | solution.py:56
  18.7 13.6 %collective-permute-start.5 = (bf16[4,64,512]{2,1,0:T(8,128)(2,1)S(1)}, bf16[4,64,512]{2,1,0:T(8,128)(2,1)S(1)}, u32[]{:S(2)}, u32[]{:S(2)}) collective-permute-start(bf16[4,64,512]{2,1,0:T(8,128)(2,1)S(1)} %get-tuple-element.9), channel_id=1, source_target_pairs={{0,12},{4,0},{8,4},{12,8},{1,13},{5,1},{9,5},{13,9},{2,14},{6,2},{... | collective-permute-start | bytes 786440 | tf_op jit(solution)/shard_map/ppermute | solution.py:56
  32.4 3.8 %collective-permute-start.6 = (bf16[4,4,64,512]{3,2,1,0:T(8,128)(2,1)S(1)}, bf16[4,4,64,512]{3,2,1,0:T(8,128)(2,1)S(1)}, u32[]{:S(2)}, u32[]{:S(2)}) collective-permute-start(bf16[4,4,64,512]{3,2,1,0:T(8,128)(2,1)S(1)} %pad_maximum_fusion.2), channel_id=1, source_target_pairs={{0,16},{16,0},{32,48},{48,32},{64,80},{80,64},{96,112},{112,96},{1... | collective-permute-start | bytes 3145736 | tf_op jit(solution)/shard_map/ppermute | solution.py:58
  35.4 1.2 copy-start.7
  35.4 1.4 copy-start.11
  37.6 10.0 %copy-start.3 = (bf16[1,176,1024]{2,1,0:T(8,128)(2,1)S(1)}, bf16[1,176,1024]{2,1,0:T(8,128)(2,1)}, u32[]{:S(2)}) copy-start(bf16[1,176,1024]{2,1,0:T(8,128)(2,1)} %param.16) | copy-start | bytes 1081348
  37.6 10.0 %copy-start.4 = (bf16[1,176,1024]{2,1,0:T(8,128)(2,1)S(1)}, bf16[1,176,1024]{2,1,0:T(8,128)(2,1)}, u32[]{:S(2)}) copy-start(bf16[1,176,1024]{2,1,0:T(8,128)(2,1)} %param.17) | copy-start | bytes 1081348
  38.7 31.6 %all-to-all-start.1 = ((bf16[16,22,1024]{2,1,0:T(8,128)(2,1)}), bf16[16,22,1024]{2,1,0:T(8,128)(2,1)S(1)}, u32[]{:S(2)}, u32[]{:S(2)}) async-start(bf16[16,22,1024]{2,1,0:T(8,128)(2,1)} %reshape.237), calls=%async_computation.1 | async-start | bytes 1572864 | tf_op jit(solution)/shard_map/all_to_all | solution.py:95
  47.6 1.0 copy-start.5
  48.6 43.0 %collective-permute-start.7 = (bf16[3,176,1024]{2,1,0:T(8,128)(2,1)S(1)}, bf16[3,176,1024]{2,1,0:T(8,128)(2,1)}, u32[]{:S(2)}, u32[]{:S(2)}) collective-permute-start(bf16[3,176,1024]{2,1,0:T(8,128)(2,1)S(1)} %constant_dynamic-update-slice_fusion), channel_id=1, source_target_pairs={{0,4},{4,8},{8,12},{12,0},{1,5},{5,9},{9,13},{13,1},{2,6},{6,10},{... | collective-permute-start | bytes 3244040 | tf_op jit(solution)/shard_map/ppermute | solution.py:75
  48.9 49.2 %collective-permute-start.8 = (bf16[3,176,1024]{2,1,0:T(8,128)(2,1)S(1)}, bf16[3,176,1024]{2,1,0:T(8,128)(2,1)}, u32[]{:S(2)}, u32[]{:S(2)}) collective-permute-start(bf16[3,176,1024]{2,1,0:T(8,128)(2,1)S(1)} %constant_dynamic-update-slice_fusion), channel_id=1, source_target_pairs={{0,8},{4,12},{8,0},{12,4},{1,9},{5,13},{9,1},{13,5},{2,10},{6,14},... | collective-permute-start | bytes 3244040 | tf_op jit(solution)/shard_map/ppermute | solution.py:75
  50.9 48.0 %collective-permute-start.9 = (bf16[3,176,1024]{2,1,0:T(8,128)(2,1)S(1)}, bf16[3,176,1024]{2,1,0:T(8,128)(2,1)}, u32[]{:S(2)}, u32[]{:S(2)}) collective-permute-start(bf16[3,176,1024]{2,1,0:T(8,128)(2,1)S(1)} %constant_dynamic-update-slice_fusion), channel_id=1, source_target_pairs={{0,12},{4,0},{8,4},{12,8},{1,13},{5,1},{9,5},{13,9},{2,14},{6,2},{... | collective-permute-start | bytes 3244040 | tf_op jit(solution)/shard_map/ppermute | solution.py:75
  70.5 18.0 %collective-permute-start.10 = (bf16[352,1024]{1,0:T(8,128)(2,1)S(1)}, bf16[352,1024]{1,0:T(8,128)(2,1)S(1)}, u32[]{:S(2)}, u32[]{:S(2)}) collective-permute-start(bf16[352,1024]{1,0:T(8,128)(2,1)S(1)} %reshape.238), channel_id=1, source_target_pairs={{0,1},{1,2},{2,3},{3,0},{4,5},{5,6},{6,7},{7,4},{8,9},{9,10},{10,1... | collective-permute-start | bytes 2162696 | tf_op jit(solution)/shard_map/ppermute | solution.py:101
  71.2 17.5 %collective-permute-start.12 = (bf16[352,1024]{1,0:T(8,128)(2,1)S(1)}, bf16[352,1024]{1,0:T(8,128)(2,1)S(1)}, u32[]{:S(2)}, u32[]{:S(2)}) collective-permute-start(bf16[352,1024]{1,0:T(8,128)(2,1)S(1)} %reshape.238), channel_id=1, source_target_pairs={{0,3},{1,0},{2,1},{3,2},{4,7},{5,4},{6,5},{7,6},{8,11},{9,8},{10,9... | collective-permute-start | bytes 2162696 | tf_op jit(solution)/shard_map/ppermute | solution.py:102
  88.5 12.6 %collective-permute-start.11 = (bf16[176,1024]{1,0:T(8,128)(2,1)S(1)}, bf16[176,1024]{1,0:T(8,128)(2,1)S(1)}, u32[]{:S(2)}, u32[]{:S(2)}) collective-permute-start(bf16[176,1024]{1,0:T(8,128)(2,1)S(1)} %slice.78), channel_id=1, source_target_pairs={{0,1},{1,2},{2,3},{3,0},{4,5},{5,6},{6,7},{7,4},{8,9},{9,10},{10,1... | collective-permute-start | bytes 1081352 | tf_op jit(solution)/shard_map/ppermute | solution.py:106
  88.8 12.3 %collective-permute-start.13 = (bf16[176,1024]{1,0:T(8,128)(2,1)S(1)}, bf16[176,1024]{1,0:T(8,128)(2,1)S(1)}, u32[]{:S(2)}, u32[]{:S(2)}) collective-permute-start(bf16[176,1024]{1,0:T(8,128)(2,1)S(1)} %slice.79), channel_id=1, source_target_pairs={{0,3},{1,0},{2,1},{3,2},{4,7},{5,4},{6,5},{7,6},{8,11},{9,8},{10,9... | collective-permute-start | bytes 1081352 | tf_op jit(solution)/shard_map/ppermute | solution.py:107
  101.0 2.0 %copy-start.1 = (bf16[3,704,1024]{2,1,0:T(8,128)(2,1)}, bf16[3,704,1024]{2,1,0:T(8,128)(2,1)S(1)}, u32[]{:S(2)}) copy-start(bf16[3,704,1024]{2,1,0:T(8,128)(2,1)S(1)} %pad_maximum_fusion) | copy-start | bytes 12976132
  103.0 1.4 copy-start.6
  116.2 25.5 %collective-permute-start.15 = (bf16[528,1024]{1,0:T(8,128)(2,1)S(1)}, bf16[528,1024]{1,0:T(8,128)(2,1)S(1)}, u32[]{:S(2)}, u32[]{:S(2)}) collective-permute-start(bf16[528,1024]{1,0:T(8,128)(2,1)S(1)} %pad_maximum_fusion.1), channel_id=1, source_target_pairs={{0,1},{1,2},{2,3},{3,0},{4,5},{5,6},{6,7},{7,4},{8,9},{9,10},{10,1... | collective-permute-start | bytes 3244040 | tf_op jit(solution)/shard_map/ppermute | solution.py:124
  117.1 24.8 %collective-permute-start.14 = (bf16[528,1024]{1,0:T(8,128)(2,1)S(1)}, bf16[528,1024]{1,0:T(8,128)(2,1)S(1)}, u32[]{:S(2)}, u32[]{:S(2)}) collective-permute-start(bf16[528,1024]{1,0:T(8,128)(2,1)S(1)} %concatenate.35), channel_id=1, source_target_pairs={{0,3},{1,0},{2,1},{3,2},{4,7},{5,4},{6,5},{7,6},{8,11},{9,8},{10,9... | collective-permute-start | bytes 3244040 | tf_op jit(solution)/shard_map/ppermute | solution.py:123
  141.7 6.0 %copy-start.8 = (bf16[528,1024]{1,0:T(8,128)(2,1)}, bf16[528,1024]{1,0:T(8,128)(2,1)S(1)}, u32[]{:S(2)}) copy-start(bf16[528,1024]{1,0:T(8,128)(2,1)S(1)} %collective-permute-done.15) | copy-start | bytes 3244036
  141.7 9.2 %collective-permute-start.17 = (bf16[176,1024]{1,0:T(8,128)(2,1)S(1)}, bf16[176,1024]{1,0:T(8,128)(2,1)S(1)}, u32[]{:S(2)}, u32[]{:S(2)}) collective-permute-start(bf16[176,1024]{1,0:T(8,128)(2,1)S(1)} %slice.85), channel_id=1, source_target_pairs={{0,1},{1,2},{2,3},{3,0},{4,5},{5,6},{6,7},{7,4},{8,9},{9,10},{10,1... | collective-permute-start | bytes 1081352 | tf_op jit(solution)/shard_map/ppermute | solution.py:126
  141.9 9.0 %collective-permute-start.16 = (bf16[176,1024]{1,0:T(8,128)(2,1)S(1)}, bf16[176,1024]{1,0:T(8,128)(2,1)}, u32[]{:S(2)}, u32[]{:S(2)}) collective-permute-start(bf16[176,1024]{1,0:T(8,128)(2,1)S(1)} %slice.84), channel_id=1, source_target_pairs={{0,3},{1,0},{2,1},{3,2},{4,7},{5,4},{6,5},{7,6},{8,11},{9,8},{10,9... | collective-permute-start | bytes 1081352 | tf_op jit(solution)/shard_map/ppermute | solution.py:125
  155.2 10.8 %copy-start.9 = (f32[1024,16]{0,1:T(8,128)S(1)}, f32[1024,16]{0,1:T(8,128)}, u32[]{:S(2)}) copy-start(f32[1024,16]{0,1:T(8,128)} %param.14) | copy-start | bytes 196612
  156.3 32.0 %all-to-all-start.2 = ((bf16[16,22,1024]{2,1,0:T(8,128)(2,1)}), bf16[16,22,1024]{2,1,0:T(8,128)(2,1)S(1)}, u32[]{:S(2)}, u32[]{:S(2)}) async-start(bf16[16,22,1024]{2,1,0:T(8,128)(2,1)} %reshape.239), calls=%async_computation.2 | async-start | bytes 1572864 | tf_op jit(solution)/shard_map/all_to_all | solution.py:136
  168.8 20.1 %copy-start.12 = (f32[1024]{0:T(1024)S(1)}, f32[1024]{0:T(1024)}, u32[]{:S(2)}) copy-start(f32[1024]{0:T(1024)} %param.19) | copy-start | bytes 12292
  188.9 0.8 copy-start.2

commit v15 on v13

--- a/solution.py
+++ b/solution.py
@@ -108,16 +108,15 @@
             ],
             axis=0,
         )
-        peer_rows = [from_below, far, from_above]
+        all_rows = [rows_in, from_below, far, from_above]
     else:
-        peer_rows = [lax.ppermute(rows_in, "tx", shift_pairs(n_tx, s)) for s in range(1, n_tx)]
-    own = expert_block(rows_in, gate_rows, up_rows, down_rows).astype(jnp.bfloat16)
-    peer_rows = jnp.concatenate(peer_rows, axis=0)
-    partial = expert_block(peer_rows, gate_rows, up_rows, down_rows).astype(jnp.bfloat16)
-    partial = partial.reshape(n_tx - 1, slot_total, width)
-    expert_sum = own.astype(jnp.float32)
+        all_rows = [rows_in] + [lax.ppermute(rows_in, "tx", shift_pairs(n_tx, s)) for s in range(1, n_tx)]
+    all_rows = jnp.concatenate(all_rows, axis=0)
+    partial = expert_block(all_rows, gate_rows, up_rows, down_rows).astype(jnp.bfloat16)
+    partial = partial.reshape(n_tx, slot_total, width)
+    expert_sum = partial[0].astype(jnp.float32)
     for s in range(1, n_tx):
-        back = lax.ppermute(partial[s - 1], "tx", shift_pairs(n_tx, -s))
+        back = lax.ppermute(partial[s], "tx", shift_pairs(n_tx, -s))
         expert_sum = expert_sum + back.astype(jnp.float32)
     expert_sum = expert_sum.astype(jnp.bfloat16)
     expert_out = expert_sum.reshape(n_expert, capacity, width)

time: 188 us -> 200 us (1.064)
  waiting for transfers between devices: 98 us -> 116 us
  matrix products: 21.4 us -> 14.7 us
  local copies, waits for them, and re-layouts: 16 us -> 13.3 us
  starting transfers between devices: 45 us -> 47.6 us
    ppermute x1, waiting for transfers between devices: 0.01 us -> 7.49 us  [per_device(): lax.ppermute(from_above[cut:], 'tx', shift_pairs(n_tx, -1))]
    ppermute x3, waiting for transfers between devices: 6.37 us -> 11.1 us  [per_device(): lax.ppermute(stacked, 'ty', shift_pairs(n_ty, s))]
    dot_general x2 -> x1, matrix products: 12.9 us -> 8.6 us  [expert_block(): return jnp.dot(hid, down_rows, preferred_element_type=jnp.float32)]
    ppermute x3, waiting for transfers between devices: 26 us -> 30.4 us  [per_device(): back = lax.ppermute(partial[s], 'tx', shift_pairs(n_tx, -s))]
    all_to_all x1, starting transfers between devices: 7.04 us -> 10.4 us  [per_device(): lax.all_to_all(expert_out, 'expert', split_axis=0, concat_axis=0, tiled=T...]
    dot_general x1 -> x0, matrix products: 3.12 us -> none  [expert_block(): lax.dot_general(inputs, up_rows, (((1,), (1,)), ((), ())), preferred_elem...]
    unnamed x30 -> x33, local copies, waits for them, and re-layouts: 5.07 us -> 3.56 us
  transfers between devices with their start and end apart: 20 -> 20, of which waited for: 11 -> 11; matrix products, arithmetic and copies ran while one was open for 10% -> 5% of each run, Pallas kernels for 0% -> 0%
where the time goes in v15:
time: 200 us; the launch traced here: 199 us
  waiting for transfers between devices  116 us (58%)
  starting transfers between devices  47.6 us (24%)
  matrix products  14.7 us (7%)
  local copies, waits for them, and re-layouts  13.3 us (7%)
  other arithmetic  6.33 us (3%)
    ppermute x3, waiting for transfers between devices, per_device(): back = lax.ppermute(partial[s], 'tx', shift_pairs(n_tx, -s))  30.4 us
    all_to_all x1, waiting for transfers between devices, per_device(): lax.all_to_all(send_slots, 'expert', split_axis=0, concat_axis=0, tiled=T...  20.2 us
    all_to_all x1, waiting for transfers between devices, per_device(): lax.all_to_all(expert_out, 'expert', split_axis=0, concat_axis=0, tiled=T...  19.4 us
    ppermute x1, waiting for transfers between devices, per_device(): from_below = lax.ppermute(rows_in, 'tx', shift_pairs(n_tx, 1))  15.2 us
    ppermute x3, waiting for transfers between devices, per_device(): lax.ppermute(near, 'ty', shift_pairs(n_ty, s))  11.9 us
    ppermute x3, waiting for transfers between devices, per_device(): lax.ppermute(stacked, 'ty', shift_pairs(n_ty, s))  11.1 us
    all_to_all x1, starting transfers between devices, per_device(): lax.all_to_all(expert_out, 'expert', split_axis=0, concat_axis=0, tiled=T...  10.4 us
    all_to_all x1, starting transfers between devices, per_device(): lax.all_to_all(send_slots, 'expert', split_axis=0, concat_axis=0, tiled=T...  8.85 us
  transfers between devices with their start and end apart: 20, of which 11 were waited for; matrix products, arithmetic and copies ran while one was open for 5% of the time, Pallas kernels for 0%

profile of v15, /device:TPU:1, one launch (start us, length us, event | category | flops | bytes accessed | tf_op | source)
XLA Modules:
  0.0 199.3 jit_solution(1915440406723784360)
XLA Ops:
  0.7 0.9 copy-done
  1.5 3.6 %collective-permute-start.1 = (bf16[64,512]{1,0:T(8,128)(2,1)S(1)}, bf16[64,512]{1,0:T(8,128)(2,1)S(1)}, u32[]{:S(2)}, u32[]{:S(2)}) collective-permute-start(bf16[64,512]{1,0:T(8,128)(2,1)S(1)} %constant_dynamic-slice_fusion), channel_id=1, source_target_pairs={{0,2},{1,3},{2,0},{3,1},{4,6},{5,7},{6,4},{7,5},{8,10},{9,11},{10,... | collective-permute-start | bytes 196616 | tf_op jit(solution)/shard_map/ppermute | solution.py:54
  5.1 0.3 collective-permute-start
  5.4 2.4 %collective-permute-start.2 = (bf16[64,512]{1,0:T(8,128)(2,1)S(1)}, bf16[64,512]{1,0:T(8,128)(2,1)S(1)}, u32[]{:S(2)}, u32[]{:S(2)}) collective-permute-start(bf16[64,512]{1,0:T(8,128)(2,1)S(1)} %constant_dynamic-slice_fusion), channel_id=1, source_target_pairs={{0,3},{1,0},{2,1},{3,2},{4,7},{5,4},{6,5},{7,6},{8,11},{9,8},{10,9... | collective-permute-start | bytes 196616 | tf_op jit(solution)/shard_map/ppermute | solution.py:54
  7.8 1.4 all_to_all.18
  9.2 0.8 copy.26
  10.0 4.3 %all-to-all-start = ((bf16[64,16,88]{2,0,1:T(8,128)(2,1)}), bf16[64,16,88]{2,0,1:T(8,128)(2,1)S(1)}, u32[]{:S(2)}, u32[]{:S(2)}) async-start(bf16[64,16,88]{2,0,1:T(8,128)(2,1)} %copy.26), calls=%async_computation | async-start | bytes 524288 | tf_op jit(solution)/shard_map/all_to_all | solution.py:59
  14.3 0.8 copy.31
  15.1 0.1 reshape.234
  15.3 0.6 reduce-window.6
  15.9 0.2 slice_reduce_fusion
  16.1 2.9 %collective-permute-start.4 = (bf16[4,64,512]{2,1,0:T(8,128)(2,1)S(1)}, bf16[4,64,512]{2,1,0:T(8,128)(2,1)S(1)}, u32[]{:S(2)}, u32[]{:S(2)}) collective-permute-start(bf16[4,64,512]{2,1,0:T(8,128)(2,1)S(1)} %get-tuple-element.12), channel_id=1, source_target_pairs={{0,8},{4,12},{8,0},{12,4},{1,9},{5,13},{9,1},{13,5},{2,10},{6,14},... | collective-permute-start | bytes 786440 | tf_op jit(solution)/shard_map/ppermute | solution.py:56
  19.1 0.3 collective-permute-start.3
  19.4 2.4 %collective-permute-start.5 = (bf16[4,64,512]{2,1,0:T(8,128)(2,1)S(1)}, bf16[4,64,512]{2,1,0:T(8,128)(2,1)S(1)}, u32[]{:S(2)}, u32[]{:S(2)}) collective-permute-start(bf16[4,64,512]{2,1,0:T(8,128)(2,1)S(1)} %get-tuple-element.12), channel_id=1, source_target_pairs={{0,12},{4,0},{8,4},{12,8},{1,13},{5,1},{9,5},{13,9},{2,14},{6,2},{... | collective-permute-start | bytes 786440 | tf_op jit(solution)/shard_map/ppermute | solution.py:56
  21.8 5.3 %collective-permute-done.4 = bf16[4,64,512]{2,1,0:T(8,128)(2,1)S(1)} collective-permute-done((bf16[4,64,512]{2,1,0:T(8,128)(2,1)S(1)}, bf16[4,64,512]{2,1,0:T(8,128)(2,1)S(1)}, u32[]{:S(2)}, u32[]{:S(2)}) %collective-permute-start.4) | collective-permute-done | bytes 262176 | tf_op jit(solution)/shard_map/ppermute | solution.py:56
  27.2 6.6 %collective-permute-done.3 = bf16[4,64,512]{2,1,0:T(8,128)(2,1)S(1)} collective-permute-done((bf16[4,64,512]{2,1,0:T(8,128)(2,1)S(1)}, bf16[4,64,512]{2,1,0:T(8,128)(2,1)S(1)}, u32[]{:S(2)}, u32[]{:S(2)}) %collective-permute-start.3) | collective-permute-done | bytes 262176 | tf_op jit(solution)/shard_map/ppermute | solution.py:56
  33.8 0.1 pad_maximum_fusion.1
  33.9 0.5 collective-permute-start.6
  34.6 0.6 gather_fusion
  35.3 0.6 gather_fusion.1
  35.9 0.4 convolution_bitcast_fusion.1
  36.3 0.5 collective-permute-done.6
  36.7 0.4 convolution_bitcast_fusion
  37.1 0.2 fusion.20
  37.3 0.1 fusion.22
  37.4 0.2 broadcast_in_dim.40
  37.6 0.1 reshape.237
  37.8 0.3 convolution_convert_fusion.1
  38.1 1.1 reshape.238
  39.2 8.9 %all-to-all-start.1 = ((bf16[16,22,1024]{2,1,0:T(8,128)(2,1)}), bf16[16,22,1024]{2,1,0:T(8,128)(2,1)S(1)}, u32[]{:S(2)}, u32[]{:S(2)}) async-start(bf16[16,22,1024]{2,1,0:T(8,128)(2,1)} %reshape.238), calls=%async_computation.1 | async-start | bytes 1572864 | tf_op jit(solution)/shard_map/all_to_all | solution.py:95
  48.2 1.6 collective-permute-start.13
  49.8 0.8 collective-permute-start.12
  50.6 20.2 %all-to-all-done.1 = bf16[16,22,1024]{2,1,0:T(8,128)(2,1)S(1)} async-done(((bf16[16,22,1024]{2,1,0:T(8,128)(2,1)}), bf16[16,22,1024]{2,1,0:T(8,128)(2,1)S(1)}, u32[]{:S(2)}, u32[]{:S(2)}) %all-to-all-start.1) | async-done | bytes 720928 | tf_op jit(solution)/shard_map/all_to_all | solution.py:95
  70.8 0.2 reshape.239
  71.0 0.9 collective-permute-start.7
  71.9 1.9 collective-permute-start.9
  73.8 15.2 %collective-permute-done.7 = bf16[352,1024]{1,0:T(8,128)(2,1)S(1)} collective-permute-done((bf16[352,1024]{1,0:T(8,128)(2,1)S(1)}, bf16[352,1024]{1,0:T(8,128)(2,1)S(1)}, u32[]{:S(2)}, u32[]{:S(2)}) %collective-permute-start.7) | collective-permute-done | bytes 720928 | tf_op jit(solution)/shard_map/ppermute | solution.py:101
  89.0 0.3 collective-permute-start.8
  89.3 11.1 %collective-permute-done.11 = bf16[3,176,1024]{2,1,0:T(8,128)(2,1)} collective-permute-done((bf16[3,176,1024]{2,1,0:T(8,128)(2,1)S(1)}, bf16[3,176,1024]{2,1,0:T(8,128)(2,1)}, u32[]{:S(2)}, u32[]{:S(2)}) %collective-permute-start.11) | collective-permute-done | bytes 1081376 | tf_op jit(solution)/shard_map/ppermute | solution.py:75
  100.4 2.2 %pad_maximum_fusion = bf16[3,704,1024]{2,1,0:T(8,128)(2,1)S(1)} fusion(bf16[3,176,1024]{2,1,0:T(8,128)(2,1)} %collective-permute-done.13, bf16[3,176,1024]{2,1,0:T(8,128)(2,1)} %collective-permute-done.12, bf16[3,176,1024]{2,1,0:T(8,128)(2,1)} %collective-permute-done.11, bf16[3,176,1024]{2,1,0:T(8,128)(2,1)S(1)} %constant_dynamic-update-slice_fusion.5), kind=kLoop, calls=%fused_computation.4 | loop fusion | flops 17301504 | bytes 8650752 | tf_op jit(solution)/shard_map/concatenate | solution.py:96
  102.6 1.9 collective-permute-start.10
  104.7 7.5 %collective-permute-done.10 = bf16[176,1024]{1,0:T(8,128)(2,1)S(1)} collective-permute-done((bf16[176,1024]{1,0:T(8,128)(2,1)S(1)}, bf16[176,1024]{1,0:T(8,128)(2,1)S(1)}, u32[]{:S(2)}, u32[]{:S(2)}) %collective-permute-start.10) | collective-permute-done | bytes 360480 | tf_op jit(solution)/shard_map/ppermute | solution.py:107
  112.3 1.6 copy-done.7
  113.9 4.4 %fusion.15 = f32[1408,704]{0,1:T(8,128)} fusion(bf16[1408,1024]{1,0:T(8,128)(2,1)S(1)} %constant_dynamic-update-slice_fusion, bf16[3,704,1024]{2,1,0:T(8,128)(2,1)S(1)} %pad_maximum_fusion), kind=kOutput, calls=%fused_computation.23 | convolution fusion | flops 2030043136 | bytes 8290304 | tf_op jit(solution)/shard_map/dot_general | solution.py:20
  118.3 8.6 %convolution_convert_fusion = bf16[1408,1024]{1,0:T(8,128)(2,1)S(1)} fusion(f32[1408,704]{0,1:T(8,128)} %fusion.15, bf16[3,704,1024]{2,1,0:T(8,128)(2,1)} %copy-done.1, bf16[1408,1024]{1,0:T(8,128)(2,1)} %copy-done.7), kind=kOutput, calls=%fused_computation.14 | convolution fusion | flops 4071440384 | bytes 12615680 | tf_op jit(solution)/shard_map/dot_general | solution.py:27
  126.9 0.2 fusion.48
  127.1 3.1 %collective-permute-start.14 = (bf16[352,1024]{1,0:T(8,128)(2,1)S(1)}, bf16[352,1024]{1,0:T(8,128)(2,1)S(1)}, u32[]{:S(2)}, u32[]{:S(2)}) collective-permute-start(bf16[352,1024]{1,0:T(8,128)(2,1)S(1)} %get-tuple-element.8), channel_id=1, source_target_pairs={{0,3},{1,0},{2,1},{3,2},{4,7},{5,4},{6,5},{7,6},{8,11},{9,8},{10,9... | collective-permute-start | bytes 2162696 | tf_op jit(solution)/shard_map/ppermute | solution.py:119
  130.2 1.3 collective-permute-start.15
  131.5 14.2 %collective-permute-done.14 = bf16[352,1024]{1,0:T(8,128)(2,1)S(1)} collective-permute-done((bf16[352,1024]{1,0:T(8,128)(2,1)S(1)}, bf16[352,1024]{1,0:T(8,128)(2,1)S(1)}, u32[]{:S(2)}, u32[]{:S(2)}) %collective-permute-start.14) | collective-permute-done | bytes 720928 | tf_op jit(solution)/shard_map/ppermute | solution.py:119
  145.7 2.9 %collective-permute-done.16 = bf16[352,1024]{1,0:T(8,128)(2,1)S(1)} collective-permute-done((bf16[352,1024]{1,0:T(8,128)(2,1)S(1)}, bf16[352,1024]{1,0:T(8,128)(2,1)S(1)}, u32[]{:S(2)}, u32[]{:S(2)}) %collective-permute-start.16) | collective-permute-done | bytes 720928 | tf_op jit(solution)/shard_map/ppermute | solution.py:119
  148.6 13.3 %collective-permute-done.15 = bf16[352,1024]{1,0:T(8,128)(2,1)S(1)} collective-permute-done((bf16[352,1024]{1,0:T(8,128)(2,1)S(1)}, bf16[352,1024]{1,0:T(8,128)(2,1)S(1)}, u32[]{:S(2)}, u32[]{:S(2)}) %collective-permute-start.15) | collective-permute-done | bytes 720928 | tf_op jit(solution)/shard_map/ppermute | solution.py:119
  161.9 1.7 add_convert_fusion
  163.5 1.1 reshape.240
  164.6 10.4 %all-to-all-start.2 = ((bf16[16,22,1024]{2,1,0:T(8,128)(2,1)}), bf16[16,22,1024]{2,1,0:T(8,128)(2,1)S(1)}, u32[]{:S(2)}, u32[]{:S(2)}) async-start(bf16[16,22,1024]{2,1,0:T(8,128)(2,1)} %reshape.240), calls=%async_computation.2 | async-start | bytes 1572864 | tf_op jit(solution)/shard_map/all_to_all | solution.py:123
  175.2 0.1 reshape.259
  175.3 0.1 iota_compare_fusion.2
  175.5 0.3 fusion.49
  175.8 2.3 %gather_fusion.2 = f32[176]{0:T(256)S(1)} fusion(f32[88,16]{0,1:T(8,128)S(1)} %fusion.32, s32[176]{0:T(256)S(1)} %reshape.259), kind=kCustom, calls=%fused_computation.2 | custom fusion | bytes 2816 | tf_op jit(solution)/shard_map/jit(take_along_axis)/gather | solution.py:82
  178.1 0.1 reshape.262
  178.4 19.4 %all-to-all-done.2 = bf16[16,22,1024]{2,1,0:T(8,128)(2,1)S(1)} async-done(((bf16[16,22,1024]{2,1,0:T(8,128)(2,1)}), bf16[16,22,1024]{2,1,0:T(8,128)(2,1)S(1)}, u32[]{:S(2)}, u32[]{:S(2)}) %all-to-all-start.2) | async-done | bytes 720928 | tf_op jit(solution)/shard_map/all_to_all | solution.py:123
  197.8 0.2 reshape.272
  198.0 0.4 fusion.16
  198.3 0.1 fusion.17
  198.5 0.8 fusion.19
  (72 shorter events, 1.2 us)
Async XLA Ops:
  0.6 0.9 copy-start
  1.5 14.5 %collective-permute-start.1 = (bf16[64,512]{1,0:T(8,128)(2,1)S(1)}, bf16[64,512]{1,0:T(8,128)(2,1)S(1)}, u32[]{:S(2)}, u32[]{:S(2)}) collective-permute-start(bf16[64,512]{1,0:T(8,128)(2,1)S(1)} %constant_dynamic-slice_fusion), channel_id=1, source_target_pairs={{0,2},{1,3},{2,0},{3,1},{4,6},{5,7},{6,4},{7,5},{8,10},{9,11},{10,... | collective-permute-start | bytes 196616 | tf_op jit(solution)/shard_map/ppermute | solution.py:54
  5.1 11.0 %collective-permute-start = (bf16[64,512]{1,0:T(8,128)(2,1)S(1)}, bf16[64,512]{1,0:T(8,128)(2,1)S(1)}, u32[]{:S(2)}, u32[]{:S(2)}) collective-permute-start(bf16[64,512]{1,0:T(8,128)(2,1)S(1)} %constant_dynamic-slice_fusion), channel_id=1, source_target_pairs={{0,1},{1,2},{2,3},{3,0},{4,5},{5,6},{6,7},{7,4},{8,9},{9,10},{10,1... | collective-permute-start | bytes 196616 | tf_op jit(solution)/shard_map/ppermute | solution.py:54
  5.4 10.7 %collective-permute-start.2 = (bf16[64,512]{1,0:T(8,128)(2,1)S(1)}, bf16[64,512]{1,0:T(8,128)(2,1)S(1)}, u32[]{:S(2)}, u32[]{:S(2)}) collective-permute-start(bf16[64,512]{1,0:T(8,128)(2,1)S(1)} %constant_dynamic-slice_fusion), channel_id=1, source_target_pairs={{0,3},{1,0},{2,1},{3,2},{4,7},{5,4},{6,5},{7,6},{8,11},{9,8},{10,9... | collective-permute-start | bytes 196616 | tf_op jit(solution)/shard_map/ppermute | solution.py:54
  10.0 24.6 %all-to-all-start = ((bf16[64,16,88]{2,0,1:T(8,128)(2,1)}), bf16[64,16,88]{2,0,1:T(8,128)(2,1)S(1)}, u32[]{:S(2)}, u32[]{:S(2)}) async-start(bf16[64,16,88]{2,0,1:T(8,128)(2,1)} %copy.26), calls=%async_computation | async-start | bytes 524288 | tf_op jit(solution)/shard_map/all_to_all | solution.py:59
  16.1 11.0 %collective-permute-start.4 = (bf16[4,64,512]{2,1,0:T(8,128)(2,1)S(1)}, bf16[4,64,512]{2,1,0:T(8,128)(2,1)S(1)}, u32[]{:S(2)}, u32[]{:S(2)}) collective-permute-start(bf16[4,64,512]{2,1,0:T(8,128)(2,1)S(1)} %get-tuple-element.12), channel_id=1, source_target_pairs={{0,8},{4,12},{8,0},{12,4},{1,9},{5,13},{9,1},{13,5},{2,10},{6,14},... | collective-permute-start | bytes 786440 | tf_op jit(solution)/shard_map/ppermute | solution.py:56
  19.1 14.7 %collective-permute-start.3 = (bf16[4,64,512]{2,1,0:T(8,128)(2,1)S(1)}, bf16[4,64,512]{2,1,0:T(8,128)(2,1)S(1)}, u32[]{:S(2)}, u32[]{:S(2)}) collective-permute-start(bf16[4,64,512]{2,1,0:T(8,128)(2,1)S(1)} %get-tuple-element.12), channel_id=1, source_target_pairs={{0,4},{4,8},{8,12},{12,0},{1,5},{5,9},{9,13},{13,1},{2,6},{6,10},{... | collective-permute-start | bytes 786440 | tf_op jit(solution)/shard_map/ppermute | solution.py:56
  19.4 14.4 %collective-permute-start.5 = (bf16[4,64,512]{2,1,0:T(8,128)(2,1)S(1)}, bf16[4,64,512]{2,1,0:T(8,128)(2,1)S(1)}, u32[]{:S(2)}, u32[]{:S(2)}) collective-permute-start(bf16[4,64,512]{2,1,0:T(8,128)(2,1)S(1)} %get-tuple-element.12), channel_id=1, source_target_pairs={{0,12},{4,0},{8,4},{12,8},{1,13},{5,1},{9,5},{13,9},{2,14},{6,2},{... | collective-permute-start | bytes 786440 | tf_op jit(solution)/shard_map/ppermute | solution.py:56
  33.8 3.3 %copy-start.8 = (bf16[88,1024]{1,0:T(8,128)(2,1)S(1)}, bf16[88,1024]{1,0:T(8,128)(2,1)}, u32[]{:S(2)}) copy-start(bf16[88,1024]{1,0:T(8,128)(2,1)} %param.10) | copy-start | bytes 540676
  33.9 3.4 %copy-start.11 = (f32[1024]{0:T(1024)S(1)}, f32[1024]{0:T(1024)}, u32[]{:S(2)}) copy-start(f32[1024]{0:T(1024)} %param.13) | copy-start | bytes 12292
  33.9 2.8 %collective-permute-start.6 = (bf16[4,4,64,512]{3,2,1,0:T(8,128)(2,1)S(1)}, bf16[4,4,64,512]{3,2,1,0:T(8,128)(2,1)S(1)}, u32[]{:S(2)}, u32[]{:S(2)}) collective-permute-start(bf16[4,4,64,512]{3,2,1,0:T(8,128)(2,1)S(1)} %pad_maximum_fusion.1), channel_id=1, source_target_pairs={{0,16},{16,0},{32,48},{48,32},{64,80},{80,64},{96,112},{112,96},{1... | collective-permute-start | bytes 3145736 | tf_op jit(solution)/shard_map/ppermute | solution.py:58
  37.3 10.8 %copy-start.4 = (bf16[1,176,1024]{2,1,0:T(8,128)(2,1)S(1)}, bf16[1,176,1024]{2,1,0:T(8,128)(2,1)}, u32[]{:S(2)}) copy-start(bf16[1,176,1024]{2,1,0:T(8,128)(2,1)} %param.16) | copy-start | bytes 1081348
  37.6 10.5 %copy-start.5 = (bf16[1,176,1024]{2,1,0:T(8,128)(2,1)S(1)}, bf16[1,176,1024]{2,1,0:T(8,128)(2,1)}, u32[]{:S(2)}) copy-start(bf16[1,176,1024]{2,1,0:T(8,128)(2,1)} %param.17) | copy-start | bytes 1081348
  37.8 10.4 %copy-start.6 = (bf16[1,176,1024]{2,1,0:T(8,128)(2,1)S(1)}, bf16[1,176,1024]{2,1,0:T(8,128)(2,1)}, u32[]{:S(2)}) copy-start(bf16[1,176,1024]{2,1,0:T(8,128)(2,1)} %param.18) | copy-start | bytes 1081348
  39.2 31.6 %all-to-all-start.1 = ((bf16[16,22,1024]{2,1,0:T(8,128)(2,1)}), bf16[16,22,1024]{2,1,0:T(8,128)(2,1)S(1)}, u32[]{:S(2)}, u32[]{:S(2)}) async-start(bf16[16,22,1024]{2,1,0:T(8,128)(2,1)} %reshape.238), calls=%async_computation.1 | async-start | bytes 1572864 | tf_op jit(solution)/shard_map/all_to_all | solution.py:95
  48.2 41.1 %collective-permute-start.13 = (bf16[3,176,1024]{2,1,0:T(8,128)(2,1)S(1)}, bf16[3,176,1024]{2,1,0:T(8,128)(2,1)}, u32[]{:S(2)}, u32[]{:S(2)}) collective-permute-start(bf16[3,176,1024]{2,1,0:T(8,128)(2,1)S(1)} %constant_dynamic-update-slice_fusion.5), channel_id=1, source_target_pairs={{0,12},{4,0},{8,4},{12,8},{1,13},{5,1},{9,5},{13,9},{2,14},{6,2},{... | collective-permute-start | bytes 3244040 | tf_op jit(solution)/shard_map/ppermute | solution.py:75
  49.8 39.5 %collective-permute-start.12 = (bf16[3,176,1024]{2,1,0:T(8,128)(2,1)S(1)}, bf16[3,176,1024]{2,1,0:T(8,128)(2,1)}, u32[]{:S(2)}, u32[]{:S(2)}) collective-permute-start(bf16[3,176,1024]{2,1,0:T(8,128)(2,1)S(1)} %constant_dynamic-update-slice_fusion.5), channel_id=1, source_target_pairs={{0,8},{4,12},{8,0},{12,4},{1,9},{5,13},{9,1},{13,5},{2,10},{6,14},... | collective-permute-start | bytes 3244040 | tf_op jit(solution)/shard_map/ppermute | solution.py:75
  50.6 49.8 %collective-permute-start.11 = (bf16[3,176,1024]{2,1,0:T(8,128)(2,1)S(1)}, bf16[3,176,1024]{2,1,0:T(8,128)(2,1)}, u32[]{:S(2)}, u32[]{:S(2)}) collective-permute-start(bf16[3,176,1024]{2,1,0:T(8,128)(2,1)S(1)} %constant_dynamic-update-slice_fusion.5), channel_id=1, source_target_pairs={{0,4},{4,8},{8,12},{12,0},{1,5},{5,9},{9,13},{13,1},{2,6},{6,10},{... | collective-permute-start | bytes 3244040 | tf_op jit(solution)/shard_map/ppermute | solution.py:75
  71.0 18.0 %collective-permute-start.7 = (bf16[352,1024]{1,0:T(8,128)(2,1)S(1)}, bf16[352,1024]{1,0:T(8,128)(2,1)S(1)}, u32[]{:S(2)}, u32[]{:S(2)}) collective-permute-start(bf16[352,1024]{1,0:T(8,128)(2,1)S(1)} %reshape.239), channel_id=1, source_target_pairs={{0,1},{1,2},{2,3},{3,0},{4,5},{5,6},{6,7},{7,4},{8,9},{9,10},{10,1... | collective-permute-start | bytes 2162696 | tf_op jit(solution)/shard_map/ppermute | solution.py:101
  71.9 30.7 %collective-permute-start.9 = (bf16[352,1024]{1,0:T(8,128)(2,1)S(1)}, bf16[352,1024]{1,0:T(8,128)(2,1)S(1)}, u32[]{:S(2)}, u32[]{:S(2)}) collective-permute-start(bf16[352,1024]{1,0:T(8,128)(2,1)S(1)} %reshape.239), channel_id=1, source_target_pairs={{0,3},{1,0},{2,1},{3,2},{4,7},{5,4},{6,5},{7,6},{8,11},{9,8},{10,9... | collective-permute-start | bytes 2162696 | tf_op jit(solution)/shard_map/ppermute | solution.py:102
  89.0 15.6 %collective-permute-start.8 = (bf16[176,1024]{1,0:T(8,128)(2,1)S(1)}, bf16[176,1024]{1,0:T(8,128)(2,1)S(1)}, u32[]{:S(2)}, u32[]{:S(2)}) collective-permute-start(bf16[176,1024]{1,0:T(8,128)(2,1)S(1)} %slice.60), channel_id=1, source_target_pairs={{0,1},{1,2},{2,3},{3,0},{4,5},{5,6},{6,7},{7,4},{8,9},{9,10},{10,1... | collective-permute-start | bytes 1081352 | tf_op jit(solution)/shard_map/ppermute | solution.py:106
  102.5 9.7 %copy-start.1 = (bf16[3,704,1024]{2,1,0:T(8,128)(2,1)}, bf16[3,704,1024]{2,1,0:T(8,128)(2,1)S(1)}, u32[]{:S(2)}) copy-start(bf16[3,704,1024]{2,1,0:T(8,128)(2,1)S(1)} %pad_maximum_fusion) | copy-start | bytes 12976132
  102.6 9.6 %collective-permute-start.10 = (bf16[176,1024]{1,0:T(8,128)(2,1)S(1)}, bf16[176,1024]{1,0:T(8,128)(2,1)S(1)}, u32[]{:S(2)}, u32[]{:S(2)}) collective-permute-start(bf16[176,1024]{1,0:T(8,128)(2,1)S(1)} %slice.61), channel_id=1, source_target_pairs={{0,3},{1,0},{2,1},{3,2},{4,7},{5,4},{6,5},{7,6},{8,11},{9,8},{10,9... | collective-permute-start | bytes 1081352 | tf_op jit(solution)/shard_map/ppermute | solution.py:107
  112.3 1.7 copy-start.7
  126.9 21.7 %copy-start.2 = (bf16[1408,1024]{1,0:T(8,128)(2,1)}, bf16[1408,1024]{1,0:T(8,128)(2,1)S(1)}, u32[]{:S(2)}) copy-start(bf16[1408,1024]{1,0:T(8,128)(2,1)S(1)} %convolution_convert_fusion) | copy-start | bytes 8650756
  127.1 18.6 %collective-permute-start.14 = (bf16[352,1024]{1,0:T(8,128)(2,1)S(1)}, bf16[352,1024]{1,0:T(8,128)(2,1)S(1)}, u32[]{:S(2)}, u32[]{:S(2)}) collective-permute-start(bf16[352,1024]{1,0:T(8,128)(2,1)S(1)} %get-tuple-element.8), channel_id=1, source_target_pairs={{0,3},{1,0},{2,1},{3,2},{4,7},{5,4},{6,5},{7,6},{8,11},{9,8},{10,9... | collective-permute-start | bytes 2162696 | tf_op jit(solution)/shard_map/ppermute | solution.py:119
  130.2 18.4 %collective-permute-start.16 = (bf16[352,1024]{1,0:T(8,128)(2,1)S(1)}, bf16[352,1024]{1,0:T(8,128)(2,1)S(1)}, u32[]{:S(2)}, u32[]{:S(2)}) collective-permute-start(bf16[352,1024]{1,0:T(8,128)(2,1)S(1)} %get-tuple-element.9), channel_id=1, source_target_pairs={{0,1},{1,2},{2,3},{3,0},{4,5},{5,6},{6,7},{7,4},{8,9},{9,10},{10,1... | collective-permute-start | bytes 2162696 | tf_op jit(solution)/shard_map/ppermute | solution.py:119
  130.2 44.8 %copy-start.10 = (s32[88,2]{0,1:T(2,128)S(1)}, s32[88,2]{0,1:T(2,128)}, u32[]{:S(2)}) copy-start(s32[88,2]{0,1:T(2,128)} %param.15) | copy-start | bytes 2116
  130.2 45.3 %copy-start.9 = (f32[1024,16]{0,1:T(8,128)S(1)}, f32[1024,16]{0,1:T(8,128)}, u32[]{:S(2)}) copy-start(f32[1024,16]{0,1:T(8,128)} %param.14) | copy-start | bytes 196612
  130.2 31.6 %collective-permute-start.15 = (bf16[352,1024]{1,0:T(8,128)(2,1)S(1)}, bf16[352,1024]{1,0:T(8,128)(2,1)S(1)}, u32[]{:S(2)}, u32[]{:S(2)}) collective-permute-start(bf16[352,1024]{1,0:T(8,128)(2,1)S(1)} %get-tuple-element.10), channel_id=1, source_target_pairs={{0,2},{1,3},{2,0},{3,1},{4,6},{5,7},{6,4},{7,5},{8,10},{9,11},{10,... | collective-permute-start | bytes 2162696 | tf_op jit(solution)/shard_map/ppermute | solution.py:119
  164.6 33.1 %all-to-all-start.2 = ((bf16[16,22,1024]{2,1,0:T(8,128)(2,1)}), bf16[16,22,1024]{2,1,0:T(8,128)(2,1)S(1)}, u32[]{:S(2)}, u32[]{:S(2)}) async-start(bf16[16,22,1024]{2,1,0:T(8,128)(2,1)} %reshape.240), calls=%async_computation.2 | async-start | bytes 1572864 | tf_op jit(solution)/shard_map/all_to_all | solution.py:123
  178.1 20.4 %copy-start.12 = (f32[1024]{0:T(1024)S(1)}, f32[1024]{0:T(1024)}, u32[]{:S(2)}) copy-start(f32[1024]{0:T(1024)} %param.19) | copy-start | bytes 12292
  198.5 0.8 copy-start.3

commit v16 on v13

--- a/solution.py
+++ b/solution.py
@@ -87,11 +87,12 @@
     earlier = jnp.cumsum(onehot, axis=0) - onehot
     slot_index = jnp.sum(earlier * onehot, axis=1)
     target = flat_ids * capacity + slot_index
-    slot_iota = jnp.arange(n_expert * capacity, dtype=jnp.int32)
-    placing = (slot_iota[:, None] == target[None, :]).astype(jnp.bfloat16)
+    slot_iota = jnp.arange(n_expert * capacity, dtype=jnp.int32).reshape(n_expert, capacity)
+    placing = (slot_iota[:, :, None] == target[None, None, :]).astype(jnp.bfloat16)
     repeated = jnp.repeat(normed, 2, axis=0)
-    send_slots = jnp.dot(placing, repeated, preferred_element_type=jnp.float32).astype(jnp.bfloat16)
-    send_slots = send_slots.reshape(n_expert, capacity, width)
+    send_slots = lax.dot_general(
+        placing, repeated, (((2,), (0,)), ((), ())), preferred_element_type=jnp.float32
+    ).astype(jnp.bfloat16)
     received = lax.all_to_all(send_slots, "expert", split_axis=0, concat_axis=0, tiled=True)
     weights = jnp.concatenate(pieces, axis=1)
     gate_rows, up_rows, down_rows = weights[0], weights[1], weights[2]
@@ -122,9 +123,8 @@
     expert_sum = expert_sum.astype(jnp.bfloat16)
     expert_out = expert_sum.reshape(n_expert, capacity, width)
     returned = lax.all_to_all(expert_out, "expert", split_axis=0, concat_axis=0, tiled=True)
-    returned = returned.reshape(slot_total, width)
     per_route = lax.dot_general(
-        placing, returned, (((0,), (0,)), ((), ())), preferred_element_type=jnp.float32
+        placing, returned, (((0, 1), (0, 1)), ((), ())), preferred_element_type=jnp.float32
     )
     per_route = per_route.reshape(row_count, 2, width)
     mixed = jnp.sum(gate_weights[:, :, None] * per_route, axis=1)

time: 188 us -> 192 us (1.021)
    ppermute x1, waiting for transfers between devices: 15.2 us -> 0.01 us  [per_device(): from_below = lax.ppermute(rows_in, 'tx', shift_pairs(n_tx, 1))]
    ppermute x1, waiting for transfers between devices: 0.01 us -> 14.8 us  [per_device(): from_above = lax.ppermute(rows_in, 'tx', shift_pairs(n_tx, -1))]
    ppermute x3, waiting for transfers between devices: 26 us -> 23.2 us  [per_device(): back = lax.ppermute(partial[s - 1], 'tx', shift_pairs(n_tx, -s))]
    ppermute x3, waiting for transfers between devices: 6.37 us -> 9.1 us  [per_device(): lax.ppermute(stacked, 'ty', shift_pairs(n_ty, s))]
    all_to_all x1, starting transfers between devices: 7.04 us -> 9.5 us  [per_device(): lax.all_to_all(expert_out, 'expert', split_axis=0, concat_axis=0, tiled=T...]
  transfers between devices with their start and end apart: 20 -> 20, of which waited for: 11 -> 10; matrix products, arithmetic and copies ran while one was open for 10% -> 10% of each run, Pallas kernels for 0% -> 0%
where the time goes in v16:
time: 192 us; the launch traced here: 191 us
  waiting for transfers between devices  99.2 us (52%)
  starting transfers between devices  46.2 us (24%)
  matrix products  22.6 us (12%)
  local copies, waits for them, and re-layouts  15.2 us (8%)
  other arithmetic  7.17 us (4%)
    ppermute x3, waiting for transfers between devices, per_device(): back = lax.ppermute(partial[s - 1], 'tx', shift_pairs(n_tx, -s))  23.2 us
    all_to_all x1, waiting for transfers between devices, per_device(): lax.all_to_all(send_slots, 'expert', split_axis=0, concat_axis=0, tiled=T...  20.2 us
    all_to_all x1, waiting for transfers between devices, per_device(): lax.all_to_all(expert_out, 'expert', split_axis=0, concat_axis=0, tiled=T...  19.5 us
    ppermute x1, waiting for transfers between devices, per_device(): from_above = lax.ppermute(rows_in, 'tx', shift_pairs(n_tx, -1))  14.8 us
    dot_general x2, matrix products, expert_block(): return jnp.dot(hid, down_rows, preferred_element_type=jnp.float32)  12.9 us
    ppermute x3, waiting for transfers between devices, per_device(): lax.ppermute(near, 'ty', shift_pairs(n_ty, s))  11.9 us
    all_to_all x1, starting transfers between devices, per_device(): lax.all_to_all(expert_out, 'expert', split_axis=0, concat_axis=0, tiled=T...  9.5 us
    ppermute x3, waiting for transfers between devices, per_device(): lax.ppermute(stacked, 'ty', shift_pairs(n_ty, s))  9.1 us
  transfers between devices with their start and end apart: 20, of which 10 were waited for; matrix products, arithmetic and copies ran while one was open for 10% of the time, Pallas kernels for 0%

profile of v16, /device:TPU:1, one launch (start us, length us, event | category | flops | bytes accessed | tf_op | source)
XLA Modules:
  0.0 191.4 jit_solution(9153659847170358625)
XLA Ops:
  0.7 0.9 copy-done
  1.5 3.6 %collective-permute-start.1 = (bf16[64,512]{1,0:T(8,128)(2,1)S(1)}, bf16[64,512]{1,0:T(8,128)(2,1)S(1)}, u32[]{:S(2)}, u32[]{:S(2)}) collective-permute-start(bf16[64,512]{1,0:T(8,128)(2,1)S(1)} %constant_dynamic-slice_fusion), channel_id=1, source_target_pairs={{0,2},{1,3},{2,0},{3,1},{4,6},{5,7},{6,4},{7,5},{8,10},{9,11},{10,... | collective-permute-start | bytes 196616 | tf_op jit(solution)/shard_map/ppermute | solution.py:54
  5.1 0.3 collective-permute-start
  5.4 2.4 %collective-permute-start.2 = (bf16[64,512]{1,0:T(8,128)(2,1)S(1)}, bf16[64,512]{1,0:T(8,128)(2,1)S(1)}, u32[]{:S(2)}, u32[]{:S(2)}) collective-permute-start(bf16[64,512]{1,0:T(8,128)(2,1)S(1)} %constant_dynamic-slice_fusion), channel_id=1, source_target_pairs={{0,3},{1,0},{2,1},{3,2},{4,7},{5,4},{6,5},{7,6},{8,11},{9,8},{10,9... | collective-permute-start | bytes 196616 | tf_op jit(solution)/shard_map/ppermute | solution.py:54
  7.8 1.4 all_to_all.18
  9.2 0.8 copy.25
  10.0 4.3 %all-to-all-start = ((bf16[64,16,88]{2,0,1:T(8,128)(2,1)}), bf16[64,16,88]{2,0,1:T(8,128)(2,1)S(1)}, u32[]{:S(2)}, u32[]{:S(2)}) async-start(bf16[64,16,88]{2,0,1:T(8,128)(2,1)} %copy.25), calls=%async_computation | async-start | bytes 524288 | tf_op jit(solution)/shard_map/all_to_all | solution.py:59
  14.3 0.8 copy.31
  15.1 0.1 reshape.213
  15.3 0.6 reduce-window.6
  15.9 0.2 slice_reduce_fusion
  16.2 2.9 %collective-permute-start.4 = (bf16[4,64,512]{2,1,0:T(8,128)(2,1)S(1)}, bf16[4,64,512]{2,1,0:T(8,128)(2,1)S(1)}, u32[]{:S(2)}, u32[]{:S(2)}) collective-permute-start(bf16[4,64,512]{2,1,0:T(8,128)(2,1)S(1)} %get-tuple-element.12), channel_id=1, source_target_pairs={{0,8},{4,12},{8,0},{12,4},{1,9},{5,13},{9,1},{13,5},{2,10},{6,14},... | collective-permute-start | bytes 786440 | tf_op jit(solution)/shard_map/ppermute | solution.py:56
  19.1 0.3 collective-permute-start.3
  19.4 2.4 %collective-permute-start.5 = (bf16[4,64,512]{2,1,0:T(8,128)(2,1)S(1)}, bf16[4,64,512]{2,1,0:T(8,128)(2,1)S(1)}, u32[]{:S(2)}, u32[]{:S(2)}) collective-permute-start(bf16[4,64,512]{2,1,0:T(8,128)(2,1)S(1)} %get-tuple-element.12), channel_id=1, source_target_pairs={{0,12},{4,0},{8,4},{12,8},{1,13},{5,1},{9,5},{13,9},{2,14},{6,2},{... | collective-permute-start | bytes 786440 | tf_op jit(solution)/shard_map/ppermute | solution.py:56
  21.9 5.3 %collective-permute-done.4 = bf16[4,64,512]{2,1,0:T(8,128)(2,1)S(1)} collective-permute-done((bf16[4,64,512]{2,1,0:T(8,128)(2,1)S(1)}, bf16[4,64,512]{2,1,0:T(8,128)(2,1)S(1)}, u32[]{:S(2)}, u32[]{:S(2)}) %collective-permute-start.4) | collective-permute-done | bytes 262176 | tf_op jit(solution)/shard_map/ppermute | solution.py:56
  27.2 6.6 %collective-permute-done.3 = bf16[4,64,512]{2,1,0:T(8,128)(2,1)S(1)} collective-permute-done((bf16[4,64,512]{2,1,0:T(8,128)(2,1)S(1)}, bf16[4,64,512]{2,1,0:T(8,128)(2,1)S(1)}, u32[]{:S(2)}, u32[]{:S(2)}) %collective-permute-start.3) | collective-permute-done | bytes 262176 | tf_op jit(solution)/shard_map/ppermute | solution.py:56
  33.8 0.1 pad_maximum_fusion.1
  33.9 0.5 collective-permute-start.6
  34.6 0.6 gather_fusion
  35.3 0.6 gather_fusion.1
  35.9 0.4 convolution_bitcast_fusion.2
  36.3 0.4 collective-permute-done.6
  36.7 0.4 convolution_bitcast_fusion.1
  37.1 0.2 fusion.36
  37.3 0.1 fusion.38
  37.4 0.2 broadcast_in_dim.39
  37.6 0.1 reshape.250
  37.8 1.3 convolution_convert_fusion.1
  39.1 8.9 %all-to-all-start.1 = ((bf16[16,22,1024]{2,1,0:T(8,128)(2,1)}), bf16[16,22,1024]{2,1,0:T(8,128)(2,1)S(1)}, u32[]{:S(2)}, u32[]{:S(2)}) async-start(bf16[16,22,1024]{2,1,0:T(8,128)(2,1)} %convolution_convert_fusion.1), calls=%async_computation.1 | async-start | bytes 1572864 | tf_op jit(solution)/shard_map/all_to_all | solution.py:96
  48.1 1.6 collective-permute-start.9
  49.7 0.8 collective-permute-start.8
  50.5 20.2 %all-to-all-done.1 = bf16[16,22,1024]{2,1,0:T(8,128)(2,1)S(1)} async-done(((bf16[16,22,1024]{2,1,0:T(8,128)(2,1)}), bf16[16,22,1024]{2,1,0:T(8,128)(2,1)S(1)}, u32[]{:S(2)}, u32[]{:S(2)}) %all-to-all-start.1) | async-done | bytes 720928 | tf_op jit(solution)/shard_map/all_to_all | solution.py:96
  70.7 0.2 reshape.217
  70.9 1.9 %collective-permute-start.12 = (bf16[352,1024]{1,0:T(8,128)(2,1)S(1)}, bf16[352,1024]{1,0:T(8,128)(2,1)S(1)}, u32[]{:S(2)}, u32[]{:S(2)}) collective-permute-start(bf16[352,1024]{1,0:T(8,128)(2,1)S(1)} %reshape.217), channel_id=1, source_target_pairs={{0,3},{1,0},{2,1},{3,2},{4,7},{5,4},{6,5},{7,6},{8,11},{9,8},{10,9... | collective-permute-start | bytes 2162696 | tf_op jit(solution)/shard_map/ppermute | solution.py:103
  72.8 14.8 %collective-permute-done.12 = bf16[352,1024]{1,0:T(8,128)(2,1)S(1)} collective-permute-done((bf16[352,1024]{1,0:T(8,128)(2,1)S(1)}, bf16[352,1024]{1,0:T(8,128)(2,1)S(1)}, u32[]{:S(2)}, u32[]{:S(2)}) %collective-permute-start.12) | collective-permute-done | bytes 720928 | tf_op jit(solution)/shard_map/ppermute | solution.py:103
  87.7 3.3 %collective-permute-start.13 = (bf16[176,1024]{1,0:T(8,128)(2,1)S(1)}, bf16[176,1024]{1,0:T(8,128)(2,1)S(1)}, u32[]{:S(2)}, u32[]{:S(2)}) collective-permute-start(bf16[176,1024]{1,0:T(8,128)(2,1)S(1)} %slice.59), channel_id=1, source_target_pairs={{0,3},{1,0},{2,1},{3,2},{4,7},{5,4},{6,5},{7,6},{8,11},{9,8},{10,9... | collective-permute-start | bytes 1081352 | tf_op jit(solution)/shard_map/ppermute | solution.py:108
  91.1 9.1 %collective-permute-done.7 = bf16[3,176,1024]{2,1,0:T(8,128)(2,1)} collective-permute-done((bf16[3,176,1024]{2,1,0:T(8,128)(2,1)S(1)}, bf16[3,176,1024]{2,1,0:T(8,128)(2,1)}, u32[]{:S(2)}, u32[]{:S(2)}) %collective-permute-start.7) | collective-permute-done | bytes 1081376 | tf_op jit(solution)/shard_map/ppermute | solution.py:75
  100.2 2.2 %pad_maximum_fusion = bf16[3,704,1024]{2,1,0:T(8,128)(2,1)S(1)} fusion(bf16[3,176,1024]{2,1,0:T(8,128)(2,1)} %collective-permute-done.9, bf16[3,176,1024]{2,1,0:T(8,128)(2,1)} %collective-permute-done.8, bf16[3,176,1024]{2,1,0:T(8,128)(2,1)} %collective-permute-done.7, bf16[3,176,1024]{2,1,0:T(8,128)(2,1)S(1)} %constant_dynamic-update-slice_fusion), kind=kLoop, calls=%fused_computation.4 | loop fusion | flops 17301504 | bytes 8650752 | tf_op jit(solution)/shard_map/concatenate | solution.py:97
  102.6 1.8 copy-done.1
  104.4 1.4 copy-done.6
  105.8 3.6 %fusion.14 = f32[1056,704]{1,0:T(8,128)} fusion(bf16[1056,1024]{1,0:T(8,128)(2,1)S(1)} %constant_dynamic-update-slice_fusion.3, bf16[3,704,1024]{2,1,0:T(8,128)(2,1)S(1)} %pad_maximum_fusion), kind=kOutput, calls=%fused_computation.27 | convolution fusion | flops 1522532352 | bytes 6578176 | tf_op jit(solution)/shard_map/dot_general | solution.py:20
  109.5 8.0 %convolution_convert_fusion = bf16[1056,1024]{1,0:T(8,128)(2,1)S(1)} fusion(f32[1056,704]{1,0:T(8,128)} %fusion.14, bf16[3,704,1024]{2,1,0:T(8,128)(2,1)} %copy-done.1, bf16[1056,1024]{1,0:T(8,128)(2,1)} %copy-done.6), kind=kOutput, calls=%fused_computation.5 | convolution fusion | flops 3053580288 | bytes 10452992 | tf_op jit(solution)/shard_map/dot_general | solution.py:27
  117.5 1.4 fusion.70
  118.9 1.8 collective-permute-start.14
  120.7 1.6 collective-permute-start.15
  122.3 3.1 %fusion.17 = f32[352,704]{1,0:T(8,128)} fusion(bf16[352,1024]{1,0:T(8,128)(2,1)S(1)} %reshape.217, bf16[3,704,1024]{2,1,0:T(8,128)(2,1)} %copy-done.1), kind=kOutput, calls=%fused_computation.30 | convolution fusion | flops 507510784 | bytes 3153920 | tf_op jit(solution)/shard_map/dot_general | solution.py:23
  125.5 4.9 %convolution_convert_fusion.2 = bf16[352,1024]{1,0:T(8,128)(2,1)} fusion(bf16[3,704,1024]{2,1,0:T(8,128)(2,1)} %copy-done.1, f32[352,704]{1,0:T(8,128)} %fusion.17, bf16[352,1024]{1,0:T(8,128)(2,1)S(1)} %reshape.217), kind=kOutput, calls=%fused_computation.25 | convolution fusion | flops 1017860096 | bytes 5406720 | tf_op jit(solution)/shard_map/dot_general | solution.py:27
  130.3 6.0 %collective-permute-done.14 = bf16[352,1024]{1,0:T(8,128)(2,1)S(1)} collective-permute-done((bf16[352,1024]{1,0:T(8,128)(2,1)}, bf16[352,1024]{1,0:T(8,128)(2,1)S(1)}, u32[]{:S(2)}, u32[]{:S(2)}) %collective-permute-start.14) | collective-permute-done | bytes 720928 | tf_op jit(solution)/shard_map/ppermute | solution.py:121
  136.3 3.8 %collective-permute-done.16 = bf16[352,1024]{1,0:T(8,128)(2,1)S(1)} collective-permute-done((bf16[352,1024]{1,0:T(8,128)(2,1)}, bf16[352,1024]{1,0:T(8,128)(2,1)S(1)}, u32[]{:S(2)}, u32[]{:S(2)}) %collective-permute-start.16) | collective-permute-done | bytes 720928 | tf_op jit(solution)/shard_map/ppermute | solution.py:121
  140.2 13.3 %collective-permute-done.15 = bf16[352,1024]{1,0:T(8,128)(2,1)S(1)} collective-permute-done((bf16[352,1024]{1,0:T(8,128)(2,1)}, bf16[352,1024]{1,0:T(8,128)(2,1)S(1)}, u32[]{:S(2)}, u32[]{:S(2)}) %collective-permute-start.15) | collective-permute-done | bytes 720928 | tf_op jit(solution)/shard_map/ppermute | solution.py:121
  153.5 1.7 add_convert_fusion
  155.2 1.1 reshape.218
  156.3 9.5 %all-to-all-start.2 = ((bf16[16,22,1024]{2,1,0:T(8,128)(2,1)}), bf16[16,22,1024]{2,1,0:T(8,128)(2,1)S(1)}, u32[]{:S(2)}, u32[]{:S(2)}) async-start(bf16[16,22,1024]{2,1,0:T(8,128)(2,1)} %reshape.218), calls=%async_computation.2 | async-start | bytes 1572864 | tf_op jit(solution)/shard_map/all_to_all | solution.py:125
  165.9 0.1 reshape.237
  166.0 0.3 fusion.71
  166.4 2.3 %gather_fusion.2 = f32[176]{0:T(256)S(1)} fusion(f32[88,16]{0,1:T(8,128)S(1)} %fusion.50, s32[176]{0:T(256)S(1)} %reshape.237), kind=kCustom, calls=%fused_computation.2 | custom fusion | bytes 2816 | tf_op jit(solution)/shard_map/jit(take_along_axis)/gather | solution.py:82
  168.6 0.1 reshape.240
  168.9 0.1 copy.30
  169.0 19.5 %all-to-all-done.2 = bf16[16,22,1024]{2,1,0:T(8,128)(2,1)S(1)} async-done(((bf16[16,22,1024]{2,1,0:T(8,128)(2,1)}), bf16[16,22,1024]{2,1,0:T(8,128)(2,1)S(1)}, u32[]{:S(2)}, u32[]{:S(2)}) %all-to-all-start.2) | async-done | bytes 720928 | tf_op jit(solution)/shard_map/all_to_all | solution.py:125
  188.5 0.6 convolution_bitcast_fusion
  189.1 0.4 reshape.219
  189.5 0.9 multiply_reduce_fusion
  190.5 0.2 fusion.33
  190.6 0.8 fusion.35
  (71 shorter events, 1.1 us)
Async XLA Ops:
  0.6 0.9 copy-start
  1.5 14.5 %collective-permute-start.1 = (bf16[64,512]{1,0:T(8,128)(2,1)S(1)}, bf16[64,512]{1,0:T(8,128)(2,1)S(1)}, u32[]{:S(2)}, u32[]{:S(2)}) collective-permute-start(bf16[64,512]{1,0:T(8,128)(2,1)S(1)} %constant_dynamic-slice_fusion), channel_id=1, source_target_pairs={{0,2},{1,3},{2,0},{3,1},{4,6},{5,7},{6,4},{7,5},{8,10},{9,11},{10,... | collective-permute-start | bytes 196616 | tf_op jit(solution)/shard_map/ppermute | solution.py:54
  5.1 11.0 %collective-permute-start = (bf16[64,512]{1,0:T(8,128)(2,1)S(1)}, bf16[64,512]{1,0:T(8,128)(2,1)S(1)}, u32[]{:S(2)}, u32[]{:S(2)}) collective-permute-start(bf16[64,512]{1,0:T(8,128)(2,1)S(1)} %constant_dynamic-slice_fusion), channel_id=1, source_target_pairs={{0,1},{1,2},{2,3},{3,0},{4,5},{5,6},{6,7},{7,4},{8,9},{9,10},{10,1... | collective-permute-start | bytes 196616 | tf_op jit(solution)/shard_map/ppermute | solution.py:54
  5.4 10.7 %collective-permute-start.2 = (bf16[64,512]{1,0:T(8,128)(2,1)S(1)}, bf16[64,512]{1,0:T(8,128)(2,1)S(1)}, u32[]{:S(2)}, u32[]{:S(2)}) collective-permute-start(bf16[64,512]{1,0:T(8,128)(2,1)S(1)} %constant_dynamic-slice_fusion), channel_id=1, source_target_pairs={{0,3},{1,0},{2,1},{3,2},{4,7},{5,4},{6,5},{7,6},{8,11},{9,8},{10,9... | collective-permute-start | bytes 196616 | tf_op jit(solution)/shard_map/ppermute | solution.py:54
  10.0 24.6 %all-to-all-start = ((bf16[64,16,88]{2,0,1:T(8,128)(2,1)}), bf16[64,16,88]{2,0,1:T(8,128)(2,1)S(1)}, u32[]{:S(2)}, u32[]{:S(2)}) async-start(bf16[64,16,88]{2,0,1:T(8,128)(2,1)} %copy.25), calls=%async_computation | async-start | bytes 524288 | tf_op jit(solution)/shard_map/all_to_all | solution.py:59
  16.2 11.0 %collective-permute-start.4 = (bf16[4,64,512]{2,1,0:T(8,128)(2,1)S(1)}, bf16[4,64,512]{2,1,0:T(8,128)(2,1)S(1)}, u32[]{:S(2)}, u32[]{:S(2)}) collective-permute-start(bf16[4,64,512]{2,1,0:T(8,128)(2,1)S(1)} %get-tuple-element.12), channel_id=1, source_target_pairs={{0,8},{4,12},{8,0},{12,4},{1,9},{5,13},{9,1},{13,5},{2,10},{6,14},... | collective-permute-start | bytes 786440 | tf_op jit(solution)/shard_map/ppermute | solution.py:56
  19.1 14.7 %collective-permute-start.3 = (bf16[4,64,512]{2,1,0:T(8,128)(2,1)S(1)}, bf16[4,64,512]{2,1,0:T(8,128)(2,1)S(1)}, u32[]{:S(2)}, u32[]{:S(2)}) collective-permute-start(bf16[4,64,512]{2,1,0:T(8,128)(2,1)S(1)} %get-tuple-element.12), channel_id=1, source_target_pairs={{0,4},{4,8},{8,12},{12,0},{1,5},{5,9},{9,13},{13,1},{2,6},{6,10},{... | collective-permute-start | bytes 786440 | tf_op jit(solution)/shard_map/ppermute | solution.py:56
  19.4 14.4 %collective-permute-start.5 = (bf16[4,64,512]{2,1,0:T(8,128)(2,1)S(1)}, bf16[4,64,512]{2,1,0:T(8,128)(2,1)S(1)}, u32[]{:S(2)}, u32[]{:S(2)}) collective-permute-start(bf16[4,64,512]{2,1,0:T(8,128)(2,1)S(1)} %get-tuple-element.12), channel_id=1, source_target_pairs={{0,12},{4,0},{8,4},{12,8},{1,13},{5,1},{9,5},{13,9},{2,14},{6,2},{... | collective-permute-start | bytes 786440 | tf_op jit(solution)/shard_map/ppermute | solution.py:56
  33.9 2.8 %collective-permute-start.6 = (bf16[4,4,64,512]{3,2,1,0:T(8,128)(2,1)S(1)}, bf16[4,4,64,512]{3,2,1,0:T(8,128)(2,1)S(1)}, u32[]{:S(2)}, u32[]{:S(2)}) collective-permute-start(bf16[4,4,64,512]{3,2,1,0:T(8,128)(2,1)S(1)} %pad_maximum_fusion.1), channel_id=1, source_target_pairs={{0,16},{16,0},{32,48},{48,32},{64,80},{80,64},{96,112},{112,96},{1... | collective-permute-start | bytes 3145736 | tf_op jit(solution)/shard_map/ppermute | solution.py:58
  34.6 2.5 %copy-start.7 = (bf16[88,1024]{1,0:T(8,128)(2,1)S(1)}, bf16[88,1024]{1,0:T(8,128)(2,1)}, u32[]{:S(2)}) copy-start(bf16[88,1024]{1,0:T(8,128)(2,1)} %param.10) | copy-start | bytes 540676
  35.3 2.0 %copy-start.10 = (f32[1024]{0:T(1024)S(1)}, f32[1024]{0:T(1024)}, u32[]{:S(2)}) copy-start(f32[1024]{0:T(1024)} %param.13) | copy-start | bytes 12292
  37.3 10.7 %copy-start.3 = (bf16[1,176,1024]{2,1,0:T(8,128)(2,1)S(1)}, bf16[1,176,1024]{2,1,0:T(8,128)(2,1)}, u32[]{:S(2)}) copy-start(bf16[1,176,1024]{2,1,0:T(8,128)(2,1)} %param.16) | copy-start | bytes 1081348
  37.6 10.4 %copy-start.4 = (bf16[1,176,1024]{2,1,0:T(8,128)(2,1)S(1)}, bf16[1,176,1024]{2,1,0:T(8,128)(2,1)}, u32[]{:S(2)}) copy-start(bf16[1,176,1024]{2,1,0:T(8,128)(2,1)} %param.17) | copy-start | bytes 1081348
  37.8 10.3 %copy-start.5 = (bf16[1,176,1024]{2,1,0:T(8,128)(2,1)S(1)}, bf16[1,176,1024]{2,1,0:T(8,128)(2,1)}, u32[]{:S(2)}) copy-start(bf16[1,176,1024]{2,1,0:T(8,128)(2,1)} %param.18) | copy-start | bytes 1081348
  39.1 31.6 %all-to-all-start.1 = ((bf16[16,22,1024]{2,1,0:T(8,128)(2,1)}), bf16[16,22,1024]{2,1,0:T(8,128)(2,1)S(1)}, u32[]{:S(2)}, u32[]{:S(2)}) async-start(bf16[16,22,1024]{2,1,0:T(8,128)(2,1)} %convolution_convert_fusion.1), calls=%async_computation.1 | async-start | bytes 1572864 | tf_op jit(solution)/shard_map/all_to_all | solution.py:96
  48.1 43.0 %collective-permute-start.9 = (bf16[3,176,1024]{2,1,0:T(8,128)(2,1)S(1)}, bf16[3,176,1024]{2,1,0:T(8,128)(2,1)}, u32[]{:S(2)}, u32[]{:S(2)}) collective-permute-start(bf16[3,176,1024]{2,1,0:T(8,128)(2,1)S(1)} %constant_dynamic-update-slice_fusion), channel_id=1, source_target_pairs={{0,12},{4,0},{8,4},{12,8},{1,13},{5,1},{9,5},{13,9},{2,14},{6,2},{... | collective-permute-start | bytes 3244040 | tf_op jit(solution)/shard_map/ppermute | solution.py:75
  49.7 41.5 %collective-permute-start.8 = (bf16[3,176,1024]{2,1,0:T(8,128)(2,1)S(1)}, bf16[3,176,1024]{2,1,0:T(8,128)(2,1)}, u32[]{:S(2)}, u32[]{:S(2)}) collective-permute-start(bf16[3,176,1024]{2,1,0:T(8,128)(2,1)S(1)} %constant_dynamic-update-slice_fusion), channel_id=1, source_target_pairs={{0,8},{4,12},{8,0},{12,4},{1,9},{5,13},{9,1},{13,5},{2,10},{6,14},... | collective-permute-start | bytes 3244040 | tf_op jit(solution)/shard_map/ppermute | solution.py:75
  50.5 49.8 %collective-permute-start.7 = (bf16[3,176,1024]{2,1,0:T(8,128)(2,1)S(1)}, bf16[3,176,1024]{2,1,0:T(8,128)(2,1)}, u32[]{:S(2)}, u32[]{:S(2)}) collective-permute-start(bf16[3,176,1024]{2,1,0:T(8,128)(2,1)S(1)} %constant_dynamic-update-slice_fusion), channel_id=1, source_target_pairs={{0,4},{4,8},{8,12},{12,0},{1,5},{5,9},{9,13},{13,1},{2,6},{6,10},{... | collective-permute-start | bytes 3244040 | tf_op jit(solution)/shard_map/ppermute | solution.py:75
  70.9 16.8 %collective-permute-start.12 = (bf16[352,1024]{1,0:T(8,128)(2,1)S(1)}, bf16[352,1024]{1,0:T(8,128)(2,1)S(1)}, u32[]{:S(2)}, u32[]{:S(2)}) collective-permute-start(bf16[352,1024]{1,0:T(8,128)(2,1)S(1)} %reshape.217), channel_id=1, source_target_pairs={{0,3},{1,0},{2,1},{3,2},{4,7},{5,4},{6,5},{7,6},{8,11},{9,8},{10,9... | collective-permute-start | bytes 2162696 | tf_op jit(solution)/shard_map/ppermute | solution.py:103
  72.8 18.2 %collective-permute-start.10 = (bf16[352,1024]{1,0:T(8,128)(2,1)S(1)}, bf16[352,1024]{1,0:T(8,128)(2,1)S(1)}, u32[]{:S(2)}, u32[]{:S(2)}) collective-permute-start(bf16[352,1024]{1,0:T(8,128)(2,1)S(1)} %reshape.217), channel_id=1, source_target_pairs={{0,1},{1,2},{2,3},{3,0},{4,5},{5,6},{6,7},{7,4},{8,9},{9,10},{10,1... | collective-permute-start | bytes 2162696 | tf_op jit(solution)/shard_map/ppermute | solution.py:102
  87.7 14.9 %collective-permute-start.13 = (bf16[176,1024]{1,0:T(8,128)(2,1)S(1)}, bf16[176,1024]{1,0:T(8,128)(2,1)S(1)}, u32[]{:S(2)}, u32[]{:S(2)}) collective-permute-start(bf16[176,1024]{1,0:T(8,128)(2,1)S(1)} %slice.59), channel_id=1, source_target_pairs={{0,3},{1,0},{2,1},{3,2},{4,7},{5,4},{6,5},{7,6},{8,11},{9,8},{10,9... | collective-permute-start | bytes 1081352 | tf_op jit(solution)/shard_map/ppermute | solution.py:108
  91.0 11.5 %collective-permute-start.11 = (bf16[176,1024]{1,0:T(8,128)(2,1)S(1)}, bf16[176,1024]{1,0:T(8,128)(2,1)S(1)}, u32[]{:S(2)}, u32[]{:S(2)}) collective-permute-start(bf16[176,1024]{1,0:T(8,128)(2,1)S(1)} %slice.58), channel_id=1, source_target_pairs={{0,1},{1,2},{2,3},{3,0},{4,5},{5,6},{6,7},{7,4},{8,9},{9,10},{10,1... | collective-permute-start | bytes 1081352 | tf_op jit(solution)/shard_map/ppermute | solution.py:107
  102.4 2.0 %copy-start.1 = (bf16[3,704,1024]{2,1,0:T(8,128)(2,1)}, bf16[3,704,1024]{2,1,0:T(8,128)(2,1)S(1)}, u32[]{:S(2)}) copy-start(bf16[3,704,1024]{2,1,0:T(8,128)(2,1)S(1)} %pad_maximum_fusion) | copy-start | bytes 12976132
  104.4 1.4 copy-start.6
  118.9 17.4 %collective-permute-start.14 = (bf16[352,1024]{1,0:T(8,128)(2,1)}, bf16[352,1024]{1,0:T(8,128)(2,1)S(1)}, u32[]{:S(2)}, u32[]{:S(2)}) collective-permute-start(bf16[352,1024]{1,0:T(8,128)(2,1)} %get-tuple-element.8), channel_id=1, source_target_pairs={{0,3},{1,0},{2,1},{3,2},{4,7},{5,4},{6,5},{7,6},{8,11},{9,8},{10,9... | collective-permute-start | bytes 2162696 | tf_op jit(solution)/shard_map/ppermute | solution.py:121
  120.7 19.4 %collective-permute-start.16 = (bf16[352,1024]{1,0:T(8,128)(2,1)}, bf16[352,1024]{1,0:T(8,128)(2,1)S(1)}, u32[]{:S(2)}, u32[]{:S(2)}) collective-permute-start(bf16[352,1024]{1,0:T(8,128)(2,1)} %get-tuple-element.9), channel_id=1, source_target_pairs={{0,1},{1,2},{2,3},{3,0},{4,5},{5,6},{6,7},{7,4},{8,9},{9,10},{10,1... | collective-permute-start | bytes 2162696 | tf_op jit(solution)/shard_map/ppermute | solution.py:121
  120.7 32.8 %collective-permute-start.15 = (bf16[352,1024]{1,0:T(8,128)(2,1)}, bf16[352,1024]{1,0:T(8,128)(2,1)S(1)}, u32[]{:S(2)}, u32[]{:S(2)}) collective-permute-start(bf16[352,1024]{1,0:T(8,128)(2,1)} %get-tuple-element.10), channel_id=1, source_target_pairs={{0,2},{1,3},{2,0},{3,1},{4,6},{5,7},{6,4},{7,5},{8,10},{9,11},{10,... | collective-permute-start | bytes 2162696 | tf_op jit(solution)/shard_map/ppermute | solution.py:121
  155.2 10.6 %copy-start.9 = (s32[88,2]{0,1:T(2,128)S(1)}, s32[88,2]{0,1:T(2,128)}, u32[]{:S(2)}) copy-start(s32[88,2]{0,1:T(2,128)} %param.15) | copy-start | bytes 2116
  155.2 10.9 %copy-start.8 = (f32[1024,16]{0,1:T(8,128)S(1)}, f32[1024,16]{0,1:T(8,128)}, u32[]{:S(2)}) copy-start(f32[1024,16]{0,1:T(8,128)} %param.14) | copy-start | bytes 196612
  156.3 32.2 %all-to-all-start.2 = ((bf16[16,22,1024]{2,1,0:T(8,128)(2,1)}), bf16[16,22,1024]{2,1,0:T(8,128)(2,1)S(1)}, u32[]{:S(2)}, u32[]{:S(2)}) async-start(bf16[16,22,1024]{2,1,0:T(8,128)(2,1)} %reshape.218), calls=%async_computation.2 | async-start | bytes 1572864 | tf_op jit(solution)/shard_map/all_to_all | solution.py:125
  189.1 1.6 copy-start.11
  190.6 0.8 copy-start.2
